TPU v7x, 256 devices: a whole 4x4x8 slice. The times are simulated.
256 devices in a mesh: embed: 8 (over x, core), hidden: 32 (over y, z).
Axes of the slice: x: 4, y: 4, z: 8, core: 2. Of those that a mesh axis runs over, the one named last changes fastest.
Arguments:
- rows_in: bfloat16 [512, 16384], P('hidden', 'embed'), may hold values from -6 to 6
- gate_weight: bfloat16 [16384, 28672], P('embed', 'hidden'), may hold values from -0.046875 to 0.046875
- up_weight: bfloat16 [16384, 28672], P('embed', 'hidden'), may hold values from -0.046875 to 0.046875
- down_weight: bfloat16 [28672, 16384], P('hidden', 'embed'), may hold values from -0.03125 to 0.03125
Outputs:
- rows_out: bfloat16 [512, 16384], P('hidden', 'embed')
All inputs are finite; a program needn't handle non-finite values.
Results may differ from a plain program's by a relative error of at most 0.0049.
Values may be sent and summed in bfloat16 or wider, within the bound.
No kernel may reach another device: no remote copies, remote signals or barrier semaphores. Data moves between devices by JAX's collectives and lax.ppermute only.
A program may use at most 64 MiB of HBM per device.

v0:
```python
import jax
import jax.numpy as jnp
from jax import lax
from jax.sharding import PartitionSpec as P


def on_device(rows_in, gate_weight, up_weight, down_weight):
    width = gate_weight.shape[1]
    piece = lax.all_gather(rows_in, "hidden", axis=0, tiled=True)
    gate_part = jnp.dot(piece, gate_weight, preferred_element_type=jnp.float32)
    up_part = jnp.dot(piece, up_weight, preferred_element_type=jnp.float32)
    partial_value = jnp.concatenate([gate_part, up_part], axis=1)
    summed = lax.psum(partial_value, "embed")
    activated = (jax.nn.silu(summed[:, :width]) * summed[:, width:]).astype(jnp.bfloat16)
    totals = lax.psum_scatter(
        jnp.dot(activated, down_weight, preferred_element_type=jnp.float32),
        "hidden",
        scatter_dimension=0,
        tiled=True,
    )
    return totals.astype(jnp.bfloat16)


def solution(mesh):
    placed = (
        P("hidden", "embed"),
        P("embed", "hidden"),
        P("embed", "hidden"),
        P("hidden", "embed"),
    )
    return jax.shard_map(
        on_device, mesh=mesh, in_specs=placed, out_specs=P("hidden", "embed"), check_vma=False
    )
```

profile of v0, /device:TPU:2, one launch (start us, length us, event | category | flops | bytes accessed | tf_op | source)
XLA Modules:
  0.0 410.9 jit_solution(4857531397653067271)
XLA Ops:
  6.5 0.0 all-gather.2.cloned.1.call-start
  6.5 0.7 all-gather.2.cloned.1.call-update
  7.3 0.0 all-reduce.2.cloned.1.call-start
  7.3 83.6 %all-gather.2.cloned.1.call-done = bf16[512,2048]{1,0:T(8,128)(2,1)} async-done(((bf16[16,2048]{1,0:T(8,128)(2,1)}), bf16[512,2048]{1,0:T(8,128)(2,1)}) %all-gather.2.cloned.1.call-update) | async-done | bytes 2097168 | tf_op jit(solution)/shard_map/all_gather | solution.py:9
  90.9 0.0 copy-start
  90.9 0.0 copy-start.1
  90.9 5.1 %fusion.6 = f32[512,896]{1,0:T(8,128)S(1)} fusion(bf16[512,2048]{1,0:T(8,128)(2,1)} %all-gather.2.cloned.1.call-done, bf16[2048,896]{1,0:T(8,128)(2,1)} %param.6), kind=kOutput, calls=%fused_computation.7 | convolution fusion | flops 1879048192 | bytes 7602176 | tf_op jit(solution)/shard_map/dot_general | solution.py:11
  96.0 0.0 copy-done
  96.0 0.0 copy-done.1
  96.0 2.3 fusion.5
  98.4 2.1 pad_maximum_fusion
  100.4 0.0 all-reduce.2.cloned.1.call-update
  100.4 0.0 reduce-scatter.2.cloned.1.call-start
  100.5 70.7 %all-reduce.2.cloned.1.call-done = f32[512,1792]{1,0:T(8,128)} async-done(((f32[512,1792]{1,0:T(8,128)}), f32[512,1792]{1,0:T(8,128)}) %all-reduce.2.cloned.1.call-update) | async-done | bytes 3670032 | tf_op jit(solution)/shard_map/psum | solution.py:13
  171.2 7.4 %fusion.1 = f32[512,2048]{1,0:T(8,128)} fusion(bf16[896,2048]{1,0:T(8,128)(2,1)} %param.7, f32[512,1792]{1,0:T(8,128)} %all-reduce.2.cloned.1.call-done), kind=kOutput, calls=%fused_computation.3 | convolution fusion | flops 1881800704 | bytes 11534336 | tf_op jit(solution)/shard_map/dot_general | solution.py:16
  178.6 0.0 reduce-scatter.2.cloned.1.call-update
  178.7 224.2 %reduce-scatter.2.cloned.1.call-done = f32[16,2048]{1,0:T(8,128)} async-done(((f32[512,2048]{1,0:T(8,128)}), f32[16,2048]{1,0:T(8,128)}) %reduce-scatter.2.cloned.1.call-update) | async-done | bytes 131088 | tf_op jit(solution)/shard_map/reduce_scatter | solution.py:15
  402.9 1.5 convert_element_type.7
Async XLA Ops:
  6.5 84.3 %all-gather.2.cloned.1.call-start = ((), (), s32[]{:S(2)}) async-start(), calls=%async_computation.1 | async-start | bytes 2162688 | tf_op jit(solution)/shard_map/all_gather | solution.py:9
  7.3 163.9 %all-reduce.2.cloned.1.call-start = ((), (), s32[]{:S(2)}) async-start(), calls=%async_computation.2 | async-start | bytes 7340032 | tf_op jit(solution)/shard_map/psum | solution.py:13
  90.9 5.2 %copy-start = (bf16[2048,896]{1,0:T(8,128)(2,1)S(1)}, bf16[2048,896]{1,0:T(8,128)(2,1)}, u32[]{:S(2)}) copy-start(bf16[2048,896]{1,0:T(8,128)(2,1)} %param.5) | copy-start | bytes 11010052
  90.9 5.2 %copy-start.1 = (bf16[512,2048]{1,0:T(8,128)(2,1)S(1)}, bf16[512,2048]{1,0:T(8,128)(2,1)}, u32[]{:S(2)}) copy-start(bf16[512,2048]{1,0:T(8,128)(2,1)} %all-gather.2.cloned.1.call-done) | copy-start | bytes 6291460
  100.4 302.4 %reduce-scatter.2.cloned.1.call-start = ((), (), s32[]{:S(2)}) async-start(), calls=%async_computation.3 | async-start | bytes 4325376 | tf_op jit(solution)/shard_map/reduce_scatter | solution.py:15
Sparse Core Ops, SparseCore 0:
  9.9 80.8 all-gather.1
  100.6 70.5 all-reduce.1
  178.8 224.0 reduce-scatter.1
where the time goes:
time: 411 us
  waiting for transfers between devices  379 us (92%)
  matrix products  14.9 us (4%)
  between operations  13.1 us (3%)
    reduce_scatter x1, waiting for transfers between devices, on_device(): lax.psum_scatter(jnp.dot(activated, down_weight, preferred_element_type=j...  224 us
    all_gather x1, waiting for transfers between devices, on_device(): piece = lax.all_gather(rows_in, 'hidden', axis=0, tiled=True)  83.6 us
    psum x1, waiting for transfers between devices, on_device(): summed = lax.psum(partial_value, 'embed')  70.7 us
  transfers between devices with their start and end apart: 3, of which 3 were waited for; matrix products, arithmetic and copies ran while one was open for 0% of the time, Pallas kernels for 0%

commit v1 on v0

v1 whole, which is shorter than its diff:
```python
import jax
import jax.numpy as jnp
from jax import lax
from jax.sharding import Mesh, PartitionSpec as P


def on_device(rows_in, gate_weight, up_weight, down_weight):
    width = gate_weight.shape[1]
    piece = lax.all_gather(rows_in, "hz", axis=0, tiled=True)
    piece = lax.all_gather(piece, "hy", axis=0, tiled=True)
    gate_part = jnp.dot(piece, gate_weight, preferred_element_type=jnp.float32)
    up_part = jnp.dot(piece, up_weight, preferred_element_type=jnp.float32)
    partial_value = jnp.concatenate([gate_part, up_part], axis=1)
    summed = lax.psum_scatter(partial_value, "embed", scatter_dimension=0, tiled=True)
    activated = (jax.nn.silu(summed[:, :width]) * summed[:, width:]).astype(jnp.bfloat16)
    activated = lax.all_gather(activated, "embed", axis=0, tiled=True)
    partial_out = jnp.dot(activated, down_weight, preferred_element_type=jnp.float32)
    totals = lax.psum_scatter(partial_out, "hy", scatter_dimension=0, tiled=True)
    totals = lax.psum_scatter(totals, "hz", scatter_dimension=0, tiled=True)
    return totals.astype(jnp.bfloat16)


def solution(mesh):
    embed, hidden = mesh.shape["embed"], mesh.shape["hidden"]
    ny = {d.coords[1] for d in mesh.devices.flat}
    ny = len(ny)
    sub = Mesh(mesh.devices.reshape(embed, ny, hidden // ny), ("embed", "hy", "hz"))
    rows = P(("hy", "hz"), "embed")
    weights = P("embed", ("hy", "hz"))
    placed = (rows, weights, weights, P(("hy", "hz"), "embed"))
    return jax.shard_map(
        on_device, mesh=sub, in_specs=placed, out_specs=rows, check_vma=False
    )
```

time: 411 us -> 240 us (0.58)
  waiting for transfers between devices: 379 us -> 161 us
  blocking collectives: 0 us -> 46.2 us
    reduce_scatter x1 -> x3, waiting for transfers between devices: 224 us -> 128 us  [the longest x1 51.3 us: on_device(): lax.psum_scatter(partial_out, 'hy', scatter_dimension=0, tiled=True)]
    psum x1 -> x0, waiting for transfers between devices: 70.7 us -> none  [on_device(): summed = lax.psum(partial_value, 'embed')]
    all_gather x1, waiting for transfers between devices: 83.6 us -> 33.1 us  [on_device(): piece = lax.all_gather(piece, 'hy', axis=0, tiled=True)]
    all_gather x0 -> x2, blocking collectives: none -> 46.2 us  [the longest x1 31.1 us: on_device(): piece = lax.all_gather(rows_in, 'hz', axis=0, tiled=True)]
  transfers between devices with their start and end apart: 3 -> 4, of which waited for: 3 -> 4; matrix products, arithmetic and copies ran while one was open for 0% -> 0% of each run, Pallas kernels for 0% -> 0%
where the time goes in v1:
time: 240 us; the launch traced here: 239 us
  waiting for transfers between devices  161 us (67%)
  blocking collectives  46.2 us (19%)
  matrix products  13.8 us (6%)
  between operations  13.2 us (6%)
  other arithmetic  4.72 us (2%)
    reduce_scatter x1, waiting for transfers between devices, on_device(): lax.psum_scatter(partial_out, 'hy', scatter_dimension=0, tiled=True)  51.3 us
    reduce_scatter x1, waiting for transfers between devices, on_device(): totals = lax.psum_scatter(totals, 'hz', scatter_dimension=0, tiled=True)  40.9 us
    reduce_scatter x1, waiting for transfers between devices, on_device(): lax.psum_scatter(partial_value, 'embed', scatter_dimension=0, tiled=True)  36.1 us
    all_gather x1, waiting for transfers between devices, on_device(): piece = lax.all_gather(piece, 'hy', axis=0, tiled=True)  33.1 us
    all_gather x1, blocking collectives, on_device(): piece = lax.all_gather(rows_in, 'hz', axis=0, tiled=True)  31.1 us
    all_gather x1, blocking collectives, on_device(): activated = lax.all_gather(activated, 'embed', axis=0, tiled=True)  15.1 us
    dot_general x1, matrix products, on_device(): jnp.dot(activated, down_weight, preferred_element_type=jnp.float32)  6.35 us
    dot_general x1, matrix products, on_device(): up_part = jnp.dot(piece, up_weight, preferred_element_type=jnp.float32)  5.14 us
  transfers between devices with their start and end apart: 4, of which 4 were waited for; matrix products, arithmetic and copies ran while one was open for 0% of the time, Pallas kernels for 0%

profile of v1, /device:TPU:2, one launch (start us, length us, event | category | flops | bytes accessed | tf_op | source)
XLA Modules:
  0.0 239.4 jit_solution(16744164856222922656)
XLA Ops:
  6.5 0.0 all-gather.2.cloned.1.call-start
  6.5 31.1 %all_gather.9 = bf16[128,2048]{1,0:T(8,128)(2,1)} all-gather(bf16[16,2048]{1,0:T(8,128)(2,1)} %param.4), channel_id=1, replica_groups=mesh['embed'=8,'hy'=4,'hz'=8] {'hz'}, dimensions={0}, use_global_device_ids=true | all-gather | bytes 589824 | tf_op jit(solution)/shard_map/all_gather | solution.py:9
  37.6 0.0 all-gather.2.cloned.1.call-update
  37.7 0.0 reduce-scatter.4.cloned.1.call-start
  37.7 33.1 %all-gather.2.cloned.1.call-done = bf16[512,2048]{1,0:T(8,128)(2,1)} async-done(((bf16[128,2048]{1,0:T(8,128)(2,1)}), bf16[512,2048]{1,0:T(8,128)(2,1)}) %all-gather.2.cloned.1.call-update) | async-done | bytes 2097168 | tf_op jit(solution)/shard_map/all_gather | solution.py:10
  70.8 0.0 copy-start
  70.8 0.0 copy-start.1
  70.8 5.1 %fusion.2 = f32[512,896]{1,0:T(8,128)S(1)} fusion(bf16[512,2048]{1,0:T(8,128)(2,1)} %all-gather.2.cloned.1.call-done, bf16[2048,896]{1,0:T(8,128)(2,1)} %param.6), kind=kOutput, calls=%fused_computation.4 | convolution fusion | flops 1879048192 | bytes 7602176 | tf_op jit(solution)/shard_map/dot_general | solution.py:12
  75.9 0.0 copy-done
  75.9 0.0 copy-done.1
  76.0 2.3 fusion.1
  78.3 2.1 pad_maximum_fusion
  80.3 0.0 reduce-scatter.4.cloned.1.call-update
  80.4 0.0 reduce-scatter.6.cloned.1.call-start
  80.4 36.1 %reduce-scatter.4.cloned.1.call-done = f32[64,1792]{1,0:T(8,128)} async-done(((f32[512,1792]{1,0:T(8,128)}), f32[64,1792]{1,0:T(8,128)}) %reduce-scatter.4.cloned.1.call-update) | async-done | bytes 458768 | tf_op jit(solution)/shard_map/reduce_scatter | solution.py:14
  116.5 1.1 fusion
  117.6 15.1 %all_gather.11 = bf16[512,896]{1,0:T(8,128)(2,1)S(1)} all-gather(bf16[64,896]{1,0:T(8,128)(2,1)S(1)} %fusion), channel_id=1, replica_groups=mesh['embed'=8,'hy'=4,'hz'=8] {'embed'}, dimensions={0}, use_global_device_ids=true | all-gather | bytes 1032192 | tf_op jit(solution)/shard_map/all_gather | solution.py:16
  132.7 6.3 %fusion.3 = f32[512,2048]{1,0:T(8,128)} fusion(bf16[512,896]{1,0:T(8,128)(2,1)S(1)} %all_gather.11, bf16[896,2048]{1,0:T(8,128)(2,1)} %param.7), kind=kOutput, calls=%fused_computation.5 | convolution fusion | flops 1879048192 | bytes 8781824 | tf_op jit(solution)/shard_map/dot_general | solution.py:17
  139.0 0.0 reduce-scatter.6.cloned.1.call-update
  139.1 0.0 reduce-scatter.8.cloned.1.call-start
  139.1 51.3 %reduce-scatter.6.cloned.1.call-done = f32[128,2048]{1,0:T(8,128)} async-done(((f32[512,2048]{1,0:T(8,128)}), f32[128,2048]{1,0:T(8,128)}) %reduce-scatter.6.cloned.1.call-update) | async-done | bytes 1048592 | tf_op jit(solution)/shard_map/reduce_scatter | solution.py:18
  190.4 0.0 reduce-scatter.8.cloned.1.call-update
  190.4 40.9 %reduce-scatter.8.cloned.1.call-done = f32[16,2048]{1,0:T(8,128)} async-done(((f32[128,2048]{1,0:T(8,128)}), f32[16,2048]{1,0:T(8,128)}) %reduce-scatter.8.cloned.1.call-update) | async-done | bytes 131088 | tf_op jit(solution)/shard_map/reduce_scatter | solution.py:19
  231.4 1.5 convert_element_type.7
Async XLA Ops:
  6.5 64.2 %all-gather.2.cloned.1.call-start = ((), (), s32[]{:S(2)}) async-start(), calls=%async_computation.3 | async-start | bytes 2621440 | tf_op jit(solution)/shard_map/all_gather | solution.py:10
  37.7 78.9 %reduce-scatter.4.cloned.1.call-start = ((), (), s32[]{:S(2)}) async-start(), calls=%async_computation.4 | async-start | bytes 4128768 | tf_op jit(solution)/shard_map/reduce_scatter | solution.py:14
  70.8 5.2 %copy-start = (bf16[2048,896]{1,0:T(8,128)(2,1)S(1)}, bf16[2048,896]{1,0:T(8,128)(2,1)}, u32[]{:S(2)}) copy-start(bf16[2048,896]{1,0:T(8,128)(2,1)} %param.5) | copy-start | bytes 11010052
  70.8 5.2 %copy-start.1 = (bf16[512,2048]{1,0:T(8,128)(2,1)S(1)}, bf16[512,2048]{1,0:T(8,128)(2,1)}, u32[]{:S(2)}) copy-start(bf16[512,2048]{1,0:T(8,128)(2,1)} %all-gather.2.cloned.1.call-done) | copy-start | bytes 6291460
  80.4 110.0 %reduce-scatter.6.cloned.1.call-start = ((), (), s32[]{:S(2)}) async-start(), calls=%async_computation.5 | async-start | bytes 5242880 | tf_op jit(solution)/shard_map/reduce_scatter | solution.py:18
  139.1 92.3 %reduce-scatter.8.cloned.1.call-start = ((), (), s32[]{:S(2)}) async-start(), calls=%async_computation.6 | async-start | bytes 1179648 | tf_op jit(solution)/shard_map/reduce_scatter | solution.py:19
Sparse Core Ops, SparseCore 0:
  37.8 32.9 all-gather.1
  80.5 35.9 reduce-scatter.3
  139.2 51.1 reduce-scatter.5
  192.9 38.3 reduce-scatter.7

commit v2 on v1

--- a/solution.py
+++ b/solution.py
@@ -15,8 +15,12 @@
     activated = (jax.nn.silu(summed[:, :width]) * summed[:, width:]).astype(jnp.bfloat16)
     activated = lax.all_gather(activated, "embed", axis=0, tiled=True)
     partial_out = jnp.dot(activated, down_weight, preferred_element_type=jnp.float32)
-    totals = lax.psum_scatter(partial_out, "hy", scatter_dimension=0, tiled=True)
-    totals = lax.psum_scatter(totals, "hz", scatter_dimension=0, tiled=True)
+    owners = lax.psum(1, ("hy", "hz"))
+    pieces = partial_out.astype(jnp.bfloat16).reshape(
+        (owners, partial_out.shape[0] // owners) + partial_out.shape[1:]
+    )
+    pieces = lax.all_to_all(pieces, ("hy", "hz"), 0, 0, tiled=True)
+    totals = pieces.astype(jnp.float32).sum(axis=0)
     return totals.astype(jnp.bfloat16)
 
 

time: 240 us -> 208 us (0.87)
  waiting for transfers between devices: 161 us -> 69.3 us
  blocking collectives: 46.2 us -> 107 us
    reduce_scatter x2 -> x0, waiting for transfers between devices: 92.2 us -> none  [the longest x1 51.3 us: on_device(): lax.psum_scatter(partial_out, 'hy', scatter_dimension=0, tiled=True)]
    all_to_all x0 -> x1, blocking collectives: none -> 61.2 us  [on_device(): pieces = lax.all_to_all(pieces, ('hy', 'hz'), 0, 0, tiled=True)]
  transfers between devices with their start and end apart: 4 -> 2, of which waited for: 4 -> 2; matrix products, arithmetic and copies ran while one was open for 0% -> 0% of each run, Pallas kernels for 0% -> 0%
where the time goes in v2:
time: 208 us; the launch traced here: 206 us
  blocking collectives  107 us (51%)
  waiting for transfers between devices  69.3 us (33%)
  between operations  13.4 us (6%)
  matrix products  11.9 us (6%)
  other arithmetic  4.13 us (2%)
    all_to_all x1, blocking collectives, on_device(): pieces = lax.all_to_all(pieces, ('hy', 'hz'), 0, 0, tiled=True)  61.2 us
    reduce_scatter x1, waiting for transfers between devices, on_device(): lax.psum_scatter(partial_value, 'embed', scatter_dimension=0, tiled=True)  36.1 us
    all_gather x1, waiting for transfers between devices, on_device(): piece = lax.all_gather(piece, 'hy', axis=0, tiled=True)  33.1 us
    all_gather x1, blocking collectives, on_device(): piece = lax.all_gather(rows_in, 'hz', axis=0, tiled=True)  31.1 us
    all_gather x1, blocking collectives, on_device(): activated = lax.all_gather(activated, 'embed', axis=0, tiled=True)  15.1 us
    dot_general x1, matrix products, on_device(): up_part = jnp.dot(piece, up_weight, preferred_element_type=jnp.float32)  5.14 us
    dot_general x1, matrix products, on_device(): jnp.dot(activated, down_weight, preferred_element_type=jnp.float32)  4.41 us
  transfers between devices with their start and end apart: 2, of which 2 were waited for; matrix products, arithmetic and copies ran while one was open for 0% of the time, Pallas kernels for 0%

profile of v2, /device:TPU:2, one launch (start us, length us, event | category | flops | bytes accessed | tf_op | source)
XLA Modules:
  0.0 206.1 jit_solution(9789712087665487801)
XLA Ops:
  6.5 0.0 all-gather.2.cloned.1.call-start
  6.5 31.1 %all_gather.9 = bf16[128,2048]{1,0:T(8,128)(2,1)} all-gather(bf16[16,2048]{1,0:T(8,128)(2,1)} %param.4), channel_id=1, replica_groups=mesh['embed'=8,'hy'=4,'hz'=8] {'hz'}, dimensions={0}, use_global_device_ids=true | all-gather | bytes 589824 | tf_op jit(solution)/shard_map/all_gather | solution.py:9
  37.6 0.0 all-gather.2.cloned.1.call-update
  37.7 0.0 reduce-scatter.2.cloned.1.call-start
  37.7 33.1 %all-gather.2.cloned.1.call-done = bf16[512,2048]{1,0:T(8,128)(2,1)} async-done(((bf16[128,2048]{1,0:T(8,128)(2,1)}), bf16[512,2048]{1,0:T(8,128)(2,1)}) %all-gather.2.cloned.1.call-update) | async-done | bytes 2097168 | tf_op jit(solution)/shard_map/all_gather | solution.py:10
  70.8 0.0 copy-start
  70.8 0.0 copy-start.1
  70.8 5.1 %fusion.2 = f32[512,896]{1,0:T(8,128)S(1)} fusion(bf16[512,2048]{1,0:T(8,128)(2,1)} %all-gather.2.cloned.1.call-done, bf16[2048,896]{1,0:T(8,128)(2,1)} %param.6), kind=kOutput, calls=%fused_computation.5 | convolution fusion | flops 1879048192 | bytes 7602176 | tf_op jit(solution)/shard_map/dot_general | solution.py:12
  75.9 0.0 copy-done
  75.9 0.0 copy-done.1
  76.0 2.3 %fusion.1 = f32[512,896]{1,0:T(8,128)S(1)} fusion(bf16[512,2048]{1,0:T(8,128)(2,1)S(1)} %copy-done.1, bf16[2048,896]{1,0:T(8,128)(2,1)S(1)} %copy-done), kind=kOutput, calls=%fused_computation.4 | convolution fusion | flops 1879048192 | bytes 7602176 | tf_op jit(solution)/shard_map/dot_general | solution.py:11
  78.3 2.1 pad_maximum_fusion
  80.3 0.0 reduce-scatter.2.cloned.1.call-update
  80.4 36.1 %reduce-scatter.2.cloned.1.call-done = f32[64,1792]{1,0:T(8,128)} async-done(((f32[512,1792]{1,0:T(8,128)}), f32[64,1792]{1,0:T(8,128)}) %reduce-scatter.2.cloned.1.call-update) | async-done | bytes 458768 | tf_op jit(solution)/shard_map/reduce_scatter | solution.py:14
  116.5 1.1 fusion
  117.6 15.1 %all_gather.11 = bf16[512,896]{1,0:T(8,128)(2,1)S(1)} all-gather(bf16[64,896]{1,0:T(8,128)(2,1)S(1)} %fusion), channel_id=1, replica_groups=mesh['embed'=8,'hy'=4,'hz'=8] {'embed'}, dimensions={0}, use_global_device_ids=true | all-gather | bytes 1032192 | tf_op jit(solution)/shard_map/all_gather | solution.py:16
  132.7 4.4 %convolution_convert_fusion = bf16[512,2048]{1,0:T(8,128)(2,1)S(1)} fusion(bf16[512,896]{1,0:T(8,128)(2,1)S(1)} %all_gather.11, bf16[896,2048]{1,0:T(8,128)(2,1)} %param.7), kind=kOutput, calls=%fused_computation.1 | convolution fusion | flops 1880096768 | bytes 6684672 | tf_op jit(solution)/shard_map/dot_general | solution.py:17
  137.1 61.2 %all_to_all.5 = bf16[32,16,2048]{2,1,0:T(8,128)(2,1)S(1)} all-to-all(bf16[32,16,2048]{2,1,0:T(8,128)(2,1)S(1)} %bitcast.7), channel_id=1, replica_groups=mesh['embed'=8,'hy'=4,'hz'=8] {'hy','hz'}, dimensions={0} | all-to-all | bytes 4194304 | tf_op jit(solution)/shard_map/all_to_all | solution.py:22
  198.3 0.9 reduce_sum.12
Async XLA Ops:
  6.5 64.2 %all-gather.2.cloned.1.call-start = ((), (), s32[]{:S(2)}) async-start(), calls=%async_computation.2 | async-start | bytes 2621440 | tf_op jit(solution)/shard_map/all_gather | solution.py:10
  37.7 78.9 %reduce-scatter.2.cloned.1.call-start = ((), (), s32[]{:S(2)}) async-start(), calls=%async_computation.3 | async-start | bytes 4128768 | tf_op jit(solution)/shard_map/reduce_scatter | solution.py:14
  70.8 5.2 %copy-start = (bf16[2048,896]{1,0:T(8,128)(2,1)S(1)}, bf16[2048,896]{1,0:T(8,128)(2,1)}, u32[]{:S(2)}) copy-start(bf16[2048,896]{1,0:T(8,128)(2,1)} %param.5) | copy-start | bytes 11010052
  70.8 5.2 %copy-start.1 = (bf16[512,2048]{1,0:T(8,128)(2,1)S(1)}, bf16[512,2048]{1,0:T(8,128)(2,1)}, u32[]{:S(2)}) copy-start(bf16[512,2048]{1,0:T(8,128)(2,1)} %all-gather.2.cloned.1.call-done) | copy-start | bytes 6291460
Sparse Core Ops, SparseCore 0:
  37.8 32.9 all-gather.1
  80.5 35.9 reduce-scatter.1

commit v3 on v2

--- a/solution.py
+++ b/solution.py
@@ -6,8 +6,11 @@
 
 def on_device(rows_in, gate_weight, up_weight, down_weight):
     width = gate_weight.shape[1]
-    piece = lax.all_gather(rows_in, "hz", axis=0, tiled=True)
-    piece = lax.all_gather(piece, "hy", axis=0, tiled=True)
+    piece = lax.all_gather(rows_in, "hy", axis=0, tiled=True)
+    piece = lax.all_gather(piece, "hz", axis=0, tiled=True)
+    piece = piece.reshape((-1, rows_in.shape[0]) + piece.shape[1:])
+    piece = piece.reshape((lax.psum(1, "hz"), lax.psum(1, "hy")) + piece.shape[1:])
+    piece = jnp.swapaxes(piece, 0, 1).reshape((-1,) + rows_in.shape[1:])
     gate_part = jnp.dot(piece, gate_weight, preferred_element_type=jnp.float32)
     up_part = jnp.dot(piece, up_weight, preferred_element_type=jnp.float32)
     partial_value = jnp.concatenate([gate_part, up_part], axis=1)

time: 208 us -> 199 us (0.957)
  blocking collectives: 107 us -> 90.6 us
  waiting for transfers between devices: 69.3 us -> 77.5 us
  matrix products: 11.9 us -> 9.07 us
  local copies, waits for them, and re-layouts: 0.01 us -> 2.67 us
    all_gather x1, blocking collectives: 31.1 us -> 14.4 us  [on_device(): piece = lax.all_gather(rows_in, 'hy', axis=0, tiled=True)]
    all_gather x1, waiting for transfers between devices: 33.1 us -> 42.7 us  [on_device(): piece = lax.all_gather(piece, 'hz', axis=0, tiled=True)]
    dot_general x1, matrix products: 5.14 us -> 2.33 us  [on_device(): up_part = jnp.dot(piece, up_weight, preferred_element_type=jnp.float32)]
where the time goes in v3:
time: 199 us; the launch traced here: 197 us
  blocking collectives  90.6 us (46%)
  waiting for transfers between devices  77.5 us (39%)
  between operations  13.4 us (7%)
  matrix products  9.07 us (5%)
  other arithmetic  4.13 us (2%)
  local copies, waits for them, and re-layouts  2.67 us (1%)
    all_to_all x1, blocking collectives, on_device(): pieces = lax.all_to_all(pieces, ('hy', 'hz'), 0, 0, tiled=True)  61.1 us
    all_gather x1, waiting for transfers between devices, on_device(): piece = lax.all_gather(piece, 'hz', axis=0, tiled=True)  42.7 us
    reduce_scatter x1, waiting for transfers between devices, on_device(): lax.psum_scatter(partial_value, 'embed', scatter_dimension=0, tiled=True)  34.7 us
    all_gather x1, blocking collectives, on_device(): activated = lax.all_gather(activated, 'embed', axis=0, tiled=True)  15.1 us
    all_gather x1, blocking collectives, on_device(): piece = lax.all_gather(rows_in, 'hy', axis=0, tiled=True)  14.4 us
    dot_general x1, matrix products, on_device(): jnp.dot(activated, down_weight, preferred_element_type=jnp.float32)  4.41 us
  transfers between devices with their start and end apart: 2, of which 2 were waited for; matrix products, arithmetic and copies ran while one was open for 0% of the time, Pallas kernels for 0%

profile of v3, /device:TPU:2, one launch (start us, length us, event | category | flops | bytes accessed | tf_op | source)
XLA Modules:
  0.0 197.4 jit_solution(12723931487141335197)
XLA Ops:
  6.5 0.0 all-gather.2.cloned.1.call-start
  6.5 14.4 %all_gather.9 = bf16[64,2048]{1,0:T(8,128)(2,1)} all-gather(bf16[16,2048]{1,0:T(8,128)(2,1)} %param.4), channel_id=1, replica_groups=mesh['embed'=8,'hy'=4,'hz'=8] {'hy'}, dimensions={0}, use_global_device_ids=true | all-gather | bytes 327680 | tf_op jit(solution)/shard_map/all_gather | solution.py:9
  21.0 0.0 all-gather.2.cloned.1.call-update
  21.0 0.0 reduce-scatter.2.cloned.1.call-start
  21.1 42.7 %all-gather.2.cloned.1.call-done = bf16[512,2048]{1,0:T(8,128)(2,1)} async-done(((bf16[64,2048]{1,0:T(8,128)(2,1)}), bf16[512,2048]{1,0:T(8,128)(2,1)}) %all-gather.2.cloned.1.call-update) | async-done | bytes 2097168 | tf_op jit(solution)/shard_map/all_gather | solution.py:10
  63.8 0.0 copy-start
  63.8 1.9 copy.5
  65.7 0.8 copy-done
  66.5 0.0 copy-start.1
  66.5 2.3 %fusion.2 = f32[512,896]{1,0:T(8,128)S(1)} fusion(bf16[512,2048]{1,0:T(8,128)(2,1)S(1)} %bitcast.12, bf16[2048,896]{1,0:T(8,128)(2,1)S(1)} %copy-done), kind=kOutput, calls=%fused_computation.5 | convolution fusion | flops 1879048192 | bytes 7602176 | tf_op jit(solution)/shard_map/dot_general | solution.py:15
  68.8 0.0 copy-done.1
  68.8 2.3 %fusion.1 = f32[512,896]{1,0:T(8,128)S(1)} fusion(bf16[512,2048]{1,0:T(8,128)(2,1)S(1)} %bitcast.13, bf16[2048,896]{1,0:T(8,128)(2,1)S(1)} %copy-done.1), kind=kOutput, calls=%fused_computation.4 | convolution fusion | flops 1879048192 | bytes 7602176 | tf_op jit(solution)/shard_map/dot_general | solution.py:14
  71.1 2.1 %pad_maximum_fusion = f32[512,1792]{1,0:T(8,128)} fusion(f32[512,896]{1,0:T(8,128)S(1)} %fusion.2, f32[512,896]{1,0:T(8,128)S(1)} %fusion.1), kind=kLoop, calls=%fused_computation | loop fusion | flops 917504 | bytes 7340032 | tf_op jit(solution)/shard_map/concatenate | solution.py:16
  73.2 0.0 reduce-scatter.2.cloned.1.call-update
  73.2 34.7 %reduce-scatter.2.cloned.1.call-done = f32[64,1792]{1,0:T(8,128)} async-done(((f32[512,1792]{1,0:T(8,128)}), f32[64,1792]{1,0:T(8,128)}) %reduce-scatter.2.cloned.1.call-update) | async-done | bytes 458768 | tf_op jit(solution)/shard_map/reduce_scatter | solution.py:17
  107.9 1.1 fusion
  109.0 15.1 %all_gather.11 = bf16[512,896]{1,0:T(8,128)(2,1)S(1)} all-gather(bf16[64,896]{1,0:T(8,128)(2,1)S(1)} %fusion), channel_id=1, replica_groups=mesh['embed'=8,'hy'=4,'hz'=8] {'embed'}, dimensions={0}, use_global_device_ids=true | all-gather | bytes 1032192 | tf_op jit(solution)/shard_map/all_gather | solution.py:19
  124.1 4.4 %convolution_convert_fusion = bf16[512,2048]{1,0:T(8,128)(2,1)S(1)} fusion(bf16[512,896]{1,0:T(8,128)(2,1)S(1)} %all_gather.11, bf16[896,2048]{1,0:T(8,128)(2,1)} %param.7), kind=kOutput, calls=%fused_computation.1 | convolution fusion | flops 1880096768 | bytes 6684672 | tf_op jit(solution)/shard_map/dot_general | solution.py:20
  128.5 61.1 %all_to_all.5 = bf16[32,16,2048]{2,1,0:T(8,128)(2,1)S(1)} all-to-all(bf16[32,16,2048]{2,1,0:T(8,128)(2,1)S(1)} %bitcast.14), channel_id=1, replica_groups=mesh['embed'=8,'hy'=4,'hz'=8] {'hy','hz'}, dimensions={0} | all-to-all | bytes 4194304 | tf_op jit(solution)/shard_map/all_to_all | solution.py:25
  189.6 0.9 reduce_sum.12
Async XLA Ops:
  6.5 57.3 %all-gather.2.cloned.1.call-start = ((), (), s32[]{:S(2)}) async-start(), calls=%async_computation.2 | async-start | bytes 2359296 | tf_op jit(solution)/shard_map/all_gather | solution.py:10
  21.0 86.9 %reduce-scatter.2.cloned.1.call-start = ((), (), s32[]{:S(2)}) async-start(), calls=%async_computation.3 | async-start | bytes 4128768 | tf_op jit(solution)/shard_map/reduce_scatter | solution.py:17
  63.8 2.7 %copy-start = (bf16[2048,896]{1,0:T(8,128)(2,1)S(1)}, bf16[2048,896]{1,0:T(8,128)(2,1)}, u32[]{:S(2)}) copy-start(bf16[2048,896]{1,0:T(8,128)(2,1)} %param.6) | copy-start | bytes 11010052
  66.5 2.3 %copy-start.1 = (bf16[2048,896]{1,0:T(8,128)(2,1)S(1)}, bf16[2048,896]{1,0:T(8,128)(2,1)}, u32[]{:S(2)}) copy-start(bf16[2048,896]{1,0:T(8,128)(2,1)} %param.5) | copy-start | bytes 11010052
Sparse Core Ops, SparseCore 0:
  21.1 42.6 all-gather.1
  73.4 34.5 reduce-scatter.1

commit v4 on v2

v4 whole, which is shorter than its diff:
```python
import jax
import jax.numpy as jnp
from jax import lax
from jax.sharding import Mesh, PartitionSpec as P

EMBED = ("ex", "ec")


def ring_rs(x, axis, n):
    k = lax.axis_index(axis)
    xs = x.reshape((n, x.shape[0] // n) + x.shape[1:])
    half = x.shape[-1] // 2
    a, b = xs[..., :half], xs[..., half:]
    take = lambda arr, i: lax.dynamic_index_in_dim(arr, i % n, 0, keepdims=False)
    fwd = [(i, (i + 1) % n) for i in range(n)]
    bwd = [(i, (i - 1) % n) for i in range(n)]
    acc_a = take(a, k - 1)
    acc_b = take(b, k + 1)
    for s in range(n - 1):
        acc_a = lax.ppermute(acc_a, axis, fwd) + take(a, k - s - 2)
        acc_b = lax.ppermute(acc_b, axis, bwd) + take(b, k + s + 2)
    return jnp.concatenate([acc_a, acc_b], axis=-1)


def ring_ag(x, axis, n):
    k = lax.axis_index(axis)
    fwd = [(i, (i + 1) % n) for i in range(n)]
    bwd = [(i, (i - 1) % n) for i in range(n)]
    nf = n // 2
    out = jnp.zeros((n,) + x.shape, x.dtype)
    put = lambda out, v, i: lax.dynamic_update_index_in_dim(out, v, i % n, 0)
    out = put(out, x, k)
    buf = x
    for s in range(nf):
        buf = lax.ppermute(buf, axis, fwd)
        out = put(out, buf, k - 1 - s)
    buf = x
    for s in range(n - 1 - nf):
        buf = lax.ppermute(buf, axis, bwd)
        out = put(out, buf, k + 1 + s)
    return out.reshape((n * x.shape[0],) + x.shape[1:])


def embed_rs(x):
    ec = lax.axis_index("ec")
    ncore = lax.psum(1, "ec")
    nx = lax.psum(1, "ex")
    xs = x.reshape((nx, ncore, x.shape[0] // (nx * ncore)) + x.shape[1:])
    mine = lax.dynamic_index_in_dim(xs, ec, 1, keepdims=False)
    other = lax.dynamic_index_in_dim(xs, 1 - ec, 1, keepdims=False)
    got = lax.ppermute(other, "ec", [(0, 1), (1, 0)])
    y = (mine + got).reshape((-1,) + x.shape[1:])
    return ring_rs(y, "ex", nx)


def on_device(rows_in, gate_weight, up_weight, down_weight):
    width = gate_weight.shape[1]
    ny = lax.psum(1, "hy")
    nz = lax.psum(1, "hz")
    piece = ring_ag(ring_ag(rows_in, "hy", ny), "hz", nz)
    gate_part = jnp.dot(piece, gate_weight, preferred_element_type=jnp.float32)
    up_part = jnp.dot(piece, up_weight, preferred_element_type=jnp.float32)
    partial_value = jnp.concatenate([gate_part, up_part], axis=1)
    summed = embed_rs(partial_value)
    activated = (jax.nn.silu(summed[:, :width]) * summed[:, width:]).astype(jnp.bfloat16)
    activated = lax.all_gather(activated, EMBED, axis=0, tiled=True)
    partial_out = jnp.dot(activated, down_weight, preferred_element_type=jnp.float32)
    pieces = partial_out.astype(jnp.bfloat16).reshape(
        (ny * nz, partial_out.shape[0] // (ny * nz)) + partial_out.shape[1:]
    )
    pieces = lax.all_to_all(pieces, ("hz", "hy"), 0, 0, tiled=True)
    totals = pieces.astype(jnp.float32).sum(axis=0)
    return totals.astype(jnp.bfloat16)


def solution(mesh):
    embed, hidden = mesh.shape["embed"], mesh.shape["hidden"]
    nx = len({d.coords[0] for d in mesh.devices.flat})
    ny = len({d.coords[1] for d in mesh.devices.flat})
    sub = Mesh(
        mesh.devices.reshape(nx, embed // nx, ny, hidden // ny),
        ("ex", "ec", "hy", "hz"),
    )
    rows = P(("hy", "hz"), EMBED)
    weights = P(EMBED, ("hy", "hz"))
    placed = (rows, weights, weights, rows)
    return jax.shard_map(
        on_device, mesh=sub, in_specs=placed, out_specs=rows, check_vma=False
    )
```

time: 208 us -> 163 us (0.78)
  blocking collectives: 107 us -> 74.3 us
  starting transfers between devices: 0.04 us -> 24 us
  waiting for transfers between devices: 69.3 us -> 47.4 us
  between operations: 13.4 us -> 0.21 us
  local copies, waits for them, and re-layouts: 0.01 us -> 4.72 us
  matrix products: 11.9 us -> 9.06 us
    ppermute x0 -> x17, waiting for transfers between devices: none -> 47.4 us  [the longest x6 28.6 us: ring_ag(): buf = lax.ppermute(buf, axis, fwd)]
    reduce_scatter x1 -> x0, waiting for transfers between devices: 36.1 us -> none  [on_device(): lax.psum_scatter(partial_value, 'embed', scatter_dimension=0, tiled=True)]
    all_gather x1 -> x0, waiting for transfers between devices: 33.1 us -> none  [on_device(): piece = lax.all_gather(piece, 'hy', axis=0, tiled=True)]
    all_gather x2 -> x1, blocking collectives: 46.2 us -> 16.3 us  [on_device(): activated = lax.all_gather(activated, EMBED, axis=0, tiled=True)]
    ppermute x0 -> x17, starting transfers between devices: none -> 24 us  [the longest x4 12.6 us: ring_ag(): buf = lax.ppermute(buf, axis, bwd)]
    all_to_all x1, blocking collectives: 61.2 us -> 58 us  [on_device(): pieces = lax.all_to_all(pieces, ('hz', 'hy'), 0, 0, tiled=True)]
    dot_general x1, matrix products: 5.14 us -> 2.33 us  [on_device(): up_part = jnp.dot(piece, up_weight, preferred_element_type=jnp.float32)]
  transfers between devices with their start and end apart: 2 -> 17, of which waited for: 2 -> 11; matrix products, arithmetic and copies ran while one was open for 0% -> 1% of each run, Pallas kernels for 0% -> 0%
where the time goes in v4:
time: 163 us
  blocking collectives  74.3 us (46%)
  waiting for transfers between devices  47.4 us (29%)
  starting transfers between devices  24 us (15%)
  matrix products  9.06 us (6%)
  local copies, waits for them, and re-layouts  4.72 us (3%)
  other arithmetic  3.1 us (2%)
    all_to_all x1, blocking collectives, on_device(): pieces = lax.all_to_all(pieces, ('hz', 'hy'), 0, 0, tiled=True)  58 us
    ppermute x6, waiting for transfers between devices, ring_ag(): buf = lax.ppermute(buf, axis, fwd)  28.6 us
    all_gather x1, blocking collectives, on_device(): activated = lax.all_gather(activated, EMBED, axis=0, tiled=True)  16.3 us
    ppermute x3, waiting for transfers between devices, ring_rs(): acc_a = lax.ppermute(acc_a, axis, fwd) + take(a, k - s - 2)  14.2 us
    ppermute x4, starting transfers between devices, ring_ag(): buf = lax.ppermute(buf, axis, bwd)  12.6 us
    ppermute x3, starting transfers between devices, ring_rs(): acc_a = lax.ppermute(acc_a, axis, fwd) + take(a, k - s - 2)  4.71 us
    dot_general x1, matrix products, on_device(): jnp.dot(activated, down_weight, preferred_element_type=jnp.float32)  4.41 us
    ppermute x1, waiting for transfers between devices, embed_rs(): got = lax.ppermute(other, 'ec', [(0, 1), (1, 0)])  3.99 us
  transfers between devices with their start and end apart: 17, of which 11 were waited for; matrix products, arithmetic and copies ran while one was open for 1% of the time, Pallas kernels for 0%

profile of v4, /device:TPU:2, one launch (start us, length us, event | category | flops | bytes accessed | tf_op | source)
XLA Modules:
  0.0 162.8 jit_solution(14195250459196878179)
XLA Ops:
  0.0 1.6 collective-permute-start
  1.6 1.7 %collective-permute-start.2 = (bf16[16,2048]{1,0:T(8,128)(2,1)}, bf16[16,2048]{1,0:T(8,128)(2,1)S(1)}, u32[]{:S(2)}, u32[]{:S(2)}) collective-permute-start(bf16[16,2048]{1,0:T(8,128)(2,1)} %param.4), channel_id=1, source_target_pairs={{0,24},{8,0},{16,8},{24,16},{1,25},{9,1},{17,9},{25,17},{2,26},{10... | collective-permute-start | bytes 196616 | tf_op jit(solution)/shard_map/ppermute | solution.py:39
  3.3 0.9 bitcast_dynamic-update-slice_fusion.11
  4.1 1.6 collective-permute-done
  5.7 0.4 collective-permute-start.1
  6.1 5.1 %collective-permute-done.1 = bf16[16,2048]{1,0:T(8,128)(2,1)S(1)} collective-permute-done((bf16[16,2048]{1,0:T(8,128)(2,1)S(1)}, bf16[16,2048]{1,0:T(8,128)(2,1)S(1)}, u32[]{:S(2)}, u32[]{:S(2)}) %collective-permute-start.1) | collective-permute-done | bytes 65568 | tf_op jit(solution)/shard_map/ppermute | solution.py:35
  11.2 0.0 collective-permute-done.2
  11.2 2.0 %collective-permute-start.3 = (bf16[64,2048]{1,0:T(8,128)(2,1)S(1)}, bf16[64,2048]{1,0:T(8,128)(2,1)S(1)}, u32[]{:S(2)}, u32[]{:S(2)}) collective-permute-start(bf16[64,2048]{1,0:T(8,128)(2,1)S(1)} %bitcast.66), channel_id=1, source_target_pairs={{0,1},{1,2},{2,3},{3,4},{4,5},{5,6},{6,7},{7,0},{8,9},{9,10},{10,1... | collective-permute-start | bytes 786440 | tf_op jit(solution)/shard_map/ppermute | solution.py:35
  13.2 4.0 %collective-permute-start.7 = (bf16[64,2048]{1,0:T(8,128)(2,1)S(1)}, bf16[64,2048]{1,0:T(8,128)(2,1)S(1)}, u32[]{:S(2)}, u32[]{:S(2)}) collective-permute-start(bf16[64,2048]{1,0:T(8,128)(2,1)S(1)} %bitcast.67), channel_id=1, source_target_pairs={{0,7},{1,0},{2,1},{3,2},{4,3},{5,4},{6,5},{7,6},{8,15},{9,8},{10,9... | collective-permute-start | bytes 786440 | tf_op jit(solution)/shard_map/ppermute | solution.py:39
  17.2 0.2 broadcast_in_dim.44
  17.5 0.0 copy-start.1
  17.5 4.0 %collective-permute-done.3 = bf16[64,2048]{1,0:T(8,128)(2,1)S(1)} collective-permute-done((bf16[64,2048]{1,0:T(8,128)(2,1)S(1)}, bf16[64,2048]{1,0:T(8,128)(2,1)S(1)}, u32[]{:S(2)}, u32[]{:S(2)}) %collective-permute-start.3) | collective-permute-done | bytes 262176 | tf_op jit(solution)/shard_map/ppermute | solution.py:35
  21.5 0.0 collective-permute-start.4
  21.5 0.0 collective-permute-done.7
  21.5 3.3 %collective-permute-start.8 = (bf16[64,2048]{1,0:T(8,128)(2,1)S(1)}, bf16[64,2048]{1,0:T(8,128)(2,1)S(1)}, u32[]{:S(2)}, u32[]{:S(2)}) collective-permute-start(bf16[64,2048]{1,0:T(8,128)(2,1)S(1)} %collective-permute-done.7), channel_id=1, source_target_pairs={{0,7},{1,0},{2,1},{3,2},{4,3},{5,4},{6,5},{7,6},{8,15},{9,8},{10,9... | collective-permute-start | bytes 786440 | tf_op jit(solution)/shard_map/ppermute | solution.py:39
  24.8 4.8 %collective-permute-done.4 = bf16[64,2048]{1,0:T(8,128)(2,1)S(1)} collective-permute-done((bf16[64,2048]{1,0:T(8,128)(2,1)S(1)}, bf16[64,2048]{1,0:T(8,128)(2,1)S(1)}, u32[]{:S(2)}, u32[]{:S(2)}) %collective-permute-start.4) | collective-permute-done | bytes 262176 | tf_op jit(solution)/shard_map/ppermute | solution.py:35
  29.6 0.0 collective-permute-start.5
  29.6 0.0 collective-permute-done.8
  29.6 3.6 %collective-permute-start.9 = (bf16[64,2048]{1,0:T(8,128)(2,1)S(1)}, bf16[64,2048]{1,0:T(8,128)(2,1)S(1)}, u32[]{:S(2)}, u32[]{:S(2)}) collective-permute-start(bf16[64,2048]{1,0:T(8,128)(2,1)S(1)} %collective-permute-done.8), channel_id=1, source_target_pairs={{0,7},{1,0},{2,1},{3,2},{4,3},{5,4},{6,5},{7,6},{8,15},{9,8},{10,9... | collective-permute-start | bytes 786440 | tf_op jit(solution)/shard_map/ppermute | solution.py:39
  33.2 5.6 %collective-permute-done.5 = bf16[64,2048]{1,0:T(8,128)(2,1)S(1)} collective-permute-done((bf16[64,2048]{1,0:T(8,128)(2,1)S(1)}, bf16[64,2048]{1,0:T(8,128)(2,1)S(1)}, u32[]{:S(2)}, u32[]{:S(2)}) %collective-permute-start.5) | collective-permute-done | bytes 262176 | tf_op jit(solution)/shard_map/ppermute | solution.py:35
  38.9 0.0 collective-permute-start.6
  38.9 7.6 %collective-permute-done.6 = bf16[64,2048]{1,0:T(8,128)(2,1)S(1)} collective-permute-done((bf16[64,2048]{1,0:T(8,128)(2,1)S(1)}, bf16[64,2048]{1,0:T(8,128)(2,1)S(1)}, u32[]{:S(2)}, u32[]{:S(2)}) %collective-permute-start.6) | collective-permute-done | bytes 262176 | tf_op jit(solution)/shard_map/ppermute | solution.py:35
  46.6 0.0 collective-permute-done.9
  46.6 0.0 copy-done.1
  46.6 0.0 copy-start.2
  46.6 2.3 %fusion.3 = f32[512,896]{1,0:T(8,128)S(1)} fusion(bf16[512,2048]{1,0:T(8,128)(2,1)S(1)} %bitcast.63, bf16[2048,896]{1,0:T(8,128)(2,1)S(1)} %copy-done.1), kind=kOutput, calls=%fused_computation.27 | convolution fusion | flops 1879048192 | bytes 7602176 | tf_op jit(solution)/shard_map/dot_general | solution.py:61
  49.0 0.0 copy-done.2
  49.0 2.3 %fusion.4 = f32[512,896]{1,0:T(8,128)S(1)} fusion(bf16[512,2048]{1,0:T(8,128)(2,1)S(1)} %bitcast.64, bf16[2048,896]{1,0:T(8,128)(2,1)S(1)} %copy-done.2), kind=kOutput, calls=%fused_computation.28 | convolution fusion | flops 1879048192 | bytes 7602176 | tf_op jit(solution)/shard_map/dot_general | solution.py:62
  51.3 0.3 pad_maximum_fusion
  51.6 0.0 copy-start
  51.6 1.8 %copy-done = f32[512,1792]{1,0:T(8,128)} copy-done((f32[512,1792]{1,0:T(8,128)}, f32[512,1792]{1,0:T(8,128)S(1)}, u32[]{:S(2)}) %copy-start) | copy-done | bytes 3670040
  53.4 1.4 dynamic-slice_bitcast_fusion
  54.8 0.0 collective-permute-start.10
  54.8 4.0 %collective-permute-done.10 = f32[4,64,1792]{2,1,0:T(8,128)S(1)} collective-permute-done((f32[4,64,1792]{2,1,0:T(8,128)}, f32[4,64,1792]{2,1,0:T(8,128)S(1)}, u32[]{:S(2)}, u32[]{:S(2)}) %collective-permute-start.10) | collective-permute-done | bytes 1835040 | tf_op jit(solution)/shard_map/ppermute | solution.py:51
  58.8 1.7 %bitcast_add_fusion = f32[4,64,1792]{2,1,0:T(8,128)S(1)} fusion(f32[4,64,1792]{2,1,0:T(8,128)S(1)} %collective-permute-done.10, f32[4,2,64,1792]{3,2,1,0:T(8,128)} %bitcast.62, s32[]{:T(128)S(6)} %select_n.177), kind=kLoop, calls=%fused_computation.2 | loop fusion | flops 458752 | bytes 5505028 | tf_op jit(solution)/shard_map/add | solution.py:52
  60.5 0.1 fusion.2
  60.7 1.6 collective-permute-start.11
  62.2 0.6 collective-permute-start.14
  62.9 5.5 %collective-permute-done.11 = f32[64,896]{1,0:T(8,128)S(1)} collective-permute-done((f32[64,896]{1,0:T(8,128)S(1)}, f32[64,896]{1,0:T(8,128)S(1)}, u32[]{:S(2)}, u32[]{:S(2)}) %collective-permute-start.11) | collective-permute-done | bytes 229408 | tf_op jit(solution)/shard_map/ppermute | solution.py:20
  68.4 1.6 collective-permute-start.12
  70.0 0.0 collective-permute-done.14
  70.0 0.6 collective-permute-start.15
  70.6 4.7 %collective-permute-done.12 = f32[64,896]{1,0:T(8,128)S(1)} collective-permute-done((f32[64,896]{1,0:T(8,128)S(1)}, f32[64,896]{1,0:T(8,128)S(1)}, u32[]{:S(2)}, u32[]{:S(2)}) %collective-permute-start.12) | collective-permute-done | bytes 229408 | tf_op jit(solution)/shard_map/ppermute | solution.py:20
  75.3 1.6 collective-permute-start.13
  76.9 0.0 collective-permute-done.15
  76.9 1.6 collective-permute-start.16
  78.5 4.0 %collective-permute-done.13 = f32[64,896]{1,0:T(8,128)S(1)} collective-permute-done((f32[64,896]{1,0:T(8,128)S(1)}, f32[64,896]{1,0:T(8,128)S(1)}, u32[]{:S(2)}, u32[]{:S(2)}) %collective-permute-start.13) | collective-permute-done | bytes 229408 | tf_op jit(solution)/shard_map/ppermute | solution.py:20
  82.5 0.5 collective-permute-done.16
  83.0 0.1 fusion.1
  83.1 16.3 %all_gather.3 = bf16[512,896]{1,0:T(8,128)(2,1)S(1)} all-gather(bf16[64,896]{1,0:T(8,128)(2,1)S(1)} %fusion.1), channel_id=1, replica_groups=mesh['ex'=4,'ec'=2,'hy'=4,'hz'=8] {'ex','ec'}, dimensions={0}, use_global_device_ids=true | all-gather | bytes 1032192 | tf_op jit(solution)/shard_map/all_gather | solution.py:66
  99.4 4.4 %convolution_convert_fusion = bf16[512,2048]{1,0:T(8,128)(2,1)S(1)} fusion(bf16[512,896]{1,0:T(8,128)(2,1)S(1)} %all_gather.3, bf16[896,2048]{1,0:T(8,128)(2,1)} %param.7), kind=kOutput, calls=%fused_computation.1 | convolution fusion | flops 1880096768 | bytes 6684672 | tf_op jit(solution)/shard_map/dot_general | solution.py:67
  103.8 58.0 %all_to_all.5 = bf16[32,16,2048]{2,1,0:T(8,128)(2,1)S(1)} all-to-all(bf16[32,16,2048]{2,1,0:T(8,128)(2,1)S(1)} %bitcast.65), channel_id=1, replica_groups=mesh['ex'=4,'ec'=2,'hy'=4,'hz'=8] {'hz','hy'}, dimensions={0} | all-to-all | bytes 4194304 | tf_op jit(solution)/shard_map/all_to_all | solution.py:71
  161.8 0.9 reduce_sum.12
  (18 shorter events, 0.4 us)
Async XLA Ops:
  0.0 5.7 %collective-permute-start = (bf16[16,2048]{1,0:T(8,128)(2,1)}, bf16[16,2048]{1,0:T(8,128)(2,1)S(1)}, u32[]{:S(2)}, u32[]{:S(2)}) collective-permute-start(bf16[16,2048]{1,0:T(8,128)(2,1)} %param.4), channel_id=1, source_target_pairs={{0,8},{8,16},{16,24},{24,0},{1,9},{9,17},{17,25},{25,1},{2,10},{10... | collective-permute-start | bytes 196616 | tf_op jit(solution)/shard_map/ppermute | solution.py:35
  1.6 9.6 %collective-permute-start.2 = (bf16[16,2048]{1,0:T(8,128)(2,1)}, bf16[16,2048]{1,0:T(8,128)(2,1)S(1)}, u32[]{:S(2)}, u32[]{:S(2)}) collective-permute-start(bf16[16,2048]{1,0:T(8,128)(2,1)} %param.4), channel_id=1, source_target_pairs={{0,24},{8,0},{16,8},{24,16},{1,25},{9,1},{17,9},{25,17},{2,26},{10... | collective-permute-start | bytes 196616 | tf_op jit(solution)/shard_map/ppermute | solution.py:39
  5.7 5.5 %collective-permute-start.1 = (bf16[16,2048]{1,0:T(8,128)(2,1)S(1)}, bf16[16,2048]{1,0:T(8,128)(2,1)S(1)}, u32[]{:S(2)}, u32[]{:S(2)}) collective-permute-start(bf16[16,2048]{1,0:T(8,128)(2,1)S(1)} %collective-permute-done), channel_id=1, source_target_pairs={{0,8},{8,16},{16,24},{24,0},{1,9},{9,17},{17,25},{25,1},{2,10},{10... | collective-permute-start | bytes 196616 | tf_op jit(solution)/shard_map/ppermute | solution.py:35
  11.2 10.3 %collective-permute-start.3 = (bf16[64,2048]{1,0:T(8,128)(2,1)S(1)}, bf16[64,2048]{1,0:T(8,128)(2,1)S(1)}, u32[]{:S(2)}, u32[]{:S(2)}) collective-permute-start(bf16[64,2048]{1,0:T(8,128)(2,1)S(1)} %bitcast.66), channel_id=1, source_target_pairs={{0,1},{1,2},{2,3},{3,4},{4,5},{5,6},{6,7},{7,0},{8,9},{9,10},{10,1... | collective-permute-start | bytes 786440 | tf_op jit(solution)/shard_map/ppermute | solution.py:35
  13.2 8.3 %collective-permute-start.7 = (bf16[64,2048]{1,0:T(8,128)(2,1)S(1)}, bf16[64,2048]{1,0:T(8,128)(2,1)S(1)}, u32[]{:S(2)}, u32[]{:S(2)}) collective-permute-start(bf16[64,2048]{1,0:T(8,128)(2,1)S(1)} %bitcast.67), channel_id=1, source_target_pairs={{0,7},{1,0},{2,1},{3,2},{4,3},{5,4},{6,5},{7,6},{8,15},{9,8},{10,9... | collective-permute-start | bytes 786440 | tf_op jit(solution)/shard_map/ppermute | solution.py:39
  17.5 29.1 %copy-start.1 = (bf16[2048,896]{1,0:T(8,128)(2,1)S(1)}, bf16[2048,896]{1,0:T(8,128)(2,1)}, u32[]{:S(2)}) copy-start(bf16[2048,896]{1,0:T(8,128)(2,1)} %param.5) | copy-start | bytes 11010052
  21.5 8.1 %collective-permute-start.4 = (bf16[64,2048]{1,0:T(8,128)(2,1)S(1)}, bf16[64,2048]{1,0:T(8,128)(2,1)S(1)}, u32[]{:S(2)}, u32[]{:S(2)}) collective-permute-start(bf16[64,2048]{1,0:T(8,128)(2,1)S(1)} %collective-permute-done.3), channel_id=1, source_target_pairs={{0,1},{1,2},{2,3},{3,4},{4,5},{5,6},{6,7},{7,0},{8,9},{9,10},{10,1... | collective-permute-start | bytes 786440 | tf_op jit(solution)/shard_map/ppermute | solution.py:35
  21.5 8.1 %collective-permute-start.8 = (bf16[64,2048]{1,0:T(8,128)(2,1)S(1)}, bf16[64,2048]{1,0:T(8,128)(2,1)S(1)}, u32[]{:S(2)}, u32[]{:S(2)}) collective-permute-start(bf16[64,2048]{1,0:T(8,128)(2,1)S(1)} %collective-permute-done.7), channel_id=1, source_target_pairs={{0,7},{1,0},{2,1},{3,2},{4,3},{5,4},{6,5},{7,6},{8,15},{9,8},{10,9... | collective-permute-start | bytes 786440 | tf_op jit(solution)/shard_map/ppermute | solution.py:39
  29.6 9.3 %collective-permute-start.5 = (bf16[64,2048]{1,0:T(8,128)(2,1)S(1)}, bf16[64,2048]{1,0:T(8,128)(2,1)S(1)}, u32[]{:S(2)}, u32[]{:S(2)}) collective-permute-start(bf16[64,2048]{1,0:T(8,128)(2,1)S(1)} %collective-permute-done.4), channel_id=1, source_target_pairs={{0,1},{1,2},{2,3},{3,4},{4,5},{5,6},{6,7},{7,0},{8,9},{9,10},{10,1... | collective-permute-start | bytes 786440 | tf_op jit(solution)/shard_map/ppermute | solution.py:35
  29.6 16.9 %collective-permute-start.9 = (bf16[64,2048]{1,0:T(8,128)(2,1)S(1)}, bf16[64,2048]{1,0:T(8,128)(2,1)S(1)}, u32[]{:S(2)}, u32[]{:S(2)}) collective-permute-start(bf16[64,2048]{1,0:T(8,128)(2,1)S(1)} %collective-permute-done.8), channel_id=1, source_target_pairs={{0,7},{1,0},{2,1},{3,2},{4,3},{5,4},{6,5},{7,6},{8,15},{9,8},{10,9... | collective-permute-start | bytes 786440 | tf_op jit(solution)/shard_map/ppermute | solution.py:39
  38.9 7.6 %collective-permute-start.6 = (bf16[64,2048]{1,0:T(8,128)(2,1)S(1)}, bf16[64,2048]{1,0:T(8,128)(2,1)S(1)}, u32[]{:S(2)}, u32[]{:S(2)}) collective-permute-start(bf16[64,2048]{1,0:T(8,128)(2,1)S(1)} %collective-permute-done.5), channel_id=1, source_target_pairs={{0,1},{1,2},{2,3},{3,4},{4,5},{5,6},{6,7},{7,0},{8,9},{9,10},{10,1... | collective-permute-start | bytes 786440 | tf_op jit(solution)/shard_map/ppermute | solution.py:35
  46.6 2.3 %copy-start.2 = (bf16[2048,896]{1,0:T(8,128)(2,1)S(1)}, bf16[2048,896]{1,0:T(8,128)(2,1)}, u32[]{:S(2)}) copy-start(bf16[2048,896]{1,0:T(8,128)(2,1)} %param.6) | copy-start | bytes 11010052
  51.6 1.8 %copy-start = (f32[512,1792]{1,0:T(8,128)}, f32[512,1792]{1,0:T(8,128)S(1)}, u32[]{:S(2)}) copy-start(f32[512,1792]{1,0:T(8,128)S(1)} %pad_maximum_fusion) | copy-start | bytes 11010052
  54.8 4.0 %collective-permute-start.10 = (f32[4,64,1792]{2,1,0:T(8,128)}, f32[4,64,1792]{2,1,0:T(8,128)S(1)}, u32[]{:S(2)}, u32[]{:S(2)}) collective-permute-start(f32[4,64,1792]{2,1,0:T(8,128)} %dynamic-slice_bitcast_fusion), channel_id=1, source_target_pairs={{0,32},{32,0},{1,33},{33,1},{2,34},{34,2},{3,35},{35,3},{4,36},{36... | collective-permute-start | bytes 5505032 | tf_op jit(solution)/shard_map/ppermute | solution.py:51
  60.7 7.7 %collective-permute-start.11 = (f32[64,896]{1,0:T(8,128)S(1)}, f32[64,896]{1,0:T(8,128)S(1)}, u32[]{:S(2)}, u32[]{:S(2)}) collective-permute-start(f32[64,896]{1,0:T(8,128)S(1)} %dynamic-slice_bitcast_fusion.2), channel_id=1, source_target_pairs={{0,64},{64,128},{128,192},{192,0},{1,65},{65,129},{129,193},{193,1... | collective-permute-start | bytes 688136 | tf_op jit(solution)/shard_map/ppermute | solution.py:20
  62.2 7.7 %collective-permute-start.14 = (f32[64,896]{1,0:T(8,128)S(1)}, f32[64,896]{1,0:T(8,128)S(1)}, u32[]{:S(2)}, u32[]{:S(2)}) collective-permute-start(f32[64,896]{1,0:T(8,128)S(1)} %dynamic-slice_bitcast_fusion.1), channel_id=1, source_target_pairs={{0,192},{64,0},{128,64},{192,128},{1,193},{65,1},{129,65},{193,129... | collective-permute-start | bytes 688136 | tf_op jit(solution)/shard_map/ppermute | solution.py:21
  68.4 6.9 %collective-permute-start.12 = (f32[64,896]{1,0:T(8,128)S(1)}, f32[64,896]{1,0:T(8,128)S(1)}, u32[]{:S(2)}, u32[]{:S(2)}) collective-permute-start(f32[64,896]{1,0:T(8,128)S(1)} %bitcast_add_fusion.6), channel_id=1, source_target_pairs={{0,64},{64,128},{128,192},{192,0},{1,65},{65,129},{129,193},{193,1... | collective-permute-start | bytes 688136 | tf_op jit(solution)/shard_map/ppermute | solution.py:20
  70.0 6.9 %collective-permute-start.15 = (f32[64,896]{1,0:T(8,128)S(1)}, f32[64,896]{1,0:T(8,128)S(1)}, u32[]{:S(2)}, u32[]{:S(2)}) collective-permute-start(f32[64,896]{1,0:T(8,128)S(1)} %bitcast_add_fusion.3), channel_id=1, source_target_pairs={{0,192},{64,0},{128,64},{192,128},{1,193},{65,1},{129,65},{193,129... | collective-permute-start | bytes 688136 | tf_op jit(solution)/shard_map/ppermute | solution.py:21
  75.3 7.2 %collective-permute-start.13 = (f32[64,896]{1,0:T(8,128)S(1)}, f32[64,896]{1,0:T(8,128)S(1)}, u32[]{:S(2)}, u32[]{:S(2)}) collective-permute-start(f32[64,896]{1,0:T(8,128)S(1)} %bitcast_add_fusion.5), channel_id=1, source_target_pairs={{0,64},{64,128},{128,192},{192,0},{1,65},{65,129},{129,193},{193,1... | collective-permute-start | bytes 688136 | tf_op jit(solution)/shard_map/ppermute | solution.py:20
  76.9 6.1 %collective-permute-start.16 = (f32[64,896]{1,0:T(8,128)S(1)}, f32[64,896]{1,0:T(8,128)S(1)}, u32[]{:S(2)}, u32[]{:S(2)}) collective-permute-start(f32[64,896]{1,0:T(8,128)S(1)} %bitcast_add_fusion.2), channel_id=1, source_target_pairs={{0,192},{64,0},{128,64},{192,128},{1,193},{65,1},{129,65},{193,129... | collective-permute-start | bytes 688136 | tf_op jit(solution)/shard_map/ppermute | solution.py:21

commit v5 on v4

--- a/solution.py
+++ b/solution.py
@@ -22,14 +22,15 @@
     return jnp.concatenate([acc_a, acc_b], axis=-1)
 
 
-def ring_ag(x, axis, n):
+def ring_ag(x, axis, n, f=lambda v: v):
     k = lax.axis_index(axis)
     fwd = [(i, (i + 1) % n) for i in range(n)]
     bwd = [(i, (i - 1) % n) for i in range(n)]
     nf = n // 2
-    out = jnp.zeros((n,) + x.shape, x.dtype)
-    put = lambda out, v, i: lax.dynamic_update_index_in_dim(out, v, i % n, 0)
-    out = put(out, x, k)
+    own = f(x)
+    out = jnp.zeros((n,) + own.shape, own.dtype)
+    put = lambda out, v, i: lax.dynamic_update_index_in_dim(out, f(v), i % n, 0)
+    out = lax.dynamic_update_index_in_dim(out, own, k, 0)
     buf = x
     for s in range(nf):
         buf = lax.ppermute(buf, axis, fwd)
@@ -38,7 +39,7 @@
     for s in range(n - 1 - nf):
         buf = lax.ppermute(buf, axis, bwd)
         out = put(out, buf, k + 1 + s)
-    return out.reshape((n * x.shape[0],) + x.shape[1:])
+    return out.reshape((n * own.shape[0],) + own.shape[1:])
 
 
 def embed_rs(x):
@@ -57,10 +58,18 @@
     width = gate_weight.shape[1]
     ny = lax.psum(1, "hy")
     nz = lax.psum(1, "hz")
-    piece = ring_ag(ring_ag(rows_in, "hy", ny), "hz", nz)
-    gate_part = jnp.dot(piece, gate_weight, preferred_element_type=jnp.float32)
-    up_part = jnp.dot(piece, up_weight, preferred_element_type=jnp.float32)
-    partial_value = jnp.concatenate([gate_part, up_part], axis=1)
+    partial_value = ring_ag(
+        ring_ag(rows_in, "hy", ny),
+        "hz",
+        nz,
+        lambda v: jnp.concatenate(
+            [
+                jnp.dot(v, gate_weight, preferred_element_type=jnp.float32),
+                jnp.dot(v, up_weight, preferred_element_type=jnp.float32),
+            ],
+            axis=1,
+        ),
+    )
     summed = embed_rs(partial_value)
     activated = (jax.nn.silu(summed[:, :width]) * summed[:, width:]).astype(jnp.bfloat16)
     activated = lax.all_gather(activated, EMBED, axis=0, tiled=True)

time: 163 us -> 161 us (0.988)
  waiting for transfers between devices: 47.4 us -> 35.1 us
  matrix products: 9.06 us -> 17.7 us
    ppermute x6, waiting for transfers between devices: 28.6 us -> 15.4 us  [ring_ag(): buf = lax.ppermute(buf, axis, fwd)]
    dot_general x2 -> x16, matrix products: 4.65 us -> 13.3 us  [the longest x8 7.66 us: on_device(): jnp.dot(v, gate_weight, preferred_element_type=jnp.float32)]
  transfers between devices with their start and end apart: 17 -> 17, of which waited for: 11 -> 13; matrix products, arithmetic and copies ran while one was open for 1% -> 8% of each run, Pallas kernels for 0% -> 0%
where the time goes in v5:
time: 161 us; the launch traced here: 160 us
  blocking collectives  74 us (46%)
  waiting for transfers between devices  35.1 us (22%)
  starting transfers between devices  24.6 us (15%)
  matrix products  17.7 us (11%)
  local copies, waits for them, and re-layouts  5.1 us (3%)
  other arithmetic  3.13 us (2%)
    all_to_all x1, blocking collectives, on_device(): pieces = lax.all_to_all(pieces, ('hz', 'hy'), 0, 0, tiled=True)  57.5 us
    all_gather x1, blocking collectives, on_device(): activated = lax.all_gather(activated, EMBED, axis=0, tiled=True)  16.5 us
    ppermute x6, waiting for transfers between devices, ring_ag(): buf = lax.ppermute(buf, axis, fwd)  15.4 us
    ppermute x3, waiting for transfers between devices, ring_rs(): acc_a = lax.ppermute(acc_a, axis, fwd) + take(a, k - s - 2)  14.2 us
    ppermute x4, starting transfers between devices, ring_ag(): buf = lax.ppermute(buf, axis, bwd)  12.9 us
    dot_general x8, matrix products, on_device(): jnp.dot(v, gate_weight, preferred_element_type=jnp.float32)  7.66 us
    dot_general x8, matrix products, on_device(): jnp.dot(v, up_weight, preferred_element_type=jnp.float32)  5.67 us
    ppermute x3, starting transfers between devices, ring_rs(): acc_a = lax.ppermute(acc_a, axis, fwd) + take(a, k - s - 2)  4.67 us
  transfers between devices with their start and end apart: 17, of which 13 were waited for; matrix products, arithmetic and copies ran while one was open for 8% of the time, Pallas kernels for 0%

profile of v5, /device:TPU:2, one launch (start us, length us, event | category | flops | bytes accessed | tf_op | source)
XLA Modules:
  0.0 160.0 jit_solution(10783877201136396382)
XLA Ops:
  0.0 1.6 collective-permute-start
  1.6 1.7 %collective-permute-start.2 = (bf16[16,2048]{1,0:T(8,128)(2,1)}, bf16[16,2048]{1,0:T(8,128)(2,1)S(1)}, u32[]{:S(2)}, u32[]{:S(2)}) collective-permute-start(bf16[16,2048]{1,0:T(8,128)(2,1)} %param.4), channel_id=1, source_target_pairs={{0,24},{8,0},{16,8},{24,16},{1,25},{9,1},{17,9},{25,17},{2,26},{10... | collective-permute-start | bytes 196616 | tf_op jit(solution)/shard_map/ppermute | solution.py:40
  3.3 0.9 bitcast_dynamic-update-slice_fusion.3
  4.1 1.6 collective-permute-done
  5.7 0.4 collective-permute-start.1
  6.1 5.1 %collective-permute-done.1 = bf16[16,2048]{1,0:T(8,128)(2,1)S(1)} collective-permute-done((bf16[16,2048]{1,0:T(8,128)(2,1)S(1)}, bf16[16,2048]{1,0:T(8,128)(2,1)S(1)}, u32[]{:S(2)}, u32[]{:S(2)}) %collective-permute-start.1) | collective-permute-done | bytes 65568 | tf_op jit(solution)/shard_map/ppermute | solution.py:36
  11.2 0.0 collective-permute-done.2
  11.2 2.0 %collective-permute-start.3 = (bf16[64,2048]{1,0:T(8,128)(2,1)S(1)}, bf16[64,2048]{1,0:T(8,128)(2,1)S(1)}, u32[]{:S(2)}, u32[]{:S(2)}) collective-permute-start(bf16[64,2048]{1,0:T(8,128)(2,1)S(1)} %bitcast.105), channel_id=1, source_target_pairs={{0,1},{1,2},{2,3},{3,4},{4,5},{5,6},{6,7},{7,0},{8,9},{9,10},{10,1... | collective-permute-start | bytes 786440 | tf_op jit(solution)/shard_map/ppermute | solution.py:36
  13.2 4.0 %collective-permute-start.7 = (bf16[64,2048]{1,0:T(8,128)(2,1)S(1)}, bf16[64,2048]{1,0:T(8,128)(2,1)S(1)}, u32[]{:S(2)}, u32[]{:S(2)}) collective-permute-start(bf16[64,2048]{1,0:T(8,128)(2,1)S(1)} %bitcast.106), channel_id=1, source_target_pairs={{0,7},{1,0},{2,1},{3,2},{4,3},{5,4},{6,5},{7,6},{8,15},{9,8},{10,9... | collective-permute-start | bytes 786440 | tf_op jit(solution)/shard_map/ppermute | solution.py:40
  17.2 2.7 %fusion.11 = f32[64,896]{1,0:T(8,128)S(1)} fusion(bf16[64,2048]{1,0:T(8,128)(2,1)S(1)} %bitcast.107, bf16[2048,896]{1,0:T(8,128)(2,1)} %param.5), kind=kOutput, calls=%fused_computation.34 | convolution fusion | flops 234881024 | bytes 4161536 | tf_op jit(solution)/shard_map/dot_general | solution.py:67
  20.0 0.0 copy-done.1
  20.0 0.0 copy-start
  20.0 0.7 fusion.12
  20.7 0.3 broadcast_in_dim.44
  21.1 0.4 collective-permute-done.3
  21.5 0.5 copy-done
  22.0 0.7 fusion.13
  22.7 0.1 collective-permute-start.4
  22.8 0.7 fusion.14
  23.5 0.0 collective-permute-done.7
  23.5 0.7 fusion.21
  24.2 0.7 fusion.22
  24.9 3.3 %collective-permute-start.8 = (bf16[64,2048]{1,0:T(8,128)(2,1)S(1)}, bf16[64,2048]{1,0:T(8,128)(2,1)S(1)}, u32[]{:S(2)}, u32[]{:S(2)}) collective-permute-start(bf16[64,2048]{1,0:T(8,128)(2,1)S(1)} %collective-permute-done.7), channel_id=1, source_target_pairs={{0,7},{1,0},{2,1},{3,2},{4,3},{5,4},{6,5},{7,6},{8,15},{9,8},{10,9... | collective-permute-start | bytes 786440 | tf_op jit(solution)/shard_map/ppermute | solution.py:40
  28.3 2.1 %collective-permute-done.4 = bf16[64,2048]{1,0:T(8,128)(2,1)S(1)} collective-permute-done((bf16[64,2048]{1,0:T(8,128)(2,1)S(1)}, bf16[64,2048]{1,0:T(8,128)(2,1)S(1)}, u32[]{:S(2)}, u32[]{:S(2)}) %collective-permute-start.4) | collective-permute-done | bytes 262176 | tf_op jit(solution)/shard_map/ppermute | solution.py:36
  30.4 0.7 fusion.15
  31.1 0.1 collective-permute-start.5
  31.2 0.7 fusion.16
  31.9 0.2 collective-permute-done.8
  32.1 0.7 fusion.23
  32.8 0.7 fusion.24
  33.6 3.9 %collective-permute-start.9 = (bf16[64,2048]{1,0:T(8,128)(2,1)S(1)}, bf16[64,2048]{1,0:T(8,128)(2,1)S(1)}, u32[]{:S(2)}, u32[]{:S(2)}) collective-permute-start(bf16[64,2048]{1,0:T(8,128)(2,1)S(1)} %collective-permute-done.8), channel_id=1, source_target_pairs={{0,7},{1,0},{2,1},{3,2},{4,3},{5,4},{6,5},{7,6},{8,15},{9,8},{10,9... | collective-permute-start | bytes 786440 | tf_op jit(solution)/shard_map/ppermute | solution.py:40
  37.5 1.5 collective-permute-done.5
  39.1 0.7 fusion.17
  39.8 0.1 collective-permute-start.6
  39.9 0.7 fusion.18
  40.6 0.8 collective-permute-done.9
  41.4 0.7 fusion.25
  42.1 0.7 fusion.26
  42.8 4.6 %collective-permute-done.6 = bf16[64,2048]{1,0:T(8,128)(2,1)S(1)} collective-permute-done((bf16[64,2048]{1,0:T(8,128)(2,1)S(1)}, bf16[64,2048]{1,0:T(8,128)(2,1)S(1)}, u32[]{:S(2)}, u32[]{:S(2)}) %collective-permute-start.6) | collective-permute-done | bytes 262176 | tf_op jit(solution)/shard_map/ppermute | solution.py:36
  47.4 0.7 fusion.19
  48.1 0.7 fusion.20
  49.1 1.8 %copy-done.2 = f32[8,64,1792]{2,1,0:T(8,128)} copy-done((f32[8,64,1792]{2,1,0:T(8,128)}, f32[8,64,1792]{2,1,0:T(8,128)S(1)}, u32[]{:S(2)}) %copy-start.2) | copy-done | bytes 3670040
  50.8 1.4 dynamic-slice_bitcast_fusion
  52.2 0.0 collective-permute-start.10
  52.2 4.0 %collective-permute-done.10 = f32[4,64,1792]{2,1,0:T(8,128)S(1)} collective-permute-done((f32[4,64,1792]{2,1,0:T(8,128)}, f32[4,64,1792]{2,1,0:T(8,128)S(1)}, u32[]{:S(2)}, u32[]{:S(2)}) %collective-permute-start.10) | collective-permute-done | bytes 1835040 | tf_op jit(solution)/shard_map/ppermute | solution.py:52
  56.2 1.7 %bitcast_add_fusion = f32[4,64,1792]{2,1,0:T(8,128)S(1)} fusion(f32[4,64,1792]{2,1,0:T(8,128)S(1)} %collective-permute-done.10, f32[4,2,64,1792]{3,2,1,0:T(8,128)} %bitcast.104, s32[]{:T(128)S(6)} %select_n.167), kind=kLoop, calls=%fused_computation.1 | loop fusion | flops 458752 | bytes 5505028 | tf_op jit(solution)/shard_map/add | solution.py:53
  57.9 0.1 fusion.10
  58.1 1.6 collective-permute-start.11
  59.7 0.6 collective-permute-start.14
  60.3 5.5 %collective-permute-done.11 = f32[64,896]{1,0:T(8,128)S(1)} collective-permute-done((f32[64,896]{1,0:T(8,128)S(1)}, f32[64,896]{1,0:T(8,128)S(1)}, u32[]{:S(2)}, u32[]{:S(2)}) %collective-permute-start.11) | collective-permute-done | bytes 229408 | tf_op jit(solution)/shard_map/ppermute | solution.py:20
  65.9 1.6 collective-permute-start.12
  67.4 0.0 collective-permute-done.14
  67.5 0.6 collective-permute-start.15
  68.1 4.7 %collective-permute-done.12 = f32[64,896]{1,0:T(8,128)S(1)} collective-permute-done((f32[64,896]{1,0:T(8,128)S(1)}, f32[64,896]{1,0:T(8,128)S(1)}, u32[]{:S(2)}, u32[]{:S(2)}) %collective-permute-start.12) | collective-permute-done | bytes 229408 | tf_op jit(solution)/shard_map/ppermute | solution.py:20
  72.8 1.6 collective-permute-start.13
  74.3 0.0 collective-permute-done.15
  74.4 1.6 collective-permute-start.16
  76.0 4.0 %collective-permute-done.13 = f32[64,896]{1,0:T(8,128)S(1)} collective-permute-done((f32[64,896]{1,0:T(8,128)S(1)}, f32[64,896]{1,0:T(8,128)S(1)}, u32[]{:S(2)}, u32[]{:S(2)}) %collective-permute-start.13) | collective-permute-done | bytes 229408 | tf_op jit(solution)/shard_map/ppermute | solution.py:20
  80.0 0.5 collective-permute-done.16
  80.5 0.1 fusion.9
  80.6 16.5 %all_gather.3 = bf16[512,896]{1,0:T(8,128)(2,1)S(1)} all-gather(bf16[64,896]{1,0:T(8,128)(2,1)S(1)} %fusion.9), channel_id=1, replica_groups=mesh['ex'=4,'ec'=2,'hy'=4,'hz'=8] {'ex','ec'}, dimensions={0}, use_global_device_ids=true | all-gather | bytes 1032192 | tf_op jit(solution)/shard_map/all_gather | solution.py:75
  97.1 4.4 %convolution_convert_fusion = bf16[512,2048]{1,0:T(8,128)(2,1)S(1)} fusion(bf16[512,896]{1,0:T(8,128)(2,1)S(1)} %all_gather.3, bf16[896,2048]{1,0:T(8,128)(2,1)} %param.7), kind=kOutput, calls=%fused_computation | convolution fusion | flops 1880096768 | bytes 6684672 | tf_op jit(solution)/shard_map/dot_general | solution.py:76
  101.5 57.5 %all_to_all.5 = bf16[32,16,2048]{2,1,0:T(8,128)(2,1)S(1)} all-to-all(bf16[32,16,2048]{2,1,0:T(8,128)(2,1)S(1)} %bitcast.109), channel_id=1, replica_groups=mesh['ex'=4,'ec'=2,'hy'=4,'hz'=8] {'hz','hy'}, dimensions={0} | all-to-all | bytes 4194304 | tf_op jit(solution)/shard_map/all_to_all | solution.py:80
  159.0 0.9 reduce_sum.12
  (20 shorter events, 0.5 us)
Async XLA Ops:
  0.0 5.7 %collective-permute-start = (bf16[16,2048]{1,0:T(8,128)(2,1)}, bf16[16,2048]{1,0:T(8,128)(2,1)S(1)}, u32[]{:S(2)}, u32[]{:S(2)}) collective-permute-start(bf16[16,2048]{1,0:T(8,128)(2,1)} %param.4), channel_id=1, source_target_pairs={{0,8},{8,16},{16,24},{24,0},{1,9},{9,17},{17,25},{25,1},{2,10},{10... | collective-permute-start | bytes 196616 | tf_op jit(solution)/shard_map/ppermute | solution.py:36
  1.6 9.6 %collective-permute-start.2 = (bf16[16,2048]{1,0:T(8,128)(2,1)}, bf16[16,2048]{1,0:T(8,128)(2,1)S(1)}, u32[]{:S(2)}, u32[]{:S(2)}) collective-permute-start(bf16[16,2048]{1,0:T(8,128)(2,1)} %param.4), channel_id=1, source_target_pairs={{0,24},{8,0},{16,8},{24,16},{1,25},{9,1},{17,9},{25,17},{2,26},{10... | collective-permute-start | bytes 196616 | tf_op jit(solution)/shard_map/ppermute | solution.py:40
  4.1 15.9 %copy-start.1 = (bf16[2048,896]{1,0:T(8,128)(2,1)S(1)}, bf16[2048,896]{1,0:T(8,128)(2,1)}, u32[]{:S(2)}) copy-start(bf16[2048,896]{1,0:T(8,128)(2,1)} %param.6) | copy-start | bytes 11010052
  5.7 5.5 %collective-permute-start.1 = (bf16[16,2048]{1,0:T(8,128)(2,1)S(1)}, bf16[16,2048]{1,0:T(8,128)(2,1)S(1)}, u32[]{:S(2)}, u32[]{:S(2)}) collective-permute-start(bf16[16,2048]{1,0:T(8,128)(2,1)S(1)} %collective-permute-done), channel_id=1, source_target_pairs={{0,8},{8,16},{16,24},{24,0},{1,9},{9,17},{17,25},{25,1},{2,10},{10... | collective-permute-start | bytes 196616 | tf_op jit(solution)/shard_map/ppermute | solution.py:36
  11.2 10.3 %collective-permute-start.3 = (bf16[64,2048]{1,0:T(8,128)(2,1)S(1)}, bf16[64,2048]{1,0:T(8,128)(2,1)S(1)}, u32[]{:S(2)}, u32[]{:S(2)}) collective-permute-start(bf16[64,2048]{1,0:T(8,128)(2,1)S(1)} %bitcast.105), channel_id=1, source_target_pairs={{0,1},{1,2},{2,3},{3,4},{4,5},{5,6},{6,7},{7,0},{8,9},{9,10},{10,1... | collective-permute-start | bytes 786440 | tf_op jit(solution)/shard_map/ppermute | solution.py:36
  13.2 10.3 %collective-permute-start.7 = (bf16[64,2048]{1,0:T(8,128)(2,1)S(1)}, bf16[64,2048]{1,0:T(8,128)(2,1)S(1)}, u32[]{:S(2)}, u32[]{:S(2)}) collective-permute-start(bf16[64,2048]{1,0:T(8,128)(2,1)S(1)} %bitcast.106), channel_id=1, source_target_pairs={{0,7},{1,0},{2,1},{3,2},{4,3},{5,4},{6,5},{7,6},{8,15},{9,8},{10,9... | collective-permute-start | bytes 786440 | tf_op jit(solution)/shard_map/ppermute | solution.py:40
  20.0 2.0 %copy-start = (bf16[2048,896]{1,0:T(8,128)(2,1)S(1)}, bf16[2048,896]{1,0:T(8,128)(2,1)}, u32[]{:S(2)}) copy-start(bf16[2048,896]{1,0:T(8,128)(2,1)} %param.5) | copy-start | bytes 11010052
  22.7 7.7 %collective-permute-start.4 = (bf16[64,2048]{1,0:T(8,128)(2,1)S(1)}, bf16[64,2048]{1,0:T(8,128)(2,1)S(1)}, u32[]{:S(2)}, u32[]{:S(2)}) collective-permute-start(bf16[64,2048]{1,0:T(8,128)(2,1)S(1)} %collective-permute-done.3), channel_id=1, source_target_pairs={{0,1},{1,2},{2,3},{3,4},{4,5},{5,6},{6,7},{7,0},{8,9},{9,10},{10,1... | collective-permute-start | bytes 786440 | tf_op jit(solution)/shard_map/ppermute | solution.py:36
  24.9 7.2 %collective-permute-start.8 = (bf16[64,2048]{1,0:T(8,128)(2,1)S(1)}, bf16[64,2048]{1,0:T(8,128)(2,1)S(1)}, u32[]{:S(2)}, u32[]{:S(2)}) collective-permute-start(bf16[64,2048]{1,0:T(8,128)(2,1)S(1)} %collective-permute-done.7), channel_id=1, source_target_pairs={{0,7},{1,0},{2,1},{3,2},{4,3},{5,4},{6,5},{7,6},{8,15},{9,8},{10,9... | collective-permute-start | bytes 786440 | tf_op jit(solution)/shard_map/ppermute | solution.py:40
  31.1 8.0 %collective-permute-start.5 = (bf16[64,2048]{1,0:T(8,128)(2,1)S(1)}, bf16[64,2048]{1,0:T(8,128)(2,1)S(1)}, u32[]{:S(2)}, u32[]{:S(2)}) collective-permute-start(bf16[64,2048]{1,0:T(8,128)(2,1)S(1)} %collective-permute-done.4), channel_id=1, source_target_pairs={{0,1},{1,2},{2,3},{3,4},{4,5},{5,6},{6,7},{7,0},{8,9},{9,10},{10,1... | collective-permute-start | bytes 786440 | tf_op jit(solution)/shard_map/ppermute | solution.py:36
  33.6 7.8 %collective-permute-start.9 = (bf16[64,2048]{1,0:T(8,128)(2,1)S(1)}, bf16[64,2048]{1,0:T(8,128)(2,1)S(1)}, u32[]{:S(2)}, u32[]{:S(2)}) collective-permute-start(bf16[64,2048]{1,0:T(8,128)(2,1)S(1)} %collective-permute-done.8), channel_id=1, source_target_pairs={{0,7},{1,0},{2,1},{3,2},{4,3},{5,4},{6,5},{7,6},{8,15},{9,8},{10,9... | collective-permute-start | bytes 786440 | tf_op jit(solution)/shard_map/ppermute | solution.py:40
  39.8 7.7 %collective-permute-start.6 = (bf16[64,2048]{1,0:T(8,128)(2,1)S(1)}, bf16[64,2048]{1,0:T(8,128)(2,1)S(1)}, u32[]{:S(2)}, u32[]{:S(2)}) collective-permute-start(bf16[64,2048]{1,0:T(8,128)(2,1)S(1)} %collective-permute-done.5), channel_id=1, source_target_pairs={{0,1},{1,2},{2,3},{3,4},{4,5},{5,6},{6,7},{7,0},{8,9},{9,10},{10,1... | collective-permute-start | bytes 786440 | tf_op jit(solution)/shard_map/ppermute | solution.py:36
  49.0 1.8 %copy-start.2 = (f32[8,64,1792]{2,1,0:T(8,128)}, f32[8,64,1792]{2,1,0:T(8,128)S(1)}, u32[]{:S(2)}) copy-start(f32[8,64,1792]{2,1,0:T(8,128)S(1)} %fusion.7) | copy-start | bytes 11010052
  52.2 4.0 %collective-permute-start.10 = (f32[4,64,1792]{2,1,0:T(8,128)}, f32[4,64,1792]{2,1,0:T(8,128)S(1)}, u32[]{:S(2)}, u32[]{:S(2)}) collective-permute-start(f32[4,64,1792]{2,1,0:T(8,128)} %dynamic-slice_bitcast_fusion), channel_id=1, source_target_pairs={{0,32},{32,0},{1,33},{33,1},{2,34},{34,2},{3,35},{35,3},{4,36},{36... | collective-permute-start | bytes 5505032 | tf_op jit(solution)/shard_map/ppermute | solution.py:52
  58.1 7.7 %collective-permute-start.11 = (f32[64,896]{1,0:T(8,128)S(1)}, f32[64,896]{1,0:T(8,128)S(1)}, u32[]{:S(2)}, u32[]{:S(2)}) collective-permute-start(f32[64,896]{1,0:T(8,128)S(1)} %dynamic-slice_bitcast_fusion.2), channel_id=1, source_target_pairs={{0,64},{64,128},{128,192},{192,0},{1,65},{65,129},{129,193},{193,1... | collective-permute-start | bytes 688136 | tf_op jit(solution)/shard_map/ppermute | solution.py:20
  59.7 7.7 %collective-permute-start.14 = (f32[64,896]{1,0:T(8,128)S(1)}, f32[64,896]{1,0:T(8,128)S(1)}, u32[]{:S(2)}, u32[]{:S(2)}) collective-permute-start(f32[64,896]{1,0:T(8,128)S(1)} %dynamic-slice_bitcast_fusion.1), channel_id=1, source_target_pairs={{0,192},{64,0},{128,64},{192,128},{1,193},{65,1},{129,65},{193,129... | collective-permute-start | bytes 688136 | tf_op jit(solution)/shard_map/ppermute | solution.py:21
  65.9 6.9 %collective-permute-start.12 = (f32[64,896]{1,0:T(8,128)S(1)}, f32[64,896]{1,0:T(8,128)S(1)}, u32[]{:S(2)}, u32[]{:S(2)}) collective-permute-start(f32[64,896]{1,0:T(8,128)S(1)} %bitcast_add_fusion.6), channel_id=1, source_target_pairs={{0,64},{64,128},{128,192},{192,0},{1,65},{65,129},{129,193},{193,1... | collective-permute-start | bytes 688136 | tf_op jit(solution)/shard_map/ppermute | solution.py:20
  67.5 6.9 %collective-permute-start.15 = (f32[64,896]{1,0:T(8,128)S(1)}, f32[64,896]{1,0:T(8,128)S(1)}, u32[]{:S(2)}, u32[]{:S(2)}) collective-permute-start(f32[64,896]{1,0:T(8,128)S(1)} %bitcast_add_fusion.3), channel_id=1, source_target_pairs={{0,192},{64,0},{128,64},{192,128},{1,193},{65,1},{129,65},{193,129... | collective-permute-start | bytes 688136 | tf_op jit(solution)/shard_map/ppermute | solution.py:21
  72.8 7.2 %collective-permute-start.13 = (f32[64,896]{1,0:T(8,128)S(1)}, f32[64,896]{1,0:T(8,128)S(1)}, u32[]{:S(2)}, u32[]{:S(2)}) collective-permute-start(f32[64,896]{1,0:T(8,128)S(1)} %bitcast_add_fusion.5), channel_id=1, source_target_pairs={{0,64},{64,128},{128,192},{192,0},{1,65},{65,129},{129,193},{193,1... | collective-permute-start | bytes 688136 | tf_op jit(solution)/shard_map/ppermute | solution.py:20
  74.4 6.1 %collective-permute-start.16 = (f32[64,896]{1,0:T(8,128)S(1)}, f32[64,896]{1,0:T(8,128)S(1)}, u32[]{:S(2)}, u32[]{:S(2)}) collective-permute-start(f32[64,896]{1,0:T(8,128)S(1)} %bitcast_add_fusion.2), channel_id=1, source_target_pairs={{0,192},{64,0},{128,64},{192,128},{1,193},{65,1},{129,65},{193,129... | collective-permute-start | bytes 688136 | tf_op jit(solution)/shard_map/ppermute | solution.py:21

commit v6 on v5

--- a/solution.py
+++ b/solution.py
@@ -42,6 +42,32 @@
     return out.reshape((n * own.shape[0],) + own.shape[1:])
 
 
+def ring_rs2(x, axis, n, chunk_axis, send_dtype):
+    k = lax.axis_index(axis)
+    take = lambda i: lax.dynamic_index_in_dim(
+        x, i % n, chunk_axis, keepdims=False
+    ).astype(jnp.float32)
+    fwd = [(i, (i + 1) % n) for i in range(n)]
+    bwd = [(i, (i - 1) % n) for i in range(n)]
+    nf = n // 2
+    nb = n - 1 - nf
+    total = take(k)
+    acc = take(k + nf)
+    for s in range(nf):
+        acc = lax.ppermute(acc.astype(send_dtype), axis, fwd).astype(jnp.float32)
+        if s < nf - 1:
+            acc = acc + take(k + nf - s - 1)
+    total = total + acc
+    if nb:
+        acc = take(k - nb)
+        for s in range(nb):
+            acc = lax.ppermute(acc.astype(send_dtype), axis, bwd).astype(jnp.float32)
+            if s < nb - 1:
+                acc = acc + take(k - nb + s + 1)
+        total = total + acc
+    return total
+
+
 def embed_rs(x):
     ec = lax.axis_index("ec")
     ncore = lax.psum(1, "ec")
@@ -74,11 +100,11 @@
     activated = (jax.nn.silu(summed[:, :width]) * summed[:, width:]).astype(jnp.bfloat16)
     activated = lax.all_gather(activated, EMBED, axis=0, tiled=True)
     partial_out = jnp.dot(activated, down_weight, preferred_element_type=jnp.float32)
-    pieces = partial_out.astype(jnp.bfloat16).reshape(
-        (ny * nz, partial_out.shape[0] // (ny * nz)) + partial_out.shape[1:]
+    blocks = partial_out.reshape(
+        (nz, ny, partial_out.shape[0] // (ny * nz)) + partial_out.shape[1:]
     )
-    pieces = lax.all_to_all(pieces, ("hz", "hy"), 0, 0, tiled=True)
-    totals = pieces.astype(jnp.float32).sum(axis=0)
+    totals = ring_rs2(blocks, "hy", ny, 1, jnp.bfloat16)
+    totals = ring_rs2(totals, "hz", nz, 0, jnp.float32)
     return totals.astype(jnp.bfloat16)
 
 

time: 161 us -> 162 us (level)
  blocking collectives: 74 us -> 16.5 us
  waiting for transfers between devices: 35.1 us -> 77.7 us
  starting transfers between devices: 24.6 us -> 38.2 us
    all_to_all x1 -> x0, blocking collectives: 57.5 us -> none  [on_device(): pieces = lax.all_to_all(pieces, ('hz', 'hy'), 0, 0, tiled=True)]
    ppermute x0 -> x10, waiting for transfers between devices: none -> 42.5 us  [the longest x6 42.5 us: ring_rs2(): acc = lax.ppermute(acc.astype(send_dtype), axis, fwd).astype(jnp.float32)]
    ppermute x0 -> x10, starting transfers between devices: none -> 13.6 us  [the longest x4 13.1 us: ring_rs2(): acc = lax.ppermute(acc.astype(send_dtype), axis, bwd).astype(jnp.float32)]
  transfers between devices with their start and end apart: 17 -> 27, of which waited for: 13 -> 19; matrix products, arithmetic and copies ran while one was open for 8% -> 8% of each run, Pallas kernels for 0% -> 0%
where the time goes in v6:
time: 162 us; the launch traced here: 160 us
  waiting for transfers between devices  77.7 us (48%)
  starting transfers between devices  38.2 us (24%)
  matrix products  17.7 us (11%)
  blocking collectives  16.5 us (10%)
  local copies, waits for them, and re-layouts  5.3 us (3%)
  other arithmetic  4.45 us (3%)
    ppermute x6, waiting for transfers between devices, ring_rs2(): acc = lax.ppermute(acc.astype(send_dtype), axis, fwd).astype(jnp.float32)  42.5 us
    all_gather x1, blocking collectives, on_device(): activated = lax.all_gather(activated, EMBED, axis=0, tiled=True)  16.5 us
    ppermute x6, waiting for transfers between devices, ring_ag(): buf = lax.ppermute(buf, axis, fwd)  15.4 us
    ppermute x3, waiting for transfers between devices, ring_rs(): acc_a = lax.ppermute(acc_a, axis, fwd) + take(a, k - s - 2)  14.2 us
    ppermute x4, starting transfers between devices, ring_rs2(): acc = lax.ppermute(acc.astype(send_dtype), axis, bwd).astype(jnp.float32)  13.1 us
    ppermute x4, starting transfers between devices, ring_ag(): buf = lax.ppermute(buf, axis, bwd)  12.9 us
    dot_general x8, matrix products, on_device(): jnp.dot(v, gate_weight, preferred_element_type=jnp.float32)  7.66 us
    dot_general x8, matrix products, on_device(): jnp.dot(v, up_weight, preferred_element_type=jnp.float32)  5.67 us
  transfers between devices with their start and end apart: 27, of which 19 were waited for; matrix products, arithmetic and copies ran while one was open for 8% of the time, Pallas kernels for 0%

profile of v6, /device:TPU:2, one launch (start us, length us, event | category | flops | bytes accessed | tf_op | source)
XLA Modules:
  0.0 160.3 jit_solution(3608440869058981773)
XLA Ops:
  0.0 1.6 collective-permute-start
  1.6 1.7 %collective-permute-start.2 = (bf16[16,2048]{1,0:T(8,128)(2,1)}, bf16[16,2048]{1,0:T(8,128)(2,1)S(1)}, u32[]{:S(2)}, u32[]{:S(2)}) collective-permute-start(bf16[16,2048]{1,0:T(8,128)(2,1)} %param.4), channel_id=1, source_target_pairs={{0,24},{8,0},{16,8},{24,16},{1,25},{9,1},{17,9},{25,17},{2,26},{10... | collective-permute-start | bytes 196616 | tf_op jit(solution)/shard_map/ppermute | solution.py:40
  3.3 0.9 bitcast_dynamic-update-slice_fusion.3
  4.1 1.6 collective-permute-done
  5.7 0.4 collective-permute-start.1
  6.1 5.1 %collective-permute-done.1 = bf16[16,2048]{1,0:T(8,128)(2,1)S(1)} collective-permute-done((bf16[16,2048]{1,0:T(8,128)(2,1)S(1)}, bf16[16,2048]{1,0:T(8,128)(2,1)S(1)}, u32[]{:S(2)}, u32[]{:S(2)}) %collective-permute-start.1) | collective-permute-done | bytes 65568 | tf_op jit(solution)/shard_map/ppermute | solution.py:36
  11.2 2.0 %collective-permute-start.3 = (bf16[64,2048]{1,0:T(8,128)(2,1)S(1)}, bf16[64,2048]{1,0:T(8,128)(2,1)S(1)}, u32[]{:S(2)}, u32[]{:S(2)}) collective-permute-start(bf16[64,2048]{1,0:T(8,128)(2,1)S(1)} %bitcast.141), channel_id=1, source_target_pairs={{0,1},{1,2},{2,3},{3,4},{4,5},{5,6},{6,7},{7,0},{8,9},{9,10},{10,1... | collective-permute-start | bytes 786440 | tf_op jit(solution)/shard_map/ppermute | solution.py:36
  13.2 4.0 %collective-permute-start.7 = (bf16[64,2048]{1,0:T(8,128)(2,1)S(1)}, bf16[64,2048]{1,0:T(8,128)(2,1)S(1)}, u32[]{:S(2)}, u32[]{:S(2)}) collective-permute-start(bf16[64,2048]{1,0:T(8,128)(2,1)S(1)} %bitcast.142), channel_id=1, source_target_pairs={{0,7},{1,0},{2,1},{3,2},{4,3},{5,4},{6,5},{7,6},{8,15},{9,8},{10,9... | collective-permute-start | bytes 786440 | tf_op jit(solution)/shard_map/ppermute | solution.py:40
  17.2 2.7 %fusion.17 = f32[64,896]{1,0:T(8,128)S(1)} fusion(bf16[64,2048]{1,0:T(8,128)(2,1)S(1)} %bitcast.143, bf16[2048,896]{1,0:T(8,128)(2,1)} %param.5), kind=kOutput, calls=%fused_computation.51 | convolution fusion | flops 234881024 | bytes 4161536 | tf_op jit(solution)/shard_map/dot_general | solution.py:93
  20.0 0.7 fusion.18
  20.7 0.3 broadcast_in_dim.44
  21.1 0.4 collective-permute-done.3
  21.5 0.5 copy-done
  22.0 0.7 fusion.19
  22.8 0.7 fusion.20
  23.5 0.7 fusion.27
  24.2 0.7 fusion.28
  24.9 3.3 %collective-permute-start.8 = (bf16[64,2048]{1,0:T(8,128)(2,1)S(1)}, bf16[64,2048]{1,0:T(8,128)(2,1)S(1)}, u32[]{:S(2)}, u32[]{:S(2)}) collective-permute-start(bf16[64,2048]{1,0:T(8,128)(2,1)S(1)} %collective-permute-done.7), channel_id=1, source_target_pairs={{0,7},{1,0},{2,1},{3,2},{4,3},{5,4},{6,5},{7,6},{8,15},{9,8},{10,9... | collective-permute-start | bytes 786440 | tf_op jit(solution)/shard_map/ppermute | solution.py:40
  28.3 2.1 %collective-permute-done.4 = bf16[64,2048]{1,0:T(8,128)(2,1)S(1)} collective-permute-done((bf16[64,2048]{1,0:T(8,128)(2,1)S(1)}, bf16[64,2048]{1,0:T(8,128)(2,1)S(1)}, u32[]{:S(2)}, u32[]{:S(2)}) %collective-permute-start.4) | collective-permute-done | bytes 262176 | tf_op jit(solution)/shard_map/ppermute | solution.py:36
  30.4 0.7 fusion.21
  31.2 0.7 fusion.22
  31.9 0.2 collective-permute-done.8
  32.1 0.7 fusion.29
  32.8 0.7 fusion.30
  33.6 3.9 %collective-permute-start.9 = (bf16[64,2048]{1,0:T(8,128)(2,1)S(1)}, bf16[64,2048]{1,0:T(8,128)(2,1)S(1)}, u32[]{:S(2)}, u32[]{:S(2)}) collective-permute-start(bf16[64,2048]{1,0:T(8,128)(2,1)S(1)} %collective-permute-done.8), channel_id=1, source_target_pairs={{0,7},{1,0},{2,1},{3,2},{4,3},{5,4},{6,5},{7,6},{8,15},{9,8},{10,9... | collective-permute-start | bytes 786440 | tf_op jit(solution)/shard_map/ppermute | solution.py:40
  37.5 1.5 collective-permute-done.5
  39.1 0.7 fusion.23
  39.9 0.7 fusion.24
  40.6 0.8 collective-permute-done.9
  41.4 0.7 fusion.31
  42.1 0.7 fusion.32
  42.8 4.6 %collective-permute-done.6 = bf16[64,2048]{1,0:T(8,128)(2,1)S(1)} collective-permute-done((bf16[64,2048]{1,0:T(8,128)(2,1)S(1)}, bf16[64,2048]{1,0:T(8,128)(2,1)S(1)}, u32[]{:S(2)}, u32[]{:S(2)}) %collective-permute-start.6) | collective-permute-done | bytes 262176 | tf_op jit(solution)/shard_map/ppermute | solution.py:36
  47.4 0.7 fusion.25
  48.1 0.7 fusion.26
  49.1 1.8 %copy-done.2 = f32[8,64,1792]{2,1,0:T(8,128)} copy-done((f32[8,64,1792]{2,1,0:T(8,128)}, f32[8,64,1792]{2,1,0:T(8,128)S(1)}, u32[]{:S(2)}) %copy-start.2) | copy-done | bytes 3670040
  50.8 1.4 dynamic-slice_bitcast_fusion
  52.2 4.0 %collective-permute-done.10 = f32[4,64,1792]{2,1,0:T(8,128)S(1)} collective-permute-done((f32[4,64,1792]{2,1,0:T(8,128)}, f32[4,64,1792]{2,1,0:T(8,128)S(1)}, u32[]{:S(2)}, u32[]{:S(2)}) %collective-permute-start.10) | collective-permute-done | bytes 1835040 | tf_op jit(solution)/shard_map/ppermute | solution.py:78
  56.2 1.7 %bitcast_add_fusion = f32[4,64,1792]{2,1,0:T(8,128)S(1)} fusion(f32[4,64,1792]{2,1,0:T(8,128)S(1)} %collective-permute-done.10, f32[4,2,64,1792]{3,2,1,0:T(8,128)} %bitcast.140, s32[]{:T(128)S(6)} %select_n.221), kind=kLoop, calls=%fused_computation | loop fusion | flops 458752 | bytes 5505028 | tf_op jit(solution)/shard_map/add | solution.py:79
  57.9 0.1 fusion.16
  58.1 1.6 collective-permute-start.11
  59.7 0.6 collective-permute-start.14
  60.3 5.5 %collective-permute-done.11 = f32[64,896]{1,0:T(8,128)S(1)} collective-permute-done((f32[64,896]{1,0:T(8,128)S(1)}, f32[64,896]{1,0:T(8,128)S(1)}, u32[]{:S(2)}, u32[]{:S(2)}) %collective-permute-start.11) | collective-permute-done | bytes 229408 | tf_op jit(solution)/shard_map/ppermute | solution.py:20
  65.9 1.6 collective-permute-start.12
  67.5 0.6 collective-permute-start.15
  68.1 4.7 %collective-permute-done.12 = f32[64,896]{1,0:T(8,128)S(1)} collective-permute-done((f32[64,896]{1,0:T(8,128)S(1)}, f32[64,896]{1,0:T(8,128)S(1)}, u32[]{:S(2)}, u32[]{:S(2)}) %collective-permute-start.12) | collective-permute-done | bytes 229408 | tf_op jit(solution)/shard_map/ppermute | solution.py:20
  72.8 1.6 collective-permute-start.13
  74.4 1.6 collective-permute-start.16
  76.0 4.0 %collective-permute-done.13 = f32[64,896]{1,0:T(8,128)S(1)} collective-permute-done((f32[64,896]{1,0:T(8,128)S(1)}, f32[64,896]{1,0:T(8,128)S(1)}, u32[]{:S(2)}, u32[]{:S(2)}) %collective-permute-start.13) | collective-permute-done | bytes 229408 | tf_op jit(solution)/shard_map/ppermute | solution.py:20
  80.0 0.5 collective-permute-done.16
  80.6 16.5 %all_gather.3 = bf16[512,896]{1,0:T(8,128)(2,1)S(1)} all-gather(bf16[64,896]{1,0:T(8,128)(2,1)S(1)} %fusion.13), channel_id=1, replica_groups=mesh['ex'=4,'ec'=2,'hy'=4,'hz'=8] {'ex','ec'}, dimensions={0}, use_global_device_ids=true | all-gather | bytes 1032192 | tf_op jit(solution)/shard_map/all_gather | solution.py:101
  97.1 4.4 %fusion.33 = f32[512,2048]{1,0:T(8,128)S(1)} fusion(bf16[512,896]{1,0:T(8,128)(2,1)S(1)} %all_gather.3, bf16[896,2048]{1,0:T(8,128)(2,1)} %param.7), kind=kOutput, calls=%fused_computation.67 | convolution fusion | flops 1879048192 | bytes 8781824 | tf_op jit(solution)/shard_map/dot_general | solution.py:102
  101.5 0.2 fusion.3
  101.8 3.2 %collective-permute-start.19 = (bf16[8,16,2048]{2,1,0:T(8,128)(2,1)S(1)}, bf16[8,16,2048]{2,1,0:T(8,128)(2,1)S(1)}, u32[]{:S(2)}, u32[]{:S(2)}) collective-permute-start(bf16[8,16,2048]{2,1,0:T(8,128)(2,1)S(1)} %get-tuple-element.6), channel_id=1, source_target_pairs={{0,24},{8,0},{16,8},{24,16},{1,25},{9,1},{17,9},{25,17},{2,26},{10... | collective-permute-start | bytes 1572872 | tf_op jit(solution)/shard_map/ppermute | solution.py:64
  105.0 12.1 %collective-permute-done.17 = bf16[8,16,2048]{2,1,0:T(8,128)(2,1)S(1)} collective-permute-done((bf16[8,16,2048]{2,1,0:T(8,128)(2,1)S(1)}, bf16[8,16,2048]{2,1,0:T(8,128)(2,1)S(1)}, u32[]{:S(2)}, u32[]{:S(2)}) %collective-permute-start.17) | collective-permute-done | bytes 524320 | tf_op jit(solution)/shard_map/ppermute | solution.py:57
  117.4 14.5 %collective-permute-done.18 = bf16[8,16,2048]{2,1,0:T(8,128)(2,1)S(1)} collective-permute-done((bf16[8,16,2048]{2,1,0:T(8,128)(2,1)S(1)}, bf16[8,16,2048]{2,1,0:T(8,128)(2,1)S(1)}, u32[]{:S(2)}, u32[]{:S(2)}) %collective-permute-start.18) | collective-permute-done | bytes 524320 | tf_op jit(solution)/shard_map/ppermute | solution.py:57
  132.0 1.4 fusion.1
  133.5 3.2 %collective-permute-start.24 = (f32[16,2048]{1,0:T(8,128)S(1)}, f32[16,2048]{1,0:T(8,128)S(1)}, u32[]{:S(2)}, u32[]{:S(2)}) collective-permute-start(f32[16,2048]{1,0:T(8,128)S(1)} %get-tuple-element.14), channel_id=1, source_target_pairs={{0,7},{1,0},{2,1},{3,2},{4,3},{5,4},{6,5},{7,6},{8,15},{9,8},{10,9... | collective-permute-start | bytes 393224 | tf_op jit(solution)/shard_map/ppermute | solution.py:64
  136.7 2.9 %collective-permute-done.20 = f32[16,2048]{1,0:T(8,128)S(1)} collective-permute-done((f32[16,2048]{1,0:T(8,128)S(1)}, f32[16,2048]{1,0:T(8,128)S(1)}, u32[]{:S(2)}, u32[]{:S(2)}) %collective-permute-start.20) | collective-permute-done | bytes 131104 | tf_op jit(solution)/shard_map/ppermute | solution.py:57
  139.8 6.2 %collective-permute-done.21 = f32[16,2048]{1,0:T(8,128)S(1)} collective-permute-done((f32[16,2048]{1,0:T(8,128)S(1)}, f32[16,2048]{1,0:T(8,128)S(1)}, u32[]{:S(2)}, u32[]{:S(2)}) %collective-permute-start.21) | collective-permute-done | bytes 131104 | tf_op jit(solution)/shard_map/ppermute | solution.py:57
  146.1 3.2 %collective-permute-start.25 = (f32[16,2048]{1,0:T(8,128)S(1)}, f32[16,2048]{1,0:T(8,128)S(1)}, u32[]{:S(2)}, u32[]{:S(2)}) collective-permute-start(f32[16,2048]{1,0:T(8,128)S(1)} %get-tuple-element.12), channel_id=1, source_target_pairs={{0,7},{1,0},{2,1},{3,2},{4,3},{5,4},{6,5},{7,6},{8,15},{9,8},{10,9... | collective-permute-start | bytes 393224 | tf_op jit(solution)/shard_map/ppermute | solution.py:64
  149.3 3.9 %collective-permute-done.22 = f32[16,2048]{1,0:T(8,128)S(1)} collective-permute-done((f32[16,2048]{1,0:T(8,128)S(1)}, f32[16,2048]{1,0:T(8,128)S(1)}, u32[]{:S(2)}, u32[]{:S(2)}) %collective-permute-start.22) | collective-permute-done | bytes 131104 | tf_op jit(solution)/shard_map/ppermute | solution.py:57
  153.3 3.4 %collective-permute-start.26 = (f32[16,2048]{1,0:T(8,128)S(1)}, f32[16,2048]{1,0:T(8,128)S(1)}, u32[]{:S(2)}, u32[]{:S(2)}) collective-permute-start(f32[16,2048]{1,0:T(8,128)S(1)} %get-tuple-element.10), channel_id=1, source_target_pairs={{0,7},{1,0},{2,1},{3,2},{4,3},{5,4},{6,5},{7,6},{8,15},{9,8},{10,9... | collective-permute-start | bytes 393224 | tf_op jit(solution)/shard_map/ppermute | solution.py:64
  156.8 2.9 %collective-permute-done.23 = f32[16,2048]{1,0:T(8,128)S(1)} collective-permute-done((f32[16,2048]{1,0:T(8,128)S(1)}, f32[16,2048]{1,0:T(8,128)S(1)}, u32[]{:S(2)}, u32[]{:S(2)}) %collective-permute-start.23) | collective-permute-done | bytes 131104 | tf_op jit(solution)/shard_map/ppermute | solution.py:57
  159.6 0.7 fusion.15
  (48 shorter events, 1.6 us)
Async XLA Ops:
  0.0 5.7 %collective-permute-start = (bf16[16,2048]{1,0:T(8,128)(2,1)}, bf16[16,2048]{1,0:T(8,128)(2,1)S(1)}, u32[]{:S(2)}, u32[]{:S(2)}) collective-permute-start(bf16[16,2048]{1,0:T(8,128)(2,1)} %param.4), channel_id=1, source_target_pairs={{0,8},{8,16},{16,24},{24,0},{1,9},{9,17},{17,25},{25,1},{2,10},{10... | collective-permute-start | bytes 196616 | tf_op jit(solution)/shard_map/ppermute | solution.py:36
  1.6 9.6 %collective-permute-start.2 = (bf16[16,2048]{1,0:T(8,128)(2,1)}, bf16[16,2048]{1,0:T(8,128)(2,1)S(1)}, u32[]{:S(2)}, u32[]{:S(2)}) collective-permute-start(bf16[16,2048]{1,0:T(8,128)(2,1)} %param.4), channel_id=1, source_target_pairs={{0,24},{8,0},{16,8},{24,16},{1,25},{9,1},{17,9},{25,17},{2,26},{10... | collective-permute-start | bytes 196616 | tf_op jit(solution)/shard_map/ppermute | solution.py:40
  4.1 15.9 %copy-start.1 = (bf16[2048,896]{1,0:T(8,128)(2,1)S(1)}, bf16[2048,896]{1,0:T(8,128)(2,1)}, u32[]{:S(2)}) copy-start(bf16[2048,896]{1,0:T(8,128)(2,1)} %param.6) | copy-start | bytes 11010052
  5.7 5.5 %collective-permute-start.1 = (bf16[16,2048]{1,0:T(8,128)(2,1)S(1)}, bf16[16,2048]{1,0:T(8,128)(2,1)S(1)}, u32[]{:S(2)}, u32[]{:S(2)}) collective-permute-start(bf16[16,2048]{1,0:T(8,128)(2,1)S(1)} %collective-permute-done), channel_id=1, source_target_pairs={{0,8},{8,16},{16,24},{24,0},{1,9},{9,17},{17,25},{25,1},{2,10},{10... | collective-permute-start | bytes 196616 | tf_op jit(solution)/shard_map/ppermute | solution.py:36
  11.2 10.3 %collective-permute-start.3 = (bf16[64,2048]{1,0:T(8,128)(2,1)S(1)}, bf16[64,2048]{1,0:T(8,128)(2,1)S(1)}, u32[]{:S(2)}, u32[]{:S(2)}) collective-permute-start(bf16[64,2048]{1,0:T(8,128)(2,1)S(1)} %bitcast.141), channel_id=1, source_target_pairs={{0,1},{1,2},{2,3},{3,4},{4,5},{5,6},{6,7},{7,0},{8,9},{9,10},{10,1... | collective-permute-start | bytes 786440 | tf_op jit(solution)/shard_map/ppermute | solution.py:36
  13.2 10.3 %collective-permute-start.7 = (bf16[64,2048]{1,0:T(8,128)(2,1)S(1)}, bf16[64,2048]{1,0:T(8,128)(2,1)S(1)}, u32[]{:S(2)}, u32[]{:S(2)}) collective-permute-start(bf16[64,2048]{1,0:T(8,128)(2,1)S(1)} %bitcast.142), channel_id=1, source_target_pairs={{0,7},{1,0},{2,1},{3,2},{4,3},{5,4},{6,5},{7,6},{8,15},{9,8},{10,9... | collective-permute-start | bytes 786440 | tf_op jit(solution)/shard_map/ppermute | solution.py:40
  20.0 2.0 %copy-start = (bf16[2048,896]{1,0:T(8,128)(2,1)S(1)}, bf16[2048,896]{1,0:T(8,128)(2,1)}, u32[]{:S(2)}) copy-start(bf16[2048,896]{1,0:T(8,128)(2,1)} %param.5) | copy-start | bytes 11010052
  22.7 7.7 %collective-permute-start.4 = (bf16[64,2048]{1,0:T(8,128)(2,1)S(1)}, bf16[64,2048]{1,0:T(8,128)(2,1)S(1)}, u32[]{:S(2)}, u32[]{:S(2)}) collective-permute-start(bf16[64,2048]{1,0:T(8,128)(2,1)S(1)} %collective-permute-done.3), channel_id=1, source_target_pairs={{0,1},{1,2},{2,3},{3,4},{4,5},{5,6},{6,7},{7,0},{8,9},{9,10},{10,1... | collective-permute-start | bytes 786440 | tf_op jit(solution)/shard_map/ppermute | solution.py:36
  24.9 7.2 %collective-permute-start.8 = (bf16[64,2048]{1,0:T(8,128)(2,1)S(1)}, bf16[64,2048]{1,0:T(8,128)(2,1)S(1)}, u32[]{:S(2)}, u32[]{:S(2)}) collective-permute-start(bf16[64,2048]{1,0:T(8,128)(2,1)S(1)} %collective-permute-done.7), channel_id=1, source_target_pairs={{0,7},{1,0},{2,1},{3,2},{4,3},{5,4},{6,5},{7,6},{8,15},{9,8},{10,9... | collective-permute-start | bytes 786440 | tf_op jit(solution)/shard_map/ppermute | solution.py:40
  31.1 8.0 %collective-permute-start.5 = (bf16[64,2048]{1,0:T(8,128)(2,1)S(1)}, bf16[64,2048]{1,0:T(8,128)(2,1)S(1)}, u32[]{:S(2)}, u32[]{:S(2)}) collective-permute-start(bf16[64,2048]{1,0:T(8,128)(2,1)S(1)} %collective-permute-done.4), channel_id=1, source_target_pairs={{0,1},{1,2},{2,3},{3,4},{4,5},{5,6},{6,7},{7,0},{8,9},{9,10},{10,1... | collective-permute-start | bytes 786440 | tf_op jit(solution)/shard_map/ppermute | solution.py:36
  33.6 7.8 %collective-permute-start.9 = (bf16[64,2048]{1,0:T(8,128)(2,1)S(1)}, bf16[64,2048]{1,0:T(8,128)(2,1)S(1)}, u32[]{:S(2)}, u32[]{:S(2)}) collective-permute-start(bf16[64,2048]{1,0:T(8,128)(2,1)S(1)} %collective-permute-done.8), channel_id=1, source_target_pairs={{0,7},{1,0},{2,1},{3,2},{4,3},{5,4},{6,5},{7,6},{8,15},{9,8},{10,9... | collective-permute-start | bytes 786440 | tf_op jit(solution)/shard_map/ppermute | solution.py:40
  39.8 7.7 %collective-permute-start.6 = (bf16[64,2048]{1,0:T(8,128)(2,1)S(1)}, bf16[64,2048]{1,0:T(8,128)(2,1)S(1)}, u32[]{:S(2)}, u32[]{:S(2)}) collective-permute-start(bf16[64,2048]{1,0:T(8,128)(2,1)S(1)} %collective-permute-done.5), channel_id=1, source_target_pairs={{0,1},{1,2},{2,3},{3,4},{4,5},{5,6},{6,7},{7,0},{8,9},{9,10},{10,1... | collective-permute-start | bytes 786440 | tf_op jit(solution)/shard_map/ppermute | solution.py:36
  49.0 1.8 %copy-start.2 = (f32[8,64,1792]{2,1,0:T(8,128)}, f32[8,64,1792]{2,1,0:T(8,128)S(1)}, u32[]{:S(2)}) copy-start(f32[8,64,1792]{2,1,0:T(8,128)S(1)} %fusion.11) | copy-start | bytes 11010052
  52.2 4.0 %collective-permute-start.10 = (f32[4,64,1792]{2,1,0:T(8,128)}, f32[4,64,1792]{2,1,0:T(8,128)S(1)}, u32[]{:S(2)}, u32[]{:S(2)}) collective-permute-start(f32[4,64,1792]{2,1,0:T(8,128)} %dynamic-slice_bitcast_fusion), channel_id=1, source_target_pairs={{0,32},{32,0},{1,33},{33,1},{2,34},{34,2},{3,35},{35,3},{4,36},{36... | collective-permute-start | bytes 5505032 | tf_op jit(solution)/shard_map/ppermute | solution.py:78
  58.1 7.7 %collective-permute-start.11 = (f32[64,896]{1,0:T(8,128)S(1)}, f32[64,896]{1,0:T(8,128)S(1)}, u32[]{:S(2)}, u32[]{:S(2)}) collective-permute-start(f32[64,896]{1,0:T(8,128)S(1)} %dynamic-slice_bitcast_fusion.2), channel_id=1, source_target_pairs={{0,64},{64,128},{128,192},{192,0},{1,65},{65,129},{129,193},{193,1... | collective-permute-start | bytes 688136 | tf_op jit(solution)/shard_map/ppermute | solution.py:20
  59.7 7.7 %collective-permute-start.14 = (f32[64,896]{1,0:T(8,128)S(1)}, f32[64,896]{1,0:T(8,128)S(1)}, u32[]{:S(2)}, u32[]{:S(2)}) collective-permute-start(f32[64,896]{1,0:T(8,128)S(1)} %dynamic-slice_bitcast_fusion.1), channel_id=1, source_target_pairs={{0,192},{64,0},{128,64},{192,128},{1,193},{65,1},{129,65},{193,129... | collective-permute-start | bytes 688136 | tf_op jit(solution)/shard_map/ppermute | solution.py:21
  65.9 6.9 %collective-permute-start.12 = (f32[64,896]{1,0:T(8,128)S(1)}, f32[64,896]{1,0:T(8,128)S(1)}, u32[]{:S(2)}, u32[]{:S(2)}) collective-permute-start(f32[64,896]{1,0:T(8,128)S(1)} %bitcast_add_fusion.8), channel_id=1, source_target_pairs={{0,64},{64,128},{128,192},{192,0},{1,65},{65,129},{129,193},{193,1... | collective-permute-start | bytes 688136 | tf_op jit(solution)/shard_map/ppermute | solution.py:20
  67.5 6.9 %collective-permute-start.15 = (f32[64,896]{1,0:T(8,128)S(1)}, f32[64,896]{1,0:T(8,128)S(1)}, u32[]{:S(2)}, u32[]{:S(2)}) collective-permute-start(f32[64,896]{1,0:T(8,128)S(1)} %bitcast_add_fusion.5), channel_id=1, source_target_pairs={{0,192},{64,0},{128,64},{192,128},{1,193},{65,1},{129,65},{193,129... | collective-permute-start | bytes 688136 | tf_op jit(solution)/shard_map/ppermute | solution.py:21
  72.8 7.2 %collective-permute-start.13 = (f32[64,896]{1,0:T(8,128)S(1)}, f32[64,896]{1,0:T(8,128)S(1)}, u32[]{:S(2)}, u32[]{:S(2)}) collective-permute-start(f32[64,896]{1,0:T(8,128)S(1)} %bitcast_add_fusion.7), channel_id=1, source_target_pairs={{0,64},{64,128},{128,192},{192,0},{1,65},{65,129},{129,193},{193,1... | collective-permute-start | bytes 688136 | tf_op jit(solution)/shard_map/ppermute | solution.py:20
  74.4 6.1 %collective-permute-start.16 = (f32[64,896]{1,0:T(8,128)S(1)}, f32[64,896]{1,0:T(8,128)S(1)}, u32[]{:S(2)}, u32[]{:S(2)}) collective-permute-start(f32[64,896]{1,0:T(8,128)S(1)} %bitcast_add_fusion.4), channel_id=1, source_target_pairs={{0,192},{64,0},{128,64},{192,128},{1,193},{65,1},{129,65},{193,129... | collective-permute-start | bytes 688136 | tf_op jit(solution)/shard_map/ppermute | solution.py:21
  101.5 15.6 %copy-start.3 = (f32[512,2048]{1,0:T(8,128)}, f32[512,2048]{1,0:T(8,128)S(1)}, u32[]{:S(2)}) copy-start(f32[512,2048]{1,0:T(8,128)S(1)} %fusion.33) | copy-start | bytes 12582916
  101.7 15.5 %collective-permute-start.17 = (bf16[8,16,2048]{2,1,0:T(8,128)(2,1)S(1)}, bf16[8,16,2048]{2,1,0:T(8,128)(2,1)S(1)}, u32[]{:S(2)}, u32[]{:S(2)}) collective-permute-start(bf16[8,16,2048]{2,1,0:T(8,128)(2,1)S(1)} %get-tuple-element.5), channel_id=1, source_target_pairs={{0,8},{8,16},{16,24},{24,0},{1,9},{9,17},{17,25},{25,1},{2,10},{10... | collective-permute-start | bytes 1572872 | tf_op jit(solution)/shard_map/ppermute | solution.py:57
  101.8 15.6 %collective-permute-start.19 = (bf16[8,16,2048]{2,1,0:T(8,128)(2,1)S(1)}, bf16[8,16,2048]{2,1,0:T(8,128)(2,1)S(1)}, u32[]{:S(2)}, u32[]{:S(2)}) collective-permute-start(bf16[8,16,2048]{2,1,0:T(8,128)(2,1)S(1)} %get-tuple-element.6), channel_id=1, source_target_pairs={{0,24},{8,0},{16,8},{24,16},{1,25},{9,1},{17,9},{25,17},{2,26},{10... | collective-permute-start | bytes 1572872 | tf_op jit(solution)/shard_map/ppermute | solution.py:64
  117.3 14.7 %collective-permute-start.18 = (bf16[8,16,2048]{2,1,0:T(8,128)(2,1)S(1)}, bf16[8,16,2048]{2,1,0:T(8,128)(2,1)S(1)}, u32[]{:S(2)}, u32[]{:S(2)}) collective-permute-start(bf16[8,16,2048]{2,1,0:T(8,128)(2,1)S(1)} %fusion), channel_id=1, source_target_pairs={{0,8},{8,16},{16,24},{24,0},{1,9},{9,17},{17,25},{25,1},{2,10},{10... | collective-permute-start | bytes 1572872 | tf_op jit(solution)/shard_map/ppermute | solution.py:57
  133.4 6.3 %collective-permute-start.20 = (f32[16,2048]{1,0:T(8,128)S(1)}, f32[16,2048]{1,0:T(8,128)S(1)}, u32[]{:S(2)}, u32[]{:S(2)}) collective-permute-start(f32[16,2048]{1,0:T(8,128)S(1)} %get-tuple-element.13), channel_id=1, source_target_pairs={{0,1},{1,2},{2,3},{3,4},{4,5},{5,6},{6,7},{7,0},{8,9},{9,10},{10,1... | collective-permute-start | bytes 393224 | tf_op jit(solution)/shard_map/ppermute | solution.py:57
  133.5 6.3 %collective-permute-start.24 = (f32[16,2048]{1,0:T(8,128)S(1)}, f32[16,2048]{1,0:T(8,128)S(1)}, u32[]{:S(2)}, u32[]{:S(2)}) collective-permute-start(f32[16,2048]{1,0:T(8,128)S(1)} %get-tuple-element.14), channel_id=1, source_target_pairs={{0,7},{1,0},{2,1},{3,2},{4,3},{5,4},{6,5},{7,6},{8,15},{9,8},{10,9... | collective-permute-start | bytes 393224 | tf_op jit(solution)/shard_map/ppermute | solution.py:64
  139.7 6.3 %collective-permute-start.21 = (f32[16,2048]{1,0:T(8,128)S(1)}, f32[16,2048]{1,0:T(8,128)S(1)}, u32[]{:S(2)}, u32[]{:S(2)}) collective-permute-start(f32[16,2048]{1,0:T(8,128)S(1)} %bitcast_add_fusion.13), channel_id=1, source_target_pairs={{0,1},{1,2},{2,3},{3,4},{4,5},{5,6},{6,7},{7,0},{8,9},{9,10},{10,1... | collective-permute-start | bytes 393224 | tf_op jit(solution)/shard_map/ppermute | solution.py:57
  146.0 7.2 %collective-permute-start.22 = (f32[16,2048]{1,0:T(8,128)S(1)}, f32[16,2048]{1,0:T(8,128)S(1)}, u32[]{:S(2)}, u32[]{:S(2)}) collective-permute-start(f32[16,2048]{1,0:T(8,128)S(1)} %get-tuple-element.11), channel_id=1, source_target_pairs={{0,1},{1,2},{2,3},{3,4},{4,5},{5,6},{6,7},{7,0},{8,9},{9,10},{10,1... | collective-permute-start | bytes 393224 | tf_op jit(solution)/shard_map/ppermute | solution.py:57
  146.1 7.1 %collective-permute-start.25 = (f32[16,2048]{1,0:T(8,128)S(1)}, f32[16,2048]{1,0:T(8,128)S(1)}, u32[]{:S(2)}, u32[]{:S(2)}) collective-permute-start(f32[16,2048]{1,0:T(8,128)S(1)} %get-tuple-element.12), channel_id=1, source_target_pairs={{0,7},{1,0},{2,1},{3,2},{4,3},{5,4},{6,5},{7,6},{8,15},{9,8},{10,9... | collective-permute-start | bytes 393224 | tf_op jit(solution)/shard_map/ppermute | solution.py:64
  153.2 6.4 %collective-permute-start.23 = (f32[16,2048]{1,0:T(8,128)S(1)}, f32[16,2048]{1,0:T(8,128)S(1)}, u32[]{:S(2)}, u32[]{:S(2)}) collective-permute-start(f32[16,2048]{1,0:T(8,128)S(1)} %get-tuple-element.9), channel_id=1, source_target_pairs={{0,1},{1,2},{2,3},{3,4},{4,5},{5,6},{6,7},{7,0},{8,9},{9,10},{10,1... | collective-permute-start | bytes 393224 | tf_op jit(solution)/shard_map/ppermute | solution.py:57
  153.3 6.3 %collective-permute-start.26 = (f32[16,2048]{1,0:T(8,128)S(1)}, f32[16,2048]{1,0:T(8,128)S(1)}, u32[]{:S(2)}, u32[]{:S(2)}) collective-permute-start(f32[16,2048]{1,0:T(8,128)S(1)} %get-tuple-element.10), channel_id=1, source_target_pairs={{0,7},{1,0},{2,1},{3,2},{4,3},{5,4},{6,5},{7,6},{8,15},{9,8},{10,9... | collective-permute-start | bytes 393224 | tf_op jit(solution)/shard_map/ppermute | solution.py:64

commit v7 on v6

--- a/solution.py
+++ b/solution.py
@@ -100,11 +100,10 @@
     activated = (jax.nn.silu(summed[:, :width]) * summed[:, width:]).astype(jnp.bfloat16)
     activated = lax.all_gather(activated, EMBED, axis=0, tiled=True)
     partial_out = jnp.dot(activated, down_weight, preferred_element_type=jnp.float32)
-    blocks = partial_out.reshape(
-        (nz, ny, partial_out.shape[0] // (ny * nz)) + partial_out.shape[1:]
-    )
-    totals = ring_rs2(blocks, "hy", ny, 1, jnp.bfloat16)
-    totals = ring_rs2(totals, "hz", nz, 0, jnp.float32)
+    blocks = partial_out.reshape((nz, -1) + partial_out.shape[1:])
+    totals = ring_rs2(blocks, "hz", nz, 0, jnp.bfloat16)
+    totals = totals.reshape((ny, -1) + totals.shape[1:])
+    totals = ring_rs2(totals, "hy", ny, 0, jnp.float32)
     return totals.astype(jnp.bfloat16)
 
 

time: 162 us -> 154 us (0.951)
  waiting for transfers between devices: 77.7 us -> 69.6 us
    ppermute x6, waiting for transfers between devices: 42.5 us -> 34.4 us  [ring_rs2(): acc = lax.ppermute(acc.astype(send_dtype), axis, fwd).astype(jnp.float32)]
  transfers between devices with their start and end apart: 27 -> 27, of which waited for: 19 -> 19; matrix products, arithmetic and copies ran while one was open for 8% -> 9% of each run, Pallas kernels for 0% -> 0%
where the time goes in v7:
time: 154 us; the launch traced here: 152 us
  waiting for transfers between devices  69.6 us (45%)
  starting transfers between devices  38 us (25%)
  matrix products  17.7 us (11%)
  blocking collectives  16.5 us (11%)
  local copies, waits for them, and re-layouts  5.21 us (3%)
  other arithmetic  4.29 us (3%)
    ppermute x6, waiting for transfers between devices, ring_rs2(): acc = lax.ppermute(acc.astype(send_dtype), axis, fwd).astype(jnp.float32)  34.4 us
    all_gather x1, blocking collectives, on_device(): activated = lax.all_gather(activated, EMBED, axis=0, tiled=True)  16.5 us
    ppermute x6, waiting for transfers between devices, ring_ag(): buf = lax.ppermute(buf, axis, fwd)  15.4 us
    ppermute x3, waiting for transfers between devices, ring_rs(): acc_a = lax.ppermute(acc_a, axis, fwd) + take(a, k - s - 2)  14.2 us
    ppermute x4, starting transfers between devices, ring_ag(): buf = lax.ppermute(buf, axis, bwd)  12.9 us
    ppermute x4, starting transfers between devices, ring_rs2(): acc = lax.ppermute(acc.astype(send_dtype), axis, bwd).astype(jnp.float32)  12.9 us
    dot_general x8, matrix products, on_device(): jnp.dot(v, gate_weight, preferred_element_type=jnp.float32)  7.66 us
    dot_general x8, matrix products, on_device(): jnp.dot(v, up_weight, preferred_element_type=jnp.float32)  5.67 us
  transfers between devices with their start and end apart: 27, of which 19 were waited for; matrix products, arithmetic and copies ran while one was open for 9% of the time, Pallas kernels for 0%

profile of v7, /device:TPU:2, one launch (start us, length us, event | category | flops | bytes accessed | tf_op | source)
XLA Modules:
  0.0 151.7 jit_solution(2826318713798246807)
XLA Ops:
  0.0 1.6 %collective-permute-start = (bf16[16,2048]{1,0:T(8,128)(2,1)}, bf16[16,2048]{1,0:T(8,128)(2,1)S(1)}, u32[]{:S(2)}, u32[]{:S(2)}) collective-permute-start(bf16[16,2048]{1,0:T(8,128)(2,1)} %param.4), channel_id=1, source_target_pairs={{0,8},{8,16},{16,24},{24,0},{1,9},{9,17},{17,25},{25,1},{2,10},{10... | collective-permute-start | bytes 196616 | tf_op jit(solution)/shard_map/ppermute | solution.py:36
  1.6 1.7 %collective-permute-start.2 = (bf16[16,2048]{1,0:T(8,128)(2,1)}, bf16[16,2048]{1,0:T(8,128)(2,1)S(1)}, u32[]{:S(2)}, u32[]{:S(2)}) collective-permute-start(bf16[16,2048]{1,0:T(8,128)(2,1)} %param.4), channel_id=1, source_target_pairs={{0,24},{8,0},{16,8},{24,16},{1,25},{9,1},{17,9},{25,17},{2,26},{10... | collective-permute-start | bytes 196616 | tf_op jit(solution)/shard_map/ppermute | solution.py:40
  3.3 0.9 bitcast_dynamic-update-slice_fusion.3
  4.1 1.6 %collective-permute-done = bf16[16,2048]{1,0:T(8,128)(2,1)S(1)} collective-permute-done((bf16[16,2048]{1,0:T(8,128)(2,1)}, bf16[16,2048]{1,0:T(8,128)(2,1)S(1)}, u32[]{:S(2)}, u32[]{:S(2)}) %collective-permute-start) | collective-permute-done | bytes 65568 | tf_op jit(solution)/shard_map/ppermute | solution.py:36
  5.7 0.4 collective-permute-start.1
  6.1 5.1 %collective-permute-done.1 = bf16[16,2048]{1,0:T(8,128)(2,1)S(1)} collective-permute-done((bf16[16,2048]{1,0:T(8,128)(2,1)S(1)}, bf16[16,2048]{1,0:T(8,128)(2,1)S(1)}, u32[]{:S(2)}, u32[]{:S(2)}) %collective-permute-start.1) | collective-permute-done | bytes 65568 | tf_op jit(solution)/shard_map/ppermute | solution.py:36
  11.2 2.0 %collective-permute-start.3 = (bf16[64,2048]{1,0:T(8,128)(2,1)S(1)}, bf16[64,2048]{1,0:T(8,128)(2,1)S(1)}, u32[]{:S(2)}, u32[]{:S(2)}) collective-permute-start(bf16[64,2048]{1,0:T(8,128)(2,1)S(1)} %bitcast.151), channel_id=1, source_target_pairs={{0,1},{1,2},{2,3},{3,4},{4,5},{5,6},{6,7},{7,0},{8,9},{9,10},{10,1... | collective-permute-start | bytes 786440 | tf_op jit(solution)/shard_map/ppermute | solution.py:36
  13.2 4.0 %collective-permute-start.7 = (bf16[64,2048]{1,0:T(8,128)(2,1)S(1)}, bf16[64,2048]{1,0:T(8,128)(2,1)S(1)}, u32[]{:S(2)}, u32[]{:S(2)}) collective-permute-start(bf16[64,2048]{1,0:T(8,128)(2,1)S(1)} %bitcast.152), channel_id=1, source_target_pairs={{0,7},{1,0},{2,1},{3,2},{4,3},{5,4},{6,5},{7,6},{8,15},{9,8},{10,9... | collective-permute-start | bytes 786440 | tf_op jit(solution)/shard_map/ppermute | solution.py:40
  17.2 2.7 %fusion.21 = f32[64,896]{1,0:T(8,128)S(1)} fusion(bf16[64,2048]{1,0:T(8,128)(2,1)S(1)} %bitcast.153, bf16[2048,896]{1,0:T(8,128)(2,1)} %param.5), kind=kOutput, calls=%fused_computation.55 | convolution fusion | flops 234881024 | bytes 4161536 | tf_op jit(solution)/shard_map/dot_general | solution.py:93
  20.0 0.7 fusion.22
  20.7 0.3 broadcast_in_dim.44
  21.1 0.4 collective-permute-done.3
  21.5 0.5 copy-done
  22.0 0.7 fusion.23
  22.8 0.7 fusion.24
  23.5 0.7 fusion.31
  24.2 0.7 fusion.32
  24.9 3.3 %collective-permute-start.8 = (bf16[64,2048]{1,0:T(8,128)(2,1)S(1)}, bf16[64,2048]{1,0:T(8,128)(2,1)S(1)}, u32[]{:S(2)}, u32[]{:S(2)}) collective-permute-start(bf16[64,2048]{1,0:T(8,128)(2,1)S(1)} %collective-permute-done.7), channel_id=1, source_target_pairs={{0,7},{1,0},{2,1},{3,2},{4,3},{5,4},{6,5},{7,6},{8,15},{9,8},{10,9... | collective-permute-start | bytes 786440 | tf_op jit(solution)/shard_map/ppermute | solution.py:40
  28.3 2.1 %collective-permute-done.4 = bf16[64,2048]{1,0:T(8,128)(2,1)S(1)} collective-permute-done((bf16[64,2048]{1,0:T(8,128)(2,1)S(1)}, bf16[64,2048]{1,0:T(8,128)(2,1)S(1)}, u32[]{:S(2)}, u32[]{:S(2)}) %collective-permute-start.4) | collective-permute-done | bytes 262176 | tf_op jit(solution)/shard_map/ppermute | solution.py:36
  30.4 0.7 fusion.25
  31.2 0.7 fusion.26
  31.9 0.2 collective-permute-done.8
  32.1 0.7 fusion.33
  32.8 0.7 fusion.34
  33.6 3.9 %collective-permute-start.9 = (bf16[64,2048]{1,0:T(8,128)(2,1)S(1)}, bf16[64,2048]{1,0:T(8,128)(2,1)S(1)}, u32[]{:S(2)}, u32[]{:S(2)}) collective-permute-start(bf16[64,2048]{1,0:T(8,128)(2,1)S(1)} %collective-permute-done.8), channel_id=1, source_target_pairs={{0,7},{1,0},{2,1},{3,2},{4,3},{5,4},{6,5},{7,6},{8,15},{9,8},{10,9... | collective-permute-start | bytes 786440 | tf_op jit(solution)/shard_map/ppermute | solution.py:40
  37.5 1.5 %collective-permute-done.5 = bf16[64,2048]{1,0:T(8,128)(2,1)S(1)} collective-permute-done((bf16[64,2048]{1,0:T(8,128)(2,1)S(1)}, bf16[64,2048]{1,0:T(8,128)(2,1)S(1)}, u32[]{:S(2)}, u32[]{:S(2)}) %collective-permute-start.5) | collective-permute-done | bytes 262176 | tf_op jit(solution)/shard_map/ppermute | solution.py:36
  39.1 0.7 fusion.27
  39.9 0.7 fusion.28
  40.6 0.8 collective-permute-done.9
  41.4 0.7 fusion.35
  42.1 0.7 fusion.36
  42.8 4.6 %collective-permute-done.6 = bf16[64,2048]{1,0:T(8,128)(2,1)S(1)} collective-permute-done((bf16[64,2048]{1,0:T(8,128)(2,1)S(1)}, bf16[64,2048]{1,0:T(8,128)(2,1)S(1)}, u32[]{:S(2)}, u32[]{:S(2)}) %collective-permute-start.6) | collective-permute-done | bytes 262176 | tf_op jit(solution)/shard_map/ppermute | solution.py:36
  47.4 0.7 fusion.29
  48.1 0.7 fusion.30
  49.1 1.8 %copy-done.2 = f32[8,64,1792]{2,1,0:T(8,128)} copy-done((f32[8,64,1792]{2,1,0:T(8,128)}, f32[8,64,1792]{2,1,0:T(8,128)S(1)}, u32[]{:S(2)}) %copy-start.2) | copy-done | bytes 3670040
  50.8 1.4 dynamic-slice_bitcast_fusion
  52.2 4.0 %collective-permute-done.10 = f32[4,64,1792]{2,1,0:T(8,128)S(1)} collective-permute-done((f32[4,64,1792]{2,1,0:T(8,128)}, f32[4,64,1792]{2,1,0:T(8,128)S(1)}, u32[]{:S(2)}, u32[]{:S(2)}) %collective-permute-start.10) | collective-permute-done | bytes 1835040 | tf_op jit(solution)/shard_map/ppermute | solution.py:78
  56.2 1.7 %bitcast_add_fusion = f32[4,64,1792]{2,1,0:T(8,128)S(1)} fusion(f32[4,64,1792]{2,1,0:T(8,128)S(1)} %collective-permute-done.10, f32[4,2,64,1792]{3,2,1,0:T(8,128)} %bitcast.145, s32[]{:T(128)S(6)} %select_n.221), kind=kLoop, calls=%fused_computation | loop fusion | flops 458752 | bytes 5505028 | tf_op jit(solution)/shard_map/add | solution.py:79
  57.9 0.1 fusion.20
  58.1 1.6 %collective-permute-start.11 = (f32[64,896]{1,0:T(8,128)S(1)}, f32[64,896]{1,0:T(8,128)S(1)}, u32[]{:S(2)}, u32[]{:S(2)}) collective-permute-start(f32[64,896]{1,0:T(8,128)S(1)} %dynamic-slice_bitcast_fusion.2), channel_id=1, source_target_pairs={{0,64},{64,128},{128,192},{192,0},{1,65},{65,129},{129,193},{193,1... | collective-permute-start | bytes 688136 | tf_op jit(solution)/shard_map/ppermute | solution.py:20
  59.7 0.6 collective-permute-start.14
  60.3 5.5 %collective-permute-done.11 = f32[64,896]{1,0:T(8,128)S(1)} collective-permute-done((f32[64,896]{1,0:T(8,128)S(1)}, f32[64,896]{1,0:T(8,128)S(1)}, u32[]{:S(2)}, u32[]{:S(2)}) %collective-permute-start.11) | collective-permute-done | bytes 229408 | tf_op jit(solution)/shard_map/ppermute | solution.py:20
  65.9 1.6 %collective-permute-start.12 = (f32[64,896]{1,0:T(8,128)S(1)}, f32[64,896]{1,0:T(8,128)S(1)}, u32[]{:S(2)}, u32[]{:S(2)}) collective-permute-start(f32[64,896]{1,0:T(8,128)S(1)} %bitcast_add_fusion.12), channel_id=1, source_target_pairs={{0,64},{64,128},{128,192},{192,0},{1,65},{65,129},{129,193},{193,1... | collective-permute-start | bytes 688136 | tf_op jit(solution)/shard_map/ppermute | solution.py:20
  67.5 0.6 collective-permute-start.15
  68.1 4.7 %collective-permute-done.12 = f32[64,896]{1,0:T(8,128)S(1)} collective-permute-done((f32[64,896]{1,0:T(8,128)S(1)}, f32[64,896]{1,0:T(8,128)S(1)}, u32[]{:S(2)}, u32[]{:S(2)}) %collective-permute-start.12) | collective-permute-done | bytes 229408 | tf_op jit(solution)/shard_map/ppermute | solution.py:20
  72.8 1.6 %collective-permute-start.13 = (f32[64,896]{1,0:T(8,128)S(1)}, f32[64,896]{1,0:T(8,128)S(1)}, u32[]{:S(2)}, u32[]{:S(2)}) collective-permute-start(f32[64,896]{1,0:T(8,128)S(1)} %bitcast_add_fusion.11), channel_id=1, source_target_pairs={{0,64},{64,128},{128,192},{192,0},{1,65},{65,129},{129,193},{193,1... | collective-permute-start | bytes 688136 | tf_op jit(solution)/shard_map/ppermute | solution.py:20
  74.4 1.6 %collective-permute-start.16 = (f32[64,896]{1,0:T(8,128)S(1)}, f32[64,896]{1,0:T(8,128)S(1)}, u32[]{:S(2)}, u32[]{:S(2)}) collective-permute-start(f32[64,896]{1,0:T(8,128)S(1)} %bitcast_add_fusion.8), channel_id=1, source_target_pairs={{0,192},{64,0},{128,64},{192,128},{1,193},{65,1},{129,65},{193,129... | collective-permute-start | bytes 688136 | tf_op jit(solution)/shard_map/ppermute | solution.py:21
  76.0 4.0 %collective-permute-done.13 = f32[64,896]{1,0:T(8,128)S(1)} collective-permute-done((f32[64,896]{1,0:T(8,128)S(1)}, f32[64,896]{1,0:T(8,128)S(1)}, u32[]{:S(2)}, u32[]{:S(2)}) %collective-permute-start.13) | collective-permute-done | bytes 229408 | tf_op jit(solution)/shard_map/ppermute | solution.py:20
  80.0 0.5 collective-permute-done.16
  80.6 16.5 %all_gather.3 = bf16[512,896]{1,0:T(8,128)(2,1)S(1)} all-gather(bf16[64,896]{1,0:T(8,128)(2,1)S(1)} %fusion.17), channel_id=1, replica_groups=mesh['ex'=4,'ec'=2,'hy'=4,'hz'=8] {'ex','ec'}, dimensions={0}, use_global_device_ids=true | all-gather | bytes 1032192 | tf_op jit(solution)/shard_map/all_gather | solution.py:101
  97.1 4.4 %fusion.37 = f32[512,2048]{1,0:T(8,128)S(1)} fusion(bf16[512,896]{1,0:T(8,128)(2,1)S(1)} %all_gather.3, bf16[896,2048]{1,0:T(8,128)(2,1)} %param.7), kind=kOutput, calls=%fused_computation.71 | convolution fusion | flops 1879048192 | bytes 8781824 | tf_op jit(solution)/shard_map/dot_general | solution.py:102
  101.7 3.2 %collective-permute-start.21 = (bf16[64,2048]{1,0:T(8,128)(2,1)S(1)}, bf16[64,2048]{1,0:T(8,128)(2,1)S(1)}, u32[]{:S(2)}, u32[]{:S(2)}) collective-permute-start(bf16[64,2048]{1,0:T(8,128)(2,1)S(1)} %get-tuple-element.10), channel_id=1, source_target_pairs={{0,7},{1,0},{2,1},{3,2},{4,3},{5,4},{6,5},{7,6},{8,15},{9,8},{10,9... | collective-permute-start | bytes 786440 | tf_op jit(solution)/shard_map/ppermute | solution.py:64
  104.9 6.5 %collective-permute-done.17 = bf16[64,2048]{1,0:T(8,128)(2,1)S(1)} collective-permute-done((bf16[64,2048]{1,0:T(8,128)(2,1)S(1)}, bf16[64,2048]{1,0:T(8,128)(2,1)S(1)}, u32[]{:S(2)}, u32[]{:S(2)}) %collective-permute-start.17) | collective-permute-done | bytes 262176 | tf_op jit(solution)/shard_map/ppermute | solution.py:57
  111.6 8.9 %collective-permute-done.18 = bf16[64,2048]{1,0:T(8,128)(2,1)S(1)} collective-permute-done((bf16[64,2048]{1,0:T(8,128)(2,1)S(1)}, bf16[64,2048]{1,0:T(8,128)(2,1)S(1)}, u32[]{:S(2)}, u32[]{:S(2)}) %collective-permute-start.18) | collective-permute-done | bytes 262176 | tf_op jit(solution)/shard_map/ppermute | solution.py:57
  120.8 3.2 %collective-permute-start.22 = (bf16[64,2048]{1,0:T(8,128)(2,1)S(1)}, bf16[64,2048]{1,0:T(8,128)(2,1)S(1)}, u32[]{:S(2)}, u32[]{:S(2)}) collective-permute-start(bf16[64,2048]{1,0:T(8,128)(2,1)S(1)} %get-tuple-element.8), channel_id=1, source_target_pairs={{0,7},{1,0},{2,1},{3,2},{4,3},{5,4},{6,5},{7,6},{8,15},{9,8},{10,9... | collective-permute-start | bytes 786440 | tf_op jit(solution)/shard_map/ppermute | solution.py:64
  124.0 4.8 %collective-permute-done.19 = bf16[64,2048]{1,0:T(8,128)(2,1)S(1)} collective-permute-done((bf16[64,2048]{1,0:T(8,128)(2,1)S(1)}, bf16[64,2048]{1,0:T(8,128)(2,1)S(1)}, u32[]{:S(2)}, u32[]{:S(2)}) %collective-permute-start.19) | collective-permute-done | bytes 262176 | tf_op jit(solution)/shard_map/ppermute | solution.py:57
  128.8 0.1 fusion.2
  129.1 3.2 %collective-permute-start.23 = (bf16[64,2048]{1,0:T(8,128)(2,1)S(1)}, bf16[64,2048]{1,0:T(8,128)(2,1)S(1)}, u32[]{:S(2)}, u32[]{:S(2)}) collective-permute-start(bf16[64,2048]{1,0:T(8,128)(2,1)S(1)} %get-tuple-element.6), channel_id=1, source_target_pairs={{0,7},{1,0},{2,1},{3,2},{4,3},{5,4},{6,5},{7,6},{8,15},{9,8},{10,9... | collective-permute-start | bytes 786440 | tf_op jit(solution)/shard_map/ppermute | solution.py:64
  132.3 4.3 %collective-permute-done.20 = bf16[64,2048]{1,0:T(8,128)(2,1)S(1)} collective-permute-done((bf16[64,2048]{1,0:T(8,128)(2,1)S(1)}, bf16[64,2048]{1,0:T(8,128)(2,1)S(1)}, u32[]{:S(2)}, u32[]{:S(2)}) %collective-permute-start.20) | collective-permute-done | bytes 262176 | tf_op jit(solution)/shard_map/ppermute | solution.py:57
  136.7 1.1 fusion.5
  137.9 3.2 %collective-permute-start.26 = (f32[16,2048]{1,0:T(8,128)S(1)}, f32[16,2048]{1,0:T(8,128)S(1)}, u32[]{:S(2)}, u32[]{:S(2)}) collective-permute-start(f32[16,2048]{1,0:T(8,128)S(1)} %get-tuple-element.14), channel_id=1, source_target_pairs={{0,24},{8,0},{16,8},{24,16},{1,25},{9,1},{17,9},{25,17},{2,26},{10... | collective-permute-start | bytes 393224 | tf_op jit(solution)/shard_map/ppermute | solution.py:64
  141.1 3.7 %collective-permute-done.24 = f32[16,2048]{1,0:T(8,128)S(1)} collective-permute-done((f32[16,2048]{1,0:T(8,128)S(1)}, f32[16,2048]{1,0:T(8,128)S(1)}, u32[]{:S(2)}, u32[]{:S(2)}) %collective-permute-start.24) | collective-permute-done | bytes 131104 | tf_op jit(solution)/shard_map/ppermute | solution.py:57
  144.9 6.1 %collective-permute-done.25 = f32[16,2048]{1,0:T(8,128)S(1)} collective-permute-done((f32[16,2048]{1,0:T(8,128)S(1)}, f32[16,2048]{1,0:T(8,128)S(1)}, u32[]{:S(2)}, u32[]{:S(2)}) %collective-permute-start.25) | collective-permute-done | bytes 131104 | tf_op jit(solution)/shard_map/ppermute | solution.py:57
  151.1 0.7 fusion.19
  (48 shorter events, 1.7 us)
Async XLA Ops:
  0.0 5.7 %collective-permute-start = (bf16[16,2048]{1,0:T(8,128)(2,1)}, bf16[16,2048]{1,0:T(8,128)(2,1)S(1)}, u32[]{:S(2)}, u32[]{:S(2)}) collective-permute-start(bf16[16,2048]{1,0:T(8,128)(2,1)} %param.4), channel_id=1, source_target_pairs={{0,8},{8,16},{16,24},{24,0},{1,9},{9,17},{17,25},{25,1},{2,10},{10... | collective-permute-start | bytes 196616 | tf_op jit(solution)/shard_map/ppermute | solution.py:36
  1.6 9.6 %collective-permute-start.2 = (bf16[16,2048]{1,0:T(8,128)(2,1)}, bf16[16,2048]{1,0:T(8,128)(2,1)S(1)}, u32[]{:S(2)}, u32[]{:S(2)}) collective-permute-start(bf16[16,2048]{1,0:T(8,128)(2,1)} %param.4), channel_id=1, source_target_pairs={{0,24},{8,0},{16,8},{24,16},{1,25},{9,1},{17,9},{25,17},{2,26},{10... | collective-permute-start | bytes 196616 | tf_op jit(solution)/shard_map/ppermute | solution.py:40
  4.1 15.9 %copy-start.1 = (bf16[2048,896]{1,0:T(8,128)(2,1)S(1)}, bf16[2048,896]{1,0:T(8,128)(2,1)}, u32[]{:S(2)}) copy-start(bf16[2048,896]{1,0:T(8,128)(2,1)} %param.6) | copy-start | bytes 11010052
  5.7 5.5 %collective-permute-start.1 = (bf16[16,2048]{1,0:T(8,128)(2,1)S(1)}, bf16[16,2048]{1,0:T(8,128)(2,1)S(1)}, u32[]{:S(2)}, u32[]{:S(2)}) collective-permute-start(bf16[16,2048]{1,0:T(8,128)(2,1)S(1)} %collective-permute-done), channel_id=1, source_target_pairs={{0,8},{8,16},{16,24},{24,0},{1,9},{9,17},{17,25},{25,1},{2,10},{10... | collective-permute-start | bytes 196616 | tf_op jit(solution)/shard_map/ppermute | solution.py:36
  11.2 10.3 %collective-permute-start.3 = (bf16[64,2048]{1,0:T(8,128)(2,1)S(1)}, bf16[64,2048]{1,0:T(8,128)(2,1)S(1)}, u32[]{:S(2)}, u32[]{:S(2)}) collective-permute-start(bf16[64,2048]{1,0:T(8,128)(2,1)S(1)} %bitcast.151), channel_id=1, source_target_pairs={{0,1},{1,2},{2,3},{3,4},{4,5},{5,6},{6,7},{7,0},{8,9},{9,10},{10,1... | collective-permute-start | bytes 786440 | tf_op jit(solution)/shard_map/ppermute | solution.py:36
  13.2 10.3 %collective-permute-start.7 = (bf16[64,2048]{1,0:T(8,128)(2,1)S(1)}, bf16[64,2048]{1,0:T(8,128)(2,1)S(1)}, u32[]{:S(2)}, u32[]{:S(2)}) collective-permute-start(bf16[64,2048]{1,0:T(8,128)(2,1)S(1)} %bitcast.152), channel_id=1, source_target_pairs={{0,7},{1,0},{2,1},{3,2},{4,3},{5,4},{6,5},{7,6},{8,15},{9,8},{10,9... | collective-permute-start | bytes 786440 | tf_op jit(solution)/shard_map/ppermute | solution.py:40
  20.0 2.0 %copy-start = (bf16[2048,896]{1,0:T(8,128)(2,1)S(1)}, bf16[2048,896]{1,0:T(8,128)(2,1)}, u32[]{:S(2)}) copy-start(bf16[2048,896]{1,0:T(8,128)(2,1)} %param.5) | copy-start | bytes 11010052
  22.7 7.7 %collective-permute-start.4 = (bf16[64,2048]{1,0:T(8,128)(2,1)S(1)}, bf16[64,2048]{1,0:T(8,128)(2,1)S(1)}, u32[]{:S(2)}, u32[]{:S(2)}) collective-permute-start(bf16[64,2048]{1,0:T(8,128)(2,1)S(1)} %collective-permute-done.3), channel_id=1, source_target_pairs={{0,1},{1,2},{2,3},{3,4},{4,5},{5,6},{6,7},{7,0},{8,9},{9,10},{10,1... | collective-permute-start | bytes 786440 | tf_op jit(solution)/shard_map/ppermute | solution.py:36
  24.9 7.2 %collective-permute-start.8 = (bf16[64,2048]{1,0:T(8,128)(2,1)S(1)}, bf16[64,2048]{1,0:T(8,128)(2,1)S(1)}, u32[]{:S(2)}, u32[]{:S(2)}) collective-permute-start(bf16[64,2048]{1,0:T(8,128)(2,1)S(1)} %collective-permute-done.7), channel_id=1, source_target_pairs={{0,7},{1,0},{2,1},{3,2},{4,3},{5,4},{6,5},{7,6},{8,15},{9,8},{10,9... | collective-permute-start | bytes 786440 | tf_op jit(solution)/shard_map/ppermute | solution.py:40
  31.1 8.0 %collective-permute-start.5 = (bf16[64,2048]{1,0:T(8,128)(2,1)S(1)}, bf16[64,2048]{1,0:T(8,128)(2,1)S(1)}, u32[]{:S(2)}, u32[]{:S(2)}) collective-permute-start(bf16[64,2048]{1,0:T(8,128)(2,1)S(1)} %collective-permute-done.4), channel_id=1, source_target_pairs={{0,1},{1,2},{2,3},{3,4},{4,5},{5,6},{6,7},{7,0},{8,9},{9,10},{10,1... | collective-permute-start | bytes 786440 | tf_op jit(solution)/shard_map/ppermute | solution.py:36
  33.6 7.8 %collective-permute-start.9 = (bf16[64,2048]{1,0:T(8,128)(2,1)S(1)}, bf16[64,2048]{1,0:T(8,128)(2,1)S(1)}, u32[]{:S(2)}, u32[]{:S(2)}) collective-permute-start(bf16[64,2048]{1,0:T(8,128)(2,1)S(1)} %collective-permute-done.8), channel_id=1, source_target_pairs={{0,7},{1,0},{2,1},{3,2},{4,3},{5,4},{6,5},{7,6},{8,15},{9,8},{10,9... | collective-permute-start | bytes 786440 | tf_op jit(solution)/shard_map/ppermute | solution.py:40
  39.8 7.7 %collective-permute-start.6 = (bf16[64,2048]{1,0:T(8,128)(2,1)S(1)}, bf16[64,2048]{1,0:T(8,128)(2,1)S(1)}, u32[]{:S(2)}, u32[]{:S(2)}) collective-permute-start(bf16[64,2048]{1,0:T(8,128)(2,1)S(1)} %collective-permute-done.5), channel_id=1, source_target_pairs={{0,1},{1,2},{2,3},{3,4},{4,5},{5,6},{6,7},{7,0},{8,9},{9,10},{10,1... | collective-permute-start | bytes 786440 | tf_op jit(solution)/shard_map/ppermute | solution.py:36
  49.0 1.8 %copy-start.2 = (f32[8,64,1792]{2,1,0:T(8,128)}, f32[8,64,1792]{2,1,0:T(8,128)S(1)}, u32[]{:S(2)}) copy-start(f32[8,64,1792]{2,1,0:T(8,128)S(1)} %fusion.13) | copy-start | bytes 11010052
  52.2 4.0 %collective-permute-start.10 = (f32[4,64,1792]{2,1,0:T(8,128)}, f32[4,64,1792]{2,1,0:T(8,128)S(1)}, u32[]{:S(2)}, u32[]{:S(2)}) collective-permute-start(f32[4,64,1792]{2,1,0:T(8,128)} %dynamic-slice_bitcast_fusion), channel_id=1, source_target_pairs={{0,32},{32,0},{1,33},{33,1},{2,34},{34,2},{3,35},{35,3},{4,36},{36... | collective-permute-start | bytes 5505032 | tf_op jit(solution)/shard_map/ppermute | solution.py:78
  58.1 7.7 %collective-permute-start.11 = (f32[64,896]{1,0:T(8,128)S(1)}, f32[64,896]{1,0:T(8,128)S(1)}, u32[]{:S(2)}, u32[]{:S(2)}) collective-permute-start(f32[64,896]{1,0:T(8,128)S(1)} %dynamic-slice_bitcast_fusion.2), channel_id=1, source_target_pairs={{0,64},{64,128},{128,192},{192,0},{1,65},{65,129},{129,193},{193,1... | collective-permute-start | bytes 688136 | tf_op jit(solution)/shard_map/ppermute | solution.py:20
  59.7 7.7 %collective-permute-start.14 = (f32[64,896]{1,0:T(8,128)S(1)}, f32[64,896]{1,0:T(8,128)S(1)}, u32[]{:S(2)}, u32[]{:S(2)}) collective-permute-start(f32[64,896]{1,0:T(8,128)S(1)} %dynamic-slice_bitcast_fusion.1), channel_id=1, source_target_pairs={{0,192},{64,0},{128,64},{192,128},{1,193},{65,1},{129,65},{193,129... | collective-permute-start | bytes 688136 | tf_op jit(solution)/shard_map/ppermute | solution.py:21
  65.9 6.9 %collective-permute-start.12 = (f32[64,896]{1,0:T(8,128)S(1)}, f32[64,896]{1,0:T(8,128)S(1)}, u32[]{:S(2)}, u32[]{:S(2)}) collective-permute-start(f32[64,896]{1,0:T(8,128)S(1)} %bitcast_add_fusion.12), channel_id=1, source_target_pairs={{0,64},{64,128},{128,192},{192,0},{1,65},{65,129},{129,193},{193,1... | collective-permute-start | bytes 688136 | tf_op jit(solution)/shard_map/ppermute | solution.py:20
  67.5 6.9 %collective-permute-start.15 = (f32[64,896]{1,0:T(8,128)S(1)}, f32[64,896]{1,0:T(8,128)S(1)}, u32[]{:S(2)}, u32[]{:S(2)}) collective-permute-start(f32[64,896]{1,0:T(8,128)S(1)} %bitcast_add_fusion.9), channel_id=1, source_target_pairs={{0,192},{64,0},{128,64},{192,128},{1,193},{65,1},{129,65},{193,129... | collective-permute-start | bytes 688136 | tf_op jit(solution)/shard_map/ppermute | solution.py:21
  72.8 7.2 %collective-permute-start.13 = (f32[64,896]{1,0:T(8,128)S(1)}, f32[64,896]{1,0:T(8,128)S(1)}, u32[]{:S(2)}, u32[]{:S(2)}) collective-permute-start(f32[64,896]{1,0:T(8,128)S(1)} %bitcast_add_fusion.11), channel_id=1, source_target_pairs={{0,64},{64,128},{128,192},{192,0},{1,65},{65,129},{129,193},{193,1... | collective-permute-start | bytes 688136 | tf_op jit(solution)/shard_map/ppermute | solution.py:20
  74.4 6.1 %collective-permute-start.16 = (f32[64,896]{1,0:T(8,128)S(1)}, f32[64,896]{1,0:T(8,128)S(1)}, u32[]{:S(2)}, u32[]{:S(2)}) collective-permute-start(f32[64,896]{1,0:T(8,128)S(1)} %bitcast_add_fusion.8), channel_id=1, source_target_pairs={{0,192},{64,0},{128,64},{192,128},{1,193},{65,1},{129,65},{193,129... | collective-permute-start | bytes 688136 | tf_op jit(solution)/shard_map/ppermute | solution.py:21
  101.5 27.3 %copy-start.3 = (f32[512,2048]{1,0:T(8,128)}, f32[512,2048]{1,0:T(8,128)S(1)}, u32[]{:S(2)}) copy-start(f32[512,2048]{1,0:T(8,128)S(1)} %fusion.37) | copy-start | bytes 12582916
  101.6 9.8 %collective-permute-start.17 = (bf16[64,2048]{1,0:T(8,128)(2,1)S(1)}, bf16[64,2048]{1,0:T(8,128)(2,1)S(1)}, u32[]{:S(2)}, u32[]{:S(2)}) collective-permute-start(bf16[64,2048]{1,0:T(8,128)(2,1)S(1)} %get-tuple-element.9), channel_id=1, source_target_pairs={{0,1},{1,2},{2,3},{3,4},{4,5},{5,6},{6,7},{7,0},{8,9},{9,10},{10,1... | collective-permute-start | bytes 786440 | tf_op jit(solution)/shard_map/ppermute | solution.py:57
  101.7 9.9 %collective-permute-start.21 = (bf16[64,2048]{1,0:T(8,128)(2,1)S(1)}, bf16[64,2048]{1,0:T(8,128)(2,1)S(1)}, u32[]{:S(2)}, u32[]{:S(2)}) collective-permute-start(bf16[64,2048]{1,0:T(8,128)(2,1)S(1)} %get-tuple-element.10), channel_id=1, source_target_pairs={{0,7},{1,0},{2,1},{3,2},{4,3},{5,4},{6,5},{7,6},{8,15},{9,8},{10,9... | collective-permute-start | bytes 786440 | tf_op jit(solution)/shard_map/ppermute | solution.py:64
  111.5 9.0 %collective-permute-start.18 = (bf16[64,2048]{1,0:T(8,128)(2,1)S(1)}, bf16[64,2048]{1,0:T(8,128)(2,1)S(1)}, u32[]{:S(2)}, u32[]{:S(2)}) collective-permute-start(bf16[64,2048]{1,0:T(8,128)(2,1)S(1)} %fusion.4), channel_id=1, source_target_pairs={{0,1},{1,2},{2,3},{3,4},{4,5},{5,6},{6,7},{7,0},{8,9},{9,10},{10,1... | collective-permute-start | bytes 786440 | tf_op jit(solution)/shard_map/ppermute | solution.py:57
  120.7 8.1 %collective-permute-start.19 = (bf16[64,2048]{1,0:T(8,128)(2,1)S(1)}, bf16[64,2048]{1,0:T(8,128)(2,1)S(1)}, u32[]{:S(2)}, u32[]{:S(2)}) collective-permute-start(bf16[64,2048]{1,0:T(8,128)(2,1)S(1)} %get-tuple-element.7), channel_id=1, source_target_pairs={{0,1},{1,2},{2,3},{3,4},{4,5},{5,6},{6,7},{7,0},{8,9},{9,10},{10,1... | collective-permute-start | bytes 786440 | tf_op jit(solution)/shard_map/ppermute | solution.py:57
  120.8 8.0 %collective-permute-start.22 = (bf16[64,2048]{1,0:T(8,128)(2,1)S(1)}, bf16[64,2048]{1,0:T(8,128)(2,1)S(1)}, u32[]{:S(2)}, u32[]{:S(2)}) collective-permute-start(bf16[64,2048]{1,0:T(8,128)(2,1)S(1)} %get-tuple-element.8), channel_id=1, source_target_pairs={{0,7},{1,0},{2,1},{3,2},{4,3},{5,4},{6,5},{7,6},{8,15},{9,8},{10,9... | collective-permute-start | bytes 786440 | tf_op jit(solution)/shard_map/ppermute | solution.py:64
  129.0 7.7 %collective-permute-start.20 = (bf16[64,2048]{1,0:T(8,128)(2,1)S(1)}, bf16[64,2048]{1,0:T(8,128)(2,1)S(1)}, u32[]{:S(2)}, u32[]{:S(2)}) collective-permute-start(bf16[64,2048]{1,0:T(8,128)(2,1)S(1)} %get-tuple-element.5), channel_id=1, source_target_pairs={{0,1},{1,2},{2,3},{3,4},{4,5},{5,6},{6,7},{7,0},{8,9},{9,10},{10,1... | collective-permute-start | bytes 786440 | tf_op jit(solution)/shard_map/ppermute | solution.py:57
  129.1 7.6 %collective-permute-start.23 = (bf16[64,2048]{1,0:T(8,128)(2,1)S(1)}, bf16[64,2048]{1,0:T(8,128)(2,1)S(1)}, u32[]{:S(2)}, u32[]{:S(2)}) collective-permute-start(bf16[64,2048]{1,0:T(8,128)(2,1)S(1)} %get-tuple-element.6), channel_id=1, source_target_pairs={{0,7},{1,0},{2,1},{3,2},{4,3},{5,4},{6,5},{7,6},{8,15},{9,8},{10,9... | collective-permute-start | bytes 786440 | tf_op jit(solution)/shard_map/ppermute | solution.py:64
  137.8 7.0 %collective-permute-start.24 = (f32[16,2048]{1,0:T(8,128)S(1)}, f32[16,2048]{1,0:T(8,128)S(1)}, u32[]{:S(2)}, u32[]{:S(2)}) collective-permute-start(f32[16,2048]{1,0:T(8,128)S(1)} %get-tuple-element.13), channel_id=1, source_target_pairs={{0,8},{8,16},{16,24},{24,0},{1,9},{9,17},{17,25},{25,1},{2,10},{10... | collective-permute-start | bytes 393224 | tf_op jit(solution)/shard_map/ppermute | solution.py:57
  137.9 7.0 %collective-permute-start.26 = (f32[16,2048]{1,0:T(8,128)S(1)}, f32[16,2048]{1,0:T(8,128)S(1)}, u32[]{:S(2)}, u32[]{:S(2)}) collective-permute-start(f32[16,2048]{1,0:T(8,128)S(1)} %get-tuple-element.14), channel_id=1, source_target_pairs={{0,24},{8,0},{16,8},{24,16},{1,25},{9,1},{17,9},{25,17},{2,26},{10... | collective-permute-start | bytes 393224 | tf_op jit(solution)/shard_map/ppermute | solution.py:64
  144.8 6.3 %collective-permute-start.25 = (f32[16,2048]{1,0:T(8,128)S(1)}, f32[16,2048]{1,0:T(8,128)S(1)}, u32[]{:S(2)}, u32[]{:S(2)}) collective-permute-start(f32[16,2048]{1,0:T(8,128)S(1)} %bitcast_add_fusion.13), channel_id=1, source_target_pairs={{0,8},{8,16},{16,24},{24,0},{1,9},{9,17},{17,25},{25,1},{2,10},{10... | collective-permute-start | bytes 393224 | tf_op jit(solution)/shard_map/ppermute | solution.py:57

commit v8 on v5

--- a/solution.py
+++ b/solution.py
@@ -4,22 +4,6 @@
 from jax.sharding import Mesh, PartitionSpec as P
 
 EMBED = ("ex", "ec")
-
-
-def ring_rs(x, axis, n):
-    k = lax.axis_index(axis)
-    xs = x.reshape((n, x.shape[0] // n) + x.shape[1:])
-    half = x.shape[-1] // 2
-    a, b = xs[..., :half], xs[..., half:]
-    take = lambda arr, i: lax.dynamic_index_in_dim(arr, i % n, 0, keepdims=False)
-    fwd = [(i, (i + 1) % n) for i in range(n)]
-    bwd = [(i, (i - 1) % n) for i in range(n)]
-    acc_a = take(a, k - 1)
-    acc_b = take(b, k + 1)
-    for s in range(n - 1):
-        acc_a = lax.ppermute(acc_a, axis, fwd) + take(a, k - s - 2)
-        acc_b = lax.ppermute(acc_b, axis, bwd) + take(b, k + s + 2)
-    return jnp.concatenate([acc_a, acc_b], axis=-1)
 
 
 def ring_ag(x, axis, n, f=lambda v: v):
@@ -42,6 +26,39 @@
     return out.reshape((n * own.shape[0],) + own.shape[1:])
 
 
+def ring_rs_bal(take, axis, n, send_dtype):
+    k = lax.axis_index(axis)
+    get = lambda i: take(i % n).astype(jnp.float32)
+    fwd = [(i, (i + 1) % n) for i in range(n)]
+    bwd = [(i, (i - 1) % n) for i in range(n)]
+    nf = n // 2
+    own = get(k)
+    h = own.shape[-1] // 2
+
+    def side(perm, sign, cols):
+        far = get(k + sign * nf)
+        acc = far[..., :h] if cols == 0 else far[..., h:]
+        for s in range(nf):
+            got = lax.ppermute(acc.astype(send_dtype), axis, perm).astype(jnp.float32)
+            if s == 0:
+                if nf == 1:
+                    return got
+                acc = get(k + sign * (nf - 1))
+                pad = [(0, 0)] * (got.ndim - 1) + ([(0, h)] if cols == 0 else [(h, 0)])
+                acc = acc + jnp.pad(got, pad)
+            elif s < nf - 1:
+                acc = get(k + sign * (nf - 1 - s)) + got
+            else:
+                acc = got
+        return acc
+
+    cw = side(fwd, 1, 0)
+    ccw = side(bwd, -1, 1)
+    if nf == 1:
+        return own + jnp.concatenate([cw, ccw], axis=-1)
+    return own + cw + ccw
+
+
 def embed_rs(x):
     ec = lax.axis_index("ec")
     ncore = lax.psum(1, "ec")
@@ -50,8 +67,10 @@
     mine = lax.dynamic_index_in_dim(xs, ec, 1, keepdims=False)
     other = lax.dynamic_index_in_dim(xs, 1 - ec, 1, keepdims=False)
     got = lax.ppermute(other, "ec", [(0, 1), (1, 0)])
-    y = (mine + got).reshape((-1,) + x.shape[1:])
-    return ring_rs(y, "ex", nx)
+    y = mine + got
+    return ring_rs_bal(
+        lambda i: lax.dynamic_index_in_dim(y, i, 0, keepdims=False), "ex", nx, jnp.float32
+    )
 
 
 def on_device(rows_in, gate_weight, up_weight, down_weight):
@@ -73,12 +92,17 @@
     summed = embed_rs(partial_value)
     activated = (jax.nn.silu(summed[:, :width]) * summed[:, width:]).astype(jnp.bfloat16)
     activated = lax.all_gather(activated, EMBED, axis=0, tiled=True)
-    partial_out = jnp.dot(activated, down_weight, preferred_element_type=jnp.float32)
-    pieces = partial_out.astype(jnp.bfloat16).reshape(
-        (ny * nz, partial_out.shape[0] // (ny * nz)) + partial_out.shape[1:]
+    act_blocks = activated.reshape((nz, -1) + activated.shape[1:])
+    project = lambda i: jnp.dot(
+        lax.dynamic_index_in_dim(act_blocks, i, 0, keepdims=False),
+        down_weight,
+        preferred_element_type=jnp.float32,
     )
-    pieces = lax.all_to_all(pieces, ("hz", "hy"), 0, 0, tiled=True)
-    totals = pieces.astype(jnp.float32).sum(axis=0)
+    totals = ring_rs_bal(project, "hz", nz, jnp.bfloat16)
+    totals = totals.reshape((ny, -1) + totals.shape[1:])
+    totals = ring_rs_bal(
+        lambda i: lax.dynamic_index_in_dim(totals, i, 0, keepdims=False), "hy", ny, jnp.float32
+    )
     return totals.astype(jnp.bfloat16)
 
 

time: 161 us -> 147 us (0.913)
  blocking collectives: 74 us -> 14.4 us
  waiting for transfers between devices: 35.1 us -> 57.8 us
  starting transfers between devices: 24.6 us -> 41.9 us
  matrix products: 17.7 us -> 22.3 us
    all_to_all x1 -> x0, blocking collectives: 57.5 us -> none  [on_device(): pieces = lax.all_to_all(pieces, ('hz', 'hy'), 0, 0, tiled=True)]
    ppermute x6 -> x16, waiting for transfers between devices: 14.7 us -> 37.6 us  [side(): got = lax.ppermute(acc.astype(send_dtype), axis, perm).astype(jnp.float32)]
    ppermute x6 -> x16, starting transfers between devices: 7.49 us -> 24.7 us  [side(): got = lax.ppermute(acc.astype(send_dtype), axis, perm).astype(jnp.float32)]
    dot_general x1 -> x9, matrix products: 4.41 us -> 8.91 us  [on_device(): jnp.dot(lax.dynamic_index_in_dim(act_blocks, i, 0, keepdims=False), down_...]
    all_gather x1, blocking collectives: 16.5 us -> 14.4 us  [on_device(): activated = lax.all_gather(activated, EMBED, axis=0, tiled=True)]
    add x5, other arithmetic: 1.8 us -> 3.51 us  [the longest x1 2.24 us: embed_rs(): y = mine + got]
  transfers between devices with their start and end apart: 17 -> 27, of which waited for: 13 -> 20; matrix products, arithmetic and copies ran while one was open for 8% -> 13% of each run, Pallas kernels for 0% -> 0%
where the time goes in v8:
time: 147 us; the launch traced here: 145 us
  waiting for transfers between devices  57.8 us (39%)
  starting transfers between devices  41.9 us (29%)
  matrix products  22.3 us (15%)
  blocking collectives  14.4 us (10%)
  other arithmetic  4.52 us (3%)
  local copies, waits for them, and re-layouts  3.8 us (3%)
    ppermute x16, waiting for transfers between devices, side(): got = lax.ppermute(acc.astype(send_dtype), axis, perm).astype(jnp.float32)  37.6 us
    ppermute x16, starting transfers between devices, side(): got = lax.ppermute(acc.astype(send_dtype), axis, perm).astype(jnp.float32)  24.7 us
    ppermute x6, waiting for transfers between devices, ring_ag(): buf = lax.ppermute(buf, axis, fwd)  15.3 us
    all_gather x1, blocking collectives, on_device(): activated = lax.all_gather(activated, EMBED, axis=0, tiled=True)  14.4 us
    ppermute x4, starting transfers between devices, ring_ag(): buf = lax.ppermute(buf, axis, bwd)  12.9 us
    dot_general x9, matrix products, on_device(): jnp.dot(lax.dynamic_index_in_dim(act_blocks, i, 0, keepdims=False), down_...  8.91 us
    dot_general x8, matrix products, on_device(): jnp.dot(v, gate_weight, preferred_element_type=jnp.float32)  7.67 us
    dot_general x8, matrix products, on_device(): jnp.dot(v, up_weight, preferred_element_type=jnp.float32)  5.67 us
  transfers between devices with their start and end apart: 27, of which 20 were waited for; matrix products, arithmetic and copies ran while one was open for 13% of the time, Pallas kernels for 0%

profile of v8, /device:TPU:2, one launch (start us, length us, event | category | flops | bytes accessed | tf_op | source)
XLA Modules:
  0.0 145.2 jit_solution(17300706280750660453)
XLA Ops:
  0.0 1.6 %collective-permute-start = (bf16[16,2048]{1,0:T(8,128)(2,1)}, bf16[16,2048]{1,0:T(8,128)(2,1)S(1)}, u32[]{:S(2)}, u32[]{:S(2)}) collective-permute-start(bf16[16,2048]{1,0:T(8,128)(2,1)} %param.4), channel_id=1, source_target_pairs={{0,8},{8,16},{16,24},{24,0},{1,9},{9,17},{17,25},{25,1},{2,10},{10... | collective-permute-start | bytes 196616 | tf_op jit(solution)/shard_map/ppermute | solution.py:20
  1.6 1.7 %collective-permute-start.2 = (bf16[16,2048]{1,0:T(8,128)(2,1)}, bf16[16,2048]{1,0:T(8,128)(2,1)S(1)}, u32[]{:S(2)}, u32[]{:S(2)}) collective-permute-start(bf16[16,2048]{1,0:T(8,128)(2,1)} %param.4), channel_id=1, source_target_pairs={{0,24},{8,0},{16,8},{24,16},{1,25},{9,1},{17,9},{25,17},{2,26},{10... | collective-permute-start | bytes 196616 | tf_op jit(solution)/shard_map/ppermute | solution.py:24
  3.3 0.9 bitcast_dynamic-update-slice_fusion.3
  4.1 1.6 %collective-permute-done = bf16[16,2048]{1,0:T(8,128)(2,1)S(1)} collective-permute-done((bf16[16,2048]{1,0:T(8,128)(2,1)}, bf16[16,2048]{1,0:T(8,128)(2,1)S(1)}, u32[]{:S(2)}, u32[]{:S(2)}) %collective-permute-start) | collective-permute-done | bytes 65568 | tf_op jit(solution)/shard_map/ppermute | solution.py:20
  6.1 5.1 %collective-permute-done.1 = bf16[16,2048]{1,0:T(8,128)(2,1)S(1)} collective-permute-done((bf16[16,2048]{1,0:T(8,128)(2,1)S(1)}, bf16[16,2048]{1,0:T(8,128)(2,1)S(1)}, u32[]{:S(2)}, u32[]{:S(2)}) %collective-permute-start.1) | collective-permute-done | bytes 65568 | tf_op jit(solution)/shard_map/ppermute | solution.py:20
  11.2 2.0 %collective-permute-start.3 = (bf16[64,2048]{1,0:T(8,128)(2,1)S(1)}, bf16[64,2048]{1,0:T(8,128)(2,1)S(1)}, u32[]{:S(2)}, u32[]{:S(2)}) collective-permute-start(bf16[64,2048]{1,0:T(8,128)(2,1)S(1)} %bitcast.168), channel_id=1, source_target_pairs={{0,1},{1,2},{2,3},{3,4},{4,5},{5,6},{6,7},{7,0},{8,9},{9,10},{10,1... | collective-permute-start | bytes 786440 | tf_op jit(solution)/shard_map/ppermute | solution.py:20
  13.2 4.0 %collective-permute-start.7 = (bf16[64,2048]{1,0:T(8,128)(2,1)S(1)}, bf16[64,2048]{1,0:T(8,128)(2,1)S(1)}, u32[]{:S(2)}, u32[]{:S(2)}) collective-permute-start(bf16[64,2048]{1,0:T(8,128)(2,1)S(1)} %bitcast.169), channel_id=1, source_target_pairs={{0,7},{1,0},{2,1},{3,2},{4,3},{5,4},{6,5},{7,6},{8,15},{9,8},{10,9... | collective-permute-start | bytes 786440 | tf_op jit(solution)/shard_map/ppermute | solution.py:24
  17.2 2.7 %fusion.60 = f32[64,896]{1,0:T(8,128)S(1)} fusion(bf16[64,2048]{1,0:T(8,128)(2,1)S(1)} %bitcast.170, bf16[2048,896]{1,0:T(8,128)(2,1)} %param.5), kind=kOutput, calls=%fused_computation.82 | convolution fusion | flops 234881024 | bytes 4161536 | tf_op jit(solution)/shard_map/dot_general | solution.py:86
  20.0 0.7 fusion.61
  22.0 0.7 fusion.62
  22.8 0.7 fusion.63
  23.5 0.7 fusion.70
  24.2 0.7 fusion.71
  24.9 3.3 %collective-permute-start.8 = (bf16[64,2048]{1,0:T(8,128)(2,1)S(1)}, bf16[64,2048]{1,0:T(8,128)(2,1)S(1)}, u32[]{:S(2)}, u32[]{:S(2)}) collective-permute-start(bf16[64,2048]{1,0:T(8,128)(2,1)S(1)} %collective-permute-done.7), channel_id=1, source_target_pairs={{0,7},{1,0},{2,1},{3,2},{4,3},{5,4},{6,5},{7,6},{8,15},{9,8},{10,9... | collective-permute-start | bytes 786440 | tf_op jit(solution)/shard_map/ppermute | solution.py:24
  28.3 2.1 %collective-permute-done.4 = bf16[64,2048]{1,0:T(8,128)(2,1)S(1)} collective-permute-done((bf16[64,2048]{1,0:T(8,128)(2,1)S(1)}, bf16[64,2048]{1,0:T(8,128)(2,1)S(1)}, u32[]{:S(2)}, u32[]{:S(2)}) %collective-permute-start.4) | collective-permute-done | bytes 262176 | tf_op jit(solution)/shard_map/ppermute | solution.py:20
  30.4 0.7 fusion.64
  31.2 0.7 fusion.65
  32.1 0.7 fusion.72
  32.8 0.7 fusion.73
  33.6 3.9 %collective-permute-start.9 = (bf16[64,2048]{1,0:T(8,128)(2,1)S(1)}, bf16[64,2048]{1,0:T(8,128)(2,1)S(1)}, u32[]{:S(2)}, u32[]{:S(2)}) collective-permute-start(bf16[64,2048]{1,0:T(8,128)(2,1)S(1)} %collective-permute-done.8), channel_id=1, source_target_pairs={{0,7},{1,0},{2,1},{3,2},{4,3},{5,4},{6,5},{7,6},{8,15},{9,8},{10,9... | collective-permute-start | bytes 786440 | tf_op jit(solution)/shard_map/ppermute | solution.py:24
  37.5 1.5 %collective-permute-done.5 = bf16[64,2048]{1,0:T(8,128)(2,1)S(1)} collective-permute-done((bf16[64,2048]{1,0:T(8,128)(2,1)S(1)}, bf16[64,2048]{1,0:T(8,128)(2,1)S(1)}, u32[]{:S(2)}, u32[]{:S(2)}) %collective-permute-start.5) | collective-permute-done | bytes 262176 | tf_op jit(solution)/shard_map/ppermute | solution.py:20
  39.1 0.7 fusion.66
  39.9 0.7 fusion.67
  40.6 0.8 collective-permute-done.9
  41.4 0.7 fusion.74
  42.1 0.7 fusion.75
  42.9 4.6 %collective-permute-done.6 = bf16[64,2048]{1,0:T(8,128)(2,1)S(1)} collective-permute-done((bf16[64,2048]{1,0:T(8,128)(2,1)S(1)}, bf16[64,2048]{1,0:T(8,128)(2,1)S(1)}, u32[]{:S(2)}, u32[]{:S(2)}) %collective-permute-start.6) | collective-permute-done | bytes 262176 | tf_op jit(solution)/shard_map/ppermute | solution.py:20
  47.4 0.7 fusion.68
  48.2 0.7 fusion.69
  49.0 1.8 %copy-done.3 = f32[8,64,1792]{2,1,0:T(8,128)} copy-done((f32[8,64,1792]{2,1,0:T(8,128)}, f32[8,64,1792]{2,1,0:T(8,128)S(1)}, u32[]{:S(2)}) %copy-start.3) | copy-done | bytes 3670040
  51.1 3.9 %collective-permute-done.10 = f32[4,64,1792]{2,1,0:T(8,128)} collective-permute-done((f32[4,64,1792]{2,1,0:T(8,128)S(1)}, f32[4,64,1792]{2,1,0:T(8,128)}, u32[]{:S(2)}, u32[]{:S(2)}) %collective-permute-start.10) | collective-permute-done | bytes 1835040 | tf_op jit(solution)/shard_map/ppermute | solution.py:69
  55.0 2.2 %bitcast_add_fusion = f32[4,64,1792]{2,1,0:T(8,128)S(1)} fusion(f32[4,64,1792]{2,1,0:T(8,128)} %collective-permute-done.10, f32[4,2,64,1792]{3,2,1,0:T(8,128)} %bitcast.155, s32[]{:T(128)S(6)} %select_n.206), kind=kLoop, calls=%fused_computation | loop fusion | flops 458752 | bytes 5505028 | tf_op jit(solution)/shard_map/add | solution.py:70
  57.3 1.6 %collective-permute-start.11 = (f32[64,896]{1,0:T(8,128)S(1)}, f32[64,896]{1,0:T(8,128)S(1)}, u32[]{:S(2)}, u32[]{:S(2)}) collective-permute-start(f32[64,896]{1,0:T(8,128)S(1)} %slice.34), channel_id=1, source_target_pairs={{0,64},{64,128},{128,192},{192,0},{1,65},{65,129},{129,193},{193,1... | collective-permute-start | bytes 688136 | tf_op jit(solution)/shard_map/ppermute | solution.py:42
  58.9 0.6 collective-permute-start.13
  59.5 5.5 %collective-permute-done.11 = f32[64,896]{1,0:T(8,128)S(1)} collective-permute-done((f32[64,896]{1,0:T(8,128)S(1)}, f32[64,896]{1,0:T(8,128)S(1)}, u32[]{:S(2)}, u32[]{:S(2)}) %collective-permute-start.11) | collective-permute-done | bytes 229408 | tf_op jit(solution)/shard_map/ppermute | solution.py:42
  65.0 1.3 collective-permute-done.13
  66.4 1.3 collective-permute-start.12
  67.7 0.8 collective-permute-start.14
  68.5 9.4 %collective-permute-done.12 = f32[64,1792]{1,0:T(8,128)S(1)} collective-permute-done((f32[64,1792]{1,0:T(8,128)S(1)}, f32[64,1792]{1,0:T(8,128)S(1)}, u32[]{:S(2)}, u32[]{:S(2)}) %collective-permute-start.12) | collective-permute-done | bytes 458784 | tf_op jit(solution)/shard_map/ppermute | solution.py:42
  77.9 1.0 collective-permute-done.14
  78.9 1.1 fusion.8
  80.1 14.4 %all_gather.3 = bf16[512,896]{1,0:T(8,128)(2,1)S(1)} all-gather(bf16[64,896]{1,0:T(8,128)(2,1)S(1)} %fusion.9), channel_id=1, replica_groups=mesh['ex'=4,'ec'=2,'hy'=4,'hz'=8] {'ex','ec'}, dimensions={0}, use_global_device_ids=true | all-gather | bytes 1032192 | tf_op jit(solution)/shard_map/all_gather | solution.py:94
  94.5 2.8 %fusion.22 = bf16[64,2048]{1,0:T(8,128)(2,1)S(1)} fusion(bf16[896,2048]{1,0:T(8,128)(2,1)} %param.7, bf16[8,64,896]{2,1,0:T(8,128)(2,1)S(1)} %bitcast.156, s32[]{:T(128)S(6)} %select_n.221), kind=kOutput, calls=%fused_computation.50 | convolution fusion | flops 234881024 | bytes 4046852 | tf_op jit(solution)/shard_map/dot_general | solution.py:96
  97.4 0.8 fusion.12
  98.2 3.5 %collective-permute-start.19 = (bf16[64,1024]{1,0:T(8,128)(2,1)S(1)}, bf16[64,1024]{1,0:T(8,128)(2,1)S(1)}, u32[]{:S(2)}, u32[]{:S(2)}) collective-permute-start(bf16[64,1024]{1,0:T(8,128)(2,1)S(1)} %slice.48), channel_id=1, source_target_pairs={{0,7},{1,0},{2,1},{3,2},{4,3},{5,4},{6,5},{7,6},{8,15},{9,8},{10,9... | collective-permute-start | bytes 393224 | tf_op jit(solution)/shard_map/ppermute | solution.py:42
  101.7 2.6 %collective-permute-done.15 = bf16[64,1024]{1,0:T(8,128)(2,1)S(1)} collective-permute-done((bf16[64,1024]{1,0:T(8,128)(2,1)S(1)}, bf16[64,1024]{1,0:T(8,128)(2,1)S(1)}, u32[]{:S(2)}, u32[]{:S(2)}) %collective-permute-start.15) | collective-permute-done | bytes 131104 | tf_op jit(solution)/shard_map/ppermute | solution.py:42
  104.4 0.8 add_convert_fusion.5
  105.2 0.8 add_convert_fusion.2
  106.0 3.3 %collective-permute-start.20 = (bf16[64,2048]{1,0:T(8,128)(2,1)S(1)}, bf16[64,2048]{1,0:T(8,128)(2,1)S(1)}, u32[]{:S(2)}, u32[]{:S(2)}) collective-permute-start(bf16[64,2048]{1,0:T(8,128)(2,1)S(1)} %add_convert_fusion.2), channel_id=1, source_target_pairs={{0,7},{1,0},{2,1},{3,2},{4,3},{5,4},{6,5},{7,6},{8,15},{9,8},{10,9... | collective-permute-start | bytes 786440 | tf_op jit(solution)/shard_map/ppermute | solution.py:42
  109.3 4.9 %collective-permute-done.16 = bf16[64,2048]{1,0:T(8,128)(2,1)S(1)} collective-permute-done((bf16[64,2048]{1,0:T(8,128)(2,1)S(1)}, bf16[64,2048]{1,0:T(8,128)(2,1)S(1)}, u32[]{:S(2)}, u32[]{:S(2)}) %collective-permute-start.16) | collective-permute-done | bytes 262176 | tf_op jit(solution)/shard_map/ppermute | solution.py:42
  114.2 0.8 add_convert_fusion.4
  115.0 0.8 add_convert_fusion.1
  115.8 3.3 %collective-permute-start.21 = (bf16[64,2048]{1,0:T(8,128)(2,1)S(1)}, bf16[64,2048]{1,0:T(8,128)(2,1)S(1)}, u32[]{:S(2)}, u32[]{:S(2)}) collective-permute-start(bf16[64,2048]{1,0:T(8,128)(2,1)S(1)} %add_convert_fusion.1), channel_id=1, source_target_pairs={{0,7},{1,0},{2,1},{3,2},{4,3},{5,4},{6,5},{7,6},{8,15},{9,8},{10,9... | collective-permute-start | bytes 786440 | tf_op jit(solution)/shard_map/ppermute | solution.py:42
  119.1 4.0 %collective-permute-done.17 = bf16[64,2048]{1,0:T(8,128)(2,1)S(1)} collective-permute-done((bf16[64,2048]{1,0:T(8,128)(2,1)S(1)}, bf16[64,2048]{1,0:T(8,128)(2,1)S(1)}, u32[]{:S(2)}, u32[]{:S(2)}) %collective-permute-start.17) | collective-permute-done | bytes 262176 | tf_op jit(solution)/shard_map/ppermute | solution.py:42
  123.1 0.8 add_convert_fusion.3
  123.9 0.8 add_convert_fusion
  124.7 3.3 %collective-permute-start.22 = (bf16[64,2048]{1,0:T(8,128)(2,1)S(1)}, bf16[64,2048]{1,0:T(8,128)(2,1)S(1)}, u32[]{:S(2)}, u32[]{:S(2)}) collective-permute-start(bf16[64,2048]{1,0:T(8,128)(2,1)S(1)} %add_convert_fusion), channel_id=1, source_target_pairs={{0,7},{1,0},{2,1},{3,2},{4,3},{5,4},{6,5},{7,6},{8,15},{9,8},{10,9... | collective-permute-start | bytes 786440 | tf_op jit(solution)/shard_map/ppermute | solution.py:42
  128.0 0.8 fusion.32
  128.8 2.7 %collective-permute-done.18 = bf16[64,2048]{1,0:T(8,128)(2,1)S(1)} collective-permute-done((bf16[64,2048]{1,0:T(8,128)(2,1)S(1)}, bf16[64,2048]{1,0:T(8,128)(2,1)S(1)}, u32[]{:S(2)}, u32[]{:S(2)}) %collective-permute-start.18) | collective-permute-done | bytes 262176 | tf_op jit(solution)/shard_map/ppermute | solution.py:42
  132.1 3.2 %collective-permute-start.25 = (f32[16,1024]{1,0:T(8,128)S(1)}, f32[16,1024]{1,0:T(8,128)S(1)}, u32[]{:S(2)}, u32[]{:S(2)}) collective-permute-start(f32[16,1024]{1,0:T(8,128)S(1)} %slice.41), channel_id=1, source_target_pairs={{0,24},{8,0},{16,8},{24,16},{1,25},{9,1},{17,9},{25,17},{2,26},{10... | collective-permute-start | bytes 196616 | tf_op jit(solution)/shard_map/ppermute | solution.py:42
  135.3 2.9 %collective-permute-done.23 = f32[16,1024]{1,0:T(8,128)S(1)} collective-permute-done((f32[16,1024]{1,0:T(8,128)S(1)}, f32[16,1024]{1,0:T(8,128)S(1)}, u32[]{:S(2)}, u32[]{:S(2)}) %collective-permute-start.23) | collective-permute-done | bytes 65568 | tf_op jit(solution)/shard_map/ppermute | solution.py:42
  138.3 3.4 %collective-permute-start.26 = (f32[16,2048]{1,0:T(8,128)S(1)}, f32[16,2048]{1,0:T(8,128)S(1)}, u32[]{:S(2)}, u32[]{:S(2)}) collective-permute-start(f32[16,2048]{1,0:T(8,128)S(1)} %get-tuple-element.10), channel_id=1, source_target_pairs={{0,24},{8,0},{16,8},{24,16},{1,25},{9,1},{17,9},{25,17},{2,26},{10... | collective-permute-start | bytes 393224 | tf_op jit(solution)/shard_map/ppermute | solution.py:42
  141.7 2.9 %collective-permute-done.24 = f32[16,2048]{1,0:T(8,128)S(1)} collective-permute-done((f32[16,2048]{1,0:T(8,128)S(1)}, f32[16,2048]{1,0:T(8,128)S(1)}, u32[]{:S(2)}, u32[]{:S(2)}) %collective-permute-start.24) | collective-permute-done | bytes 131104 | tf_op jit(solution)/shard_map/ppermute | solution.py:42
  144.6 0.7 fusion.11
  (54 shorter events, 4.0 us)
Async XLA Ops:
  0.0 5.7 %collective-permute-start = (bf16[16,2048]{1,0:T(8,128)(2,1)}, bf16[16,2048]{1,0:T(8,128)(2,1)S(1)}, u32[]{:S(2)}, u32[]{:S(2)}) collective-permute-start(bf16[16,2048]{1,0:T(8,128)(2,1)} %param.4), channel_id=1, source_target_pairs={{0,8},{8,16},{16,24},{24,0},{1,9},{9,17},{17,25},{25,1},{2,10},{10... | collective-permute-start | bytes 196616 | tf_op jit(solution)/shard_map/ppermute | solution.py:20
  1.6 9.6 %collective-permute-start.2 = (bf16[16,2048]{1,0:T(8,128)(2,1)}, bf16[16,2048]{1,0:T(8,128)(2,1)S(1)}, u32[]{:S(2)}, u32[]{:S(2)}) collective-permute-start(bf16[16,2048]{1,0:T(8,128)(2,1)} %param.4), channel_id=1, source_target_pairs={{0,24},{8,0},{16,8},{24,16},{1,25},{9,1},{17,9},{25,17},{2,26},{10... | collective-permute-start | bytes 196616 | tf_op jit(solution)/shard_map/ppermute | solution.py:24
  4.1 15.9 %copy-start.2 = (bf16[2048,896]{1,0:T(8,128)(2,1)S(1)}, bf16[2048,896]{1,0:T(8,128)(2,1)}, u32[]{:S(2)}) copy-start(bf16[2048,896]{1,0:T(8,128)(2,1)} %param.6) | copy-start | bytes 11010052
  5.7 5.5 %collective-permute-start.1 = (bf16[16,2048]{1,0:T(8,128)(2,1)S(1)}, bf16[16,2048]{1,0:T(8,128)(2,1)S(1)}, u32[]{:S(2)}, u32[]{:S(2)}) collective-permute-start(bf16[16,2048]{1,0:T(8,128)(2,1)S(1)} %collective-permute-done), channel_id=1, source_target_pairs={{0,8},{8,16},{16,24},{24,0},{1,9},{9,17},{17,25},{25,1},{2,10},{10... | collective-permute-start | bytes 196616 | tf_op jit(solution)/shard_map/ppermute | solution.py:20
  11.2 10.3 %collective-permute-start.3 = (bf16[64,2048]{1,0:T(8,128)(2,1)S(1)}, bf16[64,2048]{1,0:T(8,128)(2,1)S(1)}, u32[]{:S(2)}, u32[]{:S(2)}) collective-permute-start(bf16[64,2048]{1,0:T(8,128)(2,1)S(1)} %bitcast.168), channel_id=1, source_target_pairs={{0,1},{1,2},{2,3},{3,4},{4,5},{5,6},{6,7},{7,0},{8,9},{9,10},{10,1... | collective-permute-start | bytes 786440 | tf_op jit(solution)/shard_map/ppermute | solution.py:20
  13.2 10.3 %collective-permute-start.7 = (bf16[64,2048]{1,0:T(8,128)(2,1)S(1)}, bf16[64,2048]{1,0:T(8,128)(2,1)S(1)}, u32[]{:S(2)}, u32[]{:S(2)}) collective-permute-start(bf16[64,2048]{1,0:T(8,128)(2,1)S(1)} %bitcast.169), channel_id=1, source_target_pairs={{0,7},{1,0},{2,1},{3,2},{4,3},{5,4},{6,5},{7,6},{8,15},{9,8},{10,9... | collective-permute-start | bytes 786440 | tf_op jit(solution)/shard_map/ppermute | solution.py:24
  20.0 2.0 %copy-start.1 = (bf16[2048,896]{1,0:T(8,128)(2,1)S(1)}, bf16[2048,896]{1,0:T(8,128)(2,1)}, u32[]{:S(2)}) copy-start(bf16[2048,896]{1,0:T(8,128)(2,1)} %param.5) | copy-start | bytes 11010052
  22.7 7.7 %collective-permute-start.4 = (bf16[64,2048]{1,0:T(8,128)(2,1)S(1)}, bf16[64,2048]{1,0:T(8,128)(2,1)S(1)}, u32[]{:S(2)}, u32[]{:S(2)}) collective-permute-start(bf16[64,2048]{1,0:T(8,128)(2,1)S(1)} %collective-permute-done.3), channel_id=1, source_target_pairs={{0,1},{1,2},{2,3},{3,4},{4,5},{5,6},{6,7},{7,0},{8,9},{9,10},{10,1... | collective-permute-start | bytes 786440 | tf_op jit(solution)/shard_map/ppermute | solution.py:20
  24.9 7.2 %collective-permute-start.8 = (bf16[64,2048]{1,0:T(8,128)(2,1)S(1)}, bf16[64,2048]{1,0:T(8,128)(2,1)S(1)}, u32[]{:S(2)}, u32[]{:S(2)}) collective-permute-start(bf16[64,2048]{1,0:T(8,128)(2,1)S(1)} %collective-permute-done.7), channel_id=1, source_target_pairs={{0,7},{1,0},{2,1},{3,2},{4,3},{5,4},{6,5},{7,6},{8,15},{9,8},{10,9... | collective-permute-start | bytes 786440 | tf_op jit(solution)/shard_map/ppermute | solution.py:24
  31.1 8.0 %collective-permute-start.5 = (bf16[64,2048]{1,0:T(8,128)(2,1)S(1)}, bf16[64,2048]{1,0:T(8,128)(2,1)S(1)}, u32[]{:S(2)}, u32[]{:S(2)}) collective-permute-start(bf16[64,2048]{1,0:T(8,128)(2,1)S(1)} %collective-permute-done.4), channel_id=1, source_target_pairs={{0,1},{1,2},{2,3},{3,4},{4,5},{5,6},{6,7},{7,0},{8,9},{9,10},{10,1... | collective-permute-start | bytes 786440 | tf_op jit(solution)/shard_map/ppermute | solution.py:20
  33.6 7.8 %collective-permute-start.9 = (bf16[64,2048]{1,0:T(8,128)(2,1)S(1)}, bf16[64,2048]{1,0:T(8,128)(2,1)S(1)}, u32[]{:S(2)}, u32[]{:S(2)}) collective-permute-start(bf16[64,2048]{1,0:T(8,128)(2,1)S(1)} %collective-permute-done.8), channel_id=1, source_target_pairs={{0,7},{1,0},{2,1},{3,2},{4,3},{5,4},{6,5},{7,6},{8,15},{9,8},{10,9... | collective-permute-start | bytes 786440 | tf_op jit(solution)/shard_map/ppermute | solution.py:24
  39.8 7.7 %collective-permute-start.6 = (bf16[64,2048]{1,0:T(8,128)(2,1)S(1)}, bf16[64,2048]{1,0:T(8,128)(2,1)S(1)}, u32[]{:S(2)}, u32[]{:S(2)}) collective-permute-start(bf16[64,2048]{1,0:T(8,128)(2,1)S(1)} %collective-permute-done.5), channel_id=1, source_target_pairs={{0,1},{1,2},{2,3},{3,4},{4,5},{5,6},{6,7},{7,0},{8,9},{9,10},{10,1... | collective-permute-start | bytes 786440 | tf_op jit(solution)/shard_map/ppermute | solution.py:20
  49.0 1.8 %copy-start.3 = (f32[8,64,1792]{2,1,0:T(8,128)}, f32[8,64,1792]{2,1,0:T(8,128)S(1)}, u32[]{:S(2)}) copy-start(f32[8,64,1792]{2,1,0:T(8,128)S(1)} %fusion.7) | copy-start | bytes 11010052
  51.0 4.0 %collective-permute-start.10 = (f32[4,64,1792]{2,1,0:T(8,128)S(1)}, f32[4,64,1792]{2,1,0:T(8,128)}, u32[]{:S(2)}, u32[]{:S(2)}) collective-permute-start(f32[4,64,1792]{2,1,0:T(8,128)S(1)} %dynamic-slice_bitcast_fusion), channel_id=1, source_target_pairs={{0,32},{32,0},{1,33},{33,1},{2,34},{34,2},{3,35},{35,3},{4,36},{36... | collective-permute-start | bytes 5505032 | tf_op jit(solution)/shard_map/ppermute | solution.py:69
  57.3 7.7 %collective-permute-start.11 = (f32[64,896]{1,0:T(8,128)S(1)}, f32[64,896]{1,0:T(8,128)S(1)}, u32[]{:S(2)}, u32[]{:S(2)}) collective-permute-start(f32[64,896]{1,0:T(8,128)S(1)} %slice.34), channel_id=1, source_target_pairs={{0,64},{64,128},{128,192},{192,0},{1,65},{65,129},{129,193},{193,1... | collective-permute-start | bytes 688136 | tf_op jit(solution)/shard_map/ppermute | solution.py:42
  58.9 7.4 %collective-permute-start.13 = (f32[64,896]{1,0:T(8,128)S(1)}, f32[64,896]{1,0:T(8,128)S(1)}, u32[]{:S(2)}, u32[]{:S(2)}) collective-permute-start(f32[64,896]{1,0:T(8,128)S(1)} %slice.35), channel_id=1, source_target_pairs={{0,192},{64,0},{128,64},{192,128},{1,193},{65,1},{129,65},{193,129... | collective-permute-start | bytes 688136 | tf_op jit(solution)/shard_map/ppermute | solution.py:42
  66.4 11.5 %collective-permute-start.12 = (f32[64,1792]{1,0:T(8,128)S(1)}, f32[64,1792]{1,0:T(8,128)S(1)}, u32[]{:S(2)}, u32[]{:S(2)}) collective-permute-start(f32[64,1792]{1,0:T(8,128)S(1)} %get-tuple-element.5), channel_id=1, source_target_pairs={{0,64},{64,128},{128,192},{192,0},{1,65},{65,129},{129,193},{193,1... | collective-permute-start | bytes 1376264 | tf_op jit(solution)/shard_map/ppermute | solution.py:42
  67.7 11.2 %collective-permute-start.14 = (f32[64,1792]{1,0:T(8,128)S(1)}, f32[64,1792]{1,0:T(8,128)}, u32[]{:S(2)}, u32[]{:S(2)}) collective-permute-start(f32[64,1792]{1,0:T(8,128)S(1)} %get-tuple-element.6), channel_id=1, source_target_pairs={{0,192},{64,0},{128,64},{192,128},{1,193},{65,1},{129,65},{193,129... | collective-permute-start | bytes 1376264 | tf_op jit(solution)/shard_map/ppermute | solution.py:42
  68.5 28.9 %copy-start = (bf16[896,2048]{1,0:T(8,128)(2,1)S(1)}, bf16[896,2048]{1,0:T(8,128)(2,1)}, u32[]{:S(2)}) copy-start(bf16[896,2048]{1,0:T(8,128)(2,1)} %param.7) | copy-start | bytes 11010052
  97.3 7.0 %collective-permute-start.15 = (bf16[64,1024]{1,0:T(8,128)(2,1)S(1)}, bf16[64,1024]{1,0:T(8,128)(2,1)S(1)}, u32[]{:S(2)}, u32[]{:S(2)}) collective-permute-start(bf16[64,1024]{1,0:T(8,128)(2,1)S(1)} %slice.49), channel_id=1, source_target_pairs={{0,1},{1,2},{2,3},{3,4},{4,5},{5,6},{6,7},{7,0},{8,9},{9,10},{10,1... | collective-permute-start | bytes 393224 | tf_op jit(solution)/shard_map/ppermute | solution.py:42
  98.2 7.0 %collective-permute-start.19 = (bf16[64,1024]{1,0:T(8,128)(2,1)S(1)}, bf16[64,1024]{1,0:T(8,128)(2,1)S(1)}, u32[]{:S(2)}, u32[]{:S(2)}) collective-permute-start(bf16[64,1024]{1,0:T(8,128)(2,1)S(1)} %slice.48), channel_id=1, source_target_pairs={{0,7},{1,0},{2,1},{3,2},{4,3},{5,4},{6,5},{7,6},{8,15},{9,8},{10,9... | collective-permute-start | bytes 393224 | tf_op jit(solution)/shard_map/ppermute | solution.py:42
  105.1 9.0 %collective-permute-start.16 = (bf16[64,2048]{1,0:T(8,128)(2,1)S(1)}, bf16[64,2048]{1,0:T(8,128)(2,1)S(1)}, u32[]{:S(2)}, u32[]{:S(2)}) collective-permute-start(bf16[64,2048]{1,0:T(8,128)(2,1)S(1)} %add_convert_fusion.5), channel_id=1, source_target_pairs={{0,1},{1,2},{2,3},{3,4},{4,5},{5,6},{6,7},{7,0},{8,9},{9,10},{10,1... | collective-permute-start | bytes 786440 | tf_op jit(solution)/shard_map/ppermute | solution.py:42
  106.0 9.0 %collective-permute-start.20 = (bf16[64,2048]{1,0:T(8,128)(2,1)S(1)}, bf16[64,2048]{1,0:T(8,128)(2,1)S(1)}, u32[]{:S(2)}, u32[]{:S(2)}) collective-permute-start(bf16[64,2048]{1,0:T(8,128)(2,1)S(1)} %add_convert_fusion.2), channel_id=1, source_target_pairs={{0,7},{1,0},{2,1},{3,2},{4,3},{5,4},{6,5},{7,6},{8,15},{9,8},{10,9... | collective-permute-start | bytes 786440 | tf_op jit(solution)/shard_map/ppermute | solution.py:42
  114.9 8.1 %collective-permute-start.17 = (bf16[64,2048]{1,0:T(8,128)(2,1)S(1)}, bf16[64,2048]{1,0:T(8,128)(2,1)S(1)}, u32[]{:S(2)}, u32[]{:S(2)}) collective-permute-start(bf16[64,2048]{1,0:T(8,128)(2,1)S(1)} %add_convert_fusion.4), channel_id=1, source_target_pairs={{0,1},{1,2},{2,3},{3,4},{4,5},{5,6},{6,7},{7,0},{8,9},{9,10},{10,1... | collective-permute-start | bytes 786440 | tf_op jit(solution)/shard_map/ppermute | solution.py:42
  115.8 8.1 %collective-permute-start.21 = (bf16[64,2048]{1,0:T(8,128)(2,1)S(1)}, bf16[64,2048]{1,0:T(8,128)(2,1)S(1)}, u32[]{:S(2)}, u32[]{:S(2)}) collective-permute-start(bf16[64,2048]{1,0:T(8,128)(2,1)S(1)} %add_convert_fusion.1), channel_id=1, source_target_pairs={{0,7},{1,0},{2,1},{3,2},{4,3},{5,4},{6,5},{7,6},{8,15},{9,8},{10,9... | collective-permute-start | bytes 786440 | tf_op jit(solution)/shard_map/ppermute | solution.py:42
  123.8 7.7 %collective-permute-start.18 = (bf16[64,2048]{1,0:T(8,128)(2,1)S(1)}, bf16[64,2048]{1,0:T(8,128)(2,1)S(1)}, u32[]{:S(2)}, u32[]{:S(2)}) collective-permute-start(bf16[64,2048]{1,0:T(8,128)(2,1)S(1)} %add_convert_fusion.3), channel_id=1, source_target_pairs={{0,1},{1,2},{2,3},{3,4},{4,5},{5,6},{6,7},{7,0},{8,9},{9,10},{10,1... | collective-permute-start | bytes 786440 | tf_op jit(solution)/shard_map/ppermute | solution.py:42
  124.7 7.2 %collective-permute-start.22 = (bf16[64,2048]{1,0:T(8,128)(2,1)S(1)}, bf16[64,2048]{1,0:T(8,128)(2,1)S(1)}, u32[]{:S(2)}, u32[]{:S(2)}) collective-permute-start(bf16[64,2048]{1,0:T(8,128)(2,1)S(1)} %add_convert_fusion), channel_id=1, source_target_pairs={{0,7},{1,0},{2,1},{3,2},{4,3},{5,4},{6,5},{7,6},{8,15},{9,8},{10,9... | collective-permute-start | bytes 786440 | tf_op jit(solution)/shard_map/ppermute | solution.py:42
  132.0 6.2 %collective-permute-start.23 = (f32[16,1024]{1,0:T(8,128)S(1)}, f32[16,1024]{1,0:T(8,128)S(1)}, u32[]{:S(2)}, u32[]{:S(2)}) collective-permute-start(f32[16,1024]{1,0:T(8,128)S(1)} %slice.40), channel_id=1, source_target_pairs={{0,8},{8,16},{16,24},{24,0},{1,9},{9,17},{17,25},{25,1},{2,10},{10... | collective-permute-start | bytes 196616 | tf_op jit(solution)/shard_map/ppermute | solution.py:42
  132.1 6.1 %collective-permute-start.25 = (f32[16,1024]{1,0:T(8,128)S(1)}, f32[16,1024]{1,0:T(8,128)S(1)}, u32[]{:S(2)}, u32[]{:S(2)}) collective-permute-start(f32[16,1024]{1,0:T(8,128)S(1)} %slice.41), channel_id=1, source_target_pairs={{0,24},{8,0},{16,8},{24,16},{1,25},{9,1},{17,9},{25,17},{2,26},{10... | collective-permute-start | bytes 196616 | tf_op jit(solution)/shard_map/ppermute | solution.py:42
  138.3 6.3 %collective-permute-start.24 = (f32[16,2048]{1,0:T(8,128)S(1)}, f32[16,2048]{1,0:T(8,128)S(1)}, u32[]{:S(2)}, u32[]{:S(2)}) collective-permute-start(f32[16,2048]{1,0:T(8,128)S(1)} %get-tuple-element.9), channel_id=1, source_target_pairs={{0,8},{8,16},{16,24},{24,0},{1,9},{9,17},{17,25},{25,1},{2,10},{10... | collective-permute-start | bytes 393224 | tf_op jit(solution)/shard_map/ppermute | solution.py:42
  138.3 6.2 %collective-permute-start.26 = (f32[16,2048]{1,0:T(8,128)S(1)}, f32[16,2048]{1,0:T(8,128)S(1)}, u32[]{:S(2)}, u32[]{:S(2)}) collective-permute-start(f32[16,2048]{1,0:T(8,128)S(1)} %get-tuple-element.10), channel_id=1, source_target_pairs={{0,24},{8,0},{16,8},{24,16},{1,25},{9,1},{17,9},{25,17},{2,26},{10... | collective-permute-start | bytes 393224 | tf_op jit(solution)/shard_map/ppermute | solution.py:42

commit v9 on v8

--- a/solution.py
+++ b/solution.py
@@ -77,17 +77,12 @@
     width = gate_weight.shape[1]
     ny = lax.psum(1, "hy")
     nz = lax.psum(1, "hz")
+    both = jnp.concatenate([gate_weight, up_weight], axis=1)
     partial_value = ring_ag(
         ring_ag(rows_in, "hy", ny),
         "hz",
         nz,
-        lambda v: jnp.concatenate(
-            [
-                jnp.dot(v, gate_weight, preferred_element_type=jnp.float32),
-                jnp.dot(v, up_weight, preferred_element_type=jnp.float32),
-            ],
-            axis=1,
-        ),
+        lambda v: jnp.dot(v, both, preferred_element_type=jnp.float32),
     )
     summed = embed_rs(partial_value)
     activated = (jax.nn.silu(summed[:, :width]) * summed[:, width:]).astype(jnp.bfloat16)

time: 147 us -> 155 us (1.054)
  local copies, waits for them, and re-layouts: 3.8 us -> 10.9 us
    concatenate x0 -> x1, local copies, waits for them, and re-layouts: none -> 4.24 us  [on_device(): both = jnp.concatenate([gate_weight, up_weight], axis=1)]
    unnamed x8 -> x9, local copies, waits for them, and re-layouts: 2.31 us -> 6.04 us
    ppermute x6, waiting for transfers between devices: 15.3 us -> 17.8 us  [ring_ag(): buf = lax.ppermute(buf, axis, fwd)]
    dot_general x16 -> x8, matrix products: 13.3 us -> 14.1 us  [on_device(): jnp.dot(v, both, preferred_element_type=jnp.float32)]
  transfers between devices with their start and end apart: 27 -> 27, of which waited for: 20 -> 16; matrix products, arithmetic and copies ran while one was open for 13% -> 18% of each run, Pallas kernels for 0% -> 0%
where the time goes in v9:
time: 155 us; the launch traced here: 153 us
  waiting for transfers between devices  59.3 us (38%)
  starting transfers between devices  41 us (26%)
  matrix products  23 us (15%)
  blocking collectives  14.4 us (9%)
  local copies, waits for them, and re-layouts  10.9 us (7%)
  other arithmetic  4.23 us (3%)
    ppermute x16, waiting for transfers between devices, side(): got = lax.ppermute(acc.astype(send_dtype), axis, perm).astype(jnp.float32)  37.6 us
    ppermute x16, starting transfers between devices, side(): got = lax.ppermute(acc.astype(send_dtype), axis, perm).astype(jnp.float32)  24.7 us
    ppermute x6, waiting for transfers between devices, ring_ag(): buf = lax.ppermute(buf, axis, fwd)  17.8 us
    all_gather x1, blocking collectives, on_device(): activated = lax.all_gather(activated, EMBED, axis=0, tiled=True)  14.4 us
    dot_general x8, matrix products, on_device(): jnp.dot(v, both, preferred_element_type=jnp.float32)  14.1 us
    ppermute x4, starting transfers between devices, ring_ag(): buf = lax.ppermute(buf, axis, bwd)  12.1 us
    dot_general x9, matrix products, on_device(): jnp.dot(lax.dynamic_index_in_dim(act_blocks, i, 0, keepdims=False), down_...  8.91 us
    unnamed x9, local copies, waits for them, and re-layouts  6.04 us
  transfers between devices with their start and end apart: 27, of which 16 were waited for; matrix products, arithmetic and copies ran while one was open for 18% of the time, Pallas kernels for 0%

profile of v9, /device:TPU:2, one launch (start us, length us, event | category | flops | bytes accessed | tf_op | source)
XLA Modules:
  0.0 153.2 jit_solution(4815612351096670134)
XLA Ops:
  0.0 1.6 %collective-permute-start = (bf16[16,2048]{1,0:T(8,128)(2,1)}, bf16[16,2048]{1,0:T(8,128)(2,1)S(1)}, u32[]{:S(2)}, u32[]{:S(2)}) collective-permute-start(bf16[16,2048]{1,0:T(8,128)(2,1)} %param.4), channel_id=1, source_target_pairs={{0,8},{8,16},{16,24},{24,0},{1,9},{9,17},{17,25},{25,1},{2,10},{10... | collective-permute-start | bytes 196616 | tf_op jit(solution)/shard_map/ppermute | solution.py:20
  1.6 1.7 %collective-permute-start.2 = (bf16[16,2048]{1,0:T(8,128)(2,1)}, bf16[16,2048]{1,0:T(8,128)(2,1)S(1)}, u32[]{:S(2)}, u32[]{:S(2)}) collective-permute-start(bf16[16,2048]{1,0:T(8,128)(2,1)} %param.4), channel_id=1, source_target_pairs={{0,24},{8,0},{16,8},{24,16},{1,25},{9,1},{17,9},{25,17},{2,26},{10... | collective-permute-start | bytes 196616 | tf_op jit(solution)/shard_map/ppermute | solution.py:24
  3.2 4.3 %constant_dynamic-update-slice_fusion.1 = bf16[2048,1792]{1,0:T(8,128)(2,1)} fusion(bf16[2048,896]{1,0:T(8,128)(2,1)} %param.5), kind=kLoop, calls=%fused_computation.83 | loop fusion | bytes 7340032
  7.5 4.2 %constant_dynamic-update-slice_fusion = bf16[2048,1792]{1,0:T(8,128)(2,1)} fusion(bf16[2048,1792]{1,0:T(8,128)(2,1)} %constant_dynamic-update-slice_fusion.1, bf16[2048,896]{1,0:T(8,128)(2,1)} %param.6), kind=kLoop, calls=%fused_computation.82 | loop fusion | bytes 7340032 | tf_op jit(solution)/shard_map/concatenate | solution.py:80
  11.8 0.4 collective-permute-start.1
  12.2 5.1 %collective-permute-done.1 = bf16[16,2048]{1,0:T(8,128)(2,1)S(1)} collective-permute-done((bf16[16,2048]{1,0:T(8,128)(2,1)S(1)}, bf16[16,2048]{1,0:T(8,128)(2,1)S(1)}, u32[]{:S(2)}, u32[]{:S(2)}) %collective-permute-start.1) | collective-permute-done | bytes 65568 | tf_op jit(solution)/shard_map/ppermute | solution.py:20
  17.3 2.0 %collective-permute-start.3 = (bf16[64,2048]{1,0:T(8,128)(2,1)S(1)}, bf16[64,2048]{1,0:T(8,128)(2,1)S(1)}, u32[]{:S(2)}, u32[]{:S(2)}) collective-permute-start(bf16[64,2048]{1,0:T(8,128)(2,1)S(1)} %bitcast.152), channel_id=1, source_target_pairs={{0,1},{1,2},{2,3},{3,4},{4,5},{5,6},{6,7},{7,0},{8,9},{9,10},{10,1... | collective-permute-start | bytes 786440 | tf_op jit(solution)/shard_map/ppermute | solution.py:20
  19.3 4.0 %collective-permute-start.7 = (bf16[64,2048]{1,0:T(8,128)(2,1)S(1)}, bf16[64,2048]{1,0:T(8,128)(2,1)S(1)}, u32[]{:S(2)}, u32[]{:S(2)}) collective-permute-start(bf16[64,2048]{1,0:T(8,128)(2,1)S(1)} %bitcast.153), channel_id=1, source_target_pairs={{0,7},{1,0},{2,1},{3,2},{4,3},{5,4},{6,5},{7,6},{8,15},{9,8},{10,9... | collective-permute-start | bytes 786440 | tf_op jit(solution)/shard_map/ppermute | solution.py:24
  23.3 0.3 broadcast_in_dim.44
  23.6 4.6 %fusion.7 = f32[8,64,1792]{2,1,0:T(8,128)S(1)} fusion(f32[8,64,1792]{2,1,0:T(8,128)S(1)} %broadcast_in_dim.44, s32[]{:T(128)S(6)} %select_n.191, bf16[64,2048]{1,0:T(8,128)(2,1)S(1)} %bitcast.154, bf16[2048,1792]{1,0:T(8,128)(2,1)} %constant_dynamic-update-slice_fusion), kind=kOutput, calls=%fused_computation.15 | convolution fusion | flops 469762048 | bytes 8060932 | tf_op jit(solution)/shard_map/dot_general | solution.py:85
  28.2 0.1 collective-permute-start.4
  28.3 3.2 %collective-permute-start.8 = (bf16[64,2048]{1,0:T(8,128)(2,1)S(1)}, bf16[64,2048]{1,0:T(8,128)(2,1)S(1)}, u32[]{:S(2)}, u32[]{:S(2)}) collective-permute-start(bf16[64,2048]{1,0:T(8,128)(2,1)S(1)} %collective-permute-done.7), channel_id=1, source_target_pairs={{0,7},{1,0},{2,1},{3,2},{4,3},{5,4},{6,5},{7,6},{8,15},{9,8},{10,9... | collective-permute-start | bytes 786440 | tf_op jit(solution)/shard_map/ppermute | solution.py:24
  31.6 1.4 fusion.6
  32.9 3.0 %collective-permute-done.4 = bf16[64,2048]{1,0:T(8,128)(2,1)S(1)} collective-permute-done((bf16[64,2048]{1,0:T(8,128)(2,1)S(1)}, bf16[64,2048]{1,0:T(8,128)(2,1)S(1)}, u32[]{:S(2)}, u32[]{:S(2)}) %collective-permute-start.4) | collective-permute-done | bytes 262176 | tf_op jit(solution)/shard_map/ppermute | solution.py:20
  35.9 3.2 %collective-permute-start.9 = (bf16[64,2048]{1,0:T(8,128)(2,1)S(1)}, bf16[64,2048]{1,0:T(8,128)(2,1)S(1)}, u32[]{:S(2)}, u32[]{:S(2)}) collective-permute-start(bf16[64,2048]{1,0:T(8,128)(2,1)S(1)} %collective-permute-done.8), channel_id=1, source_target_pairs={{0,7},{1,0},{2,1},{3,2},{4,3},{5,4},{6,5},{7,6},{8,15},{9,8},{10,9... | collective-permute-start | bytes 786440 | tf_op jit(solution)/shard_map/ppermute | solution.py:24
  39.1 1.4 fusion.5
  40.5 3.5 %collective-permute-done.5 = bf16[64,2048]{1,0:T(8,128)(2,1)S(1)} collective-permute-done((bf16[64,2048]{1,0:T(8,128)(2,1)S(1)}, bf16[64,2048]{1,0:T(8,128)(2,1)S(1)}, u32[]{:S(2)}, u32[]{:S(2)}) %collective-permute-start.5) | collective-permute-done | bytes 262176 | tf_op jit(solution)/shard_map/ppermute | solution.py:20
  44.0 1.4 fusion.4
  45.4 6.2 %collective-permute-done.6 = bf16[64,2048]{1,0:T(8,128)(2,1)S(1)} collective-permute-done((bf16[64,2048]{1,0:T(8,128)(2,1)S(1)}, bf16[64,2048]{1,0:T(8,128)(2,1)S(1)}, u32[]{:S(2)}, u32[]{:S(2)}) %collective-permute-start.6) | collective-permute-done | bytes 262176 | tf_op jit(solution)/shard_map/ppermute | solution.py:20
  51.6 1.4 fusion.3
  52.9 1.4 fusion.2
  54.3 1.4 fusion.1
  55.7 1.4 fusion
  57.1 1.8 %copy-done.2 = f32[8,64,1792]{2,1,0:T(8,128)} copy-done((f32[8,64,1792]{2,1,0:T(8,128)}, f32[8,64,1792]{2,1,0:T(8,128)S(1)}, u32[]{:S(2)}) %copy-start.2) | copy-done | bytes 3670040
  58.8 0.1 dynamic-slice_bitcast_fusion
  59.0 0.1 collective-permute-start.10
  59.1 3.9 %collective-permute-done.10 = f32[4,64,1792]{2,1,0:T(8,128)} collective-permute-done((f32[4,64,1792]{2,1,0:T(8,128)S(1)}, f32[4,64,1792]{2,1,0:T(8,128)}, u32[]{:S(2)}, u32[]{:S(2)}) %collective-permute-start.10) | collective-permute-done | bytes 1835040 | tf_op jit(solution)/shard_map/ppermute | solution.py:69
  63.0 2.2 %bitcast_add_fusion = f32[4,64,1792]{2,1,0:T(8,128)S(1)} fusion(f32[4,64,1792]{2,1,0:T(8,128)} %collective-permute-done.10, f32[4,2,64,1792]{3,2,1,0:T(8,128)} %bitcast.139, s32[]{:T(128)S(6)} %select_n.206), kind=kLoop, calls=%fused_computation.16 | loop fusion | flops 458752 | bytes 5505028 | tf_op jit(solution)/shard_map/add | solution.py:70
  65.3 1.6 %collective-permute-start.11 = (f32[64,896]{1,0:T(8,128)S(1)}, f32[64,896]{1,0:T(8,128)S(1)}, u32[]{:S(2)}, u32[]{:S(2)}) collective-permute-start(f32[64,896]{1,0:T(8,128)S(1)} %slice.34), channel_id=1, source_target_pairs={{0,64},{64,128},{128,192},{192,0},{1,65},{65,129},{129,193},{193,1... | collective-permute-start | bytes 688136 | tf_op jit(solution)/shard_map/ppermute | solution.py:42
  66.9 0.6 collective-permute-start.13
  67.5 5.5 %collective-permute-done.11 = f32[64,896]{1,0:T(8,128)S(1)} collective-permute-done((f32[64,896]{1,0:T(8,128)S(1)}, f32[64,896]{1,0:T(8,128)S(1)}, u32[]{:S(2)}, u32[]{:S(2)}) %collective-permute-start.11) | collective-permute-done | bytes 229408 | tf_op jit(solution)/shard_map/ppermute | solution.py:42
  73.1 1.3 collective-permute-done.13
  74.4 1.3 collective-permute-start.12
  75.7 0.8 collective-permute-start.14
  76.5 9.4 %collective-permute-done.12 = f32[64,1792]{1,0:T(8,128)S(1)} collective-permute-done((f32[64,1792]{1,0:T(8,128)S(1)}, f32[64,1792]{1,0:T(8,128)S(1)}, u32[]{:S(2)}, u32[]{:S(2)}) %collective-permute-start.12) | collective-permute-done | bytes 458784 | tf_op jit(solution)/shard_map/ppermute | solution.py:42
  85.9 1.0 collective-permute-done.14
  87.0 1.1 fusion.8
  88.1 14.4 %all_gather.3 = bf16[512,896]{1,0:T(8,128)(2,1)S(1)} all-gather(bf16[64,896]{1,0:T(8,128)(2,1)S(1)} %fusion.9), channel_id=1, replica_groups=mesh['ex'=4,'ec'=2,'hy'=4,'hz'=8] {'ex','ec'}, dimensions={0}, use_global_device_ids=true | all-gather | bytes 1032192 | tf_op jit(solution)/shard_map/all_gather | solution.py:89
  102.5 2.8 %fusion.22 = bf16[64,2048]{1,0:T(8,128)(2,1)S(1)} fusion(bf16[896,2048]{1,0:T(8,128)(2,1)} %param.7, bf16[8,64,896]{2,1,0:T(8,128)(2,1)S(1)} %bitcast.140, s32[]{:T(128)S(6)} %select_n.221), kind=kOutput, calls=%fused_computation.50 | convolution fusion | flops 234881024 | bytes 4046852 | tf_op jit(solution)/shard_map/dot_general | solution.py:91
  105.3 0.1 collective-permute-start.15
  105.4 0.8 fusion.12
  106.2 3.5 %collective-permute-start.19 = (bf16[64,1024]{1,0:T(8,128)(2,1)S(1)}, bf16[64,1024]{1,0:T(8,128)(2,1)S(1)}, u32[]{:S(2)}, u32[]{:S(2)}) collective-permute-start(bf16[64,1024]{1,0:T(8,128)(2,1)S(1)} %slice.48), channel_id=1, source_target_pairs={{0,7},{1,0},{2,1},{3,2},{4,3},{5,4},{6,5},{7,6},{8,15},{9,8},{10,9... | collective-permute-start | bytes 393224 | tf_op jit(solution)/shard_map/ppermute | solution.py:42
  109.7 2.6 %collective-permute-done.15 = bf16[64,1024]{1,0:T(8,128)(2,1)S(1)} collective-permute-done((bf16[64,1024]{1,0:T(8,128)(2,1)S(1)}, bf16[64,1024]{1,0:T(8,128)(2,1)S(1)}, u32[]{:S(2)}, u32[]{:S(2)}) %collective-permute-start.15) | collective-permute-done | bytes 131104 | tf_op jit(solution)/shard_map/ppermute | solution.py:42
  112.4 0.8 add_convert_fusion.5
  113.2 0.1 collective-permute-start.16
  113.3 0.8 add_convert_fusion.2
  114.0 3.3 %collective-permute-start.20 = (bf16[64,2048]{1,0:T(8,128)(2,1)S(1)}, bf16[64,2048]{1,0:T(8,128)(2,1)S(1)}, u32[]{:S(2)}, u32[]{:S(2)}) collective-permute-start(bf16[64,2048]{1,0:T(8,128)(2,1)S(1)} %add_convert_fusion.2), channel_id=1, source_target_pairs={{0,7},{1,0},{2,1},{3,2},{4,3},{5,4},{6,5},{7,6},{8,15},{9,8},{10,9... | collective-permute-start | bytes 786440 | tf_op jit(solution)/shard_map/ppermute | solution.py:42
  117.3 4.9 %collective-permute-done.16 = bf16[64,2048]{1,0:T(8,128)(2,1)S(1)} collective-permute-done((bf16[64,2048]{1,0:T(8,128)(2,1)S(1)}, bf16[64,2048]{1,0:T(8,128)(2,1)S(1)}, u32[]{:S(2)}, u32[]{:S(2)}) %collective-permute-start.16) | collective-permute-done | bytes 262176 | tf_op jit(solution)/shard_map/ppermute | solution.py:42
  122.2 0.8 add_convert_fusion.4
  123.0 0.1 collective-permute-start.17
  123.1 0.8 add_convert_fusion.1
  123.8 3.3 %collective-permute-start.21 = (bf16[64,2048]{1,0:T(8,128)(2,1)S(1)}, bf16[64,2048]{1,0:T(8,128)(2,1)S(1)}, u32[]{:S(2)}, u32[]{:S(2)}) collective-permute-start(bf16[64,2048]{1,0:T(8,128)(2,1)S(1)} %add_convert_fusion.1), channel_id=1, source_target_pairs={{0,7},{1,0},{2,1},{3,2},{4,3},{5,4},{6,5},{7,6},{8,15},{9,8},{10,9... | collective-permute-start | bytes 786440 | tf_op jit(solution)/shard_map/ppermute | solution.py:42
  127.1 4.0 %collective-permute-done.17 = bf16[64,2048]{1,0:T(8,128)(2,1)S(1)} collective-permute-done((bf16[64,2048]{1,0:T(8,128)(2,1)S(1)}, bf16[64,2048]{1,0:T(8,128)(2,1)S(1)}, u32[]{:S(2)}, u32[]{:S(2)}) %collective-permute-start.17) | collective-permute-done | bytes 262176 | tf_op jit(solution)/shard_map/ppermute | solution.py:42
  131.1 0.8 add_convert_fusion.3
  132.0 0.8 add_convert_fusion
  132.7 3.3 %collective-permute-start.22 = (bf16[64,2048]{1,0:T(8,128)(2,1)S(1)}, bf16[64,2048]{1,0:T(8,128)(2,1)S(1)}, u32[]{:S(2)}, u32[]{:S(2)}) collective-permute-start(bf16[64,2048]{1,0:T(8,128)(2,1)S(1)} %add_convert_fusion), channel_id=1, source_target_pairs={{0,7},{1,0},{2,1},{3,2},{4,3},{5,4},{6,5},{7,6},{8,15},{9,8},{10,9... | collective-permute-start | bytes 786440 | tf_op jit(solution)/shard_map/ppermute | solution.py:42
  136.0 0.8 fusion.32
  136.8 2.7 %collective-permute-done.18 = bf16[64,2048]{1,0:T(8,128)(2,1)S(1)} collective-permute-done((bf16[64,2048]{1,0:T(8,128)(2,1)S(1)}, bf16[64,2048]{1,0:T(8,128)(2,1)S(1)}, u32[]{:S(2)}, u32[]{:S(2)}) %collective-permute-start.18) | collective-permute-done | bytes 262176 | tf_op jit(solution)/shard_map/ppermute | solution.py:42
  139.5 0.4 collective-permute-done.22
  140.1 3.2 %collective-permute-start.25 = (f32[16,1024]{1,0:T(8,128)S(1)}, f32[16,1024]{1,0:T(8,128)S(1)}, u32[]{:S(2)}, u32[]{:S(2)}) collective-permute-start(f32[16,1024]{1,0:T(8,128)S(1)} %slice.41), channel_id=1, source_target_pairs={{0,24},{8,0},{16,8},{24,16},{1,25},{9,1},{17,9},{25,17},{2,26},{10... | collective-permute-start | bytes 196616 | tf_op jit(solution)/shard_map/ppermute | solution.py:42
  143.4 2.9 %collective-permute-done.23 = f32[16,1024]{1,0:T(8,128)S(1)} collective-permute-done((f32[16,1024]{1,0:T(8,128)S(1)}, f32[16,1024]{1,0:T(8,128)S(1)}, u32[]{:S(2)}, u32[]{:S(2)}) %collective-permute-start.23) | collective-permute-done | bytes 65568 | tf_op jit(solution)/shard_map/ppermute | solution.py:42
  146.4 3.4 %collective-permute-start.26 = (f32[16,2048]{1,0:T(8,128)S(1)}, f32[16,2048]{1,0:T(8,128)S(1)}, u32[]{:S(2)}, u32[]{:S(2)}) collective-permute-start(f32[16,2048]{1,0:T(8,128)S(1)} %get-tuple-element.10), channel_id=1, source_target_pairs={{0,24},{8,0},{16,8},{24,16},{1,25},{9,1},{17,9},{25,17},{2,26},{10... | collective-permute-start | bytes 393224 | tf_op jit(solution)/shard_map/ppermute | solution.py:42
  149.7 2.9 %collective-permute-done.24 = f32[16,2048]{1,0:T(8,128)S(1)} collective-permute-done((f32[16,2048]{1,0:T(8,128)S(1)}, f32[16,2048]{1,0:T(8,128)S(1)}, u32[]{:S(2)}, u32[]{:S(2)}) %collective-permute-start.24) | collective-permute-done | bytes 131104 | tf_op jit(solution)/shard_map/ppermute | solution.py:42
  152.6 0.7 fusion.11
  (40 shorter events, 0.8 us)
Async XLA Ops:
  0.0 11.8 %collective-permute-start = (bf16[16,2048]{1,0:T(8,128)(2,1)}, bf16[16,2048]{1,0:T(8,128)(2,1)S(1)}, u32[]{:S(2)}, u32[]{:S(2)}) collective-permute-start(bf16[16,2048]{1,0:T(8,128)(2,1)} %param.4), channel_id=1, source_target_pairs={{0,8},{8,16},{16,24},{24,0},{1,9},{9,17},{17,25},{25,1},{2,10},{10... | collective-permute-start | bytes 196616 | tf_op jit(solution)/shard_map/ppermute | solution.py:20
  1.6 15.7 %collective-permute-start.2 = (bf16[16,2048]{1,0:T(8,128)(2,1)}, bf16[16,2048]{1,0:T(8,128)(2,1)S(1)}, u32[]{:S(2)}, u32[]{:S(2)}) collective-permute-start(bf16[16,2048]{1,0:T(8,128)(2,1)} %param.4), channel_id=1, source_target_pairs={{0,24},{8,0},{16,8},{24,16},{1,25},{9,1},{17,9},{25,17},{2,26},{10... | collective-permute-start | bytes 196616 | tf_op jit(solution)/shard_map/ppermute | solution.py:24
  3.2 4.3 %copy-start.3 = (bf16[16,2048]{1,0:T(8,128)(2,1)S(1)}, bf16[16,2048]{1,0:T(8,128)(2,1)}, u32[]{:S(2)}) copy-start(bf16[16,2048]{1,0:T(8,128)(2,1)} %param.4) | copy-start | bytes 196612
  11.8 5.5 %collective-permute-start.1 = (bf16[16,2048]{1,0:T(8,128)(2,1)S(1)}, bf16[16,2048]{1,0:T(8,128)(2,1)S(1)}, u32[]{:S(2)}, u32[]{:S(2)}) collective-permute-start(bf16[16,2048]{1,0:T(8,128)(2,1)S(1)} %collective-permute-done), channel_id=1, source_target_pairs={{0,8},{8,16},{16,24},{24,0},{1,9},{9,17},{17,25},{25,1},{2,10},{10... | collective-permute-start | bytes 196616 | tf_op jit(solution)/shard_map/ppermute | solution.py:20
  17.3 10.9 %collective-permute-start.3 = (bf16[64,2048]{1,0:T(8,128)(2,1)S(1)}, bf16[64,2048]{1,0:T(8,128)(2,1)S(1)}, u32[]{:S(2)}, u32[]{:S(2)}) collective-permute-start(bf16[64,2048]{1,0:T(8,128)(2,1)S(1)} %bitcast.152), channel_id=1, source_target_pairs={{0,1},{1,2},{2,3},{3,4},{4,5},{5,6},{6,7},{7,0},{8,9},{9,10},{10,1... | collective-permute-start | bytes 786440 | tf_op jit(solution)/shard_map/ppermute | solution.py:20
  19.3 9.0 %collective-permute-start.7 = (bf16[64,2048]{1,0:T(8,128)(2,1)S(1)}, bf16[64,2048]{1,0:T(8,128)(2,1)S(1)}, u32[]{:S(2)}, u32[]{:S(2)}) collective-permute-start(bf16[64,2048]{1,0:T(8,128)(2,1)S(1)} %bitcast.153), channel_id=1, source_target_pairs={{0,7},{1,0},{2,1},{3,2},{4,3},{5,4},{6,5},{7,6},{8,15},{9,8},{10,9... | collective-permute-start | bytes 786440 | tf_op jit(solution)/shard_map/ppermute | solution.py:24
  23.6 7.9 %copy-start = (bf16[2048,1792]{1,0:T(8,128)(2,1)S(1)}, bf16[2048,1792]{1,0:T(8,128)(2,1)}, u32[]{:S(2)}) copy-start(bf16[2048,1792]{1,0:T(8,128)(2,1)} %constant_dynamic-update-slice_fusion) | copy-start | bytes 22020100
  28.2 7.7 %collective-permute-start.4 = (bf16[64,2048]{1,0:T(8,128)(2,1)S(1)}, bf16[64,2048]{1,0:T(8,128)(2,1)S(1)}, u32[]{:S(2)}, u32[]{:S(2)}) collective-permute-start(bf16[64,2048]{1,0:T(8,128)(2,1)S(1)} %collective-permute-done.3), channel_id=1, source_target_pairs={{0,1},{1,2},{2,3},{3,4},{4,5},{5,6},{6,7},{7,0},{8,9},{9,10},{10,1... | collective-permute-start | bytes 786440 | tf_op jit(solution)/shard_map/ppermute | solution.py:20
  28.3 7.6 %collective-permute-start.8 = (bf16[64,2048]{1,0:T(8,128)(2,1)S(1)}, bf16[64,2048]{1,0:T(8,128)(2,1)S(1)}, u32[]{:S(2)}, u32[]{:S(2)}) collective-permute-start(bf16[64,2048]{1,0:T(8,128)(2,1)S(1)} %collective-permute-done.7), channel_id=1, source_target_pairs={{0,7},{1,0},{2,1},{3,2},{4,3},{5,4},{6,5},{7,6},{8,15},{9,8},{10,9... | collective-permute-start | bytes 786440 | tf_op jit(solution)/shard_map/ppermute | solution.py:24
  35.9 8.1 %collective-permute-start.5 = (bf16[64,2048]{1,0:T(8,128)(2,1)S(1)}, bf16[64,2048]{1,0:T(8,128)(2,1)S(1)}, u32[]{:S(2)}, u32[]{:S(2)}) collective-permute-start(bf16[64,2048]{1,0:T(8,128)(2,1)S(1)} %collective-permute-done.4), channel_id=1, source_target_pairs={{0,1},{1,2},{2,3},{3,4},{4,5},{5,6},{6,7},{7,0},{8,9},{9,10},{10,1... | collective-permute-start | bytes 786440 | tf_op jit(solution)/shard_map/ppermute | solution.py:20
  35.9 19.8 %collective-permute-start.9 = (bf16[64,2048]{1,0:T(8,128)(2,1)S(1)}, bf16[64,2048]{1,0:T(8,128)(2,1)S(1)}, u32[]{:S(2)}, u32[]{:S(2)}) collective-permute-start(bf16[64,2048]{1,0:T(8,128)(2,1)S(1)} %collective-permute-done.8), channel_id=1, source_target_pairs={{0,7},{1,0},{2,1},{3,2},{4,3},{5,4},{6,5},{7,6},{8,15},{9,8},{10,9... | collective-permute-start | bytes 786440 | tf_op jit(solution)/shard_map/ppermute | solution.py:24
  44.0 7.6 %collective-permute-start.6 = (bf16[64,2048]{1,0:T(8,128)(2,1)S(1)}, bf16[64,2048]{1,0:T(8,128)(2,1)S(1)}, u32[]{:S(2)}, u32[]{:S(2)}) collective-permute-start(bf16[64,2048]{1,0:T(8,128)(2,1)S(1)} %collective-permute-done.5), channel_id=1, source_target_pairs={{0,1},{1,2},{2,3},{3,4},{4,5},{5,6},{6,7},{7,0},{8,9},{9,10},{10,1... | collective-permute-start | bytes 786440 | tf_op jit(solution)/shard_map/ppermute | solution.py:20
  57.0 1.8 %copy-start.2 = (f32[8,64,1792]{2,1,0:T(8,128)}, f32[8,64,1792]{2,1,0:T(8,128)S(1)}, u32[]{:S(2)}) copy-start(f32[8,64,1792]{2,1,0:T(8,128)S(1)} %fusion) | copy-start | bytes 11010052
  59.0 4.0 %collective-permute-start.10 = (f32[4,64,1792]{2,1,0:T(8,128)S(1)}, f32[4,64,1792]{2,1,0:T(8,128)}, u32[]{:S(2)}, u32[]{:S(2)}) collective-permute-start(f32[4,64,1792]{2,1,0:T(8,128)S(1)} %dynamic-slice_bitcast_fusion), channel_id=1, source_target_pairs={{0,32},{32,0},{1,33},{33,1},{2,34},{34,2},{3,35},{35,3},{4,36},{36... | collective-permute-start | bytes 5505032 | tf_op jit(solution)/shard_map/ppermute | solution.py:69
  65.3 7.7 %collective-permute-start.11 = (f32[64,896]{1,0:T(8,128)S(1)}, f32[64,896]{1,0:T(8,128)S(1)}, u32[]{:S(2)}, u32[]{:S(2)}) collective-permute-start(f32[64,896]{1,0:T(8,128)S(1)} %slice.34), channel_id=1, source_target_pairs={{0,64},{64,128},{128,192},{192,0},{1,65},{65,129},{129,193},{193,1... | collective-permute-start | bytes 688136 | tf_op jit(solution)/shard_map/ppermute | solution.py:42
  66.9 7.4 %collective-permute-start.13 = (f32[64,896]{1,0:T(8,128)S(1)}, f32[64,896]{1,0:T(8,128)S(1)}, u32[]{:S(2)}, u32[]{:S(2)}) collective-permute-start(f32[64,896]{1,0:T(8,128)S(1)} %slice.35), channel_id=1, source_target_pairs={{0,192},{64,0},{128,64},{192,128},{1,193},{65,1},{129,65},{193,129... | collective-permute-start | bytes 688136 | tf_op jit(solution)/shard_map/ppermute | solution.py:42
  74.4 11.5 %collective-permute-start.12 = (f32[64,1792]{1,0:T(8,128)S(1)}, f32[64,1792]{1,0:T(8,128)S(1)}, u32[]{:S(2)}, u32[]{:S(2)}) collective-permute-start(f32[64,1792]{1,0:T(8,128)S(1)} %get-tuple-element.5), channel_id=1, source_target_pairs={{0,64},{64,128},{128,192},{192,0},{1,65},{65,129},{129,193},{193,1... | collective-permute-start | bytes 1376264 | tf_op jit(solution)/shard_map/ppermute | solution.py:42
  75.7 11.2 %collective-permute-start.14 = (f32[64,1792]{1,0:T(8,128)S(1)}, f32[64,1792]{1,0:T(8,128)}, u32[]{:S(2)}, u32[]{:S(2)}) collective-permute-start(f32[64,1792]{1,0:T(8,128)S(1)} %get-tuple-element.6), channel_id=1, source_target_pairs={{0,192},{64,0},{128,64},{192,128},{1,193},{65,1},{129,65},{193,129... | collective-permute-start | bytes 1376264 | tf_op jit(solution)/shard_map/ppermute | solution.py:42
  76.5 28.9 %copy-start.1 = (bf16[896,2048]{1,0:T(8,128)(2,1)S(1)}, bf16[896,2048]{1,0:T(8,128)(2,1)}, u32[]{:S(2)}) copy-start(bf16[896,2048]{1,0:T(8,128)(2,1)} %param.7) | copy-start | bytes 11010052
  105.3 7.0 %collective-permute-start.15 = (bf16[64,1024]{1,0:T(8,128)(2,1)S(1)}, bf16[64,1024]{1,0:T(8,128)(2,1)S(1)}, u32[]{:S(2)}, u32[]{:S(2)}) collective-permute-start(bf16[64,1024]{1,0:T(8,128)(2,1)S(1)} %slice.49), channel_id=1, source_target_pairs={{0,1},{1,2},{2,3},{3,4},{4,5},{5,6},{6,7},{7,0},{8,9},{9,10},{10,1... | collective-permute-start | bytes 393224 | tf_op jit(solution)/shard_map/ppermute | solution.py:42
  106.2 7.0 %collective-permute-start.19 = (bf16[64,1024]{1,0:T(8,128)(2,1)S(1)}, bf16[64,1024]{1,0:T(8,128)(2,1)S(1)}, u32[]{:S(2)}, u32[]{:S(2)}) collective-permute-start(bf16[64,1024]{1,0:T(8,128)(2,1)S(1)} %slice.48), channel_id=1, source_target_pairs={{0,7},{1,0},{2,1},{3,2},{4,3},{5,4},{6,5},{7,6},{8,15},{9,8},{10,9... | collective-permute-start | bytes 393224 | tf_op jit(solution)/shard_map/ppermute | solution.py:42
  113.2 9.0 %collective-permute-start.16 = (bf16[64,2048]{1,0:T(8,128)(2,1)S(1)}, bf16[64,2048]{1,0:T(8,128)(2,1)S(1)}, u32[]{:S(2)}, u32[]{:S(2)}) collective-permute-start(bf16[64,2048]{1,0:T(8,128)(2,1)S(1)} %add_convert_fusion.5), channel_id=1, source_target_pairs={{0,1},{1,2},{2,3},{3,4},{4,5},{5,6},{6,7},{7,0},{8,9},{9,10},{10,1... | collective-permute-start | bytes 786440 | tf_op jit(solution)/shard_map/ppermute | solution.py:42
  114.0 9.0 %collective-permute-start.20 = (bf16[64,2048]{1,0:T(8,128)(2,1)S(1)}, bf16[64,2048]{1,0:T(8,128)(2,1)S(1)}, u32[]{:S(2)}, u32[]{:S(2)}) collective-permute-start(bf16[64,2048]{1,0:T(8,128)(2,1)S(1)} %add_convert_fusion.2), channel_id=1, source_target_pairs={{0,7},{1,0},{2,1},{3,2},{4,3},{5,4},{6,5},{7,6},{8,15},{9,8},{10,9... | collective-permute-start | bytes 786440 | tf_op jit(solution)/shard_map/ppermute | solution.py:42
  123.0 8.1 %collective-permute-start.17 = (bf16[64,2048]{1,0:T(8,128)(2,1)S(1)}, bf16[64,2048]{1,0:T(8,128)(2,1)S(1)}, u32[]{:S(2)}, u32[]{:S(2)}) collective-permute-start(bf16[64,2048]{1,0:T(8,128)(2,1)S(1)} %add_convert_fusion.4), channel_id=1, source_target_pairs={{0,1},{1,2},{2,3},{3,4},{4,5},{5,6},{6,7},{7,0},{8,9},{9,10},{10,1... | collective-permute-start | bytes 786440 | tf_op jit(solution)/shard_map/ppermute | solution.py:42
  123.8 8.1 %collective-permute-start.21 = (bf16[64,2048]{1,0:T(8,128)(2,1)S(1)}, bf16[64,2048]{1,0:T(8,128)(2,1)S(1)}, u32[]{:S(2)}, u32[]{:S(2)}) collective-permute-start(bf16[64,2048]{1,0:T(8,128)(2,1)S(1)} %add_convert_fusion.1), channel_id=1, source_target_pairs={{0,7},{1,0},{2,1},{3,2},{4,3},{5,4},{6,5},{7,6},{8,15},{9,8},{10,9... | collective-permute-start | bytes 786440 | tf_op jit(solution)/shard_map/ppermute | solution.py:42
  131.9 7.7 %collective-permute-start.18 = (bf16[64,2048]{1,0:T(8,128)(2,1)S(1)}, bf16[64,2048]{1,0:T(8,128)(2,1)S(1)}, u32[]{:S(2)}, u32[]{:S(2)}) collective-permute-start(bf16[64,2048]{1,0:T(8,128)(2,1)S(1)} %add_convert_fusion.3), channel_id=1, source_target_pairs={{0,1},{1,2},{2,3},{3,4},{4,5},{5,6},{6,7},{7,0},{8,9},{9,10},{10,1... | collective-permute-start | bytes 786440 | tf_op jit(solution)/shard_map/ppermute | solution.py:42
  132.7 7.2 %collective-permute-start.22 = (bf16[64,2048]{1,0:T(8,128)(2,1)S(1)}, bf16[64,2048]{1,0:T(8,128)(2,1)S(1)}, u32[]{:S(2)}, u32[]{:S(2)}) collective-permute-start(bf16[64,2048]{1,0:T(8,128)(2,1)S(1)} %add_convert_fusion), channel_id=1, source_target_pairs={{0,7},{1,0},{2,1},{3,2},{4,3},{5,4},{6,5},{7,6},{8,15},{9,8},{10,9... | collective-permute-start | bytes 786440 | tf_op jit(solution)/shard_map/ppermute | solution.py:42
  140.0 6.2 %collective-permute-start.23 = (f32[16,1024]{1,0:T(8,128)S(1)}, f32[16,1024]{1,0:T(8,128)S(1)}, u32[]{:S(2)}, u32[]{:S(2)}) collective-permute-start(f32[16,1024]{1,0:T(8,128)S(1)} %slice.40), channel_id=1, source_target_pairs={{0,8},{8,16},{16,24},{24,0},{1,9},{9,17},{17,25},{25,1},{2,10},{10... | collective-permute-start | bytes 196616 | tf_op jit(solution)/shard_map/ppermute | solution.py:42
  140.1 6.1 %collective-permute-start.25 = (f32[16,1024]{1,0:T(8,128)S(1)}, f32[16,1024]{1,0:T(8,128)S(1)}, u32[]{:S(2)}, u32[]{:S(2)}) collective-permute-start(f32[16,1024]{1,0:T(8,128)S(1)} %slice.41), channel_id=1, source_target_pairs={{0,24},{8,0},{16,8},{24,16},{1,25},{9,1},{17,9},{25,17},{2,26},{10... | collective-permute-start | bytes 196616 | tf_op jit(solution)/shard_map/ppermute | solution.py:42
  146.3 6.3 %collective-permute-start.24 = (f32[16,2048]{1,0:T(8,128)S(1)}, f32[16,2048]{1,0:T(8,128)S(1)}, u32[]{:S(2)}, u32[]{:S(2)}) collective-permute-start(f32[16,2048]{1,0:T(8,128)S(1)} %get-tuple-element.9), channel_id=1, source_target_pairs={{0,8},{8,16},{16,24},{24,0},{1,9},{9,17},{17,25},{25,1},{2,10},{10... | collective-permute-start | bytes 393224 | tf_op jit(solution)/shard_map/ppermute | solution.py:42
  146.4 6.2 %collective-permute-start.26 = (f32[16,2048]{1,0:T(8,128)S(1)}, f32[16,2048]{1,0:T(8,128)S(1)}, u32[]{:S(2)}, u32[]{:S(2)}) collective-permute-start(f32[16,2048]{1,0:T(8,128)S(1)} %get-tuple-element.10), channel_id=1, source_target_pairs={{0,24},{8,0},{16,8},{24,16},{1,25},{9,1},{17,9},{25,17},{2,26},{10... | collective-permute-start | bytes 393224 | tf_op jit(solution)/shard_map/ppermute | solution.py:42

commit v10 on v8

--- a/solution.py
+++ b/solution.py
@@ -35,8 +35,9 @@
     own = get(k)
     h = own.shape[-1] // 2
 
+    far = get(k + nf)
+
     def side(perm, sign, cols):
-        far = get(k + sign * nf)
         acc = far[..., :h] if cols == 0 else far[..., h:]
         for s in range(nf):
             got = lax.ppermute(acc.astype(send_dtype), axis, perm).astype(jnp.float32)

time: 147 us -> 149 us (1.014)
    dot_general x9 -> x8, matrix products: 8.91 us -> 10.2 us  [on_device(): jnp.dot(lax.dynamic_index_in_dim(act_blocks, i, 0, keepdims=False), down_...]
  transfers between devices with their start and end apart: 27 -> 27, of which waited for: 20 -> 20; matrix products, arithmetic and copies ran while one was open for 13% -> 14% of each run, Pallas kernels for 0% -> 0%
where the time goes in v10:
time: 149 us; the launch traced here: 147 us
  waiting for transfers between devices  58.9 us (40%)
  starting transfers between devices  41.8 us (28%)
  matrix products  23.5 us (16%)
  blocking collectives  14.5 us (10%)
  other arithmetic  4.52 us (3%)
  local copies, waits for them, and re-layouts  3.76 us (3%)
    ppermute x16, waiting for transfers between devices, side(): got = lax.ppermute(acc.astype(send_dtype), axis, perm).astype(jnp.float32)  38.7 us
    ppermute x16, starting transfers between devices, side(): got = lax.ppermute(acc.astype(send_dtype), axis, perm).astype(jnp.float32)  24.5 us
    ppermute x6, waiting for transfers between devices, ring_ag(): buf = lax.ppermute(buf, axis, fwd)  15.3 us
    all_gather x1, blocking collectives, on_device(): activated = lax.all_gather(activated, EMBED, axis=0, tiled=True)  14.5 us
    ppermute x4, starting transfers between devices, ring_ag(): buf = lax.ppermute(buf, axis, bwd)  12.9 us
    dot_general x8, matrix products, on_device(): jnp.dot(lax.dynamic_index_in_dim(act_blocks, i, 0, keepdims=False), down_...  10.2 us
    dot_general x8, matrix products, on_device(): jnp.dot(v, gate_weight, preferred_element_type=jnp.float32)  7.67 us
    dot_general x8, matrix products, on_device(): jnp.dot(v, up_weight, preferred_element_type=jnp.float32)  5.67 us
  transfers between devices with their start and end apart: 27, of which 20 were waited for; matrix products, arithmetic and copies ran while one was open for 14% of the time, Pallas kernels for 0%

profile of v10, /device:TPU:2, one launch (start us, length us, event | category | flops | bytes accessed | tf_op | source)
XLA Modules:
  0.0 147.5 jit_solution(7257189919307146823)
XLA Ops:
  0.0 1.6 %collective-permute-start = (bf16[16,2048]{1,0:T(8,128)(2,1)}, bf16[16,2048]{1,0:T(8,128)(2,1)S(1)}, u32[]{:S(2)}, u32[]{:S(2)}) collective-permute-start(bf16[16,2048]{1,0:T(8,128)(2,1)} %param.4), channel_id=1, source_target_pairs={{0,8},{8,16},{16,24},{24,0},{1,9},{9,17},{17,25},{25,1},{2,10},{10... | collective-permute-start | bytes 196616 | tf_op jit(solution)/shard_map/ppermute | solution.py:20
  1.6 1.7 %collective-permute-start.2 = (bf16[16,2048]{1,0:T(8,128)(2,1)}, bf16[16,2048]{1,0:T(8,128)(2,1)S(1)}, u32[]{:S(2)}, u32[]{:S(2)}) collective-permute-start(bf16[16,2048]{1,0:T(8,128)(2,1)} %param.4), channel_id=1, source_target_pairs={{0,24},{8,0},{16,8},{24,16},{1,25},{9,1},{17,9},{25,17},{2,26},{10... | collective-permute-start | bytes 196616 | tf_op jit(solution)/shard_map/ppermute | solution.py:24
  3.3 0.9 bitcast_dynamic-update-slice_fusion.3
  4.1 1.6 %collective-permute-done = bf16[16,2048]{1,0:T(8,128)(2,1)S(1)} collective-permute-done((bf16[16,2048]{1,0:T(8,128)(2,1)}, bf16[16,2048]{1,0:T(8,128)(2,1)S(1)}, u32[]{:S(2)}, u32[]{:S(2)}) %collective-permute-start) | collective-permute-done | bytes 65568 | tf_op jit(solution)/shard_map/ppermute | solution.py:20
  6.1 5.1 %collective-permute-done.1 = bf16[16,2048]{1,0:T(8,128)(2,1)S(1)} collective-permute-done((bf16[16,2048]{1,0:T(8,128)(2,1)S(1)}, bf16[16,2048]{1,0:T(8,128)(2,1)S(1)}, u32[]{:S(2)}, u32[]{:S(2)}) %collective-permute-start.1) | collective-permute-done | bytes 65568 | tf_op jit(solution)/shard_map/ppermute | solution.py:20
  11.2 2.0 %collective-permute-start.3 = (bf16[64,2048]{1,0:T(8,128)(2,1)S(1)}, bf16[64,2048]{1,0:T(8,128)(2,1)S(1)}, u32[]{:S(2)}, u32[]{:S(2)}) collective-permute-start(bf16[64,2048]{1,0:T(8,128)(2,1)S(1)} %bitcast.156), channel_id=1, source_target_pairs={{0,1},{1,2},{2,3},{3,4},{4,5},{5,6},{6,7},{7,0},{8,9},{9,10},{10,1... | collective-permute-start | bytes 786440 | tf_op jit(solution)/shard_map/ppermute | solution.py:20
  13.2 4.0 %collective-permute-start.7 = (bf16[64,2048]{1,0:T(8,128)(2,1)S(1)}, bf16[64,2048]{1,0:T(8,128)(2,1)S(1)}, u32[]{:S(2)}, u32[]{:S(2)}) collective-permute-start(bf16[64,2048]{1,0:T(8,128)(2,1)S(1)} %bitcast.157), channel_id=1, source_target_pairs={{0,7},{1,0},{2,1},{3,2},{4,3},{5,4},{6,5},{7,6},{8,15},{9,8},{10,9... | collective-permute-start | bytes 786440 | tf_op jit(solution)/shard_map/ppermute | solution.py:24
  17.2 2.7 %fusion.58 = f32[64,896]{1,0:T(8,128)S(1)} fusion(bf16[64,2048]{1,0:T(8,128)(2,1)S(1)} %bitcast.158, bf16[2048,896]{1,0:T(8,128)(2,1)} %param.5), kind=kOutput, calls=%fused_computation.77 | convolution fusion | flops 234881024 | bytes 4161536 | tf_op jit(solution)/shard_map/dot_general | solution.py:87
  20.0 0.7 fusion.59
  21.5 0.5 copy-done.1
  22.0 0.7 fusion.60
  22.8 0.7 fusion.61
  23.5 0.7 fusion.68
  24.2 0.7 fusion.69
  24.9 3.3 %collective-permute-start.8 = (bf16[64,2048]{1,0:T(8,128)(2,1)S(1)}, bf16[64,2048]{1,0:T(8,128)(2,1)S(1)}, u32[]{:S(2)}, u32[]{:S(2)}) collective-permute-start(bf16[64,2048]{1,0:T(8,128)(2,1)S(1)} %collective-permute-done.7), channel_id=1, source_target_pairs={{0,7},{1,0},{2,1},{3,2},{4,3},{5,4},{6,5},{7,6},{8,15},{9,8},{10,9... | collective-permute-start | bytes 786440 | tf_op jit(solution)/shard_map/ppermute | solution.py:24
  28.3 2.1 %collective-permute-done.4 = bf16[64,2048]{1,0:T(8,128)(2,1)S(1)} collective-permute-done((bf16[64,2048]{1,0:T(8,128)(2,1)S(1)}, bf16[64,2048]{1,0:T(8,128)(2,1)S(1)}, u32[]{:S(2)}, u32[]{:S(2)}) %collective-permute-start.4) | collective-permute-done | bytes 262176 | tf_op jit(solution)/shard_map/ppermute | solution.py:20
  30.4 0.7 fusion.62
  31.2 0.7 fusion.63
  32.1 0.7 fusion.70
  32.8 0.7 fusion.71
  33.6 3.9 %collective-permute-start.9 = (bf16[64,2048]{1,0:T(8,128)(2,1)S(1)}, bf16[64,2048]{1,0:T(8,128)(2,1)S(1)}, u32[]{:S(2)}, u32[]{:S(2)}) collective-permute-start(bf16[64,2048]{1,0:T(8,128)(2,1)S(1)} %collective-permute-done.8), channel_id=1, source_target_pairs={{0,7},{1,0},{2,1},{3,2},{4,3},{5,4},{6,5},{7,6},{8,15},{9,8},{10,9... | collective-permute-start | bytes 786440 | tf_op jit(solution)/shard_map/ppermute | solution.py:24
  37.5 1.5 %collective-permute-done.5 = bf16[64,2048]{1,0:T(8,128)(2,1)S(1)} collective-permute-done((bf16[64,2048]{1,0:T(8,128)(2,1)S(1)}, bf16[64,2048]{1,0:T(8,128)(2,1)S(1)}, u32[]{:S(2)}, u32[]{:S(2)}) %collective-permute-start.5) | collective-permute-done | bytes 262176 | tf_op jit(solution)/shard_map/ppermute | solution.py:20
  39.1 0.7 fusion.64
  39.9 0.7 fusion.65
  40.6 0.8 collective-permute-done.9
  41.4 0.7 fusion.72
  42.1 0.7 fusion.73
  42.9 4.6 %collective-permute-done.6 = bf16[64,2048]{1,0:T(8,128)(2,1)S(1)} collective-permute-done((bf16[64,2048]{1,0:T(8,128)(2,1)S(1)}, bf16[64,2048]{1,0:T(8,128)(2,1)S(1)}, u32[]{:S(2)}, u32[]{:S(2)}) %collective-permute-start.6) | collective-permute-done | bytes 262176 | tf_op jit(solution)/shard_map/ppermute | solution.py:20
  47.4 0.7 fusion.66
  48.2 0.7 fusion.67
  49.0 1.8 %copy-done.3 = f32[8,64,1792]{2,1,0:T(8,128)} copy-done((f32[8,64,1792]{2,1,0:T(8,128)}, f32[8,64,1792]{2,1,0:T(8,128)S(1)}, u32[]{:S(2)}) %copy-start.3) | copy-done | bytes 3670040
  51.1 3.9 %collective-permute-done.10 = f32[4,64,1792]{2,1,0:T(8,128)} collective-permute-done((f32[4,64,1792]{2,1,0:T(8,128)S(1)}, f32[4,64,1792]{2,1,0:T(8,128)}, u32[]{:S(2)}, u32[]{:S(2)}) %collective-permute-start.10) | collective-permute-done | bytes 1835040 | tf_op jit(solution)/shard_map/ppermute | solution.py:70
  55.0 2.2 %bitcast_add_fusion = f32[4,64,1792]{2,1,0:T(8,128)S(1)} fusion(f32[4,64,1792]{2,1,0:T(8,128)} %collective-permute-done.10, f32[4,2,64,1792]{3,2,1,0:T(8,128)} %bitcast.147, s32[]{:T(128)S(6)} %select_n.193), kind=kLoop, calls=%fused_computation.1 | loop fusion | flops 458752 | bytes 5505028 | tf_op jit(solution)/shard_map/add | solution.py:71
  57.3 1.6 %collective-permute-start.11 = (f32[64,896]{1,0:T(8,128)S(1)}, f32[64,896]{1,0:T(8,128)S(1)}, u32[]{:S(2)}, u32[]{:S(2)}) collective-permute-start(f32[64,896]{1,0:T(8,128)S(1)} %get-tuple-element.9), channel_id=1, source_target_pairs={{0,64},{64,128},{128,192},{192,0},{1,65},{65,129},{129,193},{193,1... | collective-permute-start | bytes 688136 | tf_op jit(solution)/shard_map/ppermute | solution.py:43
  58.9 0.5 collective-permute-start.13
  59.4 5.6 %collective-permute-done.11 = f32[64,896]{1,0:T(8,128)S(1)} collective-permute-done((f32[64,896]{1,0:T(8,128)S(1)}, f32[64,896]{1,0:T(8,128)S(1)}, u32[]{:S(2)}, u32[]{:S(2)}) %collective-permute-start.11) | collective-permute-done | bytes 229408 | tf_op jit(solution)/shard_map/ppermute | solution.py:43
  65.0 1.2 collective-permute-done.13
  66.3 1.3 collective-permute-start.12
  67.6 0.8 collective-permute-start.14
  68.4 9.4 %collective-permute-done.12 = f32[64,1792]{1,0:T(8,128)S(1)} collective-permute-done((f32[64,1792]{1,0:T(8,128)S(1)}, f32[64,1792]{1,0:T(8,128)S(1)}, u32[]{:S(2)}, u32[]{:S(2)}) %collective-permute-start.12) | collective-permute-done | bytes 458784 | tf_op jit(solution)/shard_map/ppermute | solution.py:43
  77.8 1.0 collective-permute-done.14
  78.8 1.1 fusion.8
  80.0 14.5 %all_gather.3 = bf16[512,896]{1,0:T(8,128)(2,1)S(1)} all-gather(bf16[64,896]{1,0:T(8,128)(2,1)S(1)} %fusion.9), channel_id=1, replica_groups=mesh['ex'=4,'ec'=2,'hy'=4,'hz'=8] {'ex','ec'}, dimensions={0}, use_global_device_ids=true | all-gather | bytes 1032192 | tf_op jit(solution)/shard_map/all_gather | solution.py:95
  94.5 2.8 %convolution_convert_fusion = bf16[64,2048]{1,0:T(8,128)(2,1)S(1)} fusion(bf16[896,2048]{1,0:T(8,128)(2,1)} %param.7, bf16[8,64,896]{2,1,0:T(8,128)(2,1)S(1)} %bitcast.148, s32[]{:T(128)S(6)} %select_n.206), kind=kOutput, calls=%fused_computation | convolution fusion | flops 235012096 | bytes 4046852 | tf_op jit(solution)/shard_map/dot_general | solution.py:97
  97.5 3.2 %collective-permute-start.19 = (bf16[64,1024]{1,0:T(8,128)(2,1)S(1)}, bf16[64,1024]{1,0:T(8,128)(2,1)S(1)}, u32[]{:S(2)}, u32[]{:S(2)}) collective-permute-start(bf16[64,1024]{1,0:T(8,128)(2,1)S(1)} %get-tuple-element.12), channel_id=1, source_target_pairs={{0,7},{1,0},{2,1},{3,2},{4,3},{5,4},{6,5},{7,6},{8,15},{9,8},{10,9... | collective-permute-start | bytes 393224 | tf_op jit(solution)/shard_map/ppermute | solution.py:43
  100.6 3.7 %collective-permute-done.15 = bf16[64,1024]{1,0:T(8,128)(2,1)S(1)} collective-permute-done((bf16[64,1024]{1,0:T(8,128)(2,1)S(1)}, bf16[64,1024]{1,0:T(8,128)(2,1)S(1)}, u32[]{:S(2)}, u32[]{:S(2)}) %collective-permute-start.15) | collective-permute-done | bytes 131104 | tf_op jit(solution)/shard_map/ppermute | solution.py:43
  104.4 2.8 %add_convert_fusion.5 = bf16[64,2048]{1,0:T(8,128)(2,1)S(1)} fusion(bf16[64,1024]{1,0:T(8,128)(2,1)S(1)} %collective-permute-done.15, bf16[896,2048]{1,0:T(8,128)(2,1)} %param.7, bf16[8,64,896]{2,1,0:T(8,128)(2,1)S(1)} %bitcast.149, s32[]{:T(128)S(6)} %select_n.192), kind=kOutput, calls=%fused_computation.9 | convolution fusion | flops 235274240 | bytes 4177924 | tf_op jit(solution)/shard_map/dot_general | solution.py:97
  107.5 0.8 add_convert_fusion.2
  108.3 3.3 %collective-permute-start.20 = (bf16[64,2048]{1,0:T(8,128)(2,1)S(1)}, bf16[64,2048]{1,0:T(8,128)(2,1)S(1)}, u32[]{:S(2)}, u32[]{:S(2)}) collective-permute-start(bf16[64,2048]{1,0:T(8,128)(2,1)S(1)} %add_convert_fusion.2), channel_id=1, source_target_pairs={{0,7},{1,0},{2,1},{3,2},{4,3},{5,4},{6,5},{7,6},{8,15},{9,8},{10,9... | collective-permute-start | bytes 786440 | tf_op jit(solution)/shard_map/ppermute | solution.py:43
  111.6 4.9 %collective-permute-done.16 = bf16[64,2048]{1,0:T(8,128)(2,1)S(1)} collective-permute-done((bf16[64,2048]{1,0:T(8,128)(2,1)S(1)}, bf16[64,2048]{1,0:T(8,128)(2,1)S(1)}, u32[]{:S(2)}, u32[]{:S(2)}) %collective-permute-start.16) | collective-permute-done | bytes 262176 | tf_op jit(solution)/shard_map/ppermute | solution.py:43
  116.4 0.8 add_convert_fusion.4
  117.3 0.8 add_convert_fusion.1
  118.1 3.3 %collective-permute-start.21 = (bf16[64,2048]{1,0:T(8,128)(2,1)S(1)}, bf16[64,2048]{1,0:T(8,128)(2,1)S(1)}, u32[]{:S(2)}, u32[]{:S(2)}) collective-permute-start(bf16[64,2048]{1,0:T(8,128)(2,1)S(1)} %add_convert_fusion.1), channel_id=1, source_target_pairs={{0,7},{1,0},{2,1},{3,2},{4,3},{5,4},{6,5},{7,6},{8,15},{9,8},{10,9... | collective-permute-start | bytes 786440 | tf_op jit(solution)/shard_map/ppermute | solution.py:43
  121.4 4.0 %collective-permute-done.17 = bf16[64,2048]{1,0:T(8,128)(2,1)S(1)} collective-permute-done((bf16[64,2048]{1,0:T(8,128)(2,1)S(1)}, bf16[64,2048]{1,0:T(8,128)(2,1)S(1)}, u32[]{:S(2)}, u32[]{:S(2)}) %collective-permute-start.17) | collective-permute-done | bytes 262176 | tf_op jit(solution)/shard_map/ppermute | solution.py:43
  125.3 0.8 add_convert_fusion.3
  126.2 0.8 add_convert_fusion
  127.0 3.3 %collective-permute-start.22 = (bf16[64,2048]{1,0:T(8,128)(2,1)S(1)}, bf16[64,2048]{1,0:T(8,128)(2,1)S(1)}, u32[]{:S(2)}, u32[]{:S(2)}) collective-permute-start(bf16[64,2048]{1,0:T(8,128)(2,1)S(1)} %add_convert_fusion), channel_id=1, source_target_pairs={{0,7},{1,0},{2,1},{3,2},{4,3},{5,4},{6,5},{7,6},{8,15},{9,8},{10,9... | collective-permute-start | bytes 786440 | tf_op jit(solution)/shard_map/ppermute | solution.py:43
  130.3 0.8 fusion.29
  131.0 2.7 %collective-permute-done.18 = bf16[64,2048]{1,0:T(8,128)(2,1)S(1)} collective-permute-done((bf16[64,2048]{1,0:T(8,128)(2,1)S(1)}, bf16[64,2048]{1,0:T(8,128)(2,1)S(1)}, u32[]{:S(2)}, u32[]{:S(2)}) %collective-permute-start.18) | collective-permute-done | bytes 262176 | tf_op jit(solution)/shard_map/ppermute | solution.py:43
  134.4 3.2 %collective-permute-start.25 = (f32[16,1024]{1,0:T(8,128)S(1)}, f32[16,1024]{1,0:T(8,128)S(1)}, u32[]{:S(2)}, u32[]{:S(2)}) collective-permute-start(f32[16,1024]{1,0:T(8,128)S(1)} %get-tuple-element.14), channel_id=1, source_target_pairs={{0,24},{8,0},{16,8},{24,16},{1,25},{9,1},{17,9},{25,17},{2,26},{10... | collective-permute-start | bytes 196616 | tf_op jit(solution)/shard_map/ppermute | solution.py:43
  137.6 2.9 %collective-permute-done.23 = f32[16,1024]{1,0:T(8,128)S(1)} collective-permute-done((f32[16,1024]{1,0:T(8,128)S(1)}, f32[16,1024]{1,0:T(8,128)S(1)}, u32[]{:S(2)}, u32[]{:S(2)}) %collective-permute-start.23) | collective-permute-done | bytes 65568 | tf_op jit(solution)/shard_map/ppermute | solution.py:43
  140.6 3.4 %collective-permute-start.26 = (f32[16,2048]{1,0:T(8,128)S(1)}, f32[16,2048]{1,0:T(8,128)S(1)}, u32[]{:S(2)}, u32[]{:S(2)}) collective-permute-start(f32[16,2048]{1,0:T(8,128)S(1)} %get-tuple-element.8), channel_id=1, source_target_pairs={{0,24},{8,0},{16,8},{24,16},{1,25},{9,1},{17,9},{25,17},{2,26},{10... | collective-permute-start | bytes 393224 | tf_op jit(solution)/shard_map/ppermute | solution.py:43
  144.0 2.9 %collective-permute-done.24 = f32[16,2048]{1,0:T(8,128)S(1)} collective-permute-done((f32[16,2048]{1,0:T(8,128)S(1)}, f32[16,2048]{1,0:T(8,128)S(1)}, u32[]{:S(2)}, u32[]{:S(2)}) %collective-permute-start.24) | collective-permute-done | bytes 131104 | tf_op jit(solution)/shard_map/ppermute | solution.py:43
  146.8 0.7 fusion.11
  (50 shorter events, 3.7 us)
Async XLA Ops:
  0.0 5.7 %collective-permute-start = (bf16[16,2048]{1,0:T(8,128)(2,1)}, bf16[16,2048]{1,0:T(8,128)(2,1)S(1)}, u32[]{:S(2)}, u32[]{:S(2)}) collective-permute-start(bf16[16,2048]{1,0:T(8,128)(2,1)} %param.4), channel_id=1, source_target_pairs={{0,8},{8,16},{16,24},{24,0},{1,9},{9,17},{17,25},{25,1},{2,10},{10... | collective-permute-start | bytes 196616 | tf_op jit(solution)/shard_map/ppermute | solution.py:20
  1.6 9.6 %collective-permute-start.2 = (bf16[16,2048]{1,0:T(8,128)(2,1)}, bf16[16,2048]{1,0:T(8,128)(2,1)S(1)}, u32[]{:S(2)}, u32[]{:S(2)}) collective-permute-start(bf16[16,2048]{1,0:T(8,128)(2,1)} %param.4), channel_id=1, source_target_pairs={{0,24},{8,0},{16,8},{24,16},{1,25},{9,1},{17,9},{25,17},{2,26},{10... | collective-permute-start | bytes 196616 | tf_op jit(solution)/shard_map/ppermute | solution.py:24
  4.1 15.9 %copy-start.2 = (bf16[2048,896]{1,0:T(8,128)(2,1)S(1)}, bf16[2048,896]{1,0:T(8,128)(2,1)}, u32[]{:S(2)}) copy-start(bf16[2048,896]{1,0:T(8,128)(2,1)} %param.6) | copy-start | bytes 11010052
  5.7 5.5 %collective-permute-start.1 = (bf16[16,2048]{1,0:T(8,128)(2,1)S(1)}, bf16[16,2048]{1,0:T(8,128)(2,1)S(1)}, u32[]{:S(2)}, u32[]{:S(2)}) collective-permute-start(bf16[16,2048]{1,0:T(8,128)(2,1)S(1)} %collective-permute-done), channel_id=1, source_target_pairs={{0,8},{8,16},{16,24},{24,0},{1,9},{9,17},{17,25},{25,1},{2,10},{10... | collective-permute-start | bytes 196616 | tf_op jit(solution)/shard_map/ppermute | solution.py:20
  11.2 10.3 %collective-permute-start.3 = (bf16[64,2048]{1,0:T(8,128)(2,1)S(1)}, bf16[64,2048]{1,0:T(8,128)(2,1)S(1)}, u32[]{:S(2)}, u32[]{:S(2)}) collective-permute-start(bf16[64,2048]{1,0:T(8,128)(2,1)S(1)} %bitcast.156), channel_id=1, source_target_pairs={{0,1},{1,2},{2,3},{3,4},{4,5},{5,6},{6,7},{7,0},{8,9},{9,10},{10,1... | collective-permute-start | bytes 786440 | tf_op jit(solution)/shard_map/ppermute | solution.py:20
  13.2 10.3 %collective-permute-start.7 = (bf16[64,2048]{1,0:T(8,128)(2,1)S(1)}, bf16[64,2048]{1,0:T(8,128)(2,1)S(1)}, u32[]{:S(2)}, u32[]{:S(2)}) collective-permute-start(bf16[64,2048]{1,0:T(8,128)(2,1)S(1)} %bitcast.157), channel_id=1, source_target_pairs={{0,7},{1,0},{2,1},{3,2},{4,3},{5,4},{6,5},{7,6},{8,15},{9,8},{10,9... | collective-permute-start | bytes 786440 | tf_op jit(solution)/shard_map/ppermute | solution.py:24
  20.0 2.0 %copy-start.1 = (bf16[2048,896]{1,0:T(8,128)(2,1)S(1)}, bf16[2048,896]{1,0:T(8,128)(2,1)}, u32[]{:S(2)}) copy-start(bf16[2048,896]{1,0:T(8,128)(2,1)} %param.5) | copy-start | bytes 11010052
  22.7 7.7 %collective-permute-start.4 = (bf16[64,2048]{1,0:T(8,128)(2,1)S(1)}, bf16[64,2048]{1,0:T(8,128)(2,1)S(1)}, u32[]{:S(2)}, u32[]{:S(2)}) collective-permute-start(bf16[64,2048]{1,0:T(8,128)(2,1)S(1)} %collective-permute-done.3), channel_id=1, source_target_pairs={{0,1},{1,2},{2,3},{3,4},{4,5},{5,6},{6,7},{7,0},{8,9},{9,10},{10,1... | collective-permute-start | bytes 786440 | tf_op jit(solution)/shard_map/ppermute | solution.py:20
  24.9 7.2 %collective-permute-start.8 = (bf16[64,2048]{1,0:T(8,128)(2,1)S(1)}, bf16[64,2048]{1,0:T(8,128)(2,1)S(1)}, u32[]{:S(2)}, u32[]{:S(2)}) collective-permute-start(bf16[64,2048]{1,0:T(8,128)(2,1)S(1)} %collective-permute-done.7), channel_id=1, source_target_pairs={{0,7},{1,0},{2,1},{3,2},{4,3},{5,4},{6,5},{7,6},{8,15},{9,8},{10,9... | collective-permute-start | bytes 786440 | tf_op jit(solution)/shard_map/ppermute | solution.py:24
  31.1 8.0 %collective-permute-start.5 = (bf16[64,2048]{1,0:T(8,128)(2,1)S(1)}, bf16[64,2048]{1,0:T(8,128)(2,1)S(1)}, u32[]{:S(2)}, u32[]{:S(2)}) collective-permute-start(bf16[64,2048]{1,0:T(8,128)(2,1)S(1)} %collective-permute-done.4), channel_id=1, source_target_pairs={{0,1},{1,2},{2,3},{3,4},{4,5},{5,6},{6,7},{7,0},{8,9},{9,10},{10,1... | collective-permute-start | bytes 786440 | tf_op jit(solution)/shard_map/ppermute | solution.py:20
  33.6 7.8 %collective-permute-start.9 = (bf16[64,2048]{1,0:T(8,128)(2,1)S(1)}, bf16[64,2048]{1,0:T(8,128)(2,1)S(1)}, u32[]{:S(2)}, u32[]{:S(2)}) collective-permute-start(bf16[64,2048]{1,0:T(8,128)(2,1)S(1)} %collective-permute-done.8), channel_id=1, source_target_pairs={{0,7},{1,0},{2,1},{3,2},{4,3},{5,4},{6,5},{7,6},{8,15},{9,8},{10,9... | collective-permute-start | bytes 786440 | tf_op jit(solution)/shard_map/ppermute | solution.py:24
  39.8 7.7 %collective-permute-start.6 = (bf16[64,2048]{1,0:T(8,128)(2,1)S(1)}, bf16[64,2048]{1,0:T(8,128)(2,1)S(1)}, u32[]{:S(2)}, u32[]{:S(2)}) collective-permute-start(bf16[64,2048]{1,0:T(8,128)(2,1)S(1)} %collective-permute-done.5), channel_id=1, source_target_pairs={{0,1},{1,2},{2,3},{3,4},{4,5},{5,6},{6,7},{7,0},{8,9},{9,10},{10,1... | collective-permute-start | bytes 786440 | tf_op jit(solution)/shard_map/ppermute | solution.py:20
  49.0 1.8 %copy-start.3 = (f32[8,64,1792]{2,1,0:T(8,128)}, f32[8,64,1792]{2,1,0:T(8,128)S(1)}, u32[]{:S(2)}) copy-start(f32[8,64,1792]{2,1,0:T(8,128)S(1)} %fusion.7) | copy-start | bytes 11010052
  51.0 4.0 %collective-permute-start.10 = (f32[4,64,1792]{2,1,0:T(8,128)S(1)}, f32[4,64,1792]{2,1,0:T(8,128)}, u32[]{:S(2)}, u32[]{:S(2)}) collective-permute-start(f32[4,64,1792]{2,1,0:T(8,128)S(1)} %dynamic-slice_bitcast_fusion), channel_id=1, source_target_pairs={{0,32},{32,0},{1,33},{33,1},{2,34},{34,2},{3,35},{35,3},{4,36},{36... | collective-permute-start | bytes 5505032 | tf_op jit(solution)/shard_map/ppermute | solution.py:70
  57.3 7.7 %collective-permute-start.11 = (f32[64,896]{1,0:T(8,128)S(1)}, f32[64,896]{1,0:T(8,128)S(1)}, u32[]{:S(2)}, u32[]{:S(2)}) collective-permute-start(f32[64,896]{1,0:T(8,128)S(1)} %get-tuple-element.9), channel_id=1, source_target_pairs={{0,64},{64,128},{128,192},{192,0},{1,65},{65,129},{129,193},{193,1... | collective-permute-start | bytes 688136 | tf_op jit(solution)/shard_map/ppermute | solution.py:43
  58.9 7.4 %collective-permute-start.13 = (f32[64,896]{1,0:T(8,128)S(1)}, f32[64,896]{1,0:T(8,128)S(1)}, u32[]{:S(2)}, u32[]{:S(2)}) collective-permute-start(f32[64,896]{1,0:T(8,128)S(1)} %get-tuple-element.10), channel_id=1, source_target_pairs={{0,192},{64,0},{128,64},{192,128},{1,193},{65,1},{129,65},{193,129... | collective-permute-start | bytes 688136 | tf_op jit(solution)/shard_map/ppermute | solution.py:43
  66.3 11.5 %collective-permute-start.12 = (f32[64,1792]{1,0:T(8,128)S(1)}, f32[64,1792]{1,0:T(8,128)S(1)}, u32[]{:S(2)}, u32[]{:S(2)}) collective-permute-start(f32[64,1792]{1,0:T(8,128)S(1)} %get-tuple-element.5), channel_id=1, source_target_pairs={{0,64},{64,128},{128,192},{192,0},{1,65},{65,129},{129,193},{193,1... | collective-permute-start | bytes 1376264 | tf_op jit(solution)/shard_map/ppermute | solution.py:43
  67.6 11.2 %collective-permute-start.14 = (f32[64,1792]{1,0:T(8,128)S(1)}, f32[64,1792]{1,0:T(8,128)}, u32[]{:S(2)}, u32[]{:S(2)}) collective-permute-start(f32[64,1792]{1,0:T(8,128)S(1)} %get-tuple-element.6), channel_id=1, source_target_pairs={{0,192},{64,0},{128,64},{192,128},{1,193},{65,1},{129,65},{193,129... | collective-permute-start | bytes 1376264 | tf_op jit(solution)/shard_map/ppermute | solution.py:43
  97.3 7.0 %collective-permute-start.15 = (bf16[64,1024]{1,0:T(8,128)(2,1)S(1)}, bf16[64,1024]{1,0:T(8,128)(2,1)S(1)}, u32[]{:S(2)}, u32[]{:S(2)}) collective-permute-start(bf16[64,1024]{1,0:T(8,128)(2,1)S(1)} %get-tuple-element.11), channel_id=1, source_target_pairs={{0,1},{1,2},{2,3},{3,4},{4,5},{5,6},{6,7},{7,0},{8,9},{9,10},{10,1... | collective-permute-start | bytes 393224 | tf_op jit(solution)/shard_map/ppermute | solution.py:43
  97.4 10.0 %copy-start = (bf16[896,2048]{1,0:T(8,128)(2,1)S(1)}, bf16[896,2048]{1,0:T(8,128)(2,1)}, u32[]{:S(2)}) copy-start(bf16[896,2048]{1,0:T(8,128)(2,1)} %param.7) | copy-start | bytes 11010052
  97.5 10.0 %collective-permute-start.19 = (bf16[64,1024]{1,0:T(8,128)(2,1)S(1)}, bf16[64,1024]{1,0:T(8,128)(2,1)S(1)}, u32[]{:S(2)}, u32[]{:S(2)}) collective-permute-start(bf16[64,1024]{1,0:T(8,128)(2,1)S(1)} %get-tuple-element.12), channel_id=1, source_target_pairs={{0,7},{1,0},{2,1},{3,2},{4,3},{5,4},{6,5},{7,6},{8,15},{9,8},{10,9... | collective-permute-start | bytes 393224 | tf_op jit(solution)/shard_map/ppermute | solution.py:43
  107.2 9.3 %collective-permute-start.16 = (bf16[64,2048]{1,0:T(8,128)(2,1)S(1)}, bf16[64,2048]{1,0:T(8,128)(2,1)S(1)}, u32[]{:S(2)}, u32[]{:S(2)}) collective-permute-start(bf16[64,2048]{1,0:T(8,128)(2,1)S(1)} %add_convert_fusion.5), channel_id=1, source_target_pairs={{0,1},{1,2},{2,3},{3,4},{4,5},{5,6},{6,7},{7,0},{8,9},{9,10},{10,1... | collective-permute-start | bytes 786440 | tf_op jit(solution)/shard_map/ppermute | solution.py:43
  108.3 9.0 %collective-permute-start.20 = (bf16[64,2048]{1,0:T(8,128)(2,1)S(1)}, bf16[64,2048]{1,0:T(8,128)(2,1)S(1)}, u32[]{:S(2)}, u32[]{:S(2)}) collective-permute-start(bf16[64,2048]{1,0:T(8,128)(2,1)S(1)} %add_convert_fusion.2), channel_id=1, source_target_pairs={{0,7},{1,0},{2,1},{3,2},{4,3},{5,4},{6,5},{7,6},{8,15},{9,8},{10,9... | collective-permute-start | bytes 786440 | tf_op jit(solution)/shard_map/ppermute | solution.py:43
  117.2 8.1 %collective-permute-start.17 = (bf16[64,2048]{1,0:T(8,128)(2,1)S(1)}, bf16[64,2048]{1,0:T(8,128)(2,1)S(1)}, u32[]{:S(2)}, u32[]{:S(2)}) collective-permute-start(bf16[64,2048]{1,0:T(8,128)(2,1)S(1)} %add_convert_fusion.4), channel_id=1, source_target_pairs={{0,1},{1,2},{2,3},{3,4},{4,5},{5,6},{6,7},{7,0},{8,9},{9,10},{10,1... | collective-permute-start | bytes 786440 | tf_op jit(solution)/shard_map/ppermute | solution.py:43
  118.1 8.1 %collective-permute-start.21 = (bf16[64,2048]{1,0:T(8,128)(2,1)S(1)}, bf16[64,2048]{1,0:T(8,128)(2,1)S(1)}, u32[]{:S(2)}, u32[]{:S(2)}) collective-permute-start(bf16[64,2048]{1,0:T(8,128)(2,1)S(1)} %add_convert_fusion.1), channel_id=1, source_target_pairs={{0,7},{1,0},{2,1},{3,2},{4,3},{5,4},{6,5},{7,6},{8,15},{9,8},{10,9... | collective-permute-start | bytes 786440 | tf_op jit(solution)/shard_map/ppermute | solution.py:43
  126.1 7.7 %collective-permute-start.18 = (bf16[64,2048]{1,0:T(8,128)(2,1)S(1)}, bf16[64,2048]{1,0:T(8,128)(2,1)S(1)}, u32[]{:S(2)}, u32[]{:S(2)}) collective-permute-start(bf16[64,2048]{1,0:T(8,128)(2,1)S(1)} %add_convert_fusion.3), channel_id=1, source_target_pairs={{0,1},{1,2},{2,3},{3,4},{4,5},{5,6},{6,7},{7,0},{8,9},{9,10},{10,1... | collective-permute-start | bytes 786440 | tf_op jit(solution)/shard_map/ppermute | solution.py:43
  127.0 7.2 %collective-permute-start.22 = (bf16[64,2048]{1,0:T(8,128)(2,1)S(1)}, bf16[64,2048]{1,0:T(8,128)(2,1)S(1)}, u32[]{:S(2)}, u32[]{:S(2)}) collective-permute-start(bf16[64,2048]{1,0:T(8,128)(2,1)S(1)} %add_convert_fusion), channel_id=1, source_target_pairs={{0,7},{1,0},{2,1},{3,2},{4,3},{5,4},{6,5},{7,6},{8,15},{9,8},{10,9... | collective-permute-start | bytes 786440 | tf_op jit(solution)/shard_map/ppermute | solution.py:43
  134.3 6.2 %collective-permute-start.23 = (f32[16,1024]{1,0:T(8,128)S(1)}, f32[16,1024]{1,0:T(8,128)S(1)}, u32[]{:S(2)}, u32[]{:S(2)}) collective-permute-start(f32[16,1024]{1,0:T(8,128)S(1)} %get-tuple-element.13), channel_id=1, source_target_pairs={{0,8},{8,16},{16,24},{24,0},{1,9},{9,17},{17,25},{25,1},{2,10},{10... | collective-permute-start | bytes 196616 | tf_op jit(solution)/shard_map/ppermute | solution.py:43
  134.4 6.1 %collective-permute-start.25 = (f32[16,1024]{1,0:T(8,128)S(1)}, f32[16,1024]{1,0:T(8,128)S(1)}, u32[]{:S(2)}, u32[]{:S(2)}) collective-permute-start(f32[16,1024]{1,0:T(8,128)S(1)} %get-tuple-element.14), channel_id=1, source_target_pairs={{0,24},{8,0},{16,8},{24,16},{1,25},{9,1},{17,9},{25,17},{2,26},{10... | collective-permute-start | bytes 196616 | tf_op jit(solution)/shard_map/ppermute | solution.py:43
  140.5 6.3 %collective-permute-start.24 = (f32[16,2048]{1,0:T(8,128)S(1)}, f32[16,2048]{1,0:T(8,128)S(1)}, u32[]{:S(2)}, u32[]{:S(2)}) collective-permute-start(f32[16,2048]{1,0:T(8,128)S(1)} %get-tuple-element.7), channel_id=1, source_target_pairs={{0,8},{8,16},{16,24},{24,0},{1,9},{9,17},{17,25},{25,1},{2,10},{10... | collective-permute-start | bytes 393224 | tf_op jit(solution)/shard_map/ppermute | solution.py:43
  140.6 6.2 %collective-permute-start.26 = (f32[16,2048]{1,0:T(8,128)S(1)}, f32[16,2048]{1,0:T(8,128)S(1)}, u32[]{:S(2)}, u32[]{:S(2)}) collective-permute-start(f32[16,2048]{1,0:T(8,128)S(1)} %get-tuple-element.8), channel_id=1, source_target_pairs={{0,24},{8,0},{16,8},{24,16},{1,25},{9,1},{17,9},{25,17},{2,26},{10... | collective-permute-start | bytes 393224 | tf_op jit(solution)/shard_map/ppermute | solution.py:43

commit v11 on v8

--- a/solution.py
+++ b/solution.py
@@ -91,7 +91,8 @@
     )
     summed = embed_rs(partial_value)
     activated = (jax.nn.silu(summed[:, :width]) * summed[:, width:]).astype(jnp.bfloat16)
-    activated = lax.all_gather(activated, EMBED, axis=0, tiled=True)
+    activated = lax.all_gather(activated, "ec", axis=0, tiled=True)
+    activated = lax.all_gather(activated, "ex", axis=0, tiled=True)
     act_blocks = activated.reshape((nz, -1) + activated.shape[1:])
     project = lambda i: jnp.dot(
         lax.dynamic_index_in_dim(act_blocks, i, 0, keepdims=False),

time: 147 us -> 151 us (1.027)
  blocking collectives: 14.4 us -> 17.5 us
  matrix products: 22.3 us -> 20.2 us
  waiting for transfers between devices: 57.8 us -> 59.7 us
    all_gather x1 -> x2, blocking collectives: 14.4 us -> 17.5 us  [the longest x1 15.5 us: on_device(): activated = lax.all_gather(activated, 'ex', axis=0, tiled=True)]
    dot_general x9, matrix products: 8.91 us -> 6.85 us  [on_device(): jnp.dot(lax.dynamic_index_in_dim(act_blocks, i, 0, keepdims=False), down_...]
    ppermute x16, waiting for transfers between devices: 37.6 us -> 39.5 us  [side(): got = lax.ppermute(acc.astype(send_dtype), axis, perm).astype(jnp.float32)]
  transfers between devices with their start and end apart: 27 -> 27, of which waited for: 20 -> 22; matrix products, arithmetic and copies ran while one was open for 13% -> 11% of each run, Pallas kernels for 0% -> 0%
where the time goes in v11:
time: 151 us; the launch traced here: 149 us
  waiting for transfers between devices  59.7 us (40%)
  starting transfers between devices  42.9 us (28%)
  matrix products  20.2 us (13%)
  blocking collectives  17.5 us (12%)
  other arithmetic  4.72 us (3%)
  local copies, waits for them, and re-layouts  3.8 us (3%)
    ppermute x16, waiting for transfers between devices, side(): got = lax.ppermute(acc.astype(send_dtype), axis, perm).astype(jnp.float32)  39.5 us
    ppermute x16, starting transfers between devices, side(): got = lax.ppermute(acc.astype(send_dtype), axis, perm).astype(jnp.float32)  25.7 us
    all_gather x1, blocking collectives, on_device(): activated = lax.all_gather(activated, 'ex', axis=0, tiled=True)  15.5 us
    ppermute x6, waiting for transfers between devices, ring_ag(): buf = lax.ppermute(buf, axis, fwd)  15.3 us
    ppermute x4, starting transfers between devices, ring_ag(): buf = lax.ppermute(buf, axis, bwd)  12.9 us
    dot_general x8, matrix products, on_device(): jnp.dot(v, gate_weight, preferred_element_type=jnp.float32)  7.67 us
    dot_general x9, matrix products, on_device(): jnp.dot(lax.dynamic_index_in_dim(act_blocks, i, 0, keepdims=False), down_...  6.85 us
    dot_general x8, matrix products, on_device(): jnp.dot(v, up_weight, preferred_element_type=jnp.float32)  5.67 us
  transfers between devices with their start and end apart: 27, of which 22 were waited for; matrix products, arithmetic and copies ran while one was open for 11% of the time, Pallas kernels for 0%

profile of v11, /device:TPU:2, one launch (start us, length us, event | category | flops | bytes accessed | tf_op | source)
XLA Modules:
  0.0 149.3 jit_solution(8626487017875039608)
XLA Ops:
  0.0 1.6 %collective-permute-start = (bf16[16,2048]{1,0:T(8,128)(2,1)}, bf16[16,2048]{1,0:T(8,128)(2,1)S(1)}, u32[]{:S(2)}, u32[]{:S(2)}) collective-permute-start(bf16[16,2048]{1,0:T(8,128)(2,1)} %param.4), channel_id=1, source_target_pairs={{0,8},{8,16},{16,24},{24,0},{1,9},{9,17},{17,25},{25,1},{2,10},{10... | collective-permute-start | bytes 196616 | tf_op jit(solution)/shard_map/ppermute | solution.py:20
  1.6 1.7 %collective-permute-start.2 = (bf16[16,2048]{1,0:T(8,128)(2,1)}, bf16[16,2048]{1,0:T(8,128)(2,1)S(1)}, u32[]{:S(2)}, u32[]{:S(2)}) collective-permute-start(bf16[16,2048]{1,0:T(8,128)(2,1)} %param.4), channel_id=1, source_target_pairs={{0,24},{8,0},{16,8},{24,16},{1,25},{9,1},{17,9},{25,17},{2,26},{10... | collective-permute-start | bytes 196616 | tf_op jit(solution)/shard_map/ppermute | solution.py:24
  3.3 0.9 bitcast_dynamic-update-slice_fusion.3
  4.1 1.6 %collective-permute-done = bf16[16,2048]{1,0:T(8,128)(2,1)S(1)} collective-permute-done((bf16[16,2048]{1,0:T(8,128)(2,1)}, bf16[16,2048]{1,0:T(8,128)(2,1)S(1)}, u32[]{:S(2)}, u32[]{:S(2)}) %collective-permute-start) | collective-permute-done | bytes 65568 | tf_op jit(solution)/shard_map/ppermute | solution.py:20
  6.1 5.1 %collective-permute-done.1 = bf16[16,2048]{1,0:T(8,128)(2,1)S(1)} collective-permute-done((bf16[16,2048]{1,0:T(8,128)(2,1)S(1)}, bf16[16,2048]{1,0:T(8,128)(2,1)S(1)}, u32[]{:S(2)}, u32[]{:S(2)}) %collective-permute-start.1) | collective-permute-done | bytes 65568 | tf_op jit(solution)/shard_map/ppermute | solution.py:20
  11.2 2.0 %collective-permute-start.3 = (bf16[64,2048]{1,0:T(8,128)(2,1)S(1)}, bf16[64,2048]{1,0:T(8,128)(2,1)S(1)}, u32[]{:S(2)}, u32[]{:S(2)}) collective-permute-start(bf16[64,2048]{1,0:T(8,128)(2,1)S(1)} %bitcast.160), channel_id=1, source_target_pairs={{0,1},{1,2},{2,3},{3,4},{4,5},{5,6},{6,7},{7,0},{8,9},{9,10},{10,1... | collective-permute-start | bytes 786440 | tf_op jit(solution)/shard_map/ppermute | solution.py:20
  13.2 4.0 %collective-permute-start.7 = (bf16[64,2048]{1,0:T(8,128)(2,1)S(1)}, bf16[64,2048]{1,0:T(8,128)(2,1)S(1)}, u32[]{:S(2)}, u32[]{:S(2)}) collective-permute-start(bf16[64,2048]{1,0:T(8,128)(2,1)S(1)} %bitcast.161), channel_id=1, source_target_pairs={{0,7},{1,0},{2,1},{3,2},{4,3},{5,4},{6,5},{7,6},{8,15},{9,8},{10,9... | collective-permute-start | bytes 786440 | tf_op jit(solution)/shard_map/ppermute | solution.py:24
  17.2 2.7 %fusion.52 = f32[64,896]{1,0:T(8,128)S(1)} fusion(bf16[64,2048]{1,0:T(8,128)(2,1)S(1)} %bitcast.162, bf16[2048,896]{1,0:T(8,128)(2,1)} %param.5), kind=kOutput, calls=%fused_computation.82 | convolution fusion | flops 234881024 | bytes 4161536 | tf_op jit(solution)/shard_map/dot_general | solution.py:86
  20.0 0.7 fusion.53
  22.0 0.7 fusion.54
  22.8 0.7 fusion.55
  23.5 0.7 fusion.62
  24.2 0.7 fusion.63
  24.9 3.3 %collective-permute-start.8 = (bf16[64,2048]{1,0:T(8,128)(2,1)S(1)}, bf16[64,2048]{1,0:T(8,128)(2,1)S(1)}, u32[]{:S(2)}, u32[]{:S(2)}) collective-permute-start(bf16[64,2048]{1,0:T(8,128)(2,1)S(1)} %collective-permute-done.7), channel_id=1, source_target_pairs={{0,7},{1,0},{2,1},{3,2},{4,3},{5,4},{6,5},{7,6},{8,15},{9,8},{10,9... | collective-permute-start | bytes 786440 | tf_op jit(solution)/shard_map/ppermute | solution.py:24
  28.3 2.1 %collective-permute-done.4 = bf16[64,2048]{1,0:T(8,128)(2,1)S(1)} collective-permute-done((bf16[64,2048]{1,0:T(8,128)(2,1)S(1)}, bf16[64,2048]{1,0:T(8,128)(2,1)S(1)}, u32[]{:S(2)}, u32[]{:S(2)}) %collective-permute-start.4) | collective-permute-done | bytes 262176 | tf_op jit(solution)/shard_map/ppermute | solution.py:20
  30.4 0.7 fusion.56
  31.2 0.7 fusion.57
  32.1 0.7 fusion.64
  32.8 0.7 fusion.65
  33.6 3.9 %collective-permute-start.9 = (bf16[64,2048]{1,0:T(8,128)(2,1)S(1)}, bf16[64,2048]{1,0:T(8,128)(2,1)S(1)}, u32[]{:S(2)}, u32[]{:S(2)}) collective-permute-start(bf16[64,2048]{1,0:T(8,128)(2,1)S(1)} %collective-permute-done.8), channel_id=1, source_target_pairs={{0,7},{1,0},{2,1},{3,2},{4,3},{5,4},{6,5},{7,6},{8,15},{9,8},{10,9... | collective-permute-start | bytes 786440 | tf_op jit(solution)/shard_map/ppermute | solution.py:24
  37.5 1.5 %collective-permute-done.5 = bf16[64,2048]{1,0:T(8,128)(2,1)S(1)} collective-permute-done((bf16[64,2048]{1,0:T(8,128)(2,1)S(1)}, bf16[64,2048]{1,0:T(8,128)(2,1)S(1)}, u32[]{:S(2)}, u32[]{:S(2)}) %collective-permute-start.5) | collective-permute-done | bytes 262176 | tf_op jit(solution)/shard_map/ppermute | solution.py:20
  39.1 0.7 fusion.58
  39.9 0.7 fusion.59
  40.6 0.8 collective-permute-done.9
  41.4 0.7 fusion.66
  42.1 0.7 fusion.67
  42.9 4.6 %collective-permute-done.6 = bf16[64,2048]{1,0:T(8,128)(2,1)S(1)} collective-permute-done((bf16[64,2048]{1,0:T(8,128)(2,1)S(1)}, bf16[64,2048]{1,0:T(8,128)(2,1)S(1)}, u32[]{:S(2)}, u32[]{:S(2)}) %collective-permute-start.6) | collective-permute-done | bytes 262176 | tf_op jit(solution)/shard_map/ppermute | solution.py:20
  47.4 0.7 fusion.60
  48.2 0.7 fusion.61
  49.0 1.8 %copy-done.3 = f32[8,64,1792]{2,1,0:T(8,128)} copy-done((f32[8,64,1792]{2,1,0:T(8,128)}, f32[8,64,1792]{2,1,0:T(8,128)S(1)}, u32[]{:S(2)}) %copy-start.3) | copy-done | bytes 3670040
  51.1 3.9 %collective-permute-done.10 = f32[4,64,1792]{2,1,0:T(8,128)} collective-permute-done((f32[4,64,1792]{2,1,0:T(8,128)S(1)}, f32[4,64,1792]{2,1,0:T(8,128)}, u32[]{:S(2)}, u32[]{:S(2)}) %collective-permute-start.10) | collective-permute-done | bytes 1835040 | tf_op jit(solution)/shard_map/ppermute | solution.py:69
  55.0 2.2 %bitcast_add_fusion = f32[4,64,1792]{2,1,0:T(8,128)S(1)} fusion(f32[4,64,1792]{2,1,0:T(8,128)} %collective-permute-done.10, f32[4,2,64,1792]{3,2,1,0:T(8,128)} %bitcast.147, s32[]{:T(128)S(6)} %select_n.206), kind=kLoop, calls=%fused_computation | loop fusion | flops 458752 | bytes 5505028 | tf_op jit(solution)/shard_map/add | solution.py:70
  57.3 1.6 %collective-permute-start.11 = (f32[64,896]{1,0:T(8,128)S(1)}, f32[64,896]{1,0:T(8,128)S(1)}, u32[]{:S(2)}, u32[]{:S(2)}) collective-permute-start(f32[64,896]{1,0:T(8,128)S(1)} %slice.34), channel_id=1, source_target_pairs={{0,64},{64,128},{128,192},{192,0},{1,65},{65,129},{129,193},{193,1... | collective-permute-start | bytes 688136 | tf_op jit(solution)/shard_map/ppermute | solution.py:42
  59.5 5.5 %collective-permute-done.11 = f32[64,896]{1,0:T(8,128)S(1)} collective-permute-done((f32[64,896]{1,0:T(8,128)S(1)}, f32[64,896]{1,0:T(8,128)S(1)}, u32[]{:S(2)}, u32[]{:S(2)}) %collective-permute-start.11) | collective-permute-done | bytes 229408 | tf_op jit(solution)/shard_map/ppermute | solution.py:42
  65.0 1.3 collective-permute-done.13
  66.4 1.3 collective-permute-start.12
  67.7 0.8 collective-permute-start.14
  68.5 9.4 %collective-permute-done.12 = f32[64,1792]{1,0:T(8,128)S(1)} collective-permute-done((f32[64,1792]{1,0:T(8,128)S(1)}, f32[64,1792]{1,0:T(8,128)S(1)}, u32[]{:S(2)}, u32[]{:S(2)}) %collective-permute-start.12) | collective-permute-done | bytes 458784 | tf_op jit(solution)/shard_map/ppermute | solution.py:42
  77.9 1.0 collective-permute-done.14
  78.9 1.1 fusion.8
  80.1 2.0 %all_gather.6 = bf16[128,896]{1,0:T(8,128)(2,1)S(1)} all-gather(bf16[64,896]{1,0:T(8,128)(2,1)S(1)} %fusion.9), channel_id=1, replica_groups=mesh['ex'=4,'ec'=2,'hy'=4,'hz'=8] {'ec'}, dimensions={0}, use_global_device_ids=true | all-gather | bytes 344064 | tf_op jit(solution)/shard_map/all_gather | solution.py:94
  82.1 15.5 %all_gather.7 = bf16[512,896]{1,0:T(8,128)(2,1)S(1)} all-gather(bf16[128,896]{1,0:T(8,128)(2,1)S(1)} %all_gather.6), channel_id=1, replica_groups=mesh['ex'=4,'ec'=2,'hy'=4,'hz'=8] {'ex'}, dimensions={0}, use_global_device_ids=true | all-gather | bytes 1146880 | tf_op jit(solution)/shard_map/all_gather | solution.py:95
  97.6 0.8 fusion.28
  98.4 0.8 fusion.30
  99.1 0.8 fusion.18
  99.9 0.8 fusion.20
  100.7 0.8 fusion.22
  101.8 0.8 fusion.12
  102.6 3.3 %collective-permute-start.19 = (bf16[64,1024]{1,0:T(8,128)(2,1)S(1)}, bf16[64,1024]{1,0:T(8,128)(2,1)S(1)}, u32[]{:S(2)}, u32[]{:S(2)}) collective-permute-start(bf16[64,1024]{1,0:T(8,128)(2,1)S(1)} %slice.48), channel_id=1, source_target_pairs={{0,7},{1,0},{2,1},{3,2},{4,3},{5,4},{6,5},{7,6},{8,15},{9,8},{10,9... | collective-permute-start | bytes 393224 | tf_op jit(solution)/shard_map/ppermute | solution.py:42
  105.9 2.1 %collective-permute-done.15 = bf16[64,1024]{1,0:T(8,128)(2,1)S(1)} collective-permute-done((bf16[64,1024]{1,0:T(8,128)(2,1)S(1)}, bf16[64,1024]{1,0:T(8,128)(2,1)S(1)}, u32[]{:S(2)}, u32[]{:S(2)}) %collective-permute-start.15) | collective-permute-done | bytes 131104 | tf_op jit(solution)/shard_map/ppermute | solution.py:42
  107.9 0.8 add_convert_fusion.5
  108.8 0.8 add_convert_fusion.2
  109.6 3.3 %collective-permute-start.20 = (bf16[64,2048]{1,0:T(8,128)(2,1)S(1)}, bf16[64,2048]{1,0:T(8,128)(2,1)S(1)}, u32[]{:S(2)}, u32[]{:S(2)}) collective-permute-start(bf16[64,2048]{1,0:T(8,128)(2,1)S(1)} %add_convert_fusion.2), channel_id=1, source_target_pairs={{0,7},{1,0},{2,1},{3,2},{4,3},{5,4},{6,5},{7,6},{8,15},{9,8},{10,9... | collective-permute-start | bytes 786440 | tf_op jit(solution)/shard_map/ppermute | solution.py:42
  112.9 5.0 %collective-permute-done.16 = bf16[64,2048]{1,0:T(8,128)(2,1)S(1)} collective-permute-done((bf16[64,2048]{1,0:T(8,128)(2,1)S(1)}, bf16[64,2048]{1,0:T(8,128)(2,1)S(1)}, u32[]{:S(2)}, u32[]{:S(2)}) %collective-permute-start.16) | collective-permute-done | bytes 262176 | tf_op jit(solution)/shard_map/ppermute | solution.py:42
  118.7 3.8 %collective-permute-start.21 = (bf16[64,2048]{1,0:T(8,128)(2,1)S(1)}, bf16[64,2048]{1,0:T(8,128)(2,1)S(1)}, u32[]{:S(2)}, u32[]{:S(2)}) collective-permute-start(bf16[64,2048]{1,0:T(8,128)(2,1)S(1)} %add_convert_fusion.1), channel_id=1, source_target_pairs={{0,7},{1,0},{2,1},{3,2},{4,3},{5,4},{6,5},{7,6},{8,15},{9,8},{10,9... | collective-permute-start | bytes 786440 | tf_op jit(solution)/shard_map/ppermute | solution.py:42
  122.5 5.9 %collective-permute-done.17 = bf16[64,2048]{1,0:T(8,128)(2,1)S(1)} collective-permute-done((bf16[64,2048]{1,0:T(8,128)(2,1)S(1)}, bf16[64,2048]{1,0:T(8,128)(2,1)S(1)}, u32[]{:S(2)}, u32[]{:S(2)}) %collective-permute-start.17) | collective-permute-done | bytes 262176 | tf_op jit(solution)/shard_map/ppermute | solution.py:42
  129.0 3.8 %collective-permute-start.22 = (bf16[64,2048]{1,0:T(8,128)(2,1)S(1)}, bf16[64,2048]{1,0:T(8,128)(2,1)S(1)}, u32[]{:S(2)}, u32[]{:S(2)}) collective-permute-start(bf16[64,2048]{1,0:T(8,128)(2,1)S(1)} %add_convert_fusion), channel_id=1, source_target_pairs={{0,7},{1,0},{2,1},{3,2},{4,3},{5,4},{6,5},{7,6},{8,15},{9,8},{10,9... | collective-permute-start | bytes 786440 | tf_op jit(solution)/shard_map/ppermute | solution.py:42
  132.8 0.8 fusion.32
  133.5 2.5 %collective-permute-done.18 = bf16[64,2048]{1,0:T(8,128)(2,1)S(1)} collective-permute-done((bf16[64,2048]{1,0:T(8,128)(2,1)S(1)}, bf16[64,2048]{1,0:T(8,128)(2,1)S(1)}, u32[]{:S(2)}, u32[]{:S(2)}) %collective-permute-start.18) | collective-permute-done | bytes 262176 | tf_op jit(solution)/shard_map/ppermute | solution.py:42
  136.9 3.2 %collective-permute-start.25 = (f32[16,1024]{1,0:T(8,128)S(1)}, f32[16,1024]{1,0:T(8,128)S(1)}, u32[]{:S(2)}, u32[]{:S(2)}) collective-permute-start(f32[16,1024]{1,0:T(8,128)S(1)} %slice.41), channel_id=1, source_target_pairs={{0,24},{8,0},{16,8},{24,16},{1,25},{9,1},{17,9},{25,17},{2,26},{10... | collective-permute-start | bytes 196616 | tf_op jit(solution)/shard_map/ppermute | solution.py:42
  140.1 2.2 %collective-permute-done.23 = f32[16,1024]{1,0:T(8,128)S(1)} collective-permute-done((f32[16,1024]{1,0:T(8,128)S(1)}, f32[16,1024]{1,0:T(8,128)S(1)}, u32[]{:S(2)}, u32[]{:S(2)}) %collective-permute-start.23) | collective-permute-done | bytes 65568 | tf_op jit(solution)/shard_map/ppermute | solution.py:42
  142.5 3.3 %collective-permute-start.26 = (f32[16,2048]{1,0:T(8,128)S(1)}, f32[16,2048]{1,0:T(8,128)S(1)}, u32[]{:S(2)}, u32[]{:S(2)}) collective-permute-start(f32[16,2048]{1,0:T(8,128)S(1)} %get-tuple-element.10), channel_id=1, source_target_pairs={{0,24},{8,0},{16,8},{24,16},{1,25},{9,1},{17,9},{25,17},{2,26},{10... | collective-permute-start | bytes 393224 | tf_op jit(solution)/shard_map/ppermute | solution.py:42
  145.8 2.9 %collective-permute-done.24 = f32[16,2048]{1,0:T(8,128)S(1)} collective-permute-done((f32[16,2048]{1,0:T(8,128)S(1)}, f32[16,2048]{1,0:T(8,128)S(1)}, u32[]{:S(2)}, u32[]{:S(2)}) %collective-permute-start.24) | collective-permute-done | bytes 131104 | tf_op jit(solution)/shard_map/ppermute | solution.py:42
  148.7 0.7 fusion.11
  (59 shorter events, 6.3 us)
Async XLA Ops:
  0.0 5.7 %collective-permute-start = (bf16[16,2048]{1,0:T(8,128)(2,1)}, bf16[16,2048]{1,0:T(8,128)(2,1)S(1)}, u32[]{:S(2)}, u32[]{:S(2)}) collective-permute-start(bf16[16,2048]{1,0:T(8,128)(2,1)} %param.4), channel_id=1, source_target_pairs={{0,8},{8,16},{16,24},{24,0},{1,9},{9,17},{17,25},{25,1},{2,10},{10... | collective-permute-start | bytes 196616 | tf_op jit(solution)/shard_map/ppermute | solution.py:20
  1.6 9.6 %collective-permute-start.2 = (bf16[16,2048]{1,0:T(8,128)(2,1)}, bf16[16,2048]{1,0:T(8,128)(2,1)S(1)}, u32[]{:S(2)}, u32[]{:S(2)}) collective-permute-start(bf16[16,2048]{1,0:T(8,128)(2,1)} %param.4), channel_id=1, source_target_pairs={{0,24},{8,0},{16,8},{24,16},{1,25},{9,1},{17,9},{25,17},{2,26},{10... | collective-permute-start | bytes 196616 | tf_op jit(solution)/shard_map/ppermute | solution.py:24
  4.1 15.9 %copy-start.2 = (bf16[2048,896]{1,0:T(8,128)(2,1)S(1)}, bf16[2048,896]{1,0:T(8,128)(2,1)}, u32[]{:S(2)}) copy-start(bf16[2048,896]{1,0:T(8,128)(2,1)} %param.6) | copy-start | bytes 11010052
  5.7 5.5 %collective-permute-start.1 = (bf16[16,2048]{1,0:T(8,128)(2,1)S(1)}, bf16[16,2048]{1,0:T(8,128)(2,1)S(1)}, u32[]{:S(2)}, u32[]{:S(2)}) collective-permute-start(bf16[16,2048]{1,0:T(8,128)(2,1)S(1)} %collective-permute-done), channel_id=1, source_target_pairs={{0,8},{8,16},{16,24},{24,0},{1,9},{9,17},{17,25},{25,1},{2,10},{10... | collective-permute-start | bytes 196616 | tf_op jit(solution)/shard_map/ppermute | solution.py:20
  11.2 10.3 %collective-permute-start.3 = (bf16[64,2048]{1,0:T(8,128)(2,1)S(1)}, bf16[64,2048]{1,0:T(8,128)(2,1)S(1)}, u32[]{:S(2)}, u32[]{:S(2)}) collective-permute-start(bf16[64,2048]{1,0:T(8,128)(2,1)S(1)} %bitcast.160), channel_id=1, source_target_pairs={{0,1},{1,2},{2,3},{3,4},{4,5},{5,6},{6,7},{7,0},{8,9},{9,10},{10,1... | collective-permute-start | bytes 786440 | tf_op jit(solution)/shard_map/ppermute | solution.py:20
  13.2 10.3 %collective-permute-start.7 = (bf16[64,2048]{1,0:T(8,128)(2,1)S(1)}, bf16[64,2048]{1,0:T(8,128)(2,1)S(1)}, u32[]{:S(2)}, u32[]{:S(2)}) collective-permute-start(bf16[64,2048]{1,0:T(8,128)(2,1)S(1)} %bitcast.161), channel_id=1, source_target_pairs={{0,7},{1,0},{2,1},{3,2},{4,3},{5,4},{6,5},{7,6},{8,15},{9,8},{10,9... | collective-permute-start | bytes 786440 | tf_op jit(solution)/shard_map/ppermute | solution.py:24
  20.0 2.0 %copy-start.1 = (bf16[2048,896]{1,0:T(8,128)(2,1)S(1)}, bf16[2048,896]{1,0:T(8,128)(2,1)}, u32[]{:S(2)}) copy-start(bf16[2048,896]{1,0:T(8,128)(2,1)} %param.5) | copy-start | bytes 11010052
  22.7 7.7 %collective-permute-start.4 = (bf16[64,2048]{1,0:T(8,128)(2,1)S(1)}, bf16[64,2048]{1,0:T(8,128)(2,1)S(1)}, u32[]{:S(2)}, u32[]{:S(2)}) collective-permute-start(bf16[64,2048]{1,0:T(8,128)(2,1)S(1)} %collective-permute-done.3), channel_id=1, source_target_pairs={{0,1},{1,2},{2,3},{3,4},{4,5},{5,6},{6,7},{7,0},{8,9},{9,10},{10,1... | collective-permute-start | bytes 786440 | tf_op jit(solution)/shard_map/ppermute | solution.py:20
  24.9 7.2 %collective-permute-start.8 = (bf16[64,2048]{1,0:T(8,128)(2,1)S(1)}, bf16[64,2048]{1,0:T(8,128)(2,1)S(1)}, u32[]{:S(2)}, u32[]{:S(2)}) collective-permute-start(bf16[64,2048]{1,0:T(8,128)(2,1)S(1)} %collective-permute-done.7), channel_id=1, source_target_pairs={{0,7},{1,0},{2,1},{3,2},{4,3},{5,4},{6,5},{7,6},{8,15},{9,8},{10,9... | collective-permute-start | bytes 786440 | tf_op jit(solution)/shard_map/ppermute | solution.py:24
  31.1 8.0 %collective-permute-start.5 = (bf16[64,2048]{1,0:T(8,128)(2,1)S(1)}, bf16[64,2048]{1,0:T(8,128)(2,1)S(1)}, u32[]{:S(2)}, u32[]{:S(2)}) collective-permute-start(bf16[64,2048]{1,0:T(8,128)(2,1)S(1)} %collective-permute-done.4), channel_id=1, source_target_pairs={{0,1},{1,2},{2,3},{3,4},{4,5},{5,6},{6,7},{7,0},{8,9},{9,10},{10,1... | collective-permute-start | bytes 786440 | tf_op jit(solution)/shard_map/ppermute | solution.py:20
  33.6 7.8 %collective-permute-start.9 = (bf16[64,2048]{1,0:T(8,128)(2,1)S(1)}, bf16[64,2048]{1,0:T(8,128)(2,1)S(1)}, u32[]{:S(2)}, u32[]{:S(2)}) collective-permute-start(bf16[64,2048]{1,0:T(8,128)(2,1)S(1)} %collective-permute-done.8), channel_id=1, source_target_pairs={{0,7},{1,0},{2,1},{3,2},{4,3},{5,4},{6,5},{7,6},{8,15},{9,8},{10,9... | collective-permute-start | bytes 786440 | tf_op jit(solution)/shard_map/ppermute | solution.py:24
  39.8 7.7 %collective-permute-start.6 = (bf16[64,2048]{1,0:T(8,128)(2,1)S(1)}, bf16[64,2048]{1,0:T(8,128)(2,1)S(1)}, u32[]{:S(2)}, u32[]{:S(2)}) collective-permute-start(bf16[64,2048]{1,0:T(8,128)(2,1)S(1)} %collective-permute-done.5), channel_id=1, source_target_pairs={{0,1},{1,2},{2,3},{3,4},{4,5},{5,6},{6,7},{7,0},{8,9},{9,10},{10,1... | collective-permute-start | bytes 786440 | tf_op jit(solution)/shard_map/ppermute | solution.py:20
  49.0 1.8 %copy-start.3 = (f32[8,64,1792]{2,1,0:T(8,128)}, f32[8,64,1792]{2,1,0:T(8,128)S(1)}, u32[]{:S(2)}) copy-start(f32[8,64,1792]{2,1,0:T(8,128)S(1)} %fusion.7) | copy-start | bytes 11010052
  51.0 4.0 %collective-permute-start.10 = (f32[4,64,1792]{2,1,0:T(8,128)S(1)}, f32[4,64,1792]{2,1,0:T(8,128)}, u32[]{:S(2)}, u32[]{:S(2)}) collective-permute-start(f32[4,64,1792]{2,1,0:T(8,128)S(1)} %dynamic-slice_bitcast_fusion), channel_id=1, source_target_pairs={{0,32},{32,0},{1,33},{33,1},{2,34},{34,2},{3,35},{35,3},{4,36},{36... | collective-permute-start | bytes 5505032 | tf_op jit(solution)/shard_map/ppermute | solution.py:69
  57.3 7.7 %collective-permute-start.11 = (f32[64,896]{1,0:T(8,128)S(1)}, f32[64,896]{1,0:T(8,128)S(1)}, u32[]{:S(2)}, u32[]{:S(2)}) collective-permute-start(f32[64,896]{1,0:T(8,128)S(1)} %slice.34), channel_id=1, source_target_pairs={{0,64},{64,128},{128,192},{192,0},{1,65},{65,129},{129,193},{193,1... | collective-permute-start | bytes 688136 | tf_op jit(solution)/shard_map/ppermute | solution.py:42
  58.9 7.4 %collective-permute-start.13 = (f32[64,896]{1,0:T(8,128)S(1)}, f32[64,896]{1,0:T(8,128)S(1)}, u32[]{:S(2)}, u32[]{:S(2)}) collective-permute-start(f32[64,896]{1,0:T(8,128)S(1)} %slice.35), channel_id=1, source_target_pairs={{0,192},{64,0},{128,64},{192,128},{1,193},{65,1},{129,65},{193,129... | collective-permute-start | bytes 688136 | tf_op jit(solution)/shard_map/ppermute | solution.py:42
  66.4 11.5 %collective-permute-start.12 = (f32[64,1792]{1,0:T(8,128)S(1)}, f32[64,1792]{1,0:T(8,128)S(1)}, u32[]{:S(2)}, u32[]{:S(2)}) collective-permute-start(f32[64,1792]{1,0:T(8,128)S(1)} %get-tuple-element.5), channel_id=1, source_target_pairs={{0,64},{64,128},{128,192},{192,0},{1,65},{65,129},{129,193},{193,1... | collective-permute-start | bytes 1376264 | tf_op jit(solution)/shard_map/ppermute | solution.py:42
  67.7 11.2 %collective-permute-start.14 = (f32[64,1792]{1,0:T(8,128)S(1)}, f32[64,1792]{1,0:T(8,128)}, u32[]{:S(2)}, u32[]{:S(2)}) collective-permute-start(f32[64,1792]{1,0:T(8,128)S(1)} %get-tuple-element.6), channel_id=1, source_target_pairs={{0,192},{64,0},{128,64},{192,128},{1,193},{65,1},{129,65},{193,129... | collective-permute-start | bytes 1376264 | tf_op jit(solution)/shard_map/ppermute | solution.py:42
  68.5 29.1 %copy-start = (bf16[896,2048]{1,0:T(8,128)(2,1)S(1)}, bf16[896,2048]{1,0:T(8,128)(2,1)}, u32[]{:S(2)}) copy-start(bf16[896,2048]{1,0:T(8,128)(2,1)} %param.7) | copy-start | bytes 11010052
  101.5 6.5 %collective-permute-start.15 = (bf16[64,1024]{1,0:T(8,128)(2,1)S(1)}, bf16[64,1024]{1,0:T(8,128)(2,1)S(1)}, u32[]{:S(2)}, u32[]{:S(2)}) collective-permute-start(bf16[64,1024]{1,0:T(8,128)(2,1)S(1)} %slice.49), channel_id=1, source_target_pairs={{0,1},{1,2},{2,3},{3,4},{4,5},{5,6},{6,7},{7,0},{8,9},{9,10},{10,1... | collective-permute-start | bytes 393224 | tf_op jit(solution)/shard_map/ppermute | solution.py:42
  102.6 6.2 %collective-permute-start.19 = (bf16[64,1024]{1,0:T(8,128)(2,1)S(1)}, bf16[64,1024]{1,0:T(8,128)(2,1)S(1)}, u32[]{:S(2)}, u32[]{:S(2)}) collective-permute-start(bf16[64,1024]{1,0:T(8,128)(2,1)S(1)} %slice.48), channel_id=1, source_target_pairs={{0,7},{1,0},{2,1},{3,2},{4,3},{5,4},{6,5},{7,6},{8,15},{9,8},{10,9... | collective-permute-start | bytes 393224 | tf_op jit(solution)/shard_map/ppermute | solution.py:42
  108.7 9.2 %collective-permute-start.16 = (bf16[64,2048]{1,0:T(8,128)(2,1)S(1)}, bf16[64,2048]{1,0:T(8,128)(2,1)S(1)}, u32[]{:S(2)}, u32[]{:S(2)}) collective-permute-start(bf16[64,2048]{1,0:T(8,128)(2,1)S(1)} %add_convert_fusion.5), channel_id=1, source_target_pairs={{0,1},{1,2},{2,3},{3,4},{4,5},{5,6},{6,7},{7,0},{8,9},{9,10},{10,1... | collective-permute-start | bytes 786440 | tf_op jit(solution)/shard_map/ppermute | solution.py:42
  109.6 9.0 %collective-permute-start.20 = (bf16[64,2048]{1,0:T(8,128)(2,1)S(1)}, bf16[64,2048]{1,0:T(8,128)(2,1)S(1)}, u32[]{:S(2)}, u32[]{:S(2)}) collective-permute-start(bf16[64,2048]{1,0:T(8,128)(2,1)S(1)} %add_convert_fusion.2), channel_id=1, source_target_pairs={{0,7},{1,0},{2,1},{3,2},{4,3},{5,4},{6,5},{7,6},{8,15},{9,8},{10,9... | collective-permute-start | bytes 786440 | tf_op jit(solution)/shard_map/ppermute | solution.py:42
  118.0 10.4 %collective-permute-start.17 = (bf16[64,2048]{1,0:T(8,128)(2,1)S(1)}, bf16[64,2048]{1,0:T(8,128)(2,1)S(1)}, u32[]{:S(2)}, u32[]{:S(2)}) collective-permute-start(bf16[64,2048]{1,0:T(8,128)(2,1)S(1)} %add_convert_fusion.4), channel_id=1, source_target_pairs={{0,1},{1,2},{2,3},{3,4},{4,5},{5,6},{6,7},{7,0},{8,9},{9,10},{10,1... | collective-permute-start | bytes 786440 | tf_op jit(solution)/shard_map/ppermute | solution.py:42
  118.7 10.3 %collective-permute-start.21 = (bf16[64,2048]{1,0:T(8,128)(2,1)S(1)}, bf16[64,2048]{1,0:T(8,128)(2,1)S(1)}, u32[]{:S(2)}, u32[]{:S(2)}) collective-permute-start(bf16[64,2048]{1,0:T(8,128)(2,1)S(1)} %add_convert_fusion.1), channel_id=1, source_target_pairs={{0,7},{1,0},{2,1},{3,2},{4,3},{5,4},{6,5},{7,6},{8,15},{9,8},{10,9... | collective-permute-start | bytes 786440 | tf_op jit(solution)/shard_map/ppermute | solution.py:42
  128.4 7.7 %collective-permute-start.18 = (bf16[64,2048]{1,0:T(8,128)(2,1)S(1)}, bf16[64,2048]{1,0:T(8,128)(2,1)S(1)}, u32[]{:S(2)}, u32[]{:S(2)}) collective-permute-start(bf16[64,2048]{1,0:T(8,128)(2,1)S(1)} %add_convert_fusion.3), channel_id=1, source_target_pairs={{0,1},{1,2},{2,3},{3,4},{4,5},{5,6},{6,7},{7,0},{8,9},{9,10},{10,1... | collective-permute-start | bytes 786440 | tf_op jit(solution)/shard_map/ppermute | solution.py:42
  129.0 7.7 %collective-permute-start.22 = (bf16[64,2048]{1,0:T(8,128)(2,1)S(1)}, bf16[64,2048]{1,0:T(8,128)(2,1)S(1)}, u32[]{:S(2)}, u32[]{:S(2)}) collective-permute-start(bf16[64,2048]{1,0:T(8,128)(2,1)S(1)} %add_convert_fusion), channel_id=1, source_target_pairs={{0,7},{1,0},{2,1},{3,2},{4,3},{5,4},{6,5},{7,6},{8,15},{9,8},{10,9... | collective-permute-start | bytes 786440 | tf_op jit(solution)/shard_map/ppermute | solution.py:42
  136.8 5.6 %collective-permute-start.23 = (f32[16,1024]{1,0:T(8,128)S(1)}, f32[16,1024]{1,0:T(8,128)S(1)}, u32[]{:S(2)}, u32[]{:S(2)}) collective-permute-start(f32[16,1024]{1,0:T(8,128)S(1)} %slice.40), channel_id=1, source_target_pairs={{0,8},{8,16},{16,24},{24,0},{1,9},{9,17},{17,25},{25,1},{2,10},{10... | collective-permute-start | bytes 196616 | tf_op jit(solution)/shard_map/ppermute | solution.py:42
  136.9 5.5 %collective-permute-start.25 = (f32[16,1024]{1,0:T(8,128)S(1)}, f32[16,1024]{1,0:T(8,128)S(1)}, u32[]{:S(2)}, u32[]{:S(2)}) collective-permute-start(f32[16,1024]{1,0:T(8,128)S(1)} %slice.41), channel_id=1, source_target_pairs={{0,24},{8,0},{16,8},{24,16},{1,25},{9,1},{17,9},{25,17},{2,26},{10... | collective-permute-start | bytes 196616 | tf_op jit(solution)/shard_map/ppermute | solution.py:42
  142.4 6.3 %collective-permute-start.24 = (f32[16,2048]{1,0:T(8,128)S(1)}, f32[16,2048]{1,0:T(8,128)S(1)}, u32[]{:S(2)}, u32[]{:S(2)}) collective-permute-start(f32[16,2048]{1,0:T(8,128)S(1)} %get-tuple-element.9), channel_id=1, source_target_pairs={{0,8},{8,16},{16,24},{24,0},{1,9},{9,17},{17,25},{25,1},{2,10},{10... | collective-permute-start | bytes 393224 | tf_op jit(solution)/shard_map/ppermute | solution.py:42
  142.5 6.2 %collective-permute-start.26 = (f32[16,2048]{1,0:T(8,128)S(1)}, f32[16,2048]{1,0:T(8,128)S(1)}, u32[]{:S(2)}, u32[]{:S(2)}) collective-permute-start(f32[16,2048]{1,0:T(8,128)S(1)} %get-tuple-element.10), channel_id=1, source_target_pairs={{0,24},{8,0},{16,8},{24,16},{1,25},{9,1},{17,9},{25,17},{2,26},{10... | collective-permute-start | bytes 393224 | tf_op jit(solution)/shard_map/ppermute | solution.py:42

commit v12 on v8

--- a/solution.py
+++ b/solution.py
@@ -101,7 +101,7 @@
     totals = ring_rs_bal(project, "hz", nz, jnp.bfloat16)
     totals = totals.reshape((ny, -1) + totals.shape[1:])
     totals = ring_rs_bal(
-        lambda i: lax.dynamic_index_in_dim(totals, i, 0, keepdims=False), "hy", ny, jnp.float32
+        lambda i: lax.dynamic_index_in_dim(totals, i, 0, keepdims=False), "hy", ny, jnp.bfloat16
     )
     return totals.astype(jnp.bfloat16)
 

time: 147 us -> 145 us (0.986)
  no operation moved by 1% of the time
where the time goes in v12:
time: 145 us; the launch traced here: 144 us
  waiting for transfers between devices  56.6 us (39%)
  starting transfers between devices  41.8 us (29%)
  matrix products  22.3 us (15%)
  blocking collectives  14.4 us (10%)
  other arithmetic  4.51 us (3%)
  local copies, waits for them, and re-layouts  3.79 us (3%)
    ppermute x16, waiting for transfers between devices, side(): got = lax.ppermute(acc.astype(send_dtype), axis, perm).astype(jnp.float32)  36.3 us
    ppermute x16, starting transfers between devices, side(): got = lax.ppermute(acc.astype(send_dtype), axis, perm).astype(jnp.float32)  24.6 us
    ppermute x6, waiting for transfers between devices, ring_ag(): buf = lax.ppermute(buf, axis, fwd)  15.3 us
    all_gather x1, blocking collectives, on_device(): activated = lax.all_gather(activated, EMBED, axis=0, tiled=True)  14.4 us
    ppermute x4, starting transfers between devices, ring_ag(): buf = lax.ppermute(buf, axis, bwd)  12.9 us
    dot_general x9, matrix products, on_device(): jnp.dot(lax.dynamic_index_in_dim(act_blocks, i, 0, keepdims=False), down_...  8.91 us
    dot_general x8, matrix products, on_device(): jnp.dot(v, gate_weight, preferred_element_type=jnp.float32)  7.67 us
    dot_general x8, matrix products, on_device(): jnp.dot(v, up_weight, preferred_element_type=jnp.float32)  5.67 us
  transfers between devices with their start and end apart: 27, of which 20 were waited for; matrix products, arithmetic and copies ran while one was open for 13% of the time, Pallas kernels for 0%

profile of v12, /device:TPU:2, one launch (start us, length us, event | category | flops | bytes accessed | tf_op | source)
XLA Modules:
  0.0 143.8 jit_solution(12536663747846175876)
XLA Ops:
  0.0 1.6 %collective-permute-start = (bf16[16,2048]{1,0:T(8,128)(2,1)}, bf16[16,2048]{1,0:T(8,128)(2,1)S(1)}, u32[]{:S(2)}, u32[]{:S(2)}) collective-permute-start(bf16[16,2048]{1,0:T(8,128)(2,1)} %param.4), channel_id=1, source_target_pairs={{0,8},{8,16},{16,24},{24,0},{1,9},{9,17},{17,25},{25,1},{2,10},{10... | collective-permute-start | bytes 196616 | tf_op jit(solution)/shard_map/ppermute | solution.py:20
  1.6 1.7 %collective-permute-start.2 = (bf16[16,2048]{1,0:T(8,128)(2,1)}, bf16[16,2048]{1,0:T(8,128)(2,1)S(1)}, u32[]{:S(2)}, u32[]{:S(2)}) collective-permute-start(bf16[16,2048]{1,0:T(8,128)(2,1)} %param.4), channel_id=1, source_target_pairs={{0,24},{8,0},{16,8},{24,16},{1,25},{9,1},{17,9},{25,17},{2,26},{10... | collective-permute-start | bytes 196616 | tf_op jit(solution)/shard_map/ppermute | solution.py:24
  3.3 0.9 bitcast_dynamic-update-slice_fusion.3
  4.1 1.6 %collective-permute-done = bf16[16,2048]{1,0:T(8,128)(2,1)S(1)} collective-permute-done((bf16[16,2048]{1,0:T(8,128)(2,1)}, bf16[16,2048]{1,0:T(8,128)(2,1)S(1)}, u32[]{:S(2)}, u32[]{:S(2)}) %collective-permute-start) | collective-permute-done | bytes 65568 | tf_op jit(solution)/shard_map/ppermute | solution.py:20
  6.1 5.1 %collective-permute-done.1 = bf16[16,2048]{1,0:T(8,128)(2,1)S(1)} collective-permute-done((bf16[16,2048]{1,0:T(8,128)(2,1)S(1)}, bf16[16,2048]{1,0:T(8,128)(2,1)S(1)}, u32[]{:S(2)}, u32[]{:S(2)}) %collective-permute-start.1) | collective-permute-done | bytes 65568 | tf_op jit(solution)/shard_map/ppermute | solution.py:20
  11.2 2.0 %collective-permute-start.3 = (bf16[64,2048]{1,0:T(8,128)(2,1)S(1)}, bf16[64,2048]{1,0:T(8,128)(2,1)S(1)}, u32[]{:S(2)}, u32[]{:S(2)}) collective-permute-start(bf16[64,2048]{1,0:T(8,128)(2,1)S(1)} %bitcast.169), channel_id=1, source_target_pairs={{0,1},{1,2},{2,3},{3,4},{4,5},{5,6},{6,7},{7,0},{8,9},{9,10},{10,1... | collective-permute-start | bytes 786440 | tf_op jit(solution)/shard_map/ppermute | solution.py:20
  13.2 4.0 %collective-permute-start.7 = (bf16[64,2048]{1,0:T(8,128)(2,1)S(1)}, bf16[64,2048]{1,0:T(8,128)(2,1)S(1)}, u32[]{:S(2)}, u32[]{:S(2)}) collective-permute-start(bf16[64,2048]{1,0:T(8,128)(2,1)S(1)} %bitcast.170), channel_id=1, source_target_pairs={{0,7},{1,0},{2,1},{3,2},{4,3},{5,4},{6,5},{7,6},{8,15},{9,8},{10,9... | collective-permute-start | bytes 786440 | tf_op jit(solution)/shard_map/ppermute | solution.py:24
  17.2 2.7 %fusion.64 = f32[64,896]{1,0:T(8,128)S(1)} fusion(bf16[64,2048]{1,0:T(8,128)(2,1)S(1)} %bitcast.171, bf16[2048,896]{1,0:T(8,128)(2,1)} %param.5), kind=kOutput, calls=%fused_computation.86 | convolution fusion | flops 234881024 | bytes 4161536 | tf_op jit(solution)/shard_map/dot_general | solution.py:86
  20.0 0.7 fusion.65
  22.0 0.7 fusion.66
  22.8 0.7 fusion.67
  23.5 0.7 fusion.74
  24.2 0.7 fusion.75
  24.9 3.3 %collective-permute-start.8 = (bf16[64,2048]{1,0:T(8,128)(2,1)S(1)}, bf16[64,2048]{1,0:T(8,128)(2,1)S(1)}, u32[]{:S(2)}, u32[]{:S(2)}) collective-permute-start(bf16[64,2048]{1,0:T(8,128)(2,1)S(1)} %collective-permute-done.7), channel_id=1, source_target_pairs={{0,7},{1,0},{2,1},{3,2},{4,3},{5,4},{6,5},{7,6},{8,15},{9,8},{10,9... | collective-permute-start | bytes 786440 | tf_op jit(solution)/shard_map/ppermute | solution.py:24
  28.3 2.1 %collective-permute-done.4 = bf16[64,2048]{1,0:T(8,128)(2,1)S(1)} collective-permute-done((bf16[64,2048]{1,0:T(8,128)(2,1)S(1)}, bf16[64,2048]{1,0:T(8,128)(2,1)S(1)}, u32[]{:S(2)}, u32[]{:S(2)}) %collective-permute-start.4) | collective-permute-done | bytes 262176 | tf_op jit(solution)/shard_map/ppermute | solution.py:20
  30.4 0.7 fusion.68
  31.2 0.7 fusion.69
  32.1 0.7 fusion.76
  32.8 0.7 fusion.77
  33.6 3.9 %collective-permute-start.9 = (bf16[64,2048]{1,0:T(8,128)(2,1)S(1)}, bf16[64,2048]{1,0:T(8,128)(2,1)S(1)}, u32[]{:S(2)}, u32[]{:S(2)}) collective-permute-start(bf16[64,2048]{1,0:T(8,128)(2,1)S(1)} %collective-permute-done.8), channel_id=1, source_target_pairs={{0,7},{1,0},{2,1},{3,2},{4,3},{5,4},{6,5},{7,6},{8,15},{9,8},{10,9... | collective-permute-start | bytes 786440 | tf_op jit(solution)/shard_map/ppermute | solution.py:24
  37.5 1.5 %collective-permute-done.5 = bf16[64,2048]{1,0:T(8,128)(2,1)S(1)} collective-permute-done((bf16[64,2048]{1,0:T(8,128)(2,1)S(1)}, bf16[64,2048]{1,0:T(8,128)(2,1)S(1)}, u32[]{:S(2)}, u32[]{:S(2)}) %collective-permute-start.5) | collective-permute-done | bytes 262176 | tf_op jit(solution)/shard_map/ppermute | solution.py:20
  39.1 0.7 fusion.70
  39.9 0.7 fusion.71
  40.6 0.8 collective-permute-done.9
  41.4 0.7 fusion.78
  42.1 0.7 fusion.79
  42.9 4.6 %collective-permute-done.6 = bf16[64,2048]{1,0:T(8,128)(2,1)S(1)} collective-permute-done((bf16[64,2048]{1,0:T(8,128)(2,1)S(1)}, bf16[64,2048]{1,0:T(8,128)(2,1)S(1)}, u32[]{:S(2)}, u32[]{:S(2)}) %collective-permute-start.6) | collective-permute-done | bytes 262176 | tf_op jit(solution)/shard_map/ppermute | solution.py:20
  47.4 0.7 fusion.72
  48.2 0.7 fusion.73
  49.0 1.8 %copy-done.3 = f32[8,64,1792]{2,1,0:T(8,128)} copy-done((f32[8,64,1792]{2,1,0:T(8,128)}, f32[8,64,1792]{2,1,0:T(8,128)S(1)}, u32[]{:S(2)}) %copy-start.3) | copy-done | bytes 3670040
  51.1 3.9 %collective-permute-done.10 = f32[4,64,1792]{2,1,0:T(8,128)} collective-permute-done((f32[4,64,1792]{2,1,0:T(8,128)S(1)}, f32[4,64,1792]{2,1,0:T(8,128)}, u32[]{:S(2)}, u32[]{:S(2)}) %collective-permute-start.10) | collective-permute-done | bytes 1835040 | tf_op jit(solution)/shard_map/ppermute | solution.py:69
  55.0 2.2 %bitcast_add_fusion = f32[4,64,1792]{2,1,0:T(8,128)S(1)} fusion(f32[4,64,1792]{2,1,0:T(8,128)} %collective-permute-done.10, f32[4,2,64,1792]{3,2,1,0:T(8,128)} %bitcast.159, s32[]{:T(128)S(6)} %select_n.206), kind=kLoop, calls=%fused_computation | loop fusion | flops 458752 | bytes 5505028 | tf_op jit(solution)/shard_map/add | solution.py:70
  57.3 1.6 %collective-permute-start.11 = (f32[64,896]{1,0:T(8,128)S(1)}, f32[64,896]{1,0:T(8,128)S(1)}, u32[]{:S(2)}, u32[]{:S(2)}) collective-permute-start(f32[64,896]{1,0:T(8,128)S(1)} %slice.36), channel_id=1, source_target_pairs={{0,64},{64,128},{128,192},{192,0},{1,65},{65,129},{129,193},{193,1... | collective-permute-start | bytes 688136 | tf_op jit(solution)/shard_map/ppermute | solution.py:42
  58.9 0.6 collective-permute-start.13
  59.5 5.5 %collective-permute-done.11 = f32[64,896]{1,0:T(8,128)S(1)} collective-permute-done((f32[64,896]{1,0:T(8,128)S(1)}, f32[64,896]{1,0:T(8,128)S(1)}, u32[]{:S(2)}, u32[]{:S(2)}) %collective-permute-start.11) | collective-permute-done | bytes 229408 | tf_op jit(solution)/shard_map/ppermute | solution.py:42
  65.0 1.3 collective-permute-done.13
  66.4 1.3 collective-permute-start.12
  67.7 0.8 collective-permute-start.14
  68.5 9.4 %collective-permute-done.12 = f32[64,1792]{1,0:T(8,128)S(1)} collective-permute-done((f32[64,1792]{1,0:T(8,128)S(1)}, f32[64,1792]{1,0:T(8,128)S(1)}, u32[]{:S(2)}, u32[]{:S(2)}) %collective-permute-start.12) | collective-permute-done | bytes 458784 | tf_op jit(solution)/shard_map/ppermute | solution.py:42
  77.9 1.0 collective-permute-done.14
  78.9 1.1 fusion.8
  80.1 14.4 %all_gather.3 = bf16[512,896]{1,0:T(8,128)(2,1)S(1)} all-gather(bf16[64,896]{1,0:T(8,128)(2,1)S(1)} %fusion.9), channel_id=1, replica_groups=mesh['ex'=4,'ec'=2,'hy'=4,'hz'=8] {'ex','ec'}, dimensions={0}, use_global_device_ids=true | all-gather | bytes 1032192 | tf_op jit(solution)/shard_map/all_gather | solution.py:94
  94.5 2.8 %fusion.24 = bf16[64,2048]{1,0:T(8,128)(2,1)S(1)} fusion(bf16[896,2048]{1,0:T(8,128)(2,1)} %param.7, bf16[8,64,896]{2,1,0:T(8,128)(2,1)S(1)} %bitcast.160, s32[]{:T(128)S(6)} %select_n.221), kind=kOutput, calls=%fused_computation.52 | convolution fusion | flops 234881024 | bytes 4046852 | tf_op jit(solution)/shard_map/dot_general | solution.py:96
  97.4 0.8 fusion.14
  98.2 3.5 %collective-permute-start.19 = (bf16[64,1024]{1,0:T(8,128)(2,1)S(1)}, bf16[64,1024]{1,0:T(8,128)(2,1)S(1)}, u32[]{:S(2)}, u32[]{:S(2)}) collective-permute-start(bf16[64,1024]{1,0:T(8,128)(2,1)S(1)} %slice.50), channel_id=1, source_target_pairs={{0,7},{1,0},{2,1},{3,2},{4,3},{5,4},{6,5},{7,6},{8,15},{9,8},{10,9... | collective-permute-start | bytes 393224 | tf_op jit(solution)/shard_map/ppermute | solution.py:42
  101.7 2.6 %collective-permute-done.15 = bf16[64,1024]{1,0:T(8,128)(2,1)S(1)} collective-permute-done((bf16[64,1024]{1,0:T(8,128)(2,1)S(1)}, bf16[64,1024]{1,0:T(8,128)(2,1)S(1)}, u32[]{:S(2)}, u32[]{:S(2)}) %collective-permute-start.15) | collective-permute-done | bytes 131104 | tf_op jit(solution)/shard_map/ppermute | solution.py:42
  104.4 0.8 add_convert_fusion.5
  105.2 0.8 add_convert_fusion.2
  106.0 3.3 %collective-permute-start.20 = (bf16[64,2048]{1,0:T(8,128)(2,1)S(1)}, bf16[64,2048]{1,0:T(8,128)(2,1)S(1)}, u32[]{:S(2)}, u32[]{:S(2)}) collective-permute-start(bf16[64,2048]{1,0:T(8,128)(2,1)S(1)} %add_convert_fusion.2), channel_id=1, source_target_pairs={{0,7},{1,0},{2,1},{3,2},{4,3},{5,4},{6,5},{7,6},{8,15},{9,8},{10,9... | collective-permute-start | bytes 786440 | tf_op jit(solution)/shard_map/ppermute | solution.py:42
  109.3 4.9 %collective-permute-done.16 = bf16[64,2048]{1,0:T(8,128)(2,1)S(1)} collective-permute-done((bf16[64,2048]{1,0:T(8,128)(2,1)S(1)}, bf16[64,2048]{1,0:T(8,128)(2,1)S(1)}, u32[]{:S(2)}, u32[]{:S(2)}) %collective-permute-start.16) | collective-permute-done | bytes 262176 | tf_op jit(solution)/shard_map/ppermute | solution.py:42
  114.2 0.8 add_convert_fusion.4
  115.0 0.8 add_convert_fusion.1
  115.8 3.3 %collective-permute-start.21 = (bf16[64,2048]{1,0:T(8,128)(2,1)S(1)}, bf16[64,2048]{1,0:T(8,128)(2,1)S(1)}, u32[]{:S(2)}, u32[]{:S(2)}) collective-permute-start(bf16[64,2048]{1,0:T(8,128)(2,1)S(1)} %add_convert_fusion.1), channel_id=1, source_target_pairs={{0,7},{1,0},{2,1},{3,2},{4,3},{5,4},{6,5},{7,6},{8,15},{9,8},{10,9... | collective-permute-start | bytes 786440 | tf_op jit(solution)/shard_map/ppermute | solution.py:42
  119.1 4.0 %collective-permute-done.17 = bf16[64,2048]{1,0:T(8,128)(2,1)S(1)} collective-permute-done((bf16[64,2048]{1,0:T(8,128)(2,1)S(1)}, bf16[64,2048]{1,0:T(8,128)(2,1)S(1)}, u32[]{:S(2)}, u32[]{:S(2)}) %collective-permute-start.17) | collective-permute-done | bytes 262176 | tf_op jit(solution)/shard_map/ppermute | solution.py:42
  123.1 0.8 add_convert_fusion.3
  123.9 0.8 add_convert_fusion
  124.7 3.3 %collective-permute-start.22 = (bf16[64,2048]{1,0:T(8,128)(2,1)S(1)}, bf16[64,2048]{1,0:T(8,128)(2,1)S(1)}, u32[]{:S(2)}, u32[]{:S(2)}) collective-permute-start(bf16[64,2048]{1,0:T(8,128)(2,1)S(1)} %add_convert_fusion), channel_id=1, source_target_pairs={{0,7},{1,0},{2,1},{3,2},{4,3},{5,4},{6,5},{7,6},{8,15},{9,8},{10,9... | collective-permute-start | bytes 786440 | tf_op jit(solution)/shard_map/ppermute | solution.py:42
  128.0 0.8 fusion.34
  128.8 2.7 %collective-permute-done.18 = bf16[64,2048]{1,0:T(8,128)(2,1)S(1)} collective-permute-done((bf16[64,2048]{1,0:T(8,128)(2,1)S(1)}, bf16[64,2048]{1,0:T(8,128)(2,1)S(1)}, u32[]{:S(2)}, u32[]{:S(2)}) %collective-permute-start.18) | collective-permute-done | bytes 262176 | tf_op jit(solution)/shard_map/ppermute | solution.py:42
  132.1 3.2 %collective-permute-start.25 = (bf16[16,1024]{1,0:T(8,128)(2,1)S(1)}, bf16[16,1024]{1,0:T(8,128)(2,1)S(1)}, u32[]{:S(2)}, u32[]{:S(2)}) collective-permute-start(bf16[16,1024]{1,0:T(8,128)(2,1)S(1)} %slice.43), channel_id=1, source_target_pairs={{0,24},{8,0},{16,8},{24,16},{1,25},{9,1},{17,9},{25,17},{2,26},{10... | collective-permute-start | bytes 98312 | tf_op jit(solution)/shard_map/ppermute | solution.py:42
  135.3 2.2 %collective-permute-done.23 = bf16[16,1024]{1,0:T(8,128)(2,1)S(1)} collective-permute-done((bf16[16,1024]{1,0:T(8,128)(2,1)S(1)}, bf16[16,1024]{1,0:T(8,128)(2,1)S(1)}, u32[]{:S(2)}, u32[]{:S(2)}) %collective-permute-start.23) | collective-permute-done | bytes 32800 | tf_op jit(solution)/shard_map/ppermute | solution.py:42
  137.7 3.2 %collective-permute-start.26 = (bf16[16,2048]{1,0:T(8,128)(2,1)S(1)}, bf16[16,2048]{1,0:T(8,128)(2,1)S(1)}, u32[]{:S(2)}, u32[]{:S(2)}) collective-permute-start(bf16[16,2048]{1,0:T(8,128)(2,1)S(1)} %get-tuple-element.10), channel_id=1, source_target_pairs={{0,24},{8,0},{16,8},{24,16},{1,25},{9,1},{17,9},{25,17},{2,26},{10... | collective-permute-start | bytes 196616 | tf_op jit(solution)/shard_map/ppermute | solution.py:42
  140.9 2.2 %collective-permute-done.24 = bf16[16,2048]{1,0:T(8,128)(2,1)S(1)} collective-permute-done((bf16[16,2048]{1,0:T(8,128)(2,1)S(1)}, bf16[16,2048]{1,0:T(8,128)(2,1)S(1)}, u32[]{:S(2)}, u32[]{:S(2)}) %collective-permute-start.24) | collective-permute-done | bytes 65568 | tf_op jit(solution)/shard_map/ppermute | solution.py:42
  143.1 0.7 fusion.13
  (54 shorter events, 4.0 us)
Async XLA Ops:
  0.0 5.7 %collective-permute-start = (bf16[16,2048]{1,0:T(8,128)(2,1)}, bf16[16,2048]{1,0:T(8,128)(2,1)S(1)}, u32[]{:S(2)}, u32[]{:S(2)}) collective-permute-start(bf16[16,2048]{1,0:T(8,128)(2,1)} %param.4), channel_id=1, source_target_pairs={{0,8},{8,16},{16,24},{24,0},{1,9},{9,17},{17,25},{25,1},{2,10},{10... | collective-permute-start | bytes 196616 | tf_op jit(solution)/shard_map/ppermute | solution.py:20
  1.6 9.6 %collective-permute-start.2 = (bf16[16,2048]{1,0:T(8,128)(2,1)}, bf16[16,2048]{1,0:T(8,128)(2,1)S(1)}, u32[]{:S(2)}, u32[]{:S(2)}) collective-permute-start(bf16[16,2048]{1,0:T(8,128)(2,1)} %param.4), channel_id=1, source_target_pairs={{0,24},{8,0},{16,8},{24,16},{1,25},{9,1},{17,9},{25,17},{2,26},{10... | collective-permute-start | bytes 196616 | tf_op jit(solution)/shard_map/ppermute | solution.py:24
  4.1 15.9 %copy-start.2 = (bf16[2048,896]{1,0:T(8,128)(2,1)S(1)}, bf16[2048,896]{1,0:T(8,128)(2,1)}, u32[]{:S(2)}) copy-start(bf16[2048,896]{1,0:T(8,128)(2,1)} %param.6) | copy-start | bytes 11010052
  5.7 5.5 %collective-permute-start.1 = (bf16[16,2048]{1,0:T(8,128)(2,1)S(1)}, bf16[16,2048]{1,0:T(8,128)(2,1)S(1)}, u32[]{:S(2)}, u32[]{:S(2)}) collective-permute-start(bf16[16,2048]{1,0:T(8,128)(2,1)S(1)} %collective-permute-done), channel_id=1, source_target_pairs={{0,8},{8,16},{16,24},{24,0},{1,9},{9,17},{17,25},{25,1},{2,10},{10... | collective-permute-start | bytes 196616 | tf_op jit(solution)/shard_map/ppermute | solution.py:20
  11.2 10.3 %collective-permute-start.3 = (bf16[64,2048]{1,0:T(8,128)(2,1)S(1)}, bf16[64,2048]{1,0:T(8,128)(2,1)S(1)}, u32[]{:S(2)}, u32[]{:S(2)}) collective-permute-start(bf16[64,2048]{1,0:T(8,128)(2,1)S(1)} %bitcast.169), channel_id=1, source_target_pairs={{0,1},{1,2},{2,3},{3,4},{4,5},{5,6},{6,7},{7,0},{8,9},{9,10},{10,1... | collective-permute-start | bytes 786440 | tf_op jit(solution)/shard_map/ppermute | solution.py:20
  13.2 10.3 %collective-permute-start.7 = (bf16[64,2048]{1,0:T(8,128)(2,1)S(1)}, bf16[64,2048]{1,0:T(8,128)(2,1)S(1)}, u32[]{:S(2)}, u32[]{:S(2)}) collective-permute-start(bf16[64,2048]{1,0:T(8,128)(2,1)S(1)} %bitcast.170), channel_id=1, source_target_pairs={{0,7},{1,0},{2,1},{3,2},{4,3},{5,4},{6,5},{7,6},{8,15},{9,8},{10,9... | collective-permute-start | bytes 786440 | tf_op jit(solution)/shard_map/ppermute | solution.py:24
  20.0 2.0 %copy-start.1 = (bf16[2048,896]{1,0:T(8,128)(2,1)S(1)}, bf16[2048,896]{1,0:T(8,128)(2,1)}, u32[]{:S(2)}) copy-start(bf16[2048,896]{1,0:T(8,128)(2,1)} %param.5) | copy-start | bytes 11010052
  22.7 7.7 %collective-permute-start.4 = (bf16[64,2048]{1,0:T(8,128)(2,1)S(1)}, bf16[64,2048]{1,0:T(8,128)(2,1)S(1)}, u32[]{:S(2)}, u32[]{:S(2)}) collective-permute-start(bf16[64,2048]{1,0:T(8,128)(2,1)S(1)} %collective-permute-done.3), channel_id=1, source_target_pairs={{0,1},{1,2},{2,3},{3,4},{4,5},{5,6},{6,7},{7,0},{8,9},{9,10},{10,1... | collective-permute-start | bytes 786440 | tf_op jit(solution)/shard_map/ppermute | solution.py:20
  24.9 7.2 %collective-permute-start.8 = (bf16[64,2048]{1,0:T(8,128)(2,1)S(1)}, bf16[64,2048]{1,0:T(8,128)(2,1)S(1)}, u32[]{:S(2)}, u32[]{:S(2)}) collective-permute-start(bf16[64,2048]{1,0:T(8,128)(2,1)S(1)} %collective-permute-done.7), channel_id=1, source_target_pairs={{0,7},{1,0},{2,1},{3,2},{4,3},{5,4},{6,5},{7,6},{8,15},{9,8},{10,9... | collective-permute-start | bytes 786440 | tf_op jit(solution)/shard_map/ppermute | solution.py:24
  31.1 8.0 %collective-permute-start.5 = (bf16[64,2048]{1,0:T(8,128)(2,1)S(1)}, bf16[64,2048]{1,0:T(8,128)(2,1)S(1)}, u32[]{:S(2)}, u32[]{:S(2)}) collective-permute-start(bf16[64,2048]{1,0:T(8,128)(2,1)S(1)} %collective-permute-done.4), channel_id=1, source_target_pairs={{0,1},{1,2},{2,3},{3,4},{4,5},{5,6},{6,7},{7,0},{8,9},{9,10},{10,1... | collective-permute-start | bytes 786440 | tf_op jit(solution)/shard_map/ppermute | solution.py:20
  33.6 7.8 %collective-permute-start.9 = (bf16[64,2048]{1,0:T(8,128)(2,1)S(1)}, bf16[64,2048]{1,0:T(8,128)(2,1)S(1)}, u32[]{:S(2)}, u32[]{:S(2)}) collective-permute-start(bf16[64,2048]{1,0:T(8,128)(2,1)S(1)} %collective-permute-done.8), channel_id=1, source_target_pairs={{0,7},{1,0},{2,1},{3,2},{4,3},{5,4},{6,5},{7,6},{8,15},{9,8},{10,9... | collective-permute-start | bytes 786440 | tf_op jit(solution)/shard_map/ppermute | solution.py:24
  39.8 7.7 %collective-permute-start.6 = (bf16[64,2048]{1,0:T(8,128)(2,1)S(1)}, bf16[64,2048]{1,0:T(8,128)(2,1)S(1)}, u32[]{:S(2)}, u32[]{:S(2)}) collective-permute-start(bf16[64,2048]{1,0:T(8,128)(2,1)S(1)} %collective-permute-done.5), channel_id=1, source_target_pairs={{0,1},{1,2},{2,3},{3,4},{4,5},{5,6},{6,7},{7,0},{8,9},{9,10},{10,1... | collective-permute-start | bytes 786440 | tf_op jit(solution)/shard_map/ppermute | solution.py:20
  49.0 1.8 %copy-start.3 = (f32[8,64,1792]{2,1,0:T(8,128)}, f32[8,64,1792]{2,1,0:T(8,128)S(1)}, u32[]{:S(2)}) copy-start(f32[8,64,1792]{2,1,0:T(8,128)S(1)} %fusion.7) | copy-start | bytes 11010052
  51.0 4.0 %collective-permute-start.10 = (f32[4,64,1792]{2,1,0:T(8,128)S(1)}, f32[4,64,1792]{2,1,0:T(8,128)}, u32[]{:S(2)}, u32[]{:S(2)}) collective-permute-start(f32[4,64,1792]{2,1,0:T(8,128)S(1)} %dynamic-slice_bitcast_fusion), channel_id=1, source_target_pairs={{0,32},{32,0},{1,33},{33,1},{2,34},{34,2},{3,35},{35,3},{4,36},{36... | collective-permute-start | bytes 5505032 | tf_op jit(solution)/shard_map/ppermute | solution.py:69
  57.3 7.7 %collective-permute-start.11 = (f32[64,896]{1,0:T(8,128)S(1)}, f32[64,896]{1,0:T(8,128)S(1)}, u32[]{:S(2)}, u32[]{:S(2)}) collective-permute-start(f32[64,896]{1,0:T(8,128)S(1)} %slice.36), channel_id=1, source_target_pairs={{0,64},{64,128},{128,192},{192,0},{1,65},{65,129},{129,193},{193,1... | collective-permute-start | bytes 688136 | tf_op jit(solution)/shard_map/ppermute | solution.py:42
  58.9 7.4 %collective-permute-start.13 = (f32[64,896]{1,0:T(8,128)S(1)}, f32[64,896]{1,0:T(8,128)S(1)}, u32[]{:S(2)}, u32[]{:S(2)}) collective-permute-start(f32[64,896]{1,0:T(8,128)S(1)} %slice.37), channel_id=1, source_target_pairs={{0,192},{64,0},{128,64},{192,128},{1,193},{65,1},{129,65},{193,129... | collective-permute-start | bytes 688136 | tf_op jit(solution)/shard_map/ppermute | solution.py:42
  66.4 11.5 %collective-permute-start.12 = (f32[64,1792]{1,0:T(8,128)S(1)}, f32[64,1792]{1,0:T(8,128)S(1)}, u32[]{:S(2)}, u32[]{:S(2)}) collective-permute-start(f32[64,1792]{1,0:T(8,128)S(1)} %get-tuple-element.5), channel_id=1, source_target_pairs={{0,64},{64,128},{128,192},{192,0},{1,65},{65,129},{129,193},{193,1... | collective-permute-start | bytes 1376264 | tf_op jit(solution)/shard_map/ppermute | solution.py:42
  67.7 11.2 %collective-permute-start.14 = (f32[64,1792]{1,0:T(8,128)S(1)}, f32[64,1792]{1,0:T(8,128)}, u32[]{:S(2)}, u32[]{:S(2)}) collective-permute-start(f32[64,1792]{1,0:T(8,128)S(1)} %get-tuple-element.6), channel_id=1, source_target_pairs={{0,192},{64,0},{128,64},{192,128},{1,193},{65,1},{129,65},{193,129... | collective-permute-start | bytes 1376264 | tf_op jit(solution)/shard_map/ppermute | solution.py:42
  68.5 28.9 %copy-start = (bf16[896,2048]{1,0:T(8,128)(2,1)S(1)}, bf16[896,2048]{1,0:T(8,128)(2,1)}, u32[]{:S(2)}) copy-start(bf16[896,2048]{1,0:T(8,128)(2,1)} %param.7) | copy-start | bytes 11010052
  97.3 7.0 %collective-permute-start.15 = (bf16[64,1024]{1,0:T(8,128)(2,1)S(1)}, bf16[64,1024]{1,0:T(8,128)(2,1)S(1)}, u32[]{:S(2)}, u32[]{:S(2)}) collective-permute-start(bf16[64,1024]{1,0:T(8,128)(2,1)S(1)} %slice.51), channel_id=1, source_target_pairs={{0,1},{1,2},{2,3},{3,4},{4,5},{5,6},{6,7},{7,0},{8,9},{9,10},{10,1... | collective-permute-start | bytes 393224 | tf_op jit(solution)/shard_map/ppermute | solution.py:42
  98.2 7.0 %collective-permute-start.19 = (bf16[64,1024]{1,0:T(8,128)(2,1)S(1)}, bf16[64,1024]{1,0:T(8,128)(2,1)S(1)}, u32[]{:S(2)}, u32[]{:S(2)}) collective-permute-start(bf16[64,1024]{1,0:T(8,128)(2,1)S(1)} %slice.50), channel_id=1, source_target_pairs={{0,7},{1,0},{2,1},{3,2},{4,3},{5,4},{6,5},{7,6},{8,15},{9,8},{10,9... | collective-permute-start | bytes 393224 | tf_op jit(solution)/shard_map/ppermute | solution.py:42
  105.1 9.0 %collective-permute-start.16 = (bf16[64,2048]{1,0:T(8,128)(2,1)S(1)}, bf16[64,2048]{1,0:T(8,128)(2,1)S(1)}, u32[]{:S(2)}, u32[]{:S(2)}) collective-permute-start(bf16[64,2048]{1,0:T(8,128)(2,1)S(1)} %add_convert_fusion.5), channel_id=1, source_target_pairs={{0,1},{1,2},{2,3},{3,4},{4,5},{5,6},{6,7},{7,0},{8,9},{9,10},{10,1... | collective-permute-start | bytes 786440 | tf_op jit(solution)/shard_map/ppermute | solution.py:42
  106.0 9.0 %collective-permute-start.20 = (bf16[64,2048]{1,0:T(8,128)(2,1)S(1)}, bf16[64,2048]{1,0:T(8,128)(2,1)S(1)}, u32[]{:S(2)}, u32[]{:S(2)}) collective-permute-start(bf16[64,2048]{1,0:T(8,128)(2,1)S(1)} %add_convert_fusion.2), channel_id=1, source_target_pairs={{0,7},{1,0},{2,1},{3,2},{4,3},{5,4},{6,5},{7,6},{8,15},{9,8},{10,9... | collective-permute-start | bytes 786440 | tf_op jit(solution)/shard_map/ppermute | solution.py:42
  114.9 8.1 %collective-permute-start.17 = (bf16[64,2048]{1,0:T(8,128)(2,1)S(1)}, bf16[64,2048]{1,0:T(8,128)(2,1)S(1)}, u32[]{:S(2)}, u32[]{:S(2)}) collective-permute-start(bf16[64,2048]{1,0:T(8,128)(2,1)S(1)} %add_convert_fusion.4), channel_id=1, source_target_pairs={{0,1},{1,2},{2,3},{3,4},{4,5},{5,6},{6,7},{7,0},{8,9},{9,10},{10,1... | collective-permute-start | bytes 786440 | tf_op jit(solution)/shard_map/ppermute | solution.py:42
  115.8 8.1 %collective-permute-start.21 = (bf16[64,2048]{1,0:T(8,128)(2,1)S(1)}, bf16[64,2048]{1,0:T(8,128)(2,1)S(1)}, u32[]{:S(2)}, u32[]{:S(2)}) collective-permute-start(bf16[64,2048]{1,0:T(8,128)(2,1)S(1)} %add_convert_fusion.1), channel_id=1, source_target_pairs={{0,7},{1,0},{2,1},{3,2},{4,3},{5,4},{6,5},{7,6},{8,15},{9,8},{10,9... | collective-permute-start | bytes 786440 | tf_op jit(solution)/shard_map/ppermute | solution.py:42
  123.8 7.7 %collective-permute-start.18 = (bf16[64,2048]{1,0:T(8,128)(2,1)S(1)}, bf16[64,2048]{1,0:T(8,128)(2,1)S(1)}, u32[]{:S(2)}, u32[]{:S(2)}) collective-permute-start(bf16[64,2048]{1,0:T(8,128)(2,1)S(1)} %add_convert_fusion.3), channel_id=1, source_target_pairs={{0,1},{1,2},{2,3},{3,4},{4,5},{5,6},{6,7},{7,0},{8,9},{9,10},{10,1... | collective-permute-start | bytes 786440 | tf_op jit(solution)/shard_map/ppermute | solution.py:42
  124.7 7.2 %collective-permute-start.22 = (bf16[64,2048]{1,0:T(8,128)(2,1)S(1)}, bf16[64,2048]{1,0:T(8,128)(2,1)S(1)}, u32[]{:S(2)}, u32[]{:S(2)}) collective-permute-start(bf16[64,2048]{1,0:T(8,128)(2,1)S(1)} %add_convert_fusion), channel_id=1, source_target_pairs={{0,7},{1,0},{2,1},{3,2},{4,3},{5,4},{6,5},{7,6},{8,15},{9,8},{10,9... | collective-permute-start | bytes 786440 | tf_op jit(solution)/shard_map/ppermute | solution.py:42
  132.0 5.5 %collective-permute-start.23 = (bf16[16,1024]{1,0:T(8,128)(2,1)S(1)}, bf16[16,1024]{1,0:T(8,128)(2,1)S(1)}, u32[]{:S(2)}, u32[]{:S(2)}) collective-permute-start(bf16[16,1024]{1,0:T(8,128)(2,1)S(1)} %slice.42), channel_id=1, source_target_pairs={{0,8},{8,16},{16,24},{24,0},{1,9},{9,17},{17,25},{25,1},{2,10},{10... | collective-permute-start | bytes 98312 | tf_op jit(solution)/shard_map/ppermute | solution.py:42
  132.1 5.5 %collective-permute-start.25 = (bf16[16,1024]{1,0:T(8,128)(2,1)S(1)}, bf16[16,1024]{1,0:T(8,128)(2,1)S(1)}, u32[]{:S(2)}, u32[]{:S(2)}) collective-permute-start(bf16[16,1024]{1,0:T(8,128)(2,1)S(1)} %slice.43), channel_id=1, source_target_pairs={{0,24},{8,0},{16,8},{24,16},{1,25},{9,1},{17,9},{25,17},{2,26},{10... | collective-permute-start | bytes 98312 | tf_op jit(solution)/shard_map/ppermute | solution.py:42
  137.6 5.6 %collective-permute-start.24 = (bf16[16,2048]{1,0:T(8,128)(2,1)S(1)}, bf16[16,2048]{1,0:T(8,128)(2,1)S(1)}, u32[]{:S(2)}, u32[]{:S(2)}) collective-permute-start(bf16[16,2048]{1,0:T(8,128)(2,1)S(1)} %get-tuple-element.9), channel_id=1, source_target_pairs={{0,8},{8,16},{16,24},{24,0},{1,9},{9,17},{17,25},{25,1},{2,10},{10... | collective-permute-start | bytes 196616 | tf_op jit(solution)/shard_map/ppermute | solution.py:42
  137.7 5.5 %collective-permute-start.26 = (bf16[16,2048]{1,0:T(8,128)(2,1)S(1)}, bf16[16,2048]{1,0:T(8,128)(2,1)S(1)}, u32[]{:S(2)}, u32[]{:S(2)}) collective-permute-start(bf16[16,2048]{1,0:T(8,128)(2,1)S(1)} %get-tuple-element.10), channel_id=1, source_target_pairs={{0,24},{8,0},{16,8},{24,16},{1,25},{9,1},{17,9},{25,17},{2,26},{10... | collective-permute-start | bytes 196616 | tf_op jit(solution)/shard_map/ppermute | solution.py:42

commit v13 on v9

--- a/solution.py
+++ b/solution.py
@@ -77,16 +77,13 @@
     width = gate_weight.shape[1]
     ny = lax.psum(1, "hy")
     nz = lax.psum(1, "hz")
-    both = jnp.concatenate([gate_weight, up_weight], axis=1)
-    partial_value = ring_ag(
-        ring_ag(rows_in, "hy", ny),
-        "hz",
-        nz,
-        lambda v: jnp.dot(v, both, preferred_element_type=jnp.float32),
-    )
+    piece = ring_ag(ring_ag(rows_in, "hy", ny), "hz", nz)
+    gate_part = jnp.dot(piece, gate_weight, preferred_element_type=jnp.float32)
+    up_part = jnp.dot(piece, up_weight, preferred_element_type=jnp.float32)
+    partial_value = jnp.concatenate([gate_part, up_part], axis=1)
     summed = embed_rs(partial_value)
     activated = (jax.nn.silu(summed[:, :width]) * summed[:, width:]).astype(jnp.bfloat16)
-    activated = lax.all_gather(activated, EMBED, axis=0, tiled=True)
+    activated = ring_ag(ring_ag(activated, "ec", lax.psum(1, "ec")), "ex", lax.psum(1, "ex"))
     act_blocks = activated.reshape((nz, -1) + activated.shape[1:])
     project = lambda i: jnp.dot(
         lax.dynamic_index_in_dim(act_blocks, i, 0, keepdims=False),
@@ -96,7 +93,7 @@
     totals = ring_rs_bal(project, "hz", nz, jnp.bfloat16)
     totals = totals.reshape((ny, -1) + totals.shape[1:])
     totals = ring_rs_bal(
-        lambda i: lax.dynamic_index_in_dim(totals, i, 0, keepdims=False), "hy", ny, jnp.float32
+        lambda i: lax.dynamic_index_in_dim(totals, i, 0, keepdims=False), "hy", ny, jnp.bfloat16
     )
     return totals.astype(jnp.bfloat16)
 

time: 155 us -> 151 us (0.974)
  the two profiles are of different devices: /device:TPU:2 before, /device:TPU:120 now
where the time goes in v13:
time: 151 us
  waiting for transfers between devices  80.3 us (53%)
  starting transfers between devices  48.4 us (32%)
  matrix products  13.7 us (9%)
  other arithmetic  4.5 us (3%)
  local copies, waits for them, and re-layouts  3.63 us (2%)
    ppermute x16, waiting for transfers between devices, side(): got = lax.ppermute(acc.astype(send_dtype), axis, perm).astype(jnp.float32)  38.9 us
    ppermute x9, waiting for transfers between devices, ring_ag(): buf = lax.ppermute(buf, axis, fwd)  37.3 us
    ppermute x16, starting transfers between devices, side(): got = lax.ppermute(acc.astype(send_dtype), axis, perm).astype(jnp.float32)  27 us
    ppermute x9, starting transfers between devices, ring_ag(): buf = lax.ppermute(buf, axis, fwd)  17.2 us
    dot_general x9, matrix products, on_device(): jnp.dot(lax.dynamic_index_in_dim(act_blocks, i, 0, keepdims=False), down_...  9.04 us
    ppermute x5, starting transfers between devices, ring_ag(): buf = lax.ppermute(buf, axis, bwd)  3.98 us
    ppermute x1, waiting for transfers between devices, embed_rs(): got = lax.ppermute(other, 'ec', [(0, 1), (1, 0)])  3.86 us
  transfers between devices with their start and end apart: 31, of which 25 were waited for; matrix products, arithmetic and copies ran while one was open for 5% of the time, Pallas kernels for 0%

profile of v13, /device:TPU:120, one launch (start us, length us, event | category | flops | bytes accessed | tf_op | source)
XLA Modules:
  0.0 151.1 jit_solution(15276340338545190754)
XLA Ops:
  0.0 0.2 collective-permute-start
  0.2 1.8 %collective-permute-start.2 = (bf16[16,2048]{1,0:T(8,128)(2,1)}, bf16[16,2048]{1,0:T(8,128)(2,1)S(1)}, u32[]{:S(2)}, u32[]{:S(2)}) collective-permute-start(bf16[16,2048]{1,0:T(8,128)(2,1)} %param.4), channel_id=1, source_target_pairs={{0,24},{8,0},{16,8},{24,16},{1,25},{9,1},{17,9},{25,17},{2,26},{10... | collective-permute-start | bytes 196616 | tf_op jit(solution)/shard_map/ppermute | solution.py:24
  2.1 0.9 bitcast_dynamic-update-slice_fusion.17
  2.9 1.6 %collective-permute-done = bf16[16,2048]{1,0:T(8,128)(2,1)S(1)} collective-permute-done((bf16[16,2048]{1,0:T(8,128)(2,1)}, bf16[16,2048]{1,0:T(8,128)(2,1)S(1)}, u32[]{:S(2)}, u32[]{:S(2)}) %collective-permute-start) | collective-permute-done | bytes 65568 | tf_op jit(solution)/shard_map/ppermute | solution.py:20
  4.5 1.4 collective-permute-start.1
  5.9 2.8 %collective-permute-done.1 = bf16[16,2048]{1,0:T(8,128)(2,1)S(1)} collective-permute-done((bf16[16,2048]{1,0:T(8,128)(2,1)S(1)}, bf16[16,2048]{1,0:T(8,128)(2,1)S(1)}, u32[]{:S(2)}, u32[]{:S(2)}) %collective-permute-start.1) | collective-permute-done | bytes 65568 | tf_op jit(solution)/shard_map/ppermute | solution.py:20
  8.8 3.2 %collective-permute-start.3 = (bf16[64,2048]{1,0:T(8,128)(2,1)S(1)}, bf16[64,2048]{1,0:T(8,128)(2,1)S(1)}, u32[]{:S(2)}, u32[]{:S(2)}) collective-permute-start(bf16[64,2048]{1,0:T(8,128)(2,1)S(1)} %bitcast.146), channel_id=1, source_target_pairs={{0,1},{1,2},{2,3},{3,4},{4,5},{5,6},{6,7},{7,0},{8,9},{9,10},{10,1... | collective-permute-start | bytes 786440 | tf_op jit(solution)/shard_map/ppermute | solution.py:20
  12.0 0.2 broadcast_in_dim.72
  12.3 3.6 %collective-permute-done.3 = bf16[64,2048]{1,0:T(8,128)(2,1)S(1)} collective-permute-done((bf16[64,2048]{1,0:T(8,128)(2,1)S(1)}, bf16[64,2048]{1,0:T(8,128)(2,1)S(1)}, u32[]{:S(2)}, u32[]{:S(2)}) %collective-permute-start.3) | collective-permute-done | bytes 262176 | tf_op jit(solution)/shard_map/ppermute | solution.py:20
  15.9 3.7 %collective-permute-start.4 = (bf16[64,2048]{1,0:T(8,128)(2,1)S(1)}, bf16[64,2048]{1,0:T(8,128)(2,1)S(1)}, u32[]{:S(2)}, u32[]{:S(2)}) collective-permute-start(bf16[64,2048]{1,0:T(8,128)(2,1)S(1)} %collective-permute-done.3), channel_id=1, source_target_pairs={{0,1},{1,2},{2,3},{3,4},{4,5},{5,6},{6,7},{7,0},{8,9},{9,10},{10,1... | collective-permute-start | bytes 786440 | tf_op jit(solution)/shard_map/ppermute | solution.py:20
  19.6 4.7 %collective-permute-done.4 = bf16[64,2048]{1,0:T(8,128)(2,1)S(1)} collective-permute-done((bf16[64,2048]{1,0:T(8,128)(2,1)S(1)}, bf16[64,2048]{1,0:T(8,128)(2,1)S(1)}, u32[]{:S(2)}, u32[]{:S(2)}) %collective-permute-start.4) | collective-permute-done | bytes 262176 | tf_op jit(solution)/shard_map/ppermute | solution.py:20
  24.4 3.7 %collective-permute-start.5 = (bf16[64,2048]{1,0:T(8,128)(2,1)S(1)}, bf16[64,2048]{1,0:T(8,128)(2,1)S(1)}, u32[]{:S(2)}, u32[]{:S(2)}) collective-permute-start(bf16[64,2048]{1,0:T(8,128)(2,1)S(1)} %collective-permute-done.4), channel_id=1, source_target_pairs={{0,1},{1,2},{2,3},{3,4},{4,5},{5,6},{6,7},{7,0},{8,9},{9,10},{10,1... | collective-permute-start | bytes 786440 | tf_op jit(solution)/shard_map/ppermute | solution.py:20
  28.0 0.2 collective-permute-done.8
  28.3 5.7 %collective-permute-done.5 = bf16[64,2048]{1,0:T(8,128)(2,1)S(1)} collective-permute-done((bf16[64,2048]{1,0:T(8,128)(2,1)S(1)}, bf16[64,2048]{1,0:T(8,128)(2,1)S(1)}, u32[]{:S(2)}, u32[]{:S(2)}) %collective-permute-start.5) | collective-permute-done | bytes 262176 | tf_op jit(solution)/shard_map/ppermute | solution.py:20
  34.0 3.7 %collective-permute-start.6 = (bf16[64,2048]{1,0:T(8,128)(2,1)S(1)}, bf16[64,2048]{1,0:T(8,128)(2,1)S(1)}, u32[]{:S(2)}, u32[]{:S(2)}) collective-permute-start(bf16[64,2048]{1,0:T(8,128)(2,1)S(1)} %collective-permute-done.5), channel_id=1, source_target_pairs={{0,1},{1,2},{2,3},{3,4},{4,5},{5,6},{6,7},{7,0},{8,9},{9,10},{10,1... | collective-permute-start | bytes 786440 | tf_op jit(solution)/shard_map/ppermute | solution.py:20
  37.7 3.9 %collective-permute-done.6 = bf16[64,2048]{1,0:T(8,128)(2,1)S(1)} collective-permute-done((bf16[64,2048]{1,0:T(8,128)(2,1)S(1)}, bf16[64,2048]{1,0:T(8,128)(2,1)S(1)}, u32[]{:S(2)}, u32[]{:S(2)}) %collective-permute-start.6) | collective-permute-done | bytes 262176 | tf_op jit(solution)/shard_map/ppermute | solution.py:20
  41.7 2.3 %fusion.57 = f32[512,896]{1,0:T(8,128)S(1)} fusion(bf16[512,2048]{1,0:T(8,128)(2,1)S(1)} %bitcast.144, bf16[2048,896]{1,0:T(8,128)(2,1)S(1)} %copy-done.2), kind=kOutput, calls=%fused_computation.85 | convolution fusion | flops 1879048192 | bytes 7602176 | tf_op jit(solution)/shard_map/dot_general | solution.py:81
  44.1 2.3 %fusion.58 = f32[512,896]{1,0:T(8,128)S(1)} fusion(bf16[512,2048]{1,0:T(8,128)(2,1)S(1)} %bitcast.145, bf16[2048,896]{1,0:T(8,128)(2,1)S(1)} %copy-done.3), kind=kOutput, calls=%fused_computation.86 | convolution fusion | flops 1879048192 | bytes 7602176 | tf_op jit(solution)/shard_map/dot_general | solution.py:82
  46.4 0.3 pad_maximum_fusion
  46.7 1.8 %copy-done.1 = f32[512,1792]{1,0:T(8,128)} copy-done((f32[512,1792]{1,0:T(8,128)}, f32[512,1792]{1,0:T(8,128)S(1)}, u32[]{:S(2)}) %copy-start.1) | copy-done | bytes 3670040
  48.5 0.1 dynamic-slice_bitcast_fusion
  48.6 0.3 collective-permute-start.10
  48.9 3.9 %collective-permute-done.10 = f32[4,64,1792]{2,1,0:T(8,128)} collective-permute-done((f32[4,64,1792]{2,1,0:T(8,128)S(1)}, f32[4,64,1792]{2,1,0:T(8,128)}, u32[]{:S(2)}, u32[]{:S(2)}) %collective-permute-start.10) | collective-permute-done | bytes 1835040 | tf_op jit(solution)/shard_map/ppermute | solution.py:69
  52.8 2.2 %bitcast_add_fusion = f32[4,64,1792]{2,1,0:T(8,128)S(1)} fusion(f32[4,64,1792]{2,1,0:T(8,128)} %collective-permute-done.10, f32[4,2,64,1792]{3,2,1,0:T(8,128)} %bitcast.131, s32[]{:T(128)S(6)} %select_n.228), kind=kLoop, calls=%fused_computation.1 | loop fusion | flops 458752 | bytes 5505028 | tf_op jit(solution)/shard_map/add | solution.py:70
  55.1 1.6 %collective-permute-start.11 = (f32[64,896]{1,0:T(8,128)S(1)}, f32[64,896]{1,0:T(8,128)S(1)}, u32[]{:S(2)}, u32[]{:S(2)}) collective-permute-start(f32[64,896]{1,0:T(8,128)S(1)} %slice.36), channel_id=1, source_target_pairs={{0,64},{64,128},{128,192},{192,0},{1,65},{65,129},{129,193},{193,1... | collective-permute-start | bytes 688136 | tf_op jit(solution)/shard_map/ppermute | solution.py:42
  56.7 1.8 %collective-permute-start.13 = (f32[64,896]{1,0:T(8,128)S(1)}, f32[64,896]{1,0:T(8,128)S(1)}, u32[]{:S(2)}, u32[]{:S(2)}) collective-permute-start(f32[64,896]{1,0:T(8,128)S(1)} %slice.37), channel_id=1, source_target_pairs={{0,192},{64,0},{128,64},{192,128},{1,193},{65,1},{129,65},{193,129... | collective-permute-start | bytes 688136 | tf_op jit(solution)/shard_map/ppermute | solution.py:42
  58.5 5.5 %collective-permute-done.11 = f32[64,896]{1,0:T(8,128)S(1)} collective-permute-done((f32[64,896]{1,0:T(8,128)S(1)}, f32[64,896]{1,0:T(8,128)S(1)}, u32[]{:S(2)}, u32[]{:S(2)}) %collective-permute-start.11) | collective-permute-done | bytes 229408 | tf_op jit(solution)/shard_map/ppermute | solution.py:42
  64.2 1.6 %collective-permute-start.12 = (f32[64,1792]{1,0:T(8,128)S(1)}, f32[64,1792]{1,0:T(8,128)S(1)}, u32[]{:S(2)}, u32[]{:S(2)}) collective-permute-start(f32[64,1792]{1,0:T(8,128)S(1)} %get-tuple-element.7), channel_id=1, source_target_pairs={{0,64},{64,128},{128,192},{192,0},{1,65},{65,129},{129,193},{193,1... | collective-permute-start | bytes 1376264 | tf_op jit(solution)/shard_map/ppermute | solution.py:42
  65.8 1.7 %collective-permute-start.14 = (f32[64,1792]{1,0:T(8,128)S(1)}, f32[64,1792]{1,0:T(8,128)}, u32[]{:S(2)}, u32[]{:S(2)}) collective-permute-start(f32[64,1792]{1,0:T(8,128)S(1)} %get-tuple-element.8), channel_id=1, source_target_pairs={{0,192},{64,0},{128,64},{192,128},{1,193},{65,1},{129,65},{193,129... | collective-permute-start | bytes 1376264 | tf_op jit(solution)/shard_map/ppermute | solution.py:42
  67.6 9.6 %collective-permute-done.12 = f32[64,1792]{1,0:T(8,128)S(1)} collective-permute-done((f32[64,1792]{1,0:T(8,128)S(1)}, f32[64,1792]{1,0:T(8,128)S(1)}, u32[]{:S(2)}, u32[]{:S(2)}) %collective-permute-start.12) | collective-permute-done | bytes 458784 | tf_op jit(solution)/shard_map/ppermute | solution.py:42
  77.2 1.1 fusion
  78.5 1.3 collective-permute-done.15
  79.8 1.1 collective-permute-start.16
  81.0 2.2 %collective-permute-start.18 = (bf16[128,896]{1,0:T(8,128)(2,1)S(1)}, bf16[128,896]{1,0:T(8,128)(2,1)S(1)}, u32[]{:S(2)}, u32[]{:S(2)}) collective-permute-start(bf16[128,896]{1,0:T(8,128)(2,1)S(1)} %bitcast.150), channel_id=1, source_target_pairs={{0,192},{64,0},{128,64},{192,128},{1,193},{65,1},{129,65},{193,129... | collective-permute-start | bytes 688136 | tf_op jit(solution)/shard_map/ppermute | solution.py:24
  83.2 5.6 %collective-permute-done.16 = bf16[128,896]{1,0:T(8,128)(2,1)S(1)} collective-permute-done((bf16[128,896]{1,0:T(8,128)(2,1)S(1)}, bf16[128,896]{1,0:T(8,128)(2,1)S(1)}, u32[]{:S(2)}, u32[]{:S(2)}) %collective-permute-start.16) | collective-permute-done | bytes 229408 | tf_op jit(solution)/shard_map/ppermute | solution.py:20
  88.9 8.1 %collective-permute-done.17 = bf16[128,896]{1,0:T(8,128)(2,1)S(1)} collective-permute-done((bf16[128,896]{1,0:T(8,128)(2,1)S(1)}, bf16[128,896]{1,0:T(8,128)(2,1)S(1)}, u32[]{:S(2)}, u32[]{:S(2)}) %collective-permute-start.17) | collective-permute-done | bytes 229408 | tf_op jit(solution)/shard_map/ppermute | solution.py:20
  97.1 3.0 %fusion.20 = bf16[64,2048]{1,0:T(8,128)(2,1)S(1)} fusion(bf16[896,2048]{1,0:T(8,128)(2,1)} %param.7, bf16[8,64,896]{2,1,0:T(8,128)(2,1)S(1)} %bitcast.132, s32[]{:T(128)S(6)} %select_n.246), kind=kOutput, calls=%fused_computation.49 | convolution fusion | flops 234881024 | bytes 4046852 | tf_op jit(solution)/shard_map/dot_general | solution.py:88
  100.1 3.8 %collective-permute-start.19 = (bf16[64,1024]{1,0:T(8,128)(2,1)S(1)}, bf16[64,1024]{1,0:T(8,128)(2,1)S(1)}, u32[]{:S(2)}, u32[]{:S(2)}) collective-permute-start(bf16[64,1024]{1,0:T(8,128)(2,1)S(1)} %slice.51), channel_id=1, source_target_pairs={{0,1},{1,2},{2,3},{3,4},{4,5},{5,6},{6,7},{7,0},{8,9},{9,10},{10,1... | collective-permute-start | bytes 393224 | tf_op jit(solution)/shard_map/ppermute | solution.py:42
  103.9 0.8 fusion.6
  104.8 1.6 %collective-permute-done.19 = bf16[64,1024]{1,0:T(8,128)(2,1)S(1)} collective-permute-done((bf16[64,1024]{1,0:T(8,128)(2,1)S(1)}, bf16[64,1024]{1,0:T(8,128)(2,1)S(1)}, u32[]{:S(2)}, u32[]{:S(2)}) %collective-permute-start.19) | collective-permute-done | bytes 131104 | tf_op jit(solution)/shard_map/ppermute | solution.py:42
  106.4 0.8 add_convert_fusion.5
  107.2 3.7 %collective-permute-start.20 = (bf16[64,2048]{1,0:T(8,128)(2,1)S(1)}, bf16[64,2048]{1,0:T(8,128)(2,1)S(1)}, u32[]{:S(2)}, u32[]{:S(2)}) collective-permute-start(bf16[64,2048]{1,0:T(8,128)(2,1)S(1)} %add_convert_fusion.5), channel_id=1, source_target_pairs={{0,1},{1,2},{2,3},{3,4},{4,5},{5,6},{6,7},{7,0},{8,9},{9,10},{10,1... | collective-permute-start | bytes 786440 | tf_op jit(solution)/shard_map/ppermute | solution.py:42
  110.9 0.8 add_convert_fusion.2
  111.7 0.3 collective-permute-start.24
  112.0 2.8 %collective-permute-done.20 = bf16[64,2048]{1,0:T(8,128)(2,1)S(1)} collective-permute-done((bf16[64,2048]{1,0:T(8,128)(2,1)S(1)}, bf16[64,2048]{1,0:T(8,128)(2,1)S(1)}, u32[]{:S(2)}, u32[]{:S(2)}) %collective-permute-start.20) | collective-permute-done | bytes 262176 | tf_op jit(solution)/shard_map/ppermute | solution.py:42
  114.8 0.8 add_convert_fusion.4
  115.6 3.8 %collective-permute-start.21 = (bf16[64,2048]{1,0:T(8,128)(2,1)S(1)}, bf16[64,2048]{1,0:T(8,128)(2,1)S(1)}, u32[]{:S(2)}, u32[]{:S(2)}) collective-permute-start(bf16[64,2048]{1,0:T(8,128)(2,1)S(1)} %add_convert_fusion.4), channel_id=1, source_target_pairs={{0,1},{1,2},{2,3},{3,4},{4,5},{5,6},{6,7},{7,0},{8,9},{9,10},{10,1... | collective-permute-start | bytes 786440 | tf_op jit(solution)/shard_map/ppermute | solution.py:42
  119.3 0.2 collective-permute-done.24
  119.6 0.8 add_convert_fusion.1
  120.4 3.0 %collective-permute-done.21 = bf16[64,2048]{1,0:T(8,128)(2,1)S(1)} collective-permute-done((bf16[64,2048]{1,0:T(8,128)(2,1)S(1)}, bf16[64,2048]{1,0:T(8,128)(2,1)S(1)}, u32[]{:S(2)}, u32[]{:S(2)}) %collective-permute-start.21) | collective-permute-done | bytes 262176 | tf_op jit(solution)/shard_map/ppermute | solution.py:42
  123.4 0.8 add_convert_fusion.3
  124.2 3.8 %collective-permute-start.22 = (bf16[64,2048]{1,0:T(8,128)(2,1)S(1)}, bf16[64,2048]{1,0:T(8,128)(2,1)S(1)}, u32[]{:S(2)}, u32[]{:S(2)}) collective-permute-start(bf16[64,2048]{1,0:T(8,128)(2,1)S(1)} %add_convert_fusion.3), channel_id=1, source_target_pairs={{0,1},{1,2},{2,3},{3,4},{4,5},{5,6},{6,7},{7,0},{8,9},{9,10},{10,1... | collective-permute-start | bytes 786440 | tf_op jit(solution)/shard_map/ppermute | solution.py:42
  128.0 0.5 collective-permute-done.25
  128.5 0.8 add_convert_fusion
  129.3 0.8 fusion.34
  130.1 1.8 %collective-permute-done.22 = bf16[64,2048]{1,0:T(8,128)(2,1)S(1)} collective-permute-done((bf16[64,2048]{1,0:T(8,128)(2,1)S(1)}, bf16[64,2048]{1,0:T(8,128)(2,1)S(1)}, u32[]{:S(2)}, u32[]{:S(2)}) %collective-permute-start.22) | collective-permute-done | bytes 262176 | tf_op jit(solution)/shard_map/ppermute | solution.py:42
  131.9 5.1 %collective-permute-done.26 = bf16[64,2048]{1,0:T(8,128)(2,1)S(1)} collective-permute-done((bf16[64,2048]{1,0:T(8,128)(2,1)S(1)}, bf16[64,2048]{1,0:T(8,128)(2,1)S(1)}, u32[]{:S(2)}, u32[]{:S(2)}) %collective-permute-start.26) | collective-permute-done | bytes 262176 | tf_op jit(solution)/shard_map/ppermute | solution.py:42
  137.0 2.6 %collective-permute-start.27 = (bf16[16,1024]{1,0:T(8,128)(2,1)S(1)}, bf16[16,1024]{1,0:T(8,128)(2,1)S(1)}, u32[]{:S(2)}, u32[]{:S(2)}) collective-permute-start(bf16[16,1024]{1,0:T(8,128)(2,1)S(1)} %slice.42), channel_id=1, source_target_pairs={{0,8},{8,16},{16,24},{24,0},{1,9},{9,17},{17,25},{25,1},{2,10},{10... | collective-permute-start | bytes 98312 | tf_op jit(solution)/shard_map/ppermute | solution.py:42
  139.7 1.6 %collective-permute-done.27 = bf16[16,1024]{1,0:T(8,128)(2,1)S(1)} collective-permute-done((bf16[16,1024]{1,0:T(8,128)(2,1)S(1)}, bf16[16,1024]{1,0:T(8,128)(2,1)S(1)}, u32[]{:S(2)}, u32[]{:S(2)}) %collective-permute-start.27) | collective-permute-done | bytes 32800 | tf_op jit(solution)/shard_map/ppermute | solution.py:42
  141.2 3.5 %collective-permute-done.29 = bf16[16,1024]{1,0:T(8,128)(2,1)S(1)} collective-permute-done((bf16[16,1024]{1,0:T(8,128)(2,1)S(1)}, bf16[16,1024]{1,0:T(8,128)(2,1)S(1)}, u32[]{:S(2)}, u32[]{:S(2)}) %collective-permute-start.29) | collective-permute-done | bytes 32800 | tf_op jit(solution)/shard_map/ppermute | solution.py:42
  144.9 2.0 %collective-permute-start.30 = (bf16[16,2048]{1,0:T(8,128)(2,1)S(1)}, bf16[16,2048]{1,0:T(8,128)(2,1)S(1)}, u32[]{:S(2)}, u32[]{:S(2)}) collective-permute-start(bf16[16,2048]{1,0:T(8,128)(2,1)S(1)} %get-tuple-element.12), channel_id=1, source_target_pairs={{0,24},{8,0},{16,8},{24,16},{1,25},{9,1},{17,9},{25,17},{2,26},{10... | collective-permute-start | bytes 196616 | tf_op jit(solution)/shard_map/ppermute | solution.py:42
  146.9 2.2 %collective-permute-done.28 = bf16[16,2048]{1,0:T(8,128)(2,1)S(1)} collective-permute-done((bf16[16,2048]{1,0:T(8,128)(2,1)S(1)}, bf16[16,2048]{1,0:T(8,128)(2,1)S(1)}, u32[]{:S(2)}, u32[]{:S(2)}) %collective-permute-start.28) | collective-permute-done | bytes 65568 | tf_op jit(solution)/shard_map/ppermute | solution.py:42
  149.1 1.3 collective-permute-done.30
  150.4 0.7 fusion.5
  (55 shorter events, 1.5 us)
Async XLA Ops:
  0.0 4.5 %collective-permute-start = (bf16[16,2048]{1,0:T(8,128)(2,1)}, bf16[16,2048]{1,0:T(8,128)(2,1)S(1)}, u32[]{:S(2)}, u32[]{:S(2)}) collective-permute-start(bf16[16,2048]{1,0:T(8,128)(2,1)} %param.4), channel_id=1, source_target_pairs={{0,8},{8,16},{16,24},{24,0},{1,9},{9,17},{17,25},{25,1},{2,10},{10... | collective-permute-start | bytes 196616 | tf_op jit(solution)/shard_map/ppermute | solution.py:20
  0.2 8.5 %collective-permute-start.2 = (bf16[16,2048]{1,0:T(8,128)(2,1)}, bf16[16,2048]{1,0:T(8,128)(2,1)S(1)}, u32[]{:S(2)}, u32[]{:S(2)}) collective-permute-start(bf16[16,2048]{1,0:T(8,128)(2,1)} %param.4), channel_id=1, source_target_pairs={{0,24},{8,0},{16,8},{24,16},{1,25},{9,1},{17,9},{25,17},{2,26},{10... | collective-permute-start | bytes 196616 | tf_op jit(solution)/shard_map/ppermute | solution.py:24
  4.5 4.3 %collective-permute-start.1 = (bf16[16,2048]{1,0:T(8,128)(2,1)S(1)}, bf16[16,2048]{1,0:T(8,128)(2,1)S(1)}, u32[]{:S(2)}, u32[]{:S(2)}) collective-permute-start(bf16[16,2048]{1,0:T(8,128)(2,1)S(1)} %collective-permute-done), channel_id=1, source_target_pairs={{0,8},{8,16},{16,24},{24,0},{1,9},{9,17},{17,25},{25,1},{2,10},{10... | collective-permute-start | bytes 196616 | tf_op jit(solution)/shard_map/ppermute | solution.py:20
  8.8 7.1 %collective-permute-start.3 = (bf16[64,2048]{1,0:T(8,128)(2,1)S(1)}, bf16[64,2048]{1,0:T(8,128)(2,1)S(1)}, u32[]{:S(2)}, u32[]{:S(2)}) collective-permute-start(bf16[64,2048]{1,0:T(8,128)(2,1)S(1)} %bitcast.146), channel_id=1, source_target_pairs={{0,1},{1,2},{2,3},{3,4},{4,5},{5,6},{6,7},{7,0},{8,9},{9,10},{10,1... | collective-permute-start | bytes 786440 | tf_op jit(solution)/shard_map/ppermute | solution.py:20
  12.0 7.6 %collective-permute-start.7 = (bf16[64,2048]{1,0:T(8,128)(2,1)S(1)}, bf16[64,2048]{1,0:T(8,128)(2,1)S(1)}, u32[]{:S(2)}, u32[]{:S(2)}) collective-permute-start(bf16[64,2048]{1,0:T(8,128)(2,1)S(1)} %bitcast.147), channel_id=1, source_target_pairs={{0,7},{1,0},{2,1},{3,2},{4,3},{5,4},{6,5},{7,6},{8,15},{9,8},{10,9... | collective-permute-start | bytes 786440 | tf_op jit(solution)/shard_map/ppermute | solution.py:24
  12.2 29.5 %copy-start.2 = (bf16[2048,896]{1,0:T(8,128)(2,1)S(1)}, bf16[2048,896]{1,0:T(8,128)(2,1)}, u32[]{:S(2)}) copy-start(bf16[2048,896]{1,0:T(8,128)(2,1)} %param.5) | copy-start | bytes 11010052
  15.9 8.5 %collective-permute-start.4 = (bf16[64,2048]{1,0:T(8,128)(2,1)S(1)}, bf16[64,2048]{1,0:T(8,128)(2,1)S(1)}, u32[]{:S(2)}, u32[]{:S(2)}) collective-permute-start(bf16[64,2048]{1,0:T(8,128)(2,1)S(1)} %collective-permute-done.3), channel_id=1, source_target_pairs={{0,1},{1,2},{2,3},{3,4},{4,5},{5,6},{6,7},{7,0},{8,9},{9,10},{10,1... | collective-permute-start | bytes 786440 | tf_op jit(solution)/shard_map/ppermute | solution.py:20
  19.6 8.7 %collective-permute-start.8 = (bf16[64,2048]{1,0:T(8,128)(2,1)S(1)}, bf16[64,2048]{1,0:T(8,128)(2,1)S(1)}, u32[]{:S(2)}, u32[]{:S(2)}) collective-permute-start(bf16[64,2048]{1,0:T(8,128)(2,1)S(1)} %collective-permute-done.7), channel_id=1, source_target_pairs={{0,7},{1,0},{2,1},{3,2},{4,3},{5,4},{6,5},{7,6},{8,15},{9,8},{10,9... | collective-permute-start | bytes 786440 | tf_op jit(solution)/shard_map/ppermute | solution.py:24
  24.4 9.7 %collective-permute-start.5 = (bf16[64,2048]{1,0:T(8,128)(2,1)S(1)}, bf16[64,2048]{1,0:T(8,128)(2,1)S(1)}, u32[]{:S(2)}, u32[]{:S(2)}) collective-permute-start(bf16[64,2048]{1,0:T(8,128)(2,1)S(1)} %collective-permute-done.4), channel_id=1, source_target_pairs={{0,1},{1,2},{2,3},{3,4},{4,5},{5,6},{6,7},{7,0},{8,9},{9,10},{10,1... | collective-permute-start | bytes 786440 | tf_op jit(solution)/shard_map/ppermute | solution.py:20
  28.3 13.4 %collective-permute-start.9 = (bf16[64,2048]{1,0:T(8,128)(2,1)S(1)}, bf16[64,2048]{1,0:T(8,128)(2,1)S(1)}, u32[]{:S(2)}, u32[]{:S(2)}) collective-permute-start(bf16[64,2048]{1,0:T(8,128)(2,1)S(1)} %collective-permute-done.8), channel_id=1, source_target_pairs={{0,7},{1,0},{2,1},{3,2},{4,3},{5,4},{6,5},{7,6},{8,15},{9,8},{10,9... | collective-permute-start | bytes 786440 | tf_op jit(solution)/shard_map/ppermute | solution.py:24
  34.0 7.6 %collective-permute-start.6 = (bf16[64,2048]{1,0:T(8,128)(2,1)S(1)}, bf16[64,2048]{1,0:T(8,128)(2,1)S(1)}, u32[]{:S(2)}, u32[]{:S(2)}) collective-permute-start(bf16[64,2048]{1,0:T(8,128)(2,1)S(1)} %collective-permute-done.5), channel_id=1, source_target_pairs={{0,1},{1,2},{2,3},{3,4},{4,5},{5,6},{6,7},{7,0},{8,9},{9,10},{10,1... | collective-permute-start | bytes 786440 | tf_op jit(solution)/shard_map/ppermute | solution.py:20
  41.7 2.3 %copy-start.3 = (bf16[2048,896]{1,0:T(8,128)(2,1)S(1)}, bf16[2048,896]{1,0:T(8,128)(2,1)}, u32[]{:S(2)}) copy-start(bf16[2048,896]{1,0:T(8,128)(2,1)} %param.6) | copy-start | bytes 11010052
  46.7 1.8 %copy-start.1 = (f32[512,1792]{1,0:T(8,128)}, f32[512,1792]{1,0:T(8,128)S(1)}, u32[]{:S(2)}) copy-start(f32[512,1792]{1,0:T(8,128)S(1)} %pad_maximum_fusion) | copy-start | bytes 11010052
  48.6 4.2 %collective-permute-start.10 = (f32[4,64,1792]{2,1,0:T(8,128)S(1)}, f32[4,64,1792]{2,1,0:T(8,128)}, u32[]{:S(2)}, u32[]{:S(2)}) collective-permute-start(f32[4,64,1792]{2,1,0:T(8,128)S(1)} %dynamic-slice_bitcast_fusion), channel_id=1, source_target_pairs={{0,32},{32,0},{1,33},{33,1},{2,34},{34,2},{3,35},{35,3},{4,36},{36... | collective-permute-start | bytes 5505032 | tf_op jit(solution)/shard_map/ppermute | solution.py:69
  55.1 8.9 %collective-permute-start.11 = (f32[64,896]{1,0:T(8,128)S(1)}, f32[64,896]{1,0:T(8,128)S(1)}, u32[]{:S(2)}, u32[]{:S(2)}) collective-permute-start(f32[64,896]{1,0:T(8,128)S(1)} %slice.36), channel_id=1, source_target_pairs={{0,64},{64,128},{128,192},{192,0},{1,65},{65,129},{129,193},{193,1... | collective-permute-start | bytes 688136 | tf_op jit(solution)/shard_map/ppermute | solution.py:42
  56.7 7.4 %collective-permute-start.13 = (f32[64,896]{1,0:T(8,128)S(1)}, f32[64,896]{1,0:T(8,128)S(1)}, u32[]{:S(2)}, u32[]{:S(2)}) collective-permute-start(f32[64,896]{1,0:T(8,128)S(1)} %slice.37), channel_id=1, source_target_pairs={{0,192},{64,0},{128,64},{192,128},{1,193},{65,1},{129,65},{193,129... | collective-permute-start | bytes 688136 | tf_op jit(solution)/shard_map/ppermute | solution.py:42
  64.2 12.9 %collective-permute-start.12 = (f32[64,1792]{1,0:T(8,128)S(1)}, f32[64,1792]{1,0:T(8,128)S(1)}, u32[]{:S(2)}, u32[]{:S(2)}) collective-permute-start(f32[64,1792]{1,0:T(8,128)S(1)} %get-tuple-element.7), channel_id=1, source_target_pairs={{0,64},{64,128},{128,192},{192,0},{1,65},{65,129},{129,193},{193,1... | collective-permute-start | bytes 1376264 | tf_op jit(solution)/shard_map/ppermute | solution.py:42
  65.8 11.4 %collective-permute-start.14 = (f32[64,1792]{1,0:T(8,128)S(1)}, f32[64,1792]{1,0:T(8,128)}, u32[]{:S(2)}, u32[]{:S(2)}) collective-permute-start(f32[64,1792]{1,0:T(8,128)S(1)} %get-tuple-element.8), channel_id=1, source_target_pairs={{0,192},{64,0},{128,64},{192,128},{1,193},{65,1},{129,65},{193,129... | collective-permute-start | bytes 1376264 | tf_op jit(solution)/shard_map/ppermute | solution.py:42
  78.4 1.4 collective-permute-start.15
  79.8 9.1 %collective-permute-start.16 = (bf16[128,896]{1,0:T(8,128)(2,1)S(1)}, bf16[128,896]{1,0:T(8,128)(2,1)S(1)}, u32[]{:S(2)}, u32[]{:S(2)}) collective-permute-start(bf16[128,896]{1,0:T(8,128)(2,1)S(1)} %bitcast.149), channel_id=1, source_target_pairs={{0,64},{64,128},{128,192},{192,0},{1,65},{65,129},{129,193},{193,1... | collective-permute-start | bytes 688136 | tf_op jit(solution)/shard_map/ppermute | solution.py:20
  81.0 16.1 %collective-permute-start.18 = (bf16[128,896]{1,0:T(8,128)(2,1)S(1)}, bf16[128,896]{1,0:T(8,128)(2,1)S(1)}, u32[]{:S(2)}, u32[]{:S(2)}) collective-permute-start(bf16[128,896]{1,0:T(8,128)(2,1)S(1)} %bitcast.150), channel_id=1, source_target_pairs={{0,192},{64,0},{128,64},{192,128},{1,193},{65,1},{129,65},{193,129... | collective-permute-start | bytes 688136 | tf_op jit(solution)/shard_map/ppermute | solution.py:24
  88.9 8.2 %collective-permute-start.17 = (bf16[128,896]{1,0:T(8,128)(2,1)S(1)}, bf16[128,896]{1,0:T(8,128)(2,1)S(1)}, u32[]{:S(2)}, u32[]{:S(2)}) collective-permute-start(bf16[128,896]{1,0:T(8,128)(2,1)S(1)} %collective-permute-done.16), channel_id=1, source_target_pairs={{0,64},{64,128},{128,192},{192,0},{1,65},{65,129},{129,193},{193,1... | collective-permute-start | bytes 688136 | tf_op jit(solution)/shard_map/ppermute | solution.py:20
  97.1 6.8 %copy-start = (bf16[896,2048]{1,0:T(8,128)(2,1)S(1)}, bf16[896,2048]{1,0:T(8,128)(2,1)}, u32[]{:S(2)}) copy-start(bf16[896,2048]{1,0:T(8,128)(2,1)} %param.7) | copy-start | bytes 11010052
  100.1 6.3 %collective-permute-start.19 = (bf16[64,1024]{1,0:T(8,128)(2,1)S(1)}, bf16[64,1024]{1,0:T(8,128)(2,1)S(1)}, u32[]{:S(2)}, u32[]{:S(2)}) collective-permute-start(bf16[64,1024]{1,0:T(8,128)(2,1)S(1)} %slice.51), channel_id=1, source_target_pairs={{0,1},{1,2},{2,3},{3,4},{4,5},{5,6},{6,7},{7,0},{8,9},{9,10},{10,1... | collective-permute-start | bytes 393224 | tf_op jit(solution)/shard_map/ppermute | solution.py:42
  104.7 6.3 %collective-permute-start.23 = (bf16[64,1024]{1,0:T(8,128)(2,1)S(1)}, bf16[64,1024]{1,0:T(8,128)(2,1)S(1)}, u32[]{:S(2)}, u32[]{:S(2)}) collective-permute-start(bf16[64,1024]{1,0:T(8,128)(2,1)S(1)} %slice.50), channel_id=1, source_target_pairs={{0,7},{1,0},{2,1},{3,2},{4,3},{5,4},{6,5},{7,6},{8,15},{9,8},{10,9... | collective-permute-start | bytes 393224 | tf_op jit(solution)/shard_map/ppermute | solution.py:42
  107.2 7.6 %collective-permute-start.20 = (bf16[64,2048]{1,0:T(8,128)(2,1)S(1)}, bf16[64,2048]{1,0:T(8,128)(2,1)S(1)}, u32[]{:S(2)}, u32[]{:S(2)}) collective-permute-start(bf16[64,2048]{1,0:T(8,128)(2,1)S(1)} %add_convert_fusion.5), channel_id=1, source_target_pairs={{0,1},{1,2},{2,3},{3,4},{4,5},{5,6},{6,7},{7,0},{8,9},{9,10},{10,1... | collective-permute-start | bytes 786440 | tf_op jit(solution)/shard_map/ppermute | solution.py:42
  111.7 7.9 %collective-permute-start.24 = (bf16[64,2048]{1,0:T(8,128)(2,1)S(1)}, bf16[64,2048]{1,0:T(8,128)(2,1)S(1)}, u32[]{:S(2)}, u32[]{:S(2)}) collective-permute-start(bf16[64,2048]{1,0:T(8,128)(2,1)S(1)} %add_convert_fusion.2), channel_id=1, source_target_pairs={{0,7},{1,0},{2,1},{3,2},{4,3},{5,4},{6,5},{7,6},{8,15},{9,8},{10,9... | collective-permute-start | bytes 786440 | tf_op jit(solution)/shard_map/ppermute | solution.py:42
  115.6 7.9 %collective-permute-start.21 = (bf16[64,2048]{1,0:T(8,128)(2,1)S(1)}, bf16[64,2048]{1,0:T(8,128)(2,1)S(1)}, u32[]{:S(2)}, u32[]{:S(2)}) collective-permute-start(bf16[64,2048]{1,0:T(8,128)(2,1)S(1)} %add_convert_fusion.4), channel_id=1, source_target_pairs={{0,1},{1,2},{2,3},{3,4},{4,5},{5,6},{6,7},{7,0},{8,9},{9,10},{10,1... | collective-permute-start | bytes 786440 | tf_op jit(solution)/shard_map/ppermute | solution.py:42
  120.3 8.1 %collective-permute-start.25 = (bf16[64,2048]{1,0:T(8,128)(2,1)S(1)}, bf16[64,2048]{1,0:T(8,128)(2,1)S(1)}, u32[]{:S(2)}, u32[]{:S(2)}) collective-permute-start(bf16[64,2048]{1,0:T(8,128)(2,1)S(1)} %add_convert_fusion.1), channel_id=1, source_target_pairs={{0,7},{1,0},{2,1},{3,2},{4,3},{5,4},{6,5},{7,6},{8,15},{9,8},{10,9... | collective-permute-start | bytes 786440 | tf_op jit(solution)/shard_map/ppermute | solution.py:42
  124.2 7.7 %collective-permute-start.22 = (bf16[64,2048]{1,0:T(8,128)(2,1)S(1)}, bf16[64,2048]{1,0:T(8,128)(2,1)S(1)}, u32[]{:S(2)}, u32[]{:S(2)}) collective-permute-start(bf16[64,2048]{1,0:T(8,128)(2,1)S(1)} %add_convert_fusion.3), channel_id=1, source_target_pairs={{0,1},{1,2},{2,3},{3,4},{4,5},{5,6},{6,7},{7,0},{8,9},{9,10},{10,1... | collective-permute-start | bytes 786440 | tf_op jit(solution)/shard_map/ppermute | solution.py:42
  129.2 7.7 %collective-permute-start.26 = (bf16[64,2048]{1,0:T(8,128)(2,1)S(1)}, bf16[64,2048]{1,0:T(8,128)(2,1)S(1)}, u32[]{:S(2)}, u32[]{:S(2)}) collective-permute-start(bf16[64,2048]{1,0:T(8,128)(2,1)S(1)} %add_convert_fusion), channel_id=1, source_target_pairs={{0,7},{1,0},{2,1},{3,2},{4,3},{5,4},{6,5},{7,6},{8,15},{9,8},{10,9... | collective-permute-start | bytes 786440 | tf_op jit(solution)/shard_map/ppermute | solution.py:42
  137.0 4.2 %collective-permute-start.27 = (bf16[16,1024]{1,0:T(8,128)(2,1)S(1)}, bf16[16,1024]{1,0:T(8,128)(2,1)S(1)}, u32[]{:S(2)}, u32[]{:S(2)}) collective-permute-start(bf16[16,1024]{1,0:T(8,128)(2,1)S(1)} %slice.42), channel_id=1, source_target_pairs={{0,8},{8,16},{16,24},{24,0},{1,9},{9,17},{17,25},{25,1},{2,10},{10... | collective-permute-start | bytes 98312 | tf_op jit(solution)/shard_map/ppermute | solution.py:42
  139.6 5.1 %collective-permute-start.29 = (bf16[16,1024]{1,0:T(8,128)(2,1)S(1)}, bf16[16,1024]{1,0:T(8,128)(2,1)S(1)}, u32[]{:S(2)}, u32[]{:S(2)}) collective-permute-start(bf16[16,1024]{1,0:T(8,128)(2,1)S(1)} %slice.43), channel_id=1, source_target_pairs={{0,24},{8,0},{16,8},{24,16},{1,25},{9,1},{17,9},{25,17},{2,26},{10... | collective-permute-start | bytes 98312 | tf_op jit(solution)/shard_map/ppermute | solution.py:42
  144.8 4.3 %collective-permute-start.28 = (bf16[16,2048]{1,0:T(8,128)(2,1)S(1)}, bf16[16,2048]{1,0:T(8,128)(2,1)S(1)}, u32[]{:S(2)}, u32[]{:S(2)}) collective-permute-start(bf16[16,2048]{1,0:T(8,128)(2,1)S(1)} %get-tuple-element.11), channel_id=1, source_target_pairs={{0,8},{8,16},{16,24},{24,0},{1,9},{9,17},{17,25},{25,1},{2,10},{10... | collective-permute-start | bytes 196616 | tf_op jit(solution)/shard_map/ppermute | solution.py:42
  144.9 5.6 %collective-permute-start.30 = (bf16[16,2048]{1,0:T(8,128)(2,1)S(1)}, bf16[16,2048]{1,0:T(8,128)(2,1)S(1)}, u32[]{:S(2)}, u32[]{:S(2)}) collective-permute-start(bf16[16,2048]{1,0:T(8,128)(2,1)S(1)} %get-tuple-element.12), channel_id=1, source_target_pairs={{0,24},{8,0},{16,8},{24,16},{1,25},{9,1},{17,9},{25,17},{2,26},{10... | collective-permute-start | bytes 196616 | tf_op jit(solution)/shard_map/ppermute | solution.py:42

commit v14 on v12

--- a/solution.py
+++ b/solution.py
@@ -64,13 +64,12 @@
     ncore = lax.psum(1, "ec")
     nx = lax.psum(1, "ex")
     xs = x.reshape((nx, ncore, x.shape[0] // (nx * ncore)) + x.shape[1:])
-    mine = lax.dynamic_index_in_dim(xs, ec, 1, keepdims=False)
     other = lax.dynamic_index_in_dim(xs, 1 - ec, 1, keepdims=False)
     got = lax.ppermute(other, "ec", [(0, 1), (1, 0)])
-    y = mine + got
-    return ring_rs_bal(
-        lambda i: lax.dynamic_index_in_dim(y, i, 0, keepdims=False), "ex", nx, jnp.float32
-    )
+    piece = lambda i: lax.dynamic_index_in_dim(
+        lax.dynamic_index_in_dim(xs, i, 0, keepdims=False), ec, 0, keepdims=False
+    ) + lax.dynamic_index_in_dim(got, i, 0, keepdims=False)
+    return ring_rs_bal(piece, "ex", nx, jnp.float32)
 
 
 def on_device(rows_in, gate_weight, up_weight, down_weight):

time: 145 us -> 146 us (level)
  local copies, waits for them, and re-layouts: 3.79 us -> 6.26 us
  matrix products: 22.3 us -> 20.2 us
  blocking collectives: 14.4 us -> 16.4 us
  waiting for transfers between devices: 56.6 us -> 54.7 us
    add x1 -> x2, other arithmetic: 2.24 us -> 0.05 us  [embed_rs(): lax.dynamic_index_in_dim(lax.dynamic_index_in_dim(xs, i, 0, keepdims=Fals...]
    dot_general x9, matrix products: 8.91 us -> 6.87 us  [on_device(): jnp.dot(lax.dynamic_index_in_dim(act_blocks, i, 0, keepdims=False), down_...]
    all_gather x1, blocking collectives: 14.4 us -> 16.4 us  [on_device(): activated = lax.all_gather(activated, EMBED, axis=0, tiled=True)]
  transfers between devices with their start and end apart: 27 -> 27, of which waited for: 20 -> 19; matrix products, arithmetic and copies ran while one was open for 13% -> 14% of each run, Pallas kernels for 0% -> 0%
where the time goes in v14:
time: 146 us; the launch traced here: 144 us
  waiting for transfers between devices  54.7 us (37%)
  starting transfers between devices  42.7 us (29%)
  matrix products  20.2 us (14%)
  blocking collectives  16.4 us (11%)
  local copies, waits for them, and re-layouts  6.26 us (4%)
  other arithmetic  3.68 us (3%)
    ppermute x16, waiting for transfers between devices, side(): got = lax.ppermute(acc.astype(send_dtype), axis, perm).astype(jnp.float32)  35.6 us
    ppermute x16, starting transfers between devices, side(): got = lax.ppermute(acc.astype(send_dtype), axis, perm).astype(jnp.float32)  25.6 us
    all_gather x1, blocking collectives, on_device(): activated = lax.all_gather(activated, EMBED, axis=0, tiled=True)  16.4 us
    ppermute x6, waiting for transfers between devices, ring_ag(): buf = lax.ppermute(buf, axis, fwd)  15.3 us
    ppermute x4, starting transfers between devices, ring_ag(): buf = lax.ppermute(buf, axis, bwd)  12.9 us
    dot_general x8, matrix products, on_device(): jnp.dot(v, gate_weight, preferred_element_type=jnp.float32)  7.67 us
    dot_general x9, matrix products, on_device(): jnp.dot(lax.dynamic_index_in_dim(act_blocks, i, 0, keepdims=False), down_...  6.87 us
    dot_general x8, matrix products, on_device(): jnp.dot(v, up_weight, preferred_element_type=jnp.float32)  5.67 us
  transfers between devices with their start and end apart: 27, of which 19 were waited for; matrix products, arithmetic and copies ran while one was open for 14% of the time, Pallas kernels for 0%

profile of v14, /device:TPU:2, one launch (start us, length us, event | category | flops | bytes accessed | tf_op | source)
XLA Modules:
  0.0 144.4 jit_solution(5009697233026574689)
XLA Ops:
  0.0 1.6 %collective-permute-start = (bf16[16,2048]{1,0:T(8,128)(2,1)}, bf16[16,2048]{1,0:T(8,128)(2,1)S(1)}, u32[]{:S(2)}, u32[]{:S(2)}) collective-permute-start(bf16[16,2048]{1,0:T(8,128)(2,1)} %param.4), channel_id=1, source_target_pairs={{0,8},{8,16},{16,24},{24,0},{1,9},{9,17},{17,25},{25,1},{2,10},{10... | collective-permute-start | bytes 196616 | tf_op jit(solution)/shard_map/ppermute | solution.py:20
  1.6 1.7 %collective-permute-start.2 = (bf16[16,2048]{1,0:T(8,128)(2,1)}, bf16[16,2048]{1,0:T(8,128)(2,1)S(1)}, u32[]{:S(2)}, u32[]{:S(2)}) collective-permute-start(bf16[16,2048]{1,0:T(8,128)(2,1)} %param.4), channel_id=1, source_target_pairs={{0,24},{8,0},{16,8},{24,16},{1,25},{9,1},{17,9},{25,17},{2,26},{10... | collective-permute-start | bytes 196616 | tf_op jit(solution)/shard_map/ppermute | solution.py:24
  3.3 0.9 bitcast_dynamic-update-slice_fusion.3
  4.1 1.6 %collective-permute-done = bf16[16,2048]{1,0:T(8,128)(2,1)S(1)} collective-permute-done((bf16[16,2048]{1,0:T(8,128)(2,1)}, bf16[16,2048]{1,0:T(8,128)(2,1)S(1)}, u32[]{:S(2)}, u32[]{:S(2)}) %collective-permute-start) | collective-permute-done | bytes 65568 | tf_op jit(solution)/shard_map/ppermute | solution.py:20
  6.1 5.1 %collective-permute-done.1 = bf16[16,2048]{1,0:T(8,128)(2,1)S(1)} collective-permute-done((bf16[16,2048]{1,0:T(8,128)(2,1)S(1)}, bf16[16,2048]{1,0:T(8,128)(2,1)S(1)}, u32[]{:S(2)}, u32[]{:S(2)}) %collective-permute-start.1) | collective-permute-done | bytes 65568 | tf_op jit(solution)/shard_map/ppermute | solution.py:20
  11.2 2.0 %collective-permute-start.3 = (bf16[64,2048]{1,0:T(8,128)(2,1)S(1)}, bf16[64,2048]{1,0:T(8,128)(2,1)S(1)}, u32[]{:S(2)}, u32[]{:S(2)}) collective-permute-start(bf16[64,2048]{1,0:T(8,128)(2,1)S(1)} %bitcast.185), channel_id=1, source_target_pairs={{0,1},{1,2},{2,3},{3,4},{4,5},{5,6},{6,7},{7,0},{8,9},{9,10},{10,1... | collective-permute-start | bytes 786440 | tf_op jit(solution)/shard_map/ppermute | solution.py:20
  13.2 4.0 %collective-permute-start.7 = (bf16[64,2048]{1,0:T(8,128)(2,1)S(1)}, bf16[64,2048]{1,0:T(8,128)(2,1)S(1)}, u32[]{:S(2)}, u32[]{:S(2)}) collective-permute-start(bf16[64,2048]{1,0:T(8,128)(2,1)S(1)} %bitcast.186), channel_id=1, source_target_pairs={{0,7},{1,0},{2,1},{3,2},{4,3},{5,4},{6,5},{7,6},{8,15},{9,8},{10,9... | collective-permute-start | bytes 786440 | tf_op jit(solution)/shard_map/ppermute | solution.py:24
  17.2 2.7 %fusion.67 = f32[64,896]{1,0:T(8,128)S(1)} fusion(bf16[64,2048]{1,0:T(8,128)(2,1)S(1)} %bitcast.187, bf16[2048,896]{1,0:T(8,128)(2,1)} %param.5), kind=kOutput, calls=%fused_computation.92 | convolution fusion | flops 234881024 | bytes 4161536 | tf_op jit(solution)/shard_map/dot_general | solution.py:85
  20.0 0.7 fusion.68
  22.0 0.7 fusion.69
  22.8 0.7 fusion.70
  23.5 0.7 fusion.77
  24.2 0.7 fusion.78
  24.9 3.3 %collective-permute-start.8 = (bf16[64,2048]{1,0:T(8,128)(2,1)S(1)}, bf16[64,2048]{1,0:T(8,128)(2,1)S(1)}, u32[]{:S(2)}, u32[]{:S(2)}) collective-permute-start(bf16[64,2048]{1,0:T(8,128)(2,1)S(1)} %collective-permute-done.7), channel_id=1, source_target_pairs={{0,7},{1,0},{2,1},{3,2},{4,3},{5,4},{6,5},{7,6},{8,15},{9,8},{10,9... | collective-permute-start | bytes 786440 | tf_op jit(solution)/shard_map/ppermute | solution.py:24
  28.3 2.1 %collective-permute-done.4 = bf16[64,2048]{1,0:T(8,128)(2,1)S(1)} collective-permute-done((bf16[64,2048]{1,0:T(8,128)(2,1)S(1)}, bf16[64,2048]{1,0:T(8,128)(2,1)S(1)}, u32[]{:S(2)}, u32[]{:S(2)}) %collective-permute-start.4) | collective-permute-done | bytes 262176 | tf_op jit(solution)/shard_map/ppermute | solution.py:20
  30.4 0.7 fusion.71
  31.2 0.7 fusion.72
  32.1 0.7 fusion.79
  32.8 0.7 fusion.80
  33.6 3.9 %collective-permute-start.9 = (bf16[64,2048]{1,0:T(8,128)(2,1)S(1)}, bf16[64,2048]{1,0:T(8,128)(2,1)S(1)}, u32[]{:S(2)}, u32[]{:S(2)}) collective-permute-start(bf16[64,2048]{1,0:T(8,128)(2,1)S(1)} %collective-permute-done.8), channel_id=1, source_target_pairs={{0,7},{1,0},{2,1},{3,2},{4,3},{5,4},{6,5},{7,6},{8,15},{9,8},{10,9... | collective-permute-start | bytes 786440 | tf_op jit(solution)/shard_map/ppermute | solution.py:24
  37.5 1.5 %collective-permute-done.5 = bf16[64,2048]{1,0:T(8,128)(2,1)S(1)} collective-permute-done((bf16[64,2048]{1,0:T(8,128)(2,1)S(1)}, bf16[64,2048]{1,0:T(8,128)(2,1)S(1)}, u32[]{:S(2)}, u32[]{:S(2)}) %collective-permute-start.5) | collective-permute-done | bytes 262176 | tf_op jit(solution)/shard_map/ppermute | solution.py:20
  39.1 0.7 fusion.73
  39.9 0.7 fusion.74
  40.6 0.8 collective-permute-done.9
  41.4 0.7 fusion.81
  42.1 0.7 fusion.82
  42.9 4.6 %collective-permute-done.6 = bf16[64,2048]{1,0:T(8,128)(2,1)S(1)} collective-permute-done((bf16[64,2048]{1,0:T(8,128)(2,1)S(1)}, bf16[64,2048]{1,0:T(8,128)(2,1)S(1)}, u32[]{:S(2)}, u32[]{:S(2)}) %collective-permute-start.6) | collective-permute-done | bytes 262176 | tf_op jit(solution)/shard_map/ppermute | solution.py:20
  47.4 0.7 fusion.75
  48.2 0.7 fusion.76
  49.0 1.8 %copy-done.3 = f32[8,64,1792]{2,1,0:T(8,128)} copy-done((f32[8,64,1792]{2,1,0:T(8,128)}, f32[8,64,1792]{2,1,0:T(8,128)S(1)}, u32[]{:S(2)}) %copy-start.3) | copy-done | bytes 3670040
  50.8 1.4 dynamic-slice_bitcast_fusion
  52.2 1.2 dynamic-slice_bitcast_fusion.4
  53.5 2.8 %collective-permute-done.10 = f32[4,64,1792]{2,1,0:T(8,128)S(1)} collective-permute-done((f32[4,64,1792]{2,1,0:T(8,128)}, f32[4,64,1792]{2,1,0:T(8,128)S(1)}, u32[]{:S(2)}, u32[]{:S(2)}) %collective-permute-start.10) | collective-permute-done | bytes 1835040 | tf_op jit(solution)/shard_map/ppermute | solution.py:68
  56.3 0.6 collective-permute-start.13
  57.0 1.6 %collective-permute-start.11 = (f32[64,896]{1,0:T(8,128)S(1)}, f32[64,896]{1,0:T(8,128)S(1)}, u32[]{:S(2)}, u32[]{:S(2)}) collective-permute-start(f32[64,896]{1,0:T(8,128)S(1)} %slice_add_fusion.1), channel_id=1, source_target_pairs={{0,64},{64,128},{128,192},{192,0},{1,65},{65,129},{129,193},{193,1... | collective-permute-start | bytes 688136 | tf_op jit(solution)/shard_map/ppermute | solution.py:42
  58.5 5.5 %collective-permute-done.13 = f32[64,896]{1,0:T(8,128)S(1)} collective-permute-done((f32[64,896]{1,0:T(8,128)S(1)}, f32[64,896]{1,0:T(8,128)S(1)}, u32[]{:S(2)}, u32[]{:S(2)}) %collective-permute-start.13) | collective-permute-done | bytes 229408 | tf_op jit(solution)/shard_map/ppermute | solution.py:42
  64.1 1.4 collective-permute-done.11
  65.5 1.3 fusion.9
  67.3 2.6 %collective-permute-start.14 = (f32[64,1792]{1,0:T(8,128)S(1)}, f32[64,1792]{1,0:T(8,128)}, u32[]{:S(2)}, u32[]{:S(2)}) collective-permute-start(f32[64,1792]{1,0:T(8,128)S(1)} %get-tuple-element.6), channel_id=1, source_target_pairs={{0,192},{64,0},{128,64},{192,128},{1,193},{65,1},{129,65},{193,129... | collective-permute-start | bytes 1376264 | tf_op jit(solution)/shard_map/ppermute | solution.py:42
  69.8 9.6 %collective-permute-done.12 = f32[64,1792]{1,0:T(8,128)S(1)} collective-permute-done((f32[64,1792]{1,0:T(8,128)S(1)}, f32[64,1792]{1,0:T(8,128)S(1)}, u32[]{:S(2)}, u32[]{:S(2)}) %collective-permute-start.12) | collective-permute-done | bytes 458784 | tf_op jit(solution)/shard_map/ppermute | solution.py:42
  79.4 1.2 fusion.11
  80.8 16.4 %all_gather.3 = bf16[512,896]{1,0:T(8,128)(2,1)S(1)} all-gather(bf16[64,896]{1,0:T(8,128)(2,1)S(1)} %fusion.12), channel_id=1, replica_groups=mesh['ex'=4,'ec'=2,'hy'=4,'hz'=8] {'ex','ec'}, dimensions={0}, use_global_device_ids=true | all-gather | bytes 1032192 | tf_op jit(solution)/shard_map/all_gather | solution.py:93
  97.2 0.8 fusion.27
  98.0 0.8 fusion.17
  98.8 3.5 %collective-permute-start.19 = (bf16[64,1024]{1,0:T(8,128)(2,1)S(1)}, bf16[64,1024]{1,0:T(8,128)(2,1)S(1)}, u32[]{:S(2)}, u32[]{:S(2)}) collective-permute-start(bf16[64,1024]{1,0:T(8,128)(2,1)S(1)} %slice.56), channel_id=1, source_target_pairs={{0,7},{1,0},{2,1},{3,2},{4,3},{5,4},{6,5},{7,6},{8,15},{9,8},{10,9... | collective-permute-start | bytes 393224 | tf_op jit(solution)/shard_map/ppermute | solution.py:42
  102.3 2.6 %collective-permute-done.15 = bf16[64,1024]{1,0:T(8,128)(2,1)S(1)} collective-permute-done((bf16[64,1024]{1,0:T(8,128)(2,1)S(1)}, bf16[64,1024]{1,0:T(8,128)(2,1)S(1)}, u32[]{:S(2)}, u32[]{:S(2)}) %collective-permute-start.15) | collective-permute-done | bytes 131104 | tf_op jit(solution)/shard_map/ppermute | solution.py:42
  105.0 0.8 add_convert_fusion.5
  105.9 0.8 add_convert_fusion.2
  106.6 3.3 %collective-permute-start.20 = (bf16[64,2048]{1,0:T(8,128)(2,1)S(1)}, bf16[64,2048]{1,0:T(8,128)(2,1)S(1)}, u32[]{:S(2)}, u32[]{:S(2)}) collective-permute-start(bf16[64,2048]{1,0:T(8,128)(2,1)S(1)} %add_convert_fusion.2), channel_id=1, source_target_pairs={{0,7},{1,0},{2,1},{3,2},{4,3},{5,4},{6,5},{7,6},{8,15},{9,8},{10,9... | collective-permute-start | bytes 786440 | tf_op jit(solution)/shard_map/ppermute | solution.py:42
  109.9 4.9 %collective-permute-done.16 = bf16[64,2048]{1,0:T(8,128)(2,1)S(1)} collective-permute-done((bf16[64,2048]{1,0:T(8,128)(2,1)S(1)}, bf16[64,2048]{1,0:T(8,128)(2,1)S(1)}, u32[]{:S(2)}, u32[]{:S(2)}) %collective-permute-start.16) | collective-permute-done | bytes 262176 | tf_op jit(solution)/shard_map/ppermute | solution.py:42
  114.8 0.8 add_convert_fusion.4
  115.7 0.8 add_convert_fusion.1
  116.4 3.3 %collective-permute-start.21 = (bf16[64,2048]{1,0:T(8,128)(2,1)S(1)}, bf16[64,2048]{1,0:T(8,128)(2,1)S(1)}, u32[]{:S(2)}, u32[]{:S(2)}) collective-permute-start(bf16[64,2048]{1,0:T(8,128)(2,1)S(1)} %add_convert_fusion.1), channel_id=1, source_target_pairs={{0,7},{1,0},{2,1},{3,2},{4,3},{5,4},{6,5},{7,6},{8,15},{9,8},{10,9... | collective-permute-start | bytes 786440 | tf_op jit(solution)/shard_map/ppermute | solution.py:42
  119.7 4.0 %collective-permute-done.17 = bf16[64,2048]{1,0:T(8,128)(2,1)S(1)} collective-permute-done((bf16[64,2048]{1,0:T(8,128)(2,1)S(1)}, bf16[64,2048]{1,0:T(8,128)(2,1)S(1)}, u32[]{:S(2)}, u32[]{:S(2)}) %collective-permute-start.17) | collective-permute-done | bytes 262176 | tf_op jit(solution)/shard_map/ppermute | solution.py:42
  123.7 0.8 add_convert_fusion.3
  124.6 0.8 add_convert_fusion
  125.3 3.3 %collective-permute-start.22 = (bf16[64,2048]{1,0:T(8,128)(2,1)S(1)}, bf16[64,2048]{1,0:T(8,128)(2,1)S(1)}, u32[]{:S(2)}, u32[]{:S(2)}) collective-permute-start(bf16[64,2048]{1,0:T(8,128)(2,1)S(1)} %add_convert_fusion), channel_id=1, source_target_pairs={{0,7},{1,0},{2,1},{3,2},{4,3},{5,4},{6,5},{7,6},{8,15},{9,8},{10,9... | collective-permute-start | bytes 786440 | tf_op jit(solution)/shard_map/ppermute | solution.py:42
  128.6 0.8 fusion.37
  129.4 2.7 %collective-permute-done.18 = bf16[64,2048]{1,0:T(8,128)(2,1)S(1)} collective-permute-done((bf16[64,2048]{1,0:T(8,128)(2,1)S(1)}, bf16[64,2048]{1,0:T(8,128)(2,1)S(1)}, u32[]{:S(2)}, u32[]{:S(2)}) %collective-permute-start.18) | collective-permute-done | bytes 262176 | tf_op jit(solution)/shard_map/ppermute | solution.py:42
  132.7 3.2 %collective-permute-start.25 = (bf16[16,1024]{1,0:T(8,128)(2,1)S(1)}, bf16[16,1024]{1,0:T(8,128)(2,1)S(1)}, u32[]{:S(2)}, u32[]{:S(2)}) collective-permute-start(bf16[16,1024]{1,0:T(8,128)(2,1)S(1)} %slice.45), channel_id=1, source_target_pairs={{0,24},{8,0},{16,8},{24,16},{1,25},{9,1},{17,9},{25,17},{2,26},{10... | collective-permute-start | bytes 98312 | tf_op jit(solution)/shard_map/ppermute | solution.py:42
  136.0 2.2 %collective-permute-done.23 = bf16[16,1024]{1,0:T(8,128)(2,1)S(1)} collective-permute-done((bf16[16,1024]{1,0:T(8,128)(2,1)S(1)}, bf16[16,1024]{1,0:T(8,128)(2,1)S(1)}, u32[]{:S(2)}, u32[]{:S(2)}) %collective-permute-start.23) | collective-permute-done | bytes 32800 | tf_op jit(solution)/shard_map/ppermute | solution.py:42
  138.3 3.2 %collective-permute-start.26 = (bf16[16,2048]{1,0:T(8,128)(2,1)S(1)}, bf16[16,2048]{1,0:T(8,128)(2,1)S(1)}, u32[]{:S(2)}, u32[]{:S(2)}) collective-permute-start(bf16[16,2048]{1,0:T(8,128)(2,1)S(1)} %get-tuple-element.12), channel_id=1, source_target_pairs={{0,24},{8,0},{16,8},{24,16},{1,25},{9,1},{17,9},{25,17},{2,26},{10... | collective-permute-start | bytes 196616 | tf_op jit(solution)/shard_map/ppermute | solution.py:42
  141.5 2.2 %collective-permute-done.24 = bf16[16,2048]{1,0:T(8,128)(2,1)S(1)} collective-permute-done((bf16[16,2048]{1,0:T(8,128)(2,1)S(1)}, bf16[16,2048]{1,0:T(8,128)(2,1)S(1)}, u32[]{:S(2)}, u32[]{:S(2)}) %collective-permute-start.24) | collective-permute-done | bytes 65568 | tf_op jit(solution)/shard_map/ppermute | solution.py:42
  143.8 0.7 fusion.16
  (54 shorter events, 4.3 us)
Async XLA Ops:
  0.0 5.7 %collective-permute-start = (bf16[16,2048]{1,0:T(8,128)(2,1)}, bf16[16,2048]{1,0:T(8,128)(2,1)S(1)}, u32[]{:S(2)}, u32[]{:S(2)}) collective-permute-start(bf16[16,2048]{1,0:T(8,128)(2,1)} %param.4), channel_id=1, source_target_pairs={{0,8},{8,16},{16,24},{24,0},{1,9},{9,17},{17,25},{25,1},{2,10},{10... | collective-permute-start | bytes 196616 | tf_op jit(solution)/shard_map/ppermute | solution.py:20
  1.6 9.6 %collective-permute-start.2 = (bf16[16,2048]{1,0:T(8,128)(2,1)}, bf16[16,2048]{1,0:T(8,128)(2,1)S(1)}, u32[]{:S(2)}, u32[]{:S(2)}) collective-permute-start(bf16[16,2048]{1,0:T(8,128)(2,1)} %param.4), channel_id=1, source_target_pairs={{0,24},{8,0},{16,8},{24,16},{1,25},{9,1},{17,9},{25,17},{2,26},{10... | collective-permute-start | bytes 196616 | tf_op jit(solution)/shard_map/ppermute | solution.py:24
  4.1 15.9 %copy-start.2 = (bf16[2048,896]{1,0:T(8,128)(2,1)S(1)}, bf16[2048,896]{1,0:T(8,128)(2,1)}, u32[]{:S(2)}) copy-start(bf16[2048,896]{1,0:T(8,128)(2,1)} %param.6) | copy-start | bytes 11010052
  5.7 5.5 %collective-permute-start.1 = (bf16[16,2048]{1,0:T(8,128)(2,1)S(1)}, bf16[16,2048]{1,0:T(8,128)(2,1)S(1)}, u32[]{:S(2)}, u32[]{:S(2)}) collective-permute-start(bf16[16,2048]{1,0:T(8,128)(2,1)S(1)} %collective-permute-done), channel_id=1, source_target_pairs={{0,8},{8,16},{16,24},{24,0},{1,9},{9,17},{17,25},{25,1},{2,10},{10... | collective-permute-start | bytes 196616 | tf_op jit(solution)/shard_map/ppermute | solution.py:20
  11.2 10.3 %collective-permute-start.3 = (bf16[64,2048]{1,0:T(8,128)(2,1)S(1)}, bf16[64,2048]{1,0:T(8,128)(2,1)S(1)}, u32[]{:S(2)}, u32[]{:S(2)}) collective-permute-start(bf16[64,2048]{1,0:T(8,128)(2,1)S(1)} %bitcast.185), channel_id=1, source_target_pairs={{0,1},{1,2},{2,3},{3,4},{4,5},{5,6},{6,7},{7,0},{8,9},{9,10},{10,1... | collective-permute-start | bytes 786440 | tf_op jit(solution)/shard_map/ppermute | solution.py:20
  13.2 10.3 %collective-permute-start.7 = (bf16[64,2048]{1,0:T(8,128)(2,1)S(1)}, bf16[64,2048]{1,0:T(8,128)(2,1)S(1)}, u32[]{:S(2)}, u32[]{:S(2)}) collective-permute-start(bf16[64,2048]{1,0:T(8,128)(2,1)S(1)} %bitcast.186), channel_id=1, source_target_pairs={{0,7},{1,0},{2,1},{3,2},{4,3},{5,4},{6,5},{7,6},{8,15},{9,8},{10,9... | collective-permute-start | bytes 786440 | tf_op jit(solution)/shard_map/ppermute | solution.py:24
  20.0 2.0 %copy-start.1 = (bf16[2048,896]{1,0:T(8,128)(2,1)S(1)}, bf16[2048,896]{1,0:T(8,128)(2,1)}, u32[]{:S(2)}) copy-start(bf16[2048,896]{1,0:T(8,128)(2,1)} %param.5) | copy-start | bytes 11010052
  22.7 7.7 %collective-permute-start.4 = (bf16[64,2048]{1,0:T(8,128)(2,1)S(1)}, bf16[64,2048]{1,0:T(8,128)(2,1)S(1)}, u32[]{:S(2)}, u32[]{:S(2)}) collective-permute-start(bf16[64,2048]{1,0:T(8,128)(2,1)S(1)} %collective-permute-done.3), channel_id=1, source_target_pairs={{0,1},{1,2},{2,3},{3,4},{4,5},{5,6},{6,7},{7,0},{8,9},{9,10},{10,1... | collective-permute-start | bytes 786440 | tf_op jit(solution)/shard_map/ppermute | solution.py:20
  24.9 7.2 %collective-permute-start.8 = (bf16[64,2048]{1,0:T(8,128)(2,1)S(1)}, bf16[64,2048]{1,0:T(8,128)(2,1)S(1)}, u32[]{:S(2)}, u32[]{:S(2)}) collective-permute-start(bf16[64,2048]{1,0:T(8,128)(2,1)S(1)} %collective-permute-done.7), channel_id=1, source_target_pairs={{0,7},{1,0},{2,1},{3,2},{4,3},{5,4},{6,5},{7,6},{8,15},{9,8},{10,9... | collective-permute-start | bytes 786440 | tf_op jit(solution)/shard_map/ppermute | solution.py:24
  31.1 8.0 %collective-permute-start.5 = (bf16[64,2048]{1,0:T(8,128)(2,1)S(1)}, bf16[64,2048]{1,0:T(8,128)(2,1)S(1)}, u32[]{:S(2)}, u32[]{:S(2)}) collective-permute-start(bf16[64,2048]{1,0:T(8,128)(2,1)S(1)} %collective-permute-done.4), channel_id=1, source_target_pairs={{0,1},{1,2},{2,3},{3,4},{4,5},{5,6},{6,7},{7,0},{8,9},{9,10},{10,1... | collective-permute-start | bytes 786440 | tf_op jit(solution)/shard_map/ppermute | solution.py:20
  33.6 7.8 %collective-permute-start.9 = (bf16[64,2048]{1,0:T(8,128)(2,1)S(1)}, bf16[64,2048]{1,0:T(8,128)(2,1)S(1)}, u32[]{:S(2)}, u32[]{:S(2)}) collective-permute-start(bf16[64,2048]{1,0:T(8,128)(2,1)S(1)} %collective-permute-done.8), channel_id=1, source_target_pairs={{0,7},{1,0},{2,1},{3,2},{4,3},{5,4},{6,5},{7,6},{8,15},{9,8},{10,9... | collective-permute-start | bytes 786440 | tf_op jit(solution)/shard_map/ppermute | solution.py:24
  39.8 7.7 %collective-permute-start.6 = (bf16[64,2048]{1,0:T(8,128)(2,1)S(1)}, bf16[64,2048]{1,0:T(8,128)(2,1)S(1)}, u32[]{:S(2)}, u32[]{:S(2)}) collective-permute-start(bf16[64,2048]{1,0:T(8,128)(2,1)S(1)} %collective-permute-done.5), channel_id=1, source_target_pairs={{0,1},{1,2},{2,3},{3,4},{4,5},{5,6},{6,7},{7,0},{8,9},{9,10},{10,1... | collective-permute-start | bytes 786440 | tf_op jit(solution)/shard_map/ppermute | solution.py:20
  49.0 1.8 %copy-start.3 = (f32[8,64,1792]{2,1,0:T(8,128)}, f32[8,64,1792]{2,1,0:T(8,128)S(1)}, u32[]{:S(2)}) copy-start(f32[8,64,1792]{2,1,0:T(8,128)S(1)} %fusion.7) | copy-start | bytes 11010052
  52.2 4.0 %collective-permute-start.10 = (f32[4,64,1792]{2,1,0:T(8,128)}, f32[4,64,1792]{2,1,0:T(8,128)S(1)}, u32[]{:S(2)}, u32[]{:S(2)}) collective-permute-start(f32[4,64,1792]{2,1,0:T(8,128)} %dynamic-slice_bitcast_fusion), channel_id=1, source_target_pairs={{0,32},{32,0},{1,33},{33,1},{2,34},{34,2},{3,35},{35,3},{4,36},{36... | collective-permute-start | bytes 5505032 | tf_op jit(solution)/shard_map/ppermute | solution.py:68
  56.3 7.7 %collective-permute-start.13 = (f32[64,896]{1,0:T(8,128)S(1)}, f32[64,896]{1,0:T(8,128)S(1)}, u32[]{:S(2)}, u32[]{:S(2)}) collective-permute-start(f32[64,896]{1,0:T(8,128)S(1)} %slice_add_fusion), channel_id=1, source_target_pairs={{0,192},{64,0},{128,64},{192,128},{1,193},{65,1},{129,65},{193,129... | collective-permute-start | bytes 688136 | tf_op jit(solution)/shard_map/ppermute | solution.py:42
  57.0 8.5 %collective-permute-start.11 = (f32[64,896]{1,0:T(8,128)S(1)}, f32[64,896]{1,0:T(8,128)S(1)}, u32[]{:S(2)}, u32[]{:S(2)}) collective-permute-start(f32[64,896]{1,0:T(8,128)S(1)} %slice_add_fusion.1), channel_id=1, source_target_pairs={{0,64},{64,128},{128,192},{192,0},{1,65},{65,129},{129,193},{193,1... | collective-permute-start | bytes 688136 | tf_op jit(solution)/shard_map/ppermute | solution.py:42
  66.7 12.7 %collective-permute-start.12 = (f32[64,1792]{1,0:T(8,128)S(1)}, f32[64,1792]{1,0:T(8,128)S(1)}, u32[]{:S(2)}, u32[]{:S(2)}) collective-permute-start(f32[64,1792]{1,0:T(8,128)S(1)} %get-tuple-element.5), channel_id=1, source_target_pairs={{0,64},{64,128},{128,192},{192,0},{1,65},{65,129},{129,193},{193,1... | collective-permute-start | bytes 1376264 | tf_op jit(solution)/shard_map/ppermute | solution.py:42
  67.3 12.2 %collective-permute-start.14 = (f32[64,1792]{1,0:T(8,128)S(1)}, f32[64,1792]{1,0:T(8,128)}, u32[]{:S(2)}, u32[]{:S(2)}) collective-permute-start(f32[64,1792]{1,0:T(8,128)S(1)} %get-tuple-element.6), channel_id=1, source_target_pairs={{0,192},{64,0},{128,64},{192,128},{1,193},{65,1},{129,65},{193,129... | collective-permute-start | bytes 1376264 | tf_op jit(solution)/shard_map/ppermute | solution.py:42
  69.8 27.3 %copy-start = (bf16[896,2048]{1,0:T(8,128)(2,1)S(1)}, bf16[896,2048]{1,0:T(8,128)(2,1)}, u32[]{:S(2)}) copy-start(bf16[896,2048]{1,0:T(8,128)(2,1)} %param.7) | copy-start | bytes 11010052
  97.9 7.0 %collective-permute-start.15 = (bf16[64,1024]{1,0:T(8,128)(2,1)S(1)}, bf16[64,1024]{1,0:T(8,128)(2,1)S(1)}, u32[]{:S(2)}, u32[]{:S(2)}) collective-permute-start(bf16[64,1024]{1,0:T(8,128)(2,1)S(1)} %slice.57), channel_id=1, source_target_pairs={{0,1},{1,2},{2,3},{3,4},{4,5},{5,6},{6,7},{7,0},{8,9},{9,10},{10,1... | collective-permute-start | bytes 393224 | tf_op jit(solution)/shard_map/ppermute | solution.py:42
  98.8 7.0 %collective-permute-start.19 = (bf16[64,1024]{1,0:T(8,128)(2,1)S(1)}, bf16[64,1024]{1,0:T(8,128)(2,1)S(1)}, u32[]{:S(2)}, u32[]{:S(2)}) collective-permute-start(bf16[64,1024]{1,0:T(8,128)(2,1)S(1)} %slice.56), channel_id=1, source_target_pairs={{0,7},{1,0},{2,1},{3,2},{4,3},{5,4},{6,5},{7,6},{8,15},{9,8},{10,9... | collective-permute-start | bytes 393224 | tf_op jit(solution)/shard_map/ppermute | solution.py:42
  105.8 9.0 %collective-permute-start.16 = (bf16[64,2048]{1,0:T(8,128)(2,1)S(1)}, bf16[64,2048]{1,0:T(8,128)(2,1)S(1)}, u32[]{:S(2)}, u32[]{:S(2)}) collective-permute-start(bf16[64,2048]{1,0:T(8,128)(2,1)S(1)} %add_convert_fusion.5), channel_id=1, source_target_pairs={{0,1},{1,2},{2,3},{3,4},{4,5},{5,6},{6,7},{7,0},{8,9},{9,10},{10,1... | collective-permute-start | bytes 786440 | tf_op jit(solution)/shard_map/ppermute | solution.py:42
  106.6 9.0 %collective-permute-start.20 = (bf16[64,2048]{1,0:T(8,128)(2,1)S(1)}, bf16[64,2048]{1,0:T(8,128)(2,1)S(1)}, u32[]{:S(2)}, u32[]{:S(2)}) collective-permute-start(bf16[64,2048]{1,0:T(8,128)(2,1)S(1)} %add_convert_fusion.2), channel_id=1, source_target_pairs={{0,7},{1,0},{2,1},{3,2},{4,3},{5,4},{6,5},{7,6},{8,15},{9,8},{10,9... | collective-permute-start | bytes 786440 | tf_op jit(solution)/shard_map/ppermute | solution.py:42
  115.6 8.1 %collective-permute-start.17 = (bf16[64,2048]{1,0:T(8,128)(2,1)S(1)}, bf16[64,2048]{1,0:T(8,128)(2,1)S(1)}, u32[]{:S(2)}, u32[]{:S(2)}) collective-permute-start(bf16[64,2048]{1,0:T(8,128)(2,1)S(1)} %add_convert_fusion.4), channel_id=1, source_target_pairs={{0,1},{1,2},{2,3},{3,4},{4,5},{5,6},{6,7},{7,0},{8,9},{9,10},{10,1... | collective-permute-start | bytes 786440 | tf_op jit(solution)/shard_map/ppermute | solution.py:42
  116.4 8.1 %collective-permute-start.21 = (bf16[64,2048]{1,0:T(8,128)(2,1)S(1)}, bf16[64,2048]{1,0:T(8,128)(2,1)S(1)}, u32[]{:S(2)}, u32[]{:S(2)}) collective-permute-start(bf16[64,2048]{1,0:T(8,128)(2,1)S(1)} %add_convert_fusion.1), channel_id=1, source_target_pairs={{0,7},{1,0},{2,1},{3,2},{4,3},{5,4},{6,5},{7,6},{8,15},{9,8},{10,9... | collective-permute-start | bytes 786440 | tf_op jit(solution)/shard_map/ppermute | solution.py:42
  124.5 7.7 %collective-permute-start.18 = (bf16[64,2048]{1,0:T(8,128)(2,1)S(1)}, bf16[64,2048]{1,0:T(8,128)(2,1)S(1)}, u32[]{:S(2)}, u32[]{:S(2)}) collective-permute-start(bf16[64,2048]{1,0:T(8,128)(2,1)S(1)} %add_convert_fusion.3), channel_id=1, source_target_pairs={{0,1},{1,2},{2,3},{3,4},{4,5},{5,6},{6,7},{7,0},{8,9},{9,10},{10,1... | collective-permute-start | bytes 786440 | tf_op jit(solution)/shard_map/ppermute | solution.py:42
  125.3 7.2 %collective-permute-start.22 = (bf16[64,2048]{1,0:T(8,128)(2,1)S(1)}, bf16[64,2048]{1,0:T(8,128)(2,1)S(1)}, u32[]{:S(2)}, u32[]{:S(2)}) collective-permute-start(bf16[64,2048]{1,0:T(8,128)(2,1)S(1)} %add_convert_fusion), channel_id=1, source_target_pairs={{0,7},{1,0},{2,1},{3,2},{4,3},{5,4},{6,5},{7,6},{8,15},{9,8},{10,9... | collective-permute-start | bytes 786440 | tf_op jit(solution)/shard_map/ppermute | solution.py:42
  132.6 5.6 %collective-permute-start.23 = (bf16[16,1024]{1,0:T(8,128)(2,1)S(1)}, bf16[16,1024]{1,0:T(8,128)(2,1)S(1)}, u32[]{:S(2)}, u32[]{:S(2)}) collective-permute-start(bf16[16,1024]{1,0:T(8,128)(2,1)S(1)} %slice.44), channel_id=1, source_target_pairs={{0,8},{8,16},{16,24},{24,0},{1,9},{9,17},{17,25},{25,1},{2,10},{10... | collective-permute-start | bytes 98312 | tf_op jit(solution)/shard_map/ppermute | solution.py:42
  132.7 5.5 %collective-permute-start.25 = (bf16[16,1024]{1,0:T(8,128)(2,1)S(1)}, bf16[16,1024]{1,0:T(8,128)(2,1)S(1)}, u32[]{:S(2)}, u32[]{:S(2)}) collective-permute-start(bf16[16,1024]{1,0:T(8,128)(2,1)S(1)} %slice.45), channel_id=1, source_target_pairs={{0,24},{8,0},{16,8},{24,16},{1,25},{9,1},{17,9},{25,17},{2,26},{10... | collective-permute-start | bytes 98312 | tf_op jit(solution)/shard_map/ppermute | solution.py:42
  138.2 5.6 %collective-permute-start.24 = (bf16[16,2048]{1,0:T(8,128)(2,1)S(1)}, bf16[16,2048]{1,0:T(8,128)(2,1)S(1)}, u32[]{:S(2)}, u32[]{:S(2)}) collective-permute-start(bf16[16,2048]{1,0:T(8,128)(2,1)S(1)} %get-tuple-element.11), channel_id=1, source_target_pairs={{0,8},{8,16},{16,24},{24,0},{1,9},{9,17},{17,25},{25,1},{2,10},{10... | collective-permute-start | bytes 196616 | tf_op jit(solution)/shard_map/ppermute | solution.py:42
  138.3 5.5 %collective-permute-start.26 = (bf16[16,2048]{1,0:T(8,128)(2,1)S(1)}, bf16[16,2048]{1,0:T(8,128)(2,1)S(1)}, u32[]{:S(2)}, u32[]{:S(2)}) collective-permute-start(bf16[16,2048]{1,0:T(8,128)(2,1)S(1)} %get-tuple-element.12), channel_id=1, source_target_pairs={{0,24},{8,0},{16,8},{24,16},{1,25},{9,1},{17,9},{25,17},{2,26},{10... | collective-permute-start | bytes 196616 | tf_op jit(solution)/shard_map/ppermute | solution.py:42

commit v15 on v12

--- a/solution.py
+++ b/solution.py
@@ -93,11 +93,10 @@
     activated = (jax.nn.silu(summed[:, :width]) * summed[:, width:]).astype(jnp.bfloat16)
     activated = lax.all_gather(activated, EMBED, axis=0, tiled=True)
     act_blocks = activated.reshape((nz, -1) + activated.shape[1:])
-    project = lambda i: jnp.dot(
-        lax.dynamic_index_in_dim(act_blocks, i, 0, keepdims=False),
-        down_weight,
-        preferred_element_type=jnp.float32,
+    projected = jnp.einsum(
+        "brh,hc->brc", act_blocks, down_weight, preferred_element_type=jnp.float32
     )
+    project = lambda i: lax.dynamic_index_in_dim(projected, i, 0, keepdims=False)
     totals = ring_rs_bal(project, "hz", nz, jnp.bfloat16)
     totals = totals.reshape((ny, -1) + totals.shape[1:])
     totals = ring_rs_bal(

time: 145 us -> 160 us (1.10)
  waiting for transfers between devices: 56.6 us -> 77.7 us
  matrix products: 22.3 us -> 17.7 us
  starting transfers between devices: 41.8 us -> 38.2 us
    ppermute x16, waiting for transfers between devices: 36.3 us -> 57.5 us  [side(): got = lax.ppermute(acc.astype(send_dtype), axis, perm).astype(jnp.float32)]
    dot_general x9 -> x1, matrix products: 8.91 us -> 4.41 us  [on_device(): jnp.einsum('brh,hc->brc', act_blocks, down_weight, preferred_element_type...]
    ppermute x16, starting transfers between devices: 24.6 us -> 21 us  [side(): got = lax.ppermute(acc.astype(send_dtype), axis, perm).astype(jnp.float32)]
  transfers between devices with their start and end apart: 27 -> 27, of which waited for: 20 -> 22; matrix products, arithmetic and copies ran while one was open for 13% -> 8% of each run, Pallas kernels for 0% -> 0%
where the time goes in v15:
time: 160 us; the launch traced here: 158 us
  waiting for transfers between devices  77.7 us (49%)
  starting transfers between devices  38.2 us (24%)
  matrix products  17.7 us (11%)
  blocking collectives  14.4 us (9%)
  other arithmetic  5.88 us (4%)
  local copies, waits for them, and re-layouts  3.86 us (2%)
    ppermute x16, waiting for transfers between devices, side(): got = lax.ppermute(acc.astype(send_dtype), axis, perm).astype(jnp.float32)  57.5 us
    ppermute x16, starting transfers between devices, side(): got = lax.ppermute(acc.astype(send_dtype), axis, perm).astype(jnp.float32)  21 us
    ppermute x6, waiting for transfers between devices, ring_ag(): buf = lax.ppermute(buf, axis, fwd)  15.4 us
    all_gather x1, blocking collectives, on_device(): activated = lax.all_gather(activated, EMBED, axis=0, tiled=True)  14.4 us
    ppermute x4, starting transfers between devices, ring_ag(): buf = lax.ppermute(buf, axis, bwd)  12.9 us
    dot_general x8, matrix products, on_device(): jnp.dot(v, gate_weight, preferred_element_type=jnp.float32)  7.66 us
    dot_general x8, matrix products, on_device(): jnp.dot(v, up_weight, preferred_element_type=jnp.float32)  5.67 us
    dot_general x1, matrix products, on_device(): jnp.einsum('brh,hc->brc', act_blocks, down_weight, preferred_element_type...  4.41 us
  transfers between devices with their start and end apart: 27, of which 22 were waited for; matrix products, arithmetic and copies ran while one was open for 8% of the time, Pallas kernels for 0%

profile of v15, /device:TPU:2, one launch (start us, length us, event | category | flops | bytes accessed | tf_op | source)
XLA Modules:
  0.0 158.2 jit_solution(14596936904204878507)
XLA Ops:
  0.0 1.6 collective-permute-start
  1.6 1.7 %collective-permute-start.2 = (bf16[16,2048]{1,0:T(8,128)(2,1)}, bf16[16,2048]{1,0:T(8,128)(2,1)S(1)}, u32[]{:S(2)}, u32[]{:S(2)}) collective-permute-start(bf16[16,2048]{1,0:T(8,128)(2,1)} %param.4), channel_id=1, source_target_pairs={{0,24},{8,0},{16,8},{24,16},{1,25},{9,1},{17,9},{25,17},{2,26},{10... | collective-permute-start | bytes 196616 | tf_op jit(solution)/shard_map/ppermute | solution.py:24
  3.3 0.9 bitcast_dynamic-update-slice_fusion.3
  4.1 1.6 collective-permute-done
  5.7 0.4 collective-permute-start.1
  6.1 5.1 %collective-permute-done.1 = bf16[16,2048]{1,0:T(8,128)(2,1)S(1)} collective-permute-done((bf16[16,2048]{1,0:T(8,128)(2,1)S(1)}, bf16[16,2048]{1,0:T(8,128)(2,1)S(1)}, u32[]{:S(2)}, u32[]{:S(2)}) %collective-permute-start.1) | collective-permute-done | bytes 65568 | tf_op jit(solution)/shard_map/ppermute | solution.py:20
  11.2 2.0 %collective-permute-start.3 = (bf16[64,2048]{1,0:T(8,128)(2,1)S(1)}, bf16[64,2048]{1,0:T(8,128)(2,1)S(1)}, u32[]{:S(2)}, u32[]{:S(2)}) collective-permute-start(bf16[64,2048]{1,0:T(8,128)(2,1)S(1)} %bitcast.148), channel_id=1, source_target_pairs={{0,1},{1,2},{2,3},{3,4},{4,5},{5,6},{6,7},{7,0},{8,9},{9,10},{10,1... | collective-permute-start | bytes 786440 | tf_op jit(solution)/shard_map/ppermute | solution.py:20
  13.2 4.0 %collective-permute-start.7 = (bf16[64,2048]{1,0:T(8,128)(2,1)S(1)}, bf16[64,2048]{1,0:T(8,128)(2,1)S(1)}, u32[]{:S(2)}, u32[]{:S(2)}) collective-permute-start(bf16[64,2048]{1,0:T(8,128)(2,1)S(1)} %bitcast.149), channel_id=1, source_target_pairs={{0,7},{1,0},{2,1},{3,2},{4,3},{5,4},{6,5},{7,6},{8,15},{9,8},{10,9... | collective-permute-start | bytes 786440 | tf_op jit(solution)/shard_map/ppermute | solution.py:24
  17.2 2.7 %fusion.27 = f32[64,896]{1,0:T(8,128)S(1)} fusion(bf16[64,2048]{1,0:T(8,128)(2,1)S(1)} %bitcast.150, bf16[2048,896]{1,0:T(8,128)(2,1)} %param.5), kind=kOutput, calls=%fused_computation.61 | convolution fusion | flops 234881024 | bytes 4161536 | tf_op jit(solution)/shard_map/dot_general | solution.py:86
  20.0 0.7 fusion.28
  21.1 0.4 collective-permute-done.3
  21.5 0.5 copy-done
  22.0 0.7 fusion.29
  22.8 0.7 fusion.30
  23.5 0.7 fusion.37
  24.2 0.7 fusion.38
  24.9 3.3 %collective-permute-start.8 = (bf16[64,2048]{1,0:T(8,128)(2,1)S(1)}, bf16[64,2048]{1,0:T(8,128)(2,1)S(1)}, u32[]{:S(2)}, u32[]{:S(2)}) collective-permute-start(bf16[64,2048]{1,0:T(8,128)(2,1)S(1)} %collective-permute-done.7), channel_id=1, source_target_pairs={{0,7},{1,0},{2,1},{3,2},{4,3},{5,4},{6,5},{7,6},{8,15},{9,8},{10,9... | collective-permute-start | bytes 786440 | tf_op jit(solution)/shard_map/ppermute | solution.py:24
  28.3 2.1 %collective-permute-done.4 = bf16[64,2048]{1,0:T(8,128)(2,1)S(1)} collective-permute-done((bf16[64,2048]{1,0:T(8,128)(2,1)S(1)}, bf16[64,2048]{1,0:T(8,128)(2,1)S(1)}, u32[]{:S(2)}, u32[]{:S(2)}) %collective-permute-start.4) | collective-permute-done | bytes 262176 | tf_op jit(solution)/shard_map/ppermute | solution.py:20
  30.4 0.7 fusion.31
  31.2 0.7 fusion.32
  32.1 0.7 fusion.39
  32.8 0.7 fusion.40
  33.6 3.9 %collective-permute-start.9 = (bf16[64,2048]{1,0:T(8,128)(2,1)S(1)}, bf16[64,2048]{1,0:T(8,128)(2,1)S(1)}, u32[]{:S(2)}, u32[]{:S(2)}) collective-permute-start(bf16[64,2048]{1,0:T(8,128)(2,1)S(1)} %collective-permute-done.8), channel_id=1, source_target_pairs={{0,7},{1,0},{2,1},{3,2},{4,3},{5,4},{6,5},{7,6},{8,15},{9,8},{10,9... | collective-permute-start | bytes 786440 | tf_op jit(solution)/shard_map/ppermute | solution.py:24
  37.5 1.5 collective-permute-done.5
  39.1 0.7 fusion.33
  39.9 0.7 fusion.34
  40.6 0.8 collective-permute-done.9
  41.4 0.7 fusion.41
  42.1 0.7 fusion.42
  42.8 4.6 %collective-permute-done.6 = bf16[64,2048]{1,0:T(8,128)(2,1)S(1)} collective-permute-done((bf16[64,2048]{1,0:T(8,128)(2,1)S(1)}, bf16[64,2048]{1,0:T(8,128)(2,1)S(1)}, u32[]{:S(2)}, u32[]{:S(2)}) %collective-permute-start.6) | collective-permute-done | bytes 262176 | tf_op jit(solution)/shard_map/ppermute | solution.py:20
  47.4 0.7 fusion.35
  48.1 0.7 fusion.36
  49.1 1.8 %copy-done.2 = f32[8,64,1792]{2,1,0:T(8,128)} copy-done((f32[8,64,1792]{2,1,0:T(8,128)}, f32[8,64,1792]{2,1,0:T(8,128)S(1)}, u32[]{:S(2)}) %copy-start.2) | copy-done | bytes 3670040
  51.1 3.9 %collective-permute-done.10 = f32[4,64,1792]{2,1,0:T(8,128)} collective-permute-done((f32[4,64,1792]{2,1,0:T(8,128)S(1)}, f32[4,64,1792]{2,1,0:T(8,128)}, u32[]{:S(2)}, u32[]{:S(2)}) %collective-permute-start.10) | collective-permute-done | bytes 1835040 | tf_op jit(solution)/shard_map/ppermute | solution.py:69
  55.0 2.2 %bitcast_add_fusion = f32[4,64,1792]{2,1,0:T(8,128)S(1)} fusion(f32[4,64,1792]{2,1,0:T(8,128)} %collective-permute-done.10, f32[4,2,64,1792]{3,2,1,0:T(8,128)} %bitcast.147, s32[]{:T(128)S(6)} %select_n.206), kind=kLoop, calls=%fused_computation.2 | loop fusion | flops 458752 | bytes 5505028 | tf_op jit(solution)/shard_map/add | solution.py:70
  57.3 1.6 collective-permute-start.11
  58.9 0.6 collective-permute-start.13
  59.5 5.5 %collective-permute-done.11 = f32[64,896]{1,0:T(8,128)S(1)} collective-permute-done((f32[64,896]{1,0:T(8,128)S(1)}, f32[64,896]{1,0:T(8,128)S(1)}, u32[]{:S(2)}, u32[]{:S(2)}) %collective-permute-start.11) | collective-permute-done | bytes 229408 | tf_op jit(solution)/shard_map/ppermute | solution.py:42
  65.0 1.3 collective-permute-done.13
  66.4 1.3 collective-permute-start.12
  67.7 0.8 collective-permute-start.14
  68.5 9.4 %collective-permute-done.12 = f32[64,1792]{1,0:T(8,128)S(1)} collective-permute-done((f32[64,1792]{1,0:T(8,128)S(1)}, f32[64,1792]{1,0:T(8,128)S(1)}, u32[]{:S(2)}, u32[]{:S(2)}) %collective-permute-start.12) | collective-permute-done | bytes 458784 | tf_op jit(solution)/shard_map/ppermute | solution.py:42
  77.9 1.0 collective-permute-done.14
  78.9 1.1 fusion.17
  80.1 14.4 %all_gather.3 = bf16[512,896]{1,0:T(8,128)(2,1)S(1)} all-gather(bf16[64,896]{1,0:T(8,128)(2,1)S(1)} %fusion.20), channel_id=1, replica_groups=mesh['ex'=4,'ec'=2,'hy'=4,'hz'=8] {'ex','ec'}, dimensions={0}, use_global_device_ids=true | all-gather | bytes 1032192 | tf_op jit(solution)/shard_map/all_gather | solution.py:94
  94.5 4.4 %fusion = f32[8,64,2048]{2,1,0:T(8,128)S(1)} fusion(bf16[8,64,896]{2,1,0:T(8,128)(2,1)S(1)} %bitcast.155, bf16[896,2048]{1,0:T(8,128)(2,1)} %param.7), kind=kOutput, calls=%fused_computation | convolution fusion | flops 1879048192 | bytes 8781824 | tf_op jit(solution)/shard_map/brh,hc->brc/dot_general | solution.py:96
  99.1 6.9 %collective-permute-done.15 = bf16[64,1024]{1,0:T(8,128)(2,1)S(1)} collective-permute-done((bf16[64,1024]{1,0:T(8,128)(2,1)S(1)}, bf16[64,1024]{1,0:T(8,128)(2,1)S(1)}, u32[]{:S(2)}, u32[]{:S(2)}) %collective-permute-start.15) | collective-permute-done | bytes 131104 | tf_op jit(solution)/shard_map/ppermute | solution.py:42
  106.1 0.3 collective-permute-start.16
  106.4 9.0 %collective-permute-done.16 = bf16[64,2048]{1,0:T(8,128)(2,1)S(1)} collective-permute-done((bf16[64,2048]{1,0:T(8,128)(2,1)S(1)}, bf16[64,2048]{1,0:T(8,128)(2,1)S(1)}, u32[]{:S(2)}, u32[]{:S(2)}) %collective-permute-start.16) | collective-permute-done | bytes 262176 | tf_op jit(solution)/shard_map/ppermute | solution.py:42
  115.5 3.3 %collective-permute-start.19 = (bf16[64,1024]{1,0:T(8,128)(2,1)S(1)}, bf16[64,1024]{1,0:T(8,128)(2,1)S(1)}, u32[]{:S(2)}, u32[]{:S(2)}) collective-permute-start(bf16[64,1024]{1,0:T(8,128)(2,1)S(1)} %slice.41), channel_id=1, source_target_pairs={{0,7},{1,0},{2,1},{3,2},{4,3},{5,4},{6,5},{7,6},{8,15},{9,8},{10,9... | collective-permute-start | bytes 393224 | tf_op jit(solution)/shard_map/ppermute | solution.py:42
  118.8 2.5 %collective-permute-done.19 = bf16[64,1024]{1,0:T(8,128)(2,1)S(1)} collective-permute-done((bf16[64,1024]{1,0:T(8,128)(2,1)S(1)}, bf16[64,1024]{1,0:T(8,128)(2,1)S(1)}, u32[]{:S(2)}, u32[]{:S(2)}) %collective-permute-start.19) | collective-permute-done | bytes 131104 | tf_op jit(solution)/shard_map/ppermute | solution.py:42
  121.4 2.2 %collective-permute-done.17 = bf16[64,2048]{1,0:T(8,128)(2,1)S(1)} collective-permute-done((bf16[64,2048]{1,0:T(8,128)(2,1)S(1)}, bf16[64,2048]{1,0:T(8,128)(2,1)S(1)}, u32[]{:S(2)}, u32[]{:S(2)}) %collective-permute-start.17) | collective-permute-done | bytes 262176 | tf_op jit(solution)/shard_map/ppermute | solution.py:42
  123.7 1.5 collective-permute-start.20
  125.2 5.6 %collective-permute-done.20 = bf16[64,2048]{1,0:T(8,128)(2,1)S(1)} collective-permute-done((bf16[64,2048]{1,0:T(8,128)(2,1)S(1)}, bf16[64,2048]{1,0:T(8,128)(2,1)S(1)}, u32[]{:S(2)}, u32[]{:S(2)}) %collective-permute-start.20) | collective-permute-done | bytes 262176 | tf_op jit(solution)/shard_map/ppermute | solution.py:42
  130.8 2.1 %collective-permute-start.21 = (bf16[64,2048]{1,0:T(8,128)(2,1)S(1)}, bf16[64,2048]{1,0:T(8,128)(2,1)S(1)}, u32[]{:S(2)}, u32[]{:S(2)}) collective-permute-start(bf16[64,2048]{1,0:T(8,128)(2,1)S(1)} %fusion.3), channel_id=1, source_target_pairs={{0,7},{1,0},{2,1},{3,2},{4,3},{5,4},{6,5},{7,6},{8,15},{9,8},{10,9... | collective-permute-start | bytes 786440 | tf_op jit(solution)/shard_map/ppermute | solution.py:42
  132.9 6.1 %collective-permute-done.21 = bf16[64,2048]{1,0:T(8,128)(2,1)S(1)} collective-permute-done((bf16[64,2048]{1,0:T(8,128)(2,1)S(1)}, bf16[64,2048]{1,0:T(8,128)(2,1)S(1)}, u32[]{:S(2)}, u32[]{:S(2)}) %collective-permute-start.21) | collective-permute-done | bytes 262176 | tf_op jit(solution)/shard_map/ppermute | solution.py:42
  139.1 2.6 %collective-permute-start.22 = (bf16[64,2048]{1,0:T(8,128)(2,1)S(1)}, bf16[64,2048]{1,0:T(8,128)(2,1)S(1)}, u32[]{:S(2)}, u32[]{:S(2)}) collective-permute-start(bf16[64,2048]{1,0:T(8,128)(2,1)S(1)} %fusion.4), channel_id=1, source_target_pairs={{0,7},{1,0},{2,1},{3,2},{4,3},{5,4},{6,5},{7,6},{8,15},{9,8},{10,9... | collective-permute-start | bytes 786440 | tf_op jit(solution)/shard_map/ppermute | solution.py:42
  141.7 3.9 %collective-permute-done.22 = bf16[64,2048]{1,0:T(8,128)(2,1)S(1)} collective-permute-done((bf16[64,2048]{1,0:T(8,128)(2,1)S(1)}, bf16[64,2048]{1,0:T(8,128)(2,1)S(1)}, u32[]{:S(2)}, u32[]{:S(2)}) %collective-permute-start.22) | collective-permute-done | bytes 262176 | tf_op jit(solution)/shard_map/ppermute | solution.py:42
  145.6 1.1 fusion.8
  146.9 3.2 %collective-permute-start.25 = (bf16[16,1024]{1,0:T(8,128)(2,1)S(1)}, bf16[16,1024]{1,0:T(8,128)(2,1)S(1)}, u32[]{:S(2)}, u32[]{:S(2)}) collective-permute-start(bf16[16,1024]{1,0:T(8,128)(2,1)S(1)} %slice.43), channel_id=1, source_target_pairs={{0,24},{8,0},{16,8},{24,16},{1,25},{9,1},{17,9},{25,17},{2,26},{10... | collective-permute-start | bytes 98312 | tf_op jit(solution)/shard_map/ppermute | solution.py:42
  150.1 1.9 %collective-permute-done.23 = bf16[16,1024]{1,0:T(8,128)(2,1)S(1)} collective-permute-done((bf16[16,1024]{1,0:T(8,128)(2,1)S(1)}, bf16[16,1024]{1,0:T(8,128)(2,1)S(1)}, u32[]{:S(2)}, u32[]{:S(2)}) %collective-permute-start.23) | collective-permute-done | bytes 32800 | tf_op jit(solution)/shard_map/ppermute | solution.py:42
  152.1 3.3 %collective-permute-start.26 = (bf16[16,2048]{1,0:T(8,128)(2,1)S(1)}, bf16[16,2048]{1,0:T(8,128)(2,1)S(1)}, u32[]{:S(2)}, u32[]{:S(2)}) collective-permute-start(bf16[16,2048]{1,0:T(8,128)(2,1)S(1)} %get-tuple-element.14), channel_id=1, source_target_pairs={{0,24},{8,0},{16,8},{24,16},{1,25},{9,1},{17,9},{25,17},{2,26},{10... | collective-permute-start | bytes 196616 | tf_op jit(solution)/shard_map/ppermute | solution.py:42
  155.4 2.2 %collective-permute-done.24 = bf16[16,2048]{1,0:T(8,128)(2,1)S(1)} collective-permute-done((bf16[16,2048]{1,0:T(8,128)(2,1)S(1)}, bf16[16,2048]{1,0:T(8,128)(2,1)S(1)}, u32[]{:S(2)}, u32[]{:S(2)}) %collective-permute-start.24) | collective-permute-done | bytes 65568 | tf_op jit(solution)/shard_map/ppermute | solution.py:42
  157.6 0.7 fusion.24
  (52 shorter events, 2.4 us)
Async XLA Ops:
  0.0 5.7 %collective-permute-start = (bf16[16,2048]{1,0:T(8,128)(2,1)}, bf16[16,2048]{1,0:T(8,128)(2,1)S(1)}, u32[]{:S(2)}, u32[]{:S(2)}) collective-permute-start(bf16[16,2048]{1,0:T(8,128)(2,1)} %param.4), channel_id=1, source_target_pairs={{0,8},{8,16},{16,24},{24,0},{1,9},{9,17},{17,25},{25,1},{2,10},{10... | collective-permute-start | bytes 196616 | tf_op jit(solution)/shard_map/ppermute | solution.py:20
  1.6 9.6 %collective-permute-start.2 = (bf16[16,2048]{1,0:T(8,128)(2,1)}, bf16[16,2048]{1,0:T(8,128)(2,1)S(1)}, u32[]{:S(2)}, u32[]{:S(2)}) collective-permute-start(bf16[16,2048]{1,0:T(8,128)(2,1)} %param.4), channel_id=1, source_target_pairs={{0,24},{8,0},{16,8},{24,16},{1,25},{9,1},{17,9},{25,17},{2,26},{10... | collective-permute-start | bytes 196616 | tf_op jit(solution)/shard_map/ppermute | solution.py:24
  4.1 15.9 %copy-start.1 = (bf16[2048,896]{1,0:T(8,128)(2,1)S(1)}, bf16[2048,896]{1,0:T(8,128)(2,1)}, u32[]{:S(2)}) copy-start(bf16[2048,896]{1,0:T(8,128)(2,1)} %param.6) | copy-start | bytes 11010052
  5.7 5.5 %collective-permute-start.1 = (bf16[16,2048]{1,0:T(8,128)(2,1)S(1)}, bf16[16,2048]{1,0:T(8,128)(2,1)S(1)}, u32[]{:S(2)}, u32[]{:S(2)}) collective-permute-start(bf16[16,2048]{1,0:T(8,128)(2,1)S(1)} %collective-permute-done), channel_id=1, source_target_pairs={{0,8},{8,16},{16,24},{24,0},{1,9},{9,17},{17,25},{25,1},{2,10},{10... | collective-permute-start | bytes 196616 | tf_op jit(solution)/shard_map/ppermute | solution.py:20
  11.2 10.3 %collective-permute-start.3 = (bf16[64,2048]{1,0:T(8,128)(2,1)S(1)}, bf16[64,2048]{1,0:T(8,128)(2,1)S(1)}, u32[]{:S(2)}, u32[]{:S(2)}) collective-permute-start(bf16[64,2048]{1,0:T(8,128)(2,1)S(1)} %bitcast.148), channel_id=1, source_target_pairs={{0,1},{1,2},{2,3},{3,4},{4,5},{5,6},{6,7},{7,0},{8,9},{9,10},{10,1... | collective-permute-start | bytes 786440 | tf_op jit(solution)/shard_map/ppermute | solution.py:20
  13.2 10.3 %collective-permute-start.7 = (bf16[64,2048]{1,0:T(8,128)(2,1)S(1)}, bf16[64,2048]{1,0:T(8,128)(2,1)S(1)}, u32[]{:S(2)}, u32[]{:S(2)}) collective-permute-start(bf16[64,2048]{1,0:T(8,128)(2,1)S(1)} %bitcast.149), channel_id=1, source_target_pairs={{0,7},{1,0},{2,1},{3,2},{4,3},{5,4},{6,5},{7,6},{8,15},{9,8},{10,9... | collective-permute-start | bytes 786440 | tf_op jit(solution)/shard_map/ppermute | solution.py:24
  20.0 2.0 %copy-start = (bf16[2048,896]{1,0:T(8,128)(2,1)S(1)}, bf16[2048,896]{1,0:T(8,128)(2,1)}, u32[]{:S(2)}) copy-start(bf16[2048,896]{1,0:T(8,128)(2,1)} %param.5) | copy-start | bytes 11010052
  22.7 7.7 %collective-permute-start.4 = (bf16[64,2048]{1,0:T(8,128)(2,1)S(1)}, bf16[64,2048]{1,0:T(8,128)(2,1)S(1)}, u32[]{:S(2)}, u32[]{:S(2)}) collective-permute-start(bf16[64,2048]{1,0:T(8,128)(2,1)S(1)} %collective-permute-done.3), channel_id=1, source_target_pairs={{0,1},{1,2},{2,3},{3,4},{4,5},{5,6},{6,7},{7,0},{8,9},{9,10},{10,1... | collective-permute-start | bytes 786440 | tf_op jit(solution)/shard_map/ppermute | solution.py:20
  24.9 7.2 %collective-permute-start.8 = (bf16[64,2048]{1,0:T(8,128)(2,1)S(1)}, bf16[64,2048]{1,0:T(8,128)(2,1)S(1)}, u32[]{:S(2)}, u32[]{:S(2)}) collective-permute-start(bf16[64,2048]{1,0:T(8,128)(2,1)S(1)} %collective-permute-done.7), channel_id=1, source_target_pairs={{0,7},{1,0},{2,1},{3,2},{4,3},{5,4},{6,5},{7,6},{8,15},{9,8},{10,9... | collective-permute-start | bytes 786440 | tf_op jit(solution)/shard_map/ppermute | solution.py:24
  31.1 8.0 %collective-permute-start.5 = (bf16[64,2048]{1,0:T(8,128)(2,1)S(1)}, bf16[64,2048]{1,0:T(8,128)(2,1)S(1)}, u32[]{:S(2)}, u32[]{:S(2)}) collective-permute-start(bf16[64,2048]{1,0:T(8,128)(2,1)S(1)} %collective-permute-done.4), channel_id=1, source_target_pairs={{0,1},{1,2},{2,3},{3,4},{4,5},{5,6},{6,7},{7,0},{8,9},{9,10},{10,1... | collective-permute-start | bytes 786440 | tf_op jit(solution)/shard_map/ppermute | solution.py:20
  33.6 7.8 %collective-permute-start.9 = (bf16[64,2048]{1,0:T(8,128)(2,1)S(1)}, bf16[64,2048]{1,0:T(8,128)(2,1)S(1)}, u32[]{:S(2)}, u32[]{:S(2)}) collective-permute-start(bf16[64,2048]{1,0:T(8,128)(2,1)S(1)} %collective-permute-done.8), channel_id=1, source_target_pairs={{0,7},{1,0},{2,1},{3,2},{4,3},{5,4},{6,5},{7,6},{8,15},{9,8},{10,9... | collective-permute-start | bytes 786440 | tf_op jit(solution)/shard_map/ppermute | solution.py:24
  39.8 7.7 %collective-permute-start.6 = (bf16[64,2048]{1,0:T(8,128)(2,1)S(1)}, bf16[64,2048]{1,0:T(8,128)(2,1)S(1)}, u32[]{:S(2)}, u32[]{:S(2)}) collective-permute-start(bf16[64,2048]{1,0:T(8,128)(2,1)S(1)} %collective-permute-done.5), channel_id=1, source_target_pairs={{0,1},{1,2},{2,3},{3,4},{4,5},{5,6},{6,7},{7,0},{8,9},{9,10},{10,1... | collective-permute-start | bytes 786440 | tf_op jit(solution)/shard_map/ppermute | solution.py:20
  49.0 1.8 %copy-start.2 = (f32[8,64,1792]{2,1,0:T(8,128)}, f32[8,64,1792]{2,1,0:T(8,128)S(1)}, u32[]{:S(2)}) copy-start(f32[8,64,1792]{2,1,0:T(8,128)S(1)} %fusion.16) | copy-start | bytes 11010052
  51.0 4.0 %collective-permute-start.10 = (f32[4,64,1792]{2,1,0:T(8,128)S(1)}, f32[4,64,1792]{2,1,0:T(8,128)}, u32[]{:S(2)}, u32[]{:S(2)}) collective-permute-start(f32[4,64,1792]{2,1,0:T(8,128)S(1)} %dynamic-slice_bitcast_fusion), channel_id=1, source_target_pairs={{0,32},{32,0},{1,33},{33,1},{2,34},{34,2},{3,35},{35,3},{4,36},{36... | collective-permute-start | bytes 5505032 | tf_op jit(solution)/shard_map/ppermute | solution.py:69
  57.3 7.7 %collective-permute-start.11 = (f32[64,896]{1,0:T(8,128)S(1)}, f32[64,896]{1,0:T(8,128)S(1)}, u32[]{:S(2)}, u32[]{:S(2)}) collective-permute-start(f32[64,896]{1,0:T(8,128)S(1)} %slice.36), channel_id=1, source_target_pairs={{0,64},{64,128},{128,192},{192,0},{1,65},{65,129},{129,193},{193,1... | collective-permute-start | bytes 688136 | tf_op jit(solution)/shard_map/ppermute | solution.py:42
  58.9 7.4 %collective-permute-start.13 = (f32[64,896]{1,0:T(8,128)S(1)}, f32[64,896]{1,0:T(8,128)S(1)}, u32[]{:S(2)}, u32[]{:S(2)}) collective-permute-start(f32[64,896]{1,0:T(8,128)S(1)} %slice.37), channel_id=1, source_target_pairs={{0,192},{64,0},{128,64},{192,128},{1,193},{65,1},{129,65},{193,129... | collective-permute-start | bytes 688136 | tf_op jit(solution)/shard_map/ppermute | solution.py:42
  66.4 11.5 %collective-permute-start.12 = (f32[64,1792]{1,0:T(8,128)S(1)}, f32[64,1792]{1,0:T(8,128)S(1)}, u32[]{:S(2)}, u32[]{:S(2)}) collective-permute-start(f32[64,1792]{1,0:T(8,128)S(1)} %get-tuple-element.9), channel_id=1, source_target_pairs={{0,64},{64,128},{128,192},{192,0},{1,65},{65,129},{129,193},{193,1... | collective-permute-start | bytes 1376264 | tf_op jit(solution)/shard_map/ppermute | solution.py:42
  67.7 11.2 %collective-permute-start.14 = (f32[64,1792]{1,0:T(8,128)S(1)}, f32[64,1792]{1,0:T(8,128)}, u32[]{:S(2)}, u32[]{:S(2)}) collective-permute-start(f32[64,1792]{1,0:T(8,128)S(1)} %get-tuple-element.10), channel_id=1, source_target_pairs={{0,192},{64,0},{128,64},{192,128},{1,193},{65,1},{129,65},{193,129... | collective-permute-start | bytes 1376264 | tf_op jit(solution)/shard_map/ppermute | solution.py:42
  98.9 40.2 %copy-start.3 = (f32[8,64,2048]{2,1,0:T(8,128)}, f32[8,64,2048]{2,1,0:T(8,128)S(1)}, u32[]{:S(2)}) copy-start(f32[8,64,2048]{2,1,0:T(8,128)S(1)} %fusion) | copy-start | bytes 12582916
  99.0 7.0 %collective-permute-start.15 = (bf16[64,1024]{1,0:T(8,128)(2,1)S(1)}, bf16[64,1024]{1,0:T(8,128)(2,1)S(1)}, u32[]{:S(2)}, u32[]{:S(2)}) collective-permute-start(bf16[64,1024]{1,0:T(8,128)(2,1)S(1)} %slice.40), channel_id=1, source_target_pairs={{0,1},{1,2},{2,3},{3,4},{4,5},{5,6},{6,7},{7,0},{8,9},{9,10},{10,1... | collective-permute-start | bytes 393224 | tf_op jit(solution)/shard_map/ppermute | solution.py:42
  106.1 9.3 %collective-permute-start.16 = (bf16[64,2048]{1,0:T(8,128)(2,1)S(1)}, bf16[64,2048]{1,0:T(8,128)(2,1)S(1)}, u32[]{:S(2)}, u32[]{:S(2)}) collective-permute-start(bf16[64,2048]{1,0:T(8,128)(2,1)S(1)} %fusion.5), channel_id=1, source_target_pairs={{0,1},{1,2},{2,3},{3,4},{4,5},{5,6},{6,7},{7,0},{8,9},{9,10},{10,1... | collective-permute-start | bytes 786440 | tf_op jit(solution)/shard_map/ppermute | solution.py:42
  115.4 8.1 %collective-permute-start.17 = (bf16[64,2048]{1,0:T(8,128)(2,1)S(1)}, bf16[64,2048]{1,0:T(8,128)(2,1)S(1)}, u32[]{:S(2)}, u32[]{:S(2)}) collective-permute-start(bf16[64,2048]{1,0:T(8,128)(2,1)S(1)} %fusion.6), channel_id=1, source_target_pairs={{0,1},{1,2},{2,3},{3,4},{4,5},{5,6},{6,7},{7,0},{8,9},{9,10},{10,1... | collective-permute-start | bytes 786440 | tf_op jit(solution)/shard_map/ppermute | solution.py:42
  115.5 5.8 %collective-permute-start.19 = (bf16[64,1024]{1,0:T(8,128)(2,1)S(1)}, bf16[64,1024]{1,0:T(8,128)(2,1)S(1)}, u32[]{:S(2)}, u32[]{:S(2)}) collective-permute-start(bf16[64,1024]{1,0:T(8,128)(2,1)S(1)} %slice.41), channel_id=1, source_target_pairs={{0,7},{1,0},{2,1},{3,2},{4,3},{5,4},{6,5},{7,6},{8,15},{9,8},{10,9... | collective-permute-start | bytes 393224 | tf_op jit(solution)/shard_map/ppermute | solution.py:42
  123.7 7.1 %collective-permute-start.20 = (bf16[64,2048]{1,0:T(8,128)(2,1)S(1)}, bf16[64,2048]{1,0:T(8,128)(2,1)S(1)}, u32[]{:S(2)}, u32[]{:S(2)}) collective-permute-start(bf16[64,2048]{1,0:T(8,128)(2,1)S(1)} %get-tuple-element.6), channel_id=1, source_target_pairs={{0,7},{1,0},{2,1},{3,2},{4,3},{5,4},{6,5},{7,6},{8,15},{9,8},{10,9... | collective-permute-start | bytes 786440 | tf_op jit(solution)/shard_map/ppermute | solution.py:42
  130.8 8.2 %collective-permute-start.21 = (bf16[64,2048]{1,0:T(8,128)(2,1)S(1)}, bf16[64,2048]{1,0:T(8,128)(2,1)S(1)}, u32[]{:S(2)}, u32[]{:S(2)}) collective-permute-start(bf16[64,2048]{1,0:T(8,128)(2,1)S(1)} %fusion.3), channel_id=1, source_target_pairs={{0,7},{1,0},{2,1},{3,2},{4,3},{5,4},{6,5},{7,6},{8,15},{9,8},{10,9... | collective-permute-start | bytes 786440 | tf_op jit(solution)/shard_map/ppermute | solution.py:42
  132.9 8.8 %collective-permute-start.18 = (bf16[64,2048]{1,0:T(8,128)(2,1)S(1)}, bf16[64,2048]{1,0:T(8,128)(2,1)S(1)}, u32[]{:S(2)}, u32[]{:S(2)}) collective-permute-start(bf16[64,2048]{1,0:T(8,128)(2,1)S(1)} %get-tuple-element.5), channel_id=1, source_target_pairs={{0,1},{1,2},{2,3},{3,4},{4,5},{5,6},{6,7},{7,0},{8,9},{9,10},{10,1... | collective-permute-start | bytes 786440 | tf_op jit(solution)/shard_map/ppermute | solution.py:42
  139.1 6.5 %collective-permute-start.22 = (bf16[64,2048]{1,0:T(8,128)(2,1)S(1)}, bf16[64,2048]{1,0:T(8,128)(2,1)S(1)}, u32[]{:S(2)}, u32[]{:S(2)}) collective-permute-start(bf16[64,2048]{1,0:T(8,128)(2,1)S(1)} %fusion.4), channel_id=1, source_target_pairs={{0,7},{1,0},{2,1},{3,2},{4,3},{5,4},{6,5},{7,6},{8,15},{9,8},{10,9... | collective-permute-start | bytes 786440 | tf_op jit(solution)/shard_map/ppermute | solution.py:42
  146.8 5.2 %collective-permute-start.23 = (bf16[16,1024]{1,0:T(8,128)(2,1)S(1)}, bf16[16,1024]{1,0:T(8,128)(2,1)S(1)}, u32[]{:S(2)}, u32[]{:S(2)}) collective-permute-start(bf16[16,1024]{1,0:T(8,128)(2,1)S(1)} %slice.42), channel_id=1, source_target_pairs={{0,8},{8,16},{16,24},{24,0},{1,9},{9,17},{17,25},{25,1},{2,10},{10... | collective-permute-start | bytes 98312 | tf_op jit(solution)/shard_map/ppermute | solution.py:42
  146.9 5.1 %collective-permute-start.25 = (bf16[16,1024]{1,0:T(8,128)(2,1)S(1)}, bf16[16,1024]{1,0:T(8,128)(2,1)S(1)}, u32[]{:S(2)}, u32[]{:S(2)}) collective-permute-start(bf16[16,1024]{1,0:T(8,128)(2,1)S(1)} %slice.43), channel_id=1, source_target_pairs={{0,24},{8,0},{16,8},{24,16},{1,25},{9,1},{17,9},{25,17},{2,26},{10... | collective-permute-start | bytes 98312 | tf_op jit(solution)/shard_map/ppermute | solution.py:42
  152.0 5.6 %collective-permute-start.24 = (bf16[16,2048]{1,0:T(8,128)(2,1)S(1)}, bf16[16,2048]{1,0:T(8,128)(2,1)S(1)}, u32[]{:S(2)}, u32[]{:S(2)}) collective-permute-start(bf16[16,2048]{1,0:T(8,128)(2,1)S(1)} %get-tuple-element.13), channel_id=1, source_target_pairs={{0,8},{8,16},{16,24},{24,0},{1,9},{9,17},{17,25},{25,1},{2,10},{10... | collective-permute-start | bytes 196616 | tf_op jit(solution)/shard_map/ppermute | solution.py:42
  152.1 5.5 %collective-permute-start.26 = (bf16[16,2048]{1,0:T(8,128)(2,1)S(1)}, bf16[16,2048]{1,0:T(8,128)(2,1)S(1)}, u32[]{:S(2)}, u32[]{:S(2)}) collective-permute-start(bf16[16,2048]{1,0:T(8,128)(2,1)S(1)} %get-tuple-element.14), channel_id=1, source_target_pairs={{0,24},{8,0},{16,8},{24,16},{1,25},{9,1},{17,9},{25,17},{2,26},{10... | collective-permute-start | bytes 196616 | tf_op jit(solution)/shard_map/ppermute | solution.py:42

commit v16 on v12

--- a/solution.py
+++ b/solution.py
@@ -35,8 +35,9 @@
     own = get(k)
     h = own.shape[-1] // 2
 
+    far = get(k + nf)
+
     def side(perm, sign, cols):
-        far = get(k + sign * nf)
         acc = far[..., :h] if cols == 0 else far[..., h:]
         for s in range(nf):
             got = lax.ppermute(acc.astype(send_dtype), axis, perm).astype(jnp.float32)

time: 145 us -> 148 us (1.021)
    dot_general x9 -> x8, matrix products: 8.91 us -> 10.2 us  [on_device(): jnp.dot(lax.dynamic_index_in_dim(act_blocks, i, 0, keepdims=False), down_...]
  transfers between devices with their start and end apart: 27 -> 27, of which waited for: 20 -> 20; matrix products, arithmetic and copies ran while one was open for 13% -> 14% of each run, Pallas kernels for 0% -> 0%
where the time goes in v16:
time: 148 us; the launch traced here: 146 us
  waiting for transfers between devices  57.7 us (39%)
  starting transfers between devices  41.6 us (28%)
  matrix products  23.5 us (16%)
  blocking collectives  14.5 us (10%)
  other arithmetic  4.51 us (3%)
  local copies, waits for them, and re-layouts  3.76 us (3%)
    ppermute x16, waiting for transfers between devices, side(): got = lax.ppermute(acc.astype(send_dtype), axis, perm).astype(jnp.float32)  37.4 us
    ppermute x16, starting transfers between devices, side(): got = lax.ppermute(acc.astype(send_dtype), axis, perm).astype(jnp.float32)  24.4 us
    ppermute x6, waiting for transfers between devices, ring_ag(): buf = lax.ppermute(buf, axis, fwd)  15.3 us
    all_gather x1, blocking collectives, on_device(): activated = lax.all_gather(activated, EMBED, axis=0, tiled=True)  14.5 us
    ppermute x4, starting transfers between devices, ring_ag(): buf = lax.ppermute(buf, axis, bwd)  12.9 us
    dot_general x8, matrix products, on_device(): jnp.dot(lax.dynamic_index_in_dim(act_blocks, i, 0, keepdims=False), down_...  10.2 us
    dot_general x8, matrix products, on_device(): jnp.dot(v, gate_weight, preferred_element_type=jnp.float32)  7.67 us
    dot_general x8, matrix products, on_device(): jnp.dot(v, up_weight, preferred_element_type=jnp.float32)  5.67 us
  transfers between devices with their start and end apart: 27, of which 20 were waited for; matrix products, arithmetic and copies ran while one was open for 14% of the time, Pallas kernels for 0%

profile of v16, /device:TPU:2, one launch (start us, length us, event | category | flops | bytes accessed | tf_op | source)
XLA Modules:
  0.0 146.1 jit_solution(8452634923310357136)
XLA Ops:
  0.0 1.6 %collective-permute-start = (bf16[16,2048]{1,0:T(8,128)(2,1)}, bf16[16,2048]{1,0:T(8,128)(2,1)S(1)}, u32[]{:S(2)}, u32[]{:S(2)}) collective-permute-start(bf16[16,2048]{1,0:T(8,128)(2,1)} %param.4), channel_id=1, source_target_pairs={{0,8},{8,16},{16,24},{24,0},{1,9},{9,17},{17,25},{25,1},{2,10},{10... | collective-permute-start | bytes 196616 | tf_op jit(solution)/shard_map/ppermute | solution.py:20
  1.6 1.7 %collective-permute-start.2 = (bf16[16,2048]{1,0:T(8,128)(2,1)}, bf16[16,2048]{1,0:T(8,128)(2,1)S(1)}, u32[]{:S(2)}, u32[]{:S(2)}) collective-permute-start(bf16[16,2048]{1,0:T(8,128)(2,1)} %param.4), channel_id=1, source_target_pairs={{0,24},{8,0},{16,8},{24,16},{1,25},{9,1},{17,9},{25,17},{2,26},{10... | collective-permute-start | bytes 196616 | tf_op jit(solution)/shard_map/ppermute | solution.py:24
  3.3 0.9 bitcast_dynamic-update-slice_fusion.3
  4.1 1.6 %collective-permute-done = bf16[16,2048]{1,0:T(8,128)(2,1)S(1)} collective-permute-done((bf16[16,2048]{1,0:T(8,128)(2,1)}, bf16[16,2048]{1,0:T(8,128)(2,1)S(1)}, u32[]{:S(2)}, u32[]{:S(2)}) %collective-permute-start) | collective-permute-done | bytes 65568 | tf_op jit(solution)/shard_map/ppermute | solution.py:20
  6.1 5.1 %collective-permute-done.1 = bf16[16,2048]{1,0:T(8,128)(2,1)S(1)} collective-permute-done((bf16[16,2048]{1,0:T(8,128)(2,1)S(1)}, bf16[16,2048]{1,0:T(8,128)(2,1)S(1)}, u32[]{:S(2)}, u32[]{:S(2)}) %collective-permute-start.1) | collective-permute-done | bytes 65568 | tf_op jit(solution)/shard_map/ppermute | solution.py:20
  11.2 2.0 %collective-permute-start.3 = (bf16[64,2048]{1,0:T(8,128)(2,1)S(1)}, bf16[64,2048]{1,0:T(8,128)(2,1)S(1)}, u32[]{:S(2)}, u32[]{:S(2)}) collective-permute-start(bf16[64,2048]{1,0:T(8,128)(2,1)S(1)} %bitcast.160), channel_id=1, source_target_pairs={{0,1},{1,2},{2,3},{3,4},{4,5},{5,6},{6,7},{7,0},{8,9},{9,10},{10,1... | collective-permute-start | bytes 786440 | tf_op jit(solution)/shard_map/ppermute | solution.py:20
  13.2 4.0 %collective-permute-start.7 = (bf16[64,2048]{1,0:T(8,128)(2,1)S(1)}, bf16[64,2048]{1,0:T(8,128)(2,1)S(1)}, u32[]{:S(2)}, u32[]{:S(2)}) collective-permute-start(bf16[64,2048]{1,0:T(8,128)(2,1)S(1)} %bitcast.161), channel_id=1, source_target_pairs={{0,7},{1,0},{2,1},{3,2},{4,3},{5,4},{6,5},{7,6},{8,15},{9,8},{10,9... | collective-permute-start | bytes 786440 | tf_op jit(solution)/shard_map/ppermute | solution.py:24
  17.2 2.7 %fusion.61 = f32[64,896]{1,0:T(8,128)S(1)} fusion(bf16[64,2048]{1,0:T(8,128)(2,1)S(1)} %bitcast.162, bf16[2048,896]{1,0:T(8,128)(2,1)} %param.5), kind=kOutput, calls=%fused_computation.80 | convolution fusion | flops 234881024 | bytes 4161536 | tf_op jit(solution)/shard_map/dot_general | solution.py:87
  20.0 0.7 fusion.62
  21.5 0.5 copy-done.1
  22.0 0.7 fusion.63
  22.8 0.7 fusion.64
  23.5 0.7 fusion.71
  24.2 0.7 fusion.72
  24.9 3.3 %collective-permute-start.8 = (bf16[64,2048]{1,0:T(8,128)(2,1)S(1)}, bf16[64,2048]{1,0:T(8,128)(2,1)S(1)}, u32[]{:S(2)}, u32[]{:S(2)}) collective-permute-start(bf16[64,2048]{1,0:T(8,128)(2,1)S(1)} %collective-permute-done.7), channel_id=1, source_target_pairs={{0,7},{1,0},{2,1},{3,2},{4,3},{5,4},{6,5},{7,6},{8,15},{9,8},{10,9... | collective-permute-start | bytes 786440 | tf_op jit(solution)/shard_map/ppermute | solution.py:24
  28.3 2.1 %collective-permute-done.4 = bf16[64,2048]{1,0:T(8,128)(2,1)S(1)} collective-permute-done((bf16[64,2048]{1,0:T(8,128)(2,1)S(1)}, bf16[64,2048]{1,0:T(8,128)(2,1)S(1)}, u32[]{:S(2)}, u32[]{:S(2)}) %collective-permute-start.4) | collective-permute-done | bytes 262176 | tf_op jit(solution)/shard_map/ppermute | solution.py:20
  30.4 0.7 fusion.65
  31.2 0.7 fusion.66
  32.1 0.7 fusion.73
  32.8 0.7 fusion.74
  33.6 3.9 %collective-permute-start.9 = (bf16[64,2048]{1,0:T(8,128)(2,1)S(1)}, bf16[64,2048]{1,0:T(8,128)(2,1)S(1)}, u32[]{:S(2)}, u32[]{:S(2)}) collective-permute-start(bf16[64,2048]{1,0:T(8,128)(2,1)S(1)} %collective-permute-done.8), channel_id=1, source_target_pairs={{0,7},{1,0},{2,1},{3,2},{4,3},{5,4},{6,5},{7,6},{8,15},{9,8},{10,9... | collective-permute-start | bytes 786440 | tf_op jit(solution)/shard_map/ppermute | solution.py:24
  37.5 1.5 %collective-permute-done.5 = bf16[64,2048]{1,0:T(8,128)(2,1)S(1)} collective-permute-done((bf16[64,2048]{1,0:T(8,128)(2,1)S(1)}, bf16[64,2048]{1,0:T(8,128)(2,1)S(1)}, u32[]{:S(2)}, u32[]{:S(2)}) %collective-permute-start.5) | collective-permute-done | bytes 262176 | tf_op jit(solution)/shard_map/ppermute | solution.py:20
  39.1 0.7 fusion.67
  39.9 0.7 fusion.68
  40.6 0.8 collective-permute-done.9
  41.4 0.7 fusion.75
  42.1 0.7 fusion.76
  42.9 4.6 %collective-permute-done.6 = bf16[64,2048]{1,0:T(8,128)(2,1)S(1)} collective-permute-done((bf16[64,2048]{1,0:T(8,128)(2,1)S(1)}, bf16[64,2048]{1,0:T(8,128)(2,1)S(1)}, u32[]{:S(2)}, u32[]{:S(2)}) %collective-permute-start.6) | collective-permute-done | bytes 262176 | tf_op jit(solution)/shard_map/ppermute | solution.py:20
  47.4 0.7 fusion.69
  48.2 0.7 fusion.70
  49.0 1.8 %copy-done.3 = f32[8,64,1792]{2,1,0:T(8,128)} copy-done((f32[8,64,1792]{2,1,0:T(8,128)}, f32[8,64,1792]{2,1,0:T(8,128)S(1)}, u32[]{:S(2)}) %copy-start.3) | copy-done | bytes 3670040
  51.1 3.9 %collective-permute-done.10 = f32[4,64,1792]{2,1,0:T(8,128)} collective-permute-done((f32[4,64,1792]{2,1,0:T(8,128)S(1)}, f32[4,64,1792]{2,1,0:T(8,128)}, u32[]{:S(2)}, u32[]{:S(2)}) %collective-permute-start.10) | collective-permute-done | bytes 1835040 | tf_op jit(solution)/shard_map/ppermute | solution.py:70
  55.0 2.2 %bitcast_add_fusion = f32[4,64,1792]{2,1,0:T(8,128)S(1)} fusion(f32[4,64,1792]{2,1,0:T(8,128)} %collective-permute-done.10, f32[4,2,64,1792]{3,2,1,0:T(8,128)} %bitcast.151, s32[]{:T(128)S(6)} %select_n.193), kind=kLoop, calls=%fused_computation.1 | loop fusion | flops 458752 | bytes 5505028 | tf_op jit(solution)/shard_map/add | solution.py:71
  57.3 1.6 %collective-permute-start.11 = (f32[64,896]{1,0:T(8,128)S(1)}, f32[64,896]{1,0:T(8,128)S(1)}, u32[]{:S(2)}, u32[]{:S(2)}) collective-permute-start(f32[64,896]{1,0:T(8,128)S(1)} %get-tuple-element.9), channel_id=1, source_target_pairs={{0,64},{64,128},{128,192},{192,0},{1,65},{65,129},{129,193},{193,1... | collective-permute-start | bytes 688136 | tf_op jit(solution)/shard_map/ppermute | solution.py:43
  58.9 0.5 collective-permute-start.13
  59.4 5.6 %collective-permute-done.11 = f32[64,896]{1,0:T(8,128)S(1)} collective-permute-done((f32[64,896]{1,0:T(8,128)S(1)}, f32[64,896]{1,0:T(8,128)S(1)}, u32[]{:S(2)}, u32[]{:S(2)}) %collective-permute-start.11) | collective-permute-done | bytes 229408 | tf_op jit(solution)/shard_map/ppermute | solution.py:43
  65.0 1.2 collective-permute-done.13
  66.3 1.3 collective-permute-start.12
  67.6 0.8 collective-permute-start.14
  68.4 9.4 %collective-permute-done.12 = f32[64,1792]{1,0:T(8,128)S(1)} collective-permute-done((f32[64,1792]{1,0:T(8,128)S(1)}, f32[64,1792]{1,0:T(8,128)S(1)}, u32[]{:S(2)}, u32[]{:S(2)}) %collective-permute-start.12) | collective-permute-done | bytes 458784 | tf_op jit(solution)/shard_map/ppermute | solution.py:43
  77.8 1.0 collective-permute-done.14
  78.8 1.1 fusion.8
  80.0 14.5 %all_gather.3 = bf16[512,896]{1,0:T(8,128)(2,1)S(1)} all-gather(bf16[64,896]{1,0:T(8,128)(2,1)S(1)} %fusion.9), channel_id=1, replica_groups=mesh['ex'=4,'ec'=2,'hy'=4,'hz'=8] {'ex','ec'}, dimensions={0}, use_global_device_ids=true | all-gather | bytes 1032192 | tf_op jit(solution)/shard_map/all_gather | solution.py:95
  94.5 2.8 %convolution_convert_fusion = bf16[64,2048]{1,0:T(8,128)(2,1)S(1)} fusion(bf16[896,2048]{1,0:T(8,128)(2,1)} %param.7, bf16[8,64,896]{2,1,0:T(8,128)(2,1)S(1)} %bitcast.152, s32[]{:T(128)S(6)} %select_n.206), kind=kOutput, calls=%fused_computation | convolution fusion | flops 235012096 | bytes 4046852 | tf_op jit(solution)/shard_map/dot_general | solution.py:97
  97.5 3.2 %collective-permute-start.19 = (bf16[64,1024]{1,0:T(8,128)(2,1)S(1)}, bf16[64,1024]{1,0:T(8,128)(2,1)S(1)}, u32[]{:S(2)}, u32[]{:S(2)}) collective-permute-start(bf16[64,1024]{1,0:T(8,128)(2,1)S(1)} %get-tuple-element.12), channel_id=1, source_target_pairs={{0,7},{1,0},{2,1},{3,2},{4,3},{5,4},{6,5},{7,6},{8,15},{9,8},{10,9... | collective-permute-start | bytes 393224 | tf_op jit(solution)/shard_map/ppermute | solution.py:43
  100.6 3.7 %collective-permute-done.15 = bf16[64,1024]{1,0:T(8,128)(2,1)S(1)} collective-permute-done((bf16[64,1024]{1,0:T(8,128)(2,1)S(1)}, bf16[64,1024]{1,0:T(8,128)(2,1)S(1)}, u32[]{:S(2)}, u32[]{:S(2)}) %collective-permute-start.15) | collective-permute-done | bytes 131104 | tf_op jit(solution)/shard_map/ppermute | solution.py:43
  104.4 2.8 %add_convert_fusion.5 = bf16[64,2048]{1,0:T(8,128)(2,1)S(1)} fusion(bf16[64,1024]{1,0:T(8,128)(2,1)S(1)} %collective-permute-done.15, bf16[896,2048]{1,0:T(8,128)(2,1)} %param.7, bf16[8,64,896]{2,1,0:T(8,128)(2,1)S(1)} %bitcast.153, s32[]{:T(128)S(6)} %select_n.192), kind=kOutput, calls=%fused_computation.9 | convolution fusion | flops 235274240 | bytes 4177924 | tf_op jit(solution)/shard_map/dot_general | solution.py:97
  107.5 0.8 add_convert_fusion.2
  108.3 3.3 %collective-permute-start.20 = (bf16[64,2048]{1,0:T(8,128)(2,1)S(1)}, bf16[64,2048]{1,0:T(8,128)(2,1)S(1)}, u32[]{:S(2)}, u32[]{:S(2)}) collective-permute-start(bf16[64,2048]{1,0:T(8,128)(2,1)S(1)} %add_convert_fusion.2), channel_id=1, source_target_pairs={{0,7},{1,0},{2,1},{3,2},{4,3},{5,4},{6,5},{7,6},{8,15},{9,8},{10,9... | collective-permute-start | bytes 786440 | tf_op jit(solution)/shard_map/ppermute | solution.py:43
  111.6 4.9 %collective-permute-done.16 = bf16[64,2048]{1,0:T(8,128)(2,1)S(1)} collective-permute-done((bf16[64,2048]{1,0:T(8,128)(2,1)S(1)}, bf16[64,2048]{1,0:T(8,128)(2,1)S(1)}, u32[]{:S(2)}, u32[]{:S(2)}) %collective-permute-start.16) | collective-permute-done | bytes 262176 | tf_op jit(solution)/shard_map/ppermute | solution.py:43
  116.4 0.8 add_convert_fusion.4
  117.3 0.8 add_convert_fusion.1
  118.1 3.3 %collective-permute-start.21 = (bf16[64,2048]{1,0:T(8,128)(2,1)S(1)}, bf16[64,2048]{1,0:T(8,128)(2,1)S(1)}, u32[]{:S(2)}, u32[]{:S(2)}) collective-permute-start(bf16[64,2048]{1,0:T(8,128)(2,1)S(1)} %add_convert_fusion.1), channel_id=1, source_target_pairs={{0,7},{1,0},{2,1},{3,2},{4,3},{5,4},{6,5},{7,6},{8,15},{9,8},{10,9... | collective-permute-start | bytes 786440 | tf_op jit(solution)/shard_map/ppermute | solution.py:43
  121.4 4.0 %collective-permute-done.17 = bf16[64,2048]{1,0:T(8,128)(2,1)S(1)} collective-permute-done((bf16[64,2048]{1,0:T(8,128)(2,1)S(1)}, bf16[64,2048]{1,0:T(8,128)(2,1)S(1)}, u32[]{:S(2)}, u32[]{:S(2)}) %collective-permute-start.17) | collective-permute-done | bytes 262176 | tf_op jit(solution)/shard_map/ppermute | solution.py:43
  125.3 0.8 add_convert_fusion.3
  126.2 0.8 add_convert_fusion
  127.0 3.3 %collective-permute-start.22 = (bf16[64,2048]{1,0:T(8,128)(2,1)S(1)}, bf16[64,2048]{1,0:T(8,128)(2,1)S(1)}, u32[]{:S(2)}, u32[]{:S(2)}) collective-permute-start(bf16[64,2048]{1,0:T(8,128)(2,1)S(1)} %add_convert_fusion), channel_id=1, source_target_pairs={{0,7},{1,0},{2,1},{3,2},{4,3},{5,4},{6,5},{7,6},{8,15},{9,8},{10,9... | collective-permute-start | bytes 786440 | tf_op jit(solution)/shard_map/ppermute | solution.py:43
  130.3 0.8 fusion.31
  131.0 2.7 %collective-permute-done.18 = bf16[64,2048]{1,0:T(8,128)(2,1)S(1)} collective-permute-done((bf16[64,2048]{1,0:T(8,128)(2,1)S(1)}, bf16[64,2048]{1,0:T(8,128)(2,1)S(1)}, u32[]{:S(2)}, u32[]{:S(2)}) %collective-permute-start.18) | collective-permute-done | bytes 262176 | tf_op jit(solution)/shard_map/ppermute | solution.py:43
  134.4 3.2 %collective-permute-start.25 = (bf16[16,1024]{1,0:T(8,128)(2,1)S(1)}, bf16[16,1024]{1,0:T(8,128)(2,1)S(1)}, u32[]{:S(2)}, u32[]{:S(2)}) collective-permute-start(bf16[16,1024]{1,0:T(8,128)(2,1)S(1)} %get-tuple-element.14), channel_id=1, source_target_pairs={{0,24},{8,0},{16,8},{24,16},{1,25},{9,1},{17,9},{25,17},{2,26},{10... | collective-permute-start | bytes 98312 | tf_op jit(solution)/shard_map/ppermute | solution.py:43
  137.6 2.2 %collective-permute-done.23 = bf16[16,1024]{1,0:T(8,128)(2,1)S(1)} collective-permute-done((bf16[16,1024]{1,0:T(8,128)(2,1)S(1)}, bf16[16,1024]{1,0:T(8,128)(2,1)S(1)}, u32[]{:S(2)}, u32[]{:S(2)}) %collective-permute-start.23) | collective-permute-done | bytes 32800 | tf_op jit(solution)/shard_map/ppermute | solution.py:43
  139.9 3.2 %collective-permute-start.26 = (bf16[16,2048]{1,0:T(8,128)(2,1)S(1)}, bf16[16,2048]{1,0:T(8,128)(2,1)S(1)}, u32[]{:S(2)}, u32[]{:S(2)}) collective-permute-start(bf16[16,2048]{1,0:T(8,128)(2,1)S(1)} %get-tuple-element.8), channel_id=1, source_target_pairs={{0,24},{8,0},{16,8},{24,16},{1,25},{9,1},{17,9},{25,17},{2,26},{10... | collective-permute-start | bytes 196616 | tf_op jit(solution)/shard_map/ppermute | solution.py:43
  143.2 2.2 %collective-permute-done.24 = bf16[16,2048]{1,0:T(8,128)(2,1)S(1)} collective-permute-done((bf16[16,2048]{1,0:T(8,128)(2,1)S(1)}, bf16[16,2048]{1,0:T(8,128)(2,1)S(1)}, u32[]{:S(2)}, u32[]{:S(2)}) %collective-permute-start.24) | collective-permute-done | bytes 65568 | tf_op jit(solution)/shard_map/ppermute | solution.py:43
  145.4 0.7 fusion.13
  (50 shorter events, 3.7 us)
Async XLA Ops:
  0.0 5.7 %collective-permute-start = (bf16[16,2048]{1,0:T(8,128)(2,1)}, bf16[16,2048]{1,0:T(8,128)(2,1)S(1)}, u32[]{:S(2)}, u32[]{:S(2)}) collective-permute-start(bf16[16,2048]{1,0:T(8,128)(2,1)} %param.4), channel_id=1, source_target_pairs={{0,8},{8,16},{16,24},{24,0},{1,9},{9,17},{17,25},{25,1},{2,10},{10... | collective-permute-start | bytes 196616 | tf_op jit(solution)/shard_map/ppermute | solution.py:20
  1.6 9.6 %collective-permute-start.2 = (bf16[16,2048]{1,0:T(8,128)(2,1)}, bf16[16,2048]{1,0:T(8,128)(2,1)S(1)}, u32[]{:S(2)}, u32[]{:S(2)}) collective-permute-start(bf16[16,2048]{1,0:T(8,128)(2,1)} %param.4), channel_id=1, source_target_pairs={{0,24},{8,0},{16,8},{24,16},{1,25},{9,1},{17,9},{25,17},{2,26},{10... | collective-permute-start | bytes 196616 | tf_op jit(solution)/shard_map/ppermute | solution.py:24
  4.1 15.9 %copy-start.2 = (bf16[2048,896]{1,0:T(8,128)(2,1)S(1)}, bf16[2048,896]{1,0:T(8,128)(2,1)}, u32[]{:S(2)}) copy-start(bf16[2048,896]{1,0:T(8,128)(2,1)} %param.6) | copy-start | bytes 11010052
  5.7 5.5 %collective-permute-start.1 = (bf16[16,2048]{1,0:T(8,128)(2,1)S(1)}, bf16[16,2048]{1,0:T(8,128)(2,1)S(1)}, u32[]{:S(2)}, u32[]{:S(2)}) collective-permute-start(bf16[16,2048]{1,0:T(8,128)(2,1)S(1)} %collective-permute-done), channel_id=1, source_target_pairs={{0,8},{8,16},{16,24},{24,0},{1,9},{9,17},{17,25},{25,1},{2,10},{10... | collective-permute-start | bytes 196616 | tf_op jit(solution)/shard_map/ppermute | solution.py:20
  11.2 10.3 %collective-permute-start.3 = (bf16[64,2048]{1,0:T(8,128)(2,1)S(1)}, bf16[64,2048]{1,0:T(8,128)(2,1)S(1)}, u32[]{:S(2)}, u32[]{:S(2)}) collective-permute-start(bf16[64,2048]{1,0:T(8,128)(2,1)S(1)} %bitcast.160), channel_id=1, source_target_pairs={{0,1},{1,2},{2,3},{3,4},{4,5},{5,6},{6,7},{7,0},{8,9},{9,10},{10,1... | collective-permute-start | bytes 786440 | tf_op jit(solution)/shard_map/ppermute | solution.py:20
  13.2 10.3 %collective-permute-start.7 = (bf16[64,2048]{1,0:T(8,128)(2,1)S(1)}, bf16[64,2048]{1,0:T(8,128)(2,1)S(1)}, u32[]{:S(2)}, u32[]{:S(2)}) collective-permute-start(bf16[64,2048]{1,0:T(8,128)(2,1)S(1)} %bitcast.161), channel_id=1, source_target_pairs={{0,7},{1,0},{2,1},{3,2},{4,3},{5,4},{6,5},{7,6},{8,15},{9,8},{10,9... | collective-permute-start | bytes 786440 | tf_op jit(solution)/shard_map/ppermute | solution.py:24
  20.0 2.0 %copy-start.1 = (bf16[2048,896]{1,0:T(8,128)(2,1)S(1)}, bf16[2048,896]{1,0:T(8,128)(2,1)}, u32[]{:S(2)}) copy-start(bf16[2048,896]{1,0:T(8,128)(2,1)} %param.5) | copy-start | bytes 11010052
  22.7 7.7 %collective-permute-start.4 = (bf16[64,2048]{1,0:T(8,128)(2,1)S(1)}, bf16[64,2048]{1,0:T(8,128)(2,1)S(1)}, u32[]{:S(2)}, u32[]{:S(2)}) collective-permute-start(bf16[64,2048]{1,0:T(8,128)(2,1)S(1)} %collective-permute-done.3), channel_id=1, source_target_pairs={{0,1},{1,2},{2,3},{3,4},{4,5},{5,6},{6,7},{7,0},{8,9},{9,10},{10,1... | collective-permute-start | bytes 786440 | tf_op jit(solution)/shard_map/ppermute | solution.py:20
  24.9 7.2 %collective-permute-start.8 = (bf16[64,2048]{1,0:T(8,128)(2,1)S(1)}, bf16[64,2048]{1,0:T(8,128)(2,1)S(1)}, u32[]{:S(2)}, u32[]{:S(2)}) collective-permute-start(bf16[64,2048]{1,0:T(8,128)(2,1)S(1)} %collective-permute-done.7), channel_id=1, source_target_pairs={{0,7},{1,0},{2,1},{3,2},{4,3},{5,4},{6,5},{7,6},{8,15},{9,8},{10,9... | collective-permute-start | bytes 786440 | tf_op jit(solution)/shard_map/ppermute | solution.py:24
  31.1 8.0 %collective-permute-start.5 = (bf16[64,2048]{1,0:T(8,128)(2,1)S(1)}, bf16[64,2048]{1,0:T(8,128)(2,1)S(1)}, u32[]{:S(2)}, u32[]{:S(2)}) collective-permute-start(bf16[64,2048]{1,0:T(8,128)(2,1)S(1)} %collective-permute-done.4), channel_id=1, source_target_pairs={{0,1},{1,2},{2,3},{3,4},{4,5},{5,6},{6,7},{7,0},{8,9},{9,10},{10,1... | collective-permute-start | bytes 786440 | tf_op jit(solution)/shard_map/ppermute | solution.py:20
  33.6 7.8 %collective-permute-start.9 = (bf16[64,2048]{1,0:T(8,128)(2,1)S(1)}, bf16[64,2048]{1,0:T(8,128)(2,1)S(1)}, u32[]{:S(2)}, u32[]{:S(2)}) collective-permute-start(bf16[64,2048]{1,0:T(8,128)(2,1)S(1)} %collective-permute-done.8), channel_id=1, source_target_pairs={{0,7},{1,0},{2,1},{3,2},{4,3},{5,4},{6,5},{7,6},{8,15},{9,8},{10,9... | collective-permute-start | bytes 786440 | tf_op jit(solution)/shard_map/ppermute | solution.py:24
  39.8 7.7 %collective-permute-start.6 = (bf16[64,2048]{1,0:T(8,128)(2,1)S(1)}, bf16[64,2048]{1,0:T(8,128)(2,1)S(1)}, u32[]{:S(2)}, u32[]{:S(2)}) collective-permute-start(bf16[64,2048]{1,0:T(8,128)(2,1)S(1)} %collective-permute-done.5), channel_id=1, source_target_pairs={{0,1},{1,2},{2,3},{3,4},{4,5},{5,6},{6,7},{7,0},{8,9},{9,10},{10,1... | collective-permute-start | bytes 786440 | tf_op jit(solution)/shard_map/ppermute | solution.py:20
  49.0 1.8 %copy-start.3 = (f32[8,64,1792]{2,1,0:T(8,128)}, f32[8,64,1792]{2,1,0:T(8,128)S(1)}, u32[]{:S(2)}) copy-start(f32[8,64,1792]{2,1,0:T(8,128)S(1)} %fusion.7) | copy-start | bytes 11010052
  51.0 4.0 %collective-permute-start.10 = (f32[4,64,1792]{2,1,0:T(8,128)S(1)}, f32[4,64,1792]{2,1,0:T(8,128)}, u32[]{:S(2)}, u32[]{:S(2)}) collective-permute-start(f32[4,64,1792]{2,1,0:T(8,128)S(1)} %dynamic-slice_bitcast_fusion), channel_id=1, source_target_pairs={{0,32},{32,0},{1,33},{33,1},{2,34},{34,2},{3,35},{35,3},{4,36},{36... | collective-permute-start | bytes 5505032 | tf_op jit(solution)/shard_map/ppermute | solution.py:70
  57.3 7.7 %collective-permute-start.11 = (f32[64,896]{1,0:T(8,128)S(1)}, f32[64,896]{1,0:T(8,128)S(1)}, u32[]{:S(2)}, u32[]{:S(2)}) collective-permute-start(f32[64,896]{1,0:T(8,128)S(1)} %get-tuple-element.9), channel_id=1, source_target_pairs={{0,64},{64,128},{128,192},{192,0},{1,65},{65,129},{129,193},{193,1... | collective-permute-start | bytes 688136 | tf_op jit(solution)/shard_map/ppermute | solution.py:43
  58.9 7.4 %collective-permute-start.13 = (f32[64,896]{1,0:T(8,128)S(1)}, f32[64,896]{1,0:T(8,128)S(1)}, u32[]{:S(2)}, u32[]{:S(2)}) collective-permute-start(f32[64,896]{1,0:T(8,128)S(1)} %get-tuple-element.10), channel_id=1, source_target_pairs={{0,192},{64,0},{128,64},{192,128},{1,193},{65,1},{129,65},{193,129... | collective-permute-start | bytes 688136 | tf_op jit(solution)/shard_map/ppermute | solution.py:43
  66.3 11.5 %collective-permute-start.12 = (f32[64,1792]{1,0:T(8,128)S(1)}, f32[64,1792]{1,0:T(8,128)S(1)}, u32[]{:S(2)}, u32[]{:S(2)}) collective-permute-start(f32[64,1792]{1,0:T(8,128)S(1)} %get-tuple-element.5), channel_id=1, source_target_pairs={{0,64},{64,128},{128,192},{192,0},{1,65},{65,129},{129,193},{193,1... | collective-permute-start | bytes 1376264 | tf_op jit(solution)/shard_map/ppermute | solution.py:43
  67.6 11.2 %collective-permute-start.14 = (f32[64,1792]{1,0:T(8,128)S(1)}, f32[64,1792]{1,0:T(8,128)}, u32[]{:S(2)}, u32[]{:S(2)}) collective-permute-start(f32[64,1792]{1,0:T(8,128)S(1)} %get-tuple-element.6), channel_id=1, source_target_pairs={{0,192},{64,0},{128,64},{192,128},{1,193},{65,1},{129,65},{193,129... | collective-permute-start | bytes 1376264 | tf_op jit(solution)/shard_map/ppermute | solution.py:43
  97.3 7.0 %collective-permute-start.15 = (bf16[64,1024]{1,0:T(8,128)(2,1)S(1)}, bf16[64,1024]{1,0:T(8,128)(2,1)S(1)}, u32[]{:S(2)}, u32[]{:S(2)}) collective-permute-start(bf16[64,1024]{1,0:T(8,128)(2,1)S(1)} %get-tuple-element.11), channel_id=1, source_target_pairs={{0,1},{1,2},{2,3},{3,4},{4,5},{5,6},{6,7},{7,0},{8,9},{9,10},{10,1... | collective-permute-start | bytes 393224 | tf_op jit(solution)/shard_map/ppermute | solution.py:43
  97.4 10.0 %copy-start = (bf16[896,2048]{1,0:T(8,128)(2,1)S(1)}, bf16[896,2048]{1,0:T(8,128)(2,1)}, u32[]{:S(2)}) copy-start(bf16[896,2048]{1,0:T(8,128)(2,1)} %param.7) | copy-start | bytes 11010052
  97.5 10.0 %collective-permute-start.19 = (bf16[64,1024]{1,0:T(8,128)(2,1)S(1)}, bf16[64,1024]{1,0:T(8,128)(2,1)S(1)}, u32[]{:S(2)}, u32[]{:S(2)}) collective-permute-start(bf16[64,1024]{1,0:T(8,128)(2,1)S(1)} %get-tuple-element.12), channel_id=1, source_target_pairs={{0,7},{1,0},{2,1},{3,2},{4,3},{5,4},{6,5},{7,6},{8,15},{9,8},{10,9... | collective-permute-start | bytes 393224 | tf_op jit(solution)/shard_map/ppermute | solution.py:43
  107.2 9.3 %collective-permute-start.16 = (bf16[64,2048]{1,0:T(8,128)(2,1)S(1)}, bf16[64,2048]{1,0:T(8,128)(2,1)S(1)}, u32[]{:S(2)}, u32[]{:S(2)}) collective-permute-start(bf16[64,2048]{1,0:T(8,128)(2,1)S(1)} %add_convert_fusion.5), channel_id=1, source_target_pairs={{0,1},{1,2},{2,3},{3,4},{4,5},{5,6},{6,7},{7,0},{8,9},{9,10},{10,1... | collective-permute-start | bytes 786440 | tf_op jit(solution)/shard_map/ppermute | solution.py:43
  108.3 9.0 %collective-permute-start.20 = (bf16[64,2048]{1,0:T(8,128)(2,1)S(1)}, bf16[64,2048]{1,0:T(8,128)(2,1)S(1)}, u32[]{:S(2)}, u32[]{:S(2)}) collective-permute-start(bf16[64,2048]{1,0:T(8,128)(2,1)S(1)} %add_convert_fusion.2), channel_id=1, source_target_pairs={{0,7},{1,0},{2,1},{3,2},{4,3},{5,4},{6,5},{7,6},{8,15},{9,8},{10,9... | collective-permute-start | bytes 786440 | tf_op jit(solution)/shard_map/ppermute | solution.py:43
  117.2 8.1 %collective-permute-start.17 = (bf16[64,2048]{1,0:T(8,128)(2,1)S(1)}, bf16[64,2048]{1,0:T(8,128)(2,1)S(1)}, u32[]{:S(2)}, u32[]{:S(2)}) collective-permute-start(bf16[64,2048]{1,0:T(8,128)(2,1)S(1)} %add_convert_fusion.4), channel_id=1, source_target_pairs={{0,1},{1,2},{2,3},{3,4},{4,5},{5,6},{6,7},{7,0},{8,9},{9,10},{10,1... | collective-permute-start | bytes 786440 | tf_op jit(solution)/shard_map/ppermute | solution.py:43
  118.1 8.1 %collective-permute-start.21 = (bf16[64,2048]{1,0:T(8,128)(2,1)S(1)}, bf16[64,2048]{1,0:T(8,128)(2,1)S(1)}, u32[]{:S(2)}, u32[]{:S(2)}) collective-permute-start(bf16[64,2048]{1,0:T(8,128)(2,1)S(1)} %add_convert_fusion.1), channel_id=1, source_target_pairs={{0,7},{1,0},{2,1},{3,2},{4,3},{5,4},{6,5},{7,6},{8,15},{9,8},{10,9... | collective-permute-start | bytes 786440 | tf_op jit(solution)/shard_map/ppermute | solution.py:43
  126.1 7.7 %collective-permute-start.18 = (bf16[64,2048]{1,0:T(8,128)(2,1)S(1)}, bf16[64,2048]{1,0:T(8,128)(2,1)S(1)}, u32[]{:S(2)}, u32[]{:S(2)}) collective-permute-start(bf16[64,2048]{1,0:T(8,128)(2,1)S(1)} %add_convert_fusion.3), channel_id=1, source_target_pairs={{0,1},{1,2},{2,3},{3,4},{4,5},{5,6},{6,7},{7,0},{8,9},{9,10},{10,1... | collective-permute-start | bytes 786440 | tf_op jit(solution)/shard_map/ppermute | solution.py:43
  127.0 7.2 %collective-permute-start.22 = (bf16[64,2048]{1,0:T(8,128)(2,1)S(1)}, bf16[64,2048]{1,0:T(8,128)(2,1)S(1)}, u32[]{:S(2)}, u32[]{:S(2)}) collective-permute-start(bf16[64,2048]{1,0:T(8,128)(2,1)S(1)} %add_convert_fusion), channel_id=1, source_target_pairs={{0,7},{1,0},{2,1},{3,2},{4,3},{5,4},{6,5},{7,6},{8,15},{9,8},{10,9... | collective-permute-start | bytes 786440 | tf_op jit(solution)/shard_map/ppermute | solution.py:43
  134.3 5.6 %collective-permute-start.23 = (bf16[16,1024]{1,0:T(8,128)(2,1)S(1)}, bf16[16,1024]{1,0:T(8,128)(2,1)S(1)}, u32[]{:S(2)}, u32[]{:S(2)}) collective-permute-start(bf16[16,1024]{1,0:T(8,128)(2,1)S(1)} %get-tuple-element.13), channel_id=1, source_target_pairs={{0,8},{8,16},{16,24},{24,0},{1,9},{9,17},{17,25},{25,1},{2,10},{10... | collective-permute-start | bytes 98312 | tf_op jit(solution)/shard_map/ppermute | solution.py:43
  134.4 5.5 %collective-permute-start.25 = (bf16[16,1024]{1,0:T(8,128)(2,1)S(1)}, bf16[16,1024]{1,0:T(8,128)(2,1)S(1)}, u32[]{:S(2)}, u32[]{:S(2)}) collective-permute-start(bf16[16,1024]{1,0:T(8,128)(2,1)S(1)} %get-tuple-element.14), channel_id=1, source_target_pairs={{0,24},{8,0},{16,8},{24,16},{1,25},{9,1},{17,9},{25,17},{2,26},{10... | collective-permute-start | bytes 98312 | tf_op jit(solution)/shard_map/ppermute | solution.py:43
  139.8 5.6 %collective-permute-start.24 = (bf16[16,2048]{1,0:T(8,128)(2,1)S(1)}, bf16[16,2048]{1,0:T(8,128)(2,1)S(1)}, u32[]{:S(2)}, u32[]{:S(2)}) collective-permute-start(bf16[16,2048]{1,0:T(8,128)(2,1)S(1)} %get-tuple-element.7), channel_id=1, source_target_pairs={{0,8},{8,16},{16,24},{24,0},{1,9},{9,17},{17,25},{25,1},{2,10},{10... | collective-permute-start | bytes 196616 | tf_op jit(solution)/shard_map/ppermute | solution.py:43
  139.9 5.5 %collective-permute-start.26 = (bf16[16,2048]{1,0:T(8,128)(2,1)S(1)}, bf16[16,2048]{1,0:T(8,128)(2,1)S(1)}, u32[]{:S(2)}, u32[]{:S(2)}) collective-permute-start(bf16[16,2048]{1,0:T(8,128)(2,1)S(1)} %get-tuple-element.8), channel_id=1, source_target_pairs={{0,24},{8,0},{16,8},{24,16},{1,25},{9,1},{17,9},{25,17},{2,26},{10... | collective-permute-start | bytes 196616 | tf_op jit(solution)/shard_map/ppermute | solution.py:43

commit v17 on v12

--- a/solution.py
+++ b/solution.py
@@ -15,14 +15,14 @@
     out = jnp.zeros((n,) + own.shape, own.dtype)
     put = lambda out, v, i: lax.dynamic_update_index_in_dim(out, f(v), i % n, 0)
     out = lax.dynamic_update_index_in_dim(out, own, k, 0)
-    buf = x
+    buf_f = buf_b = x
     for s in range(nf):
-        buf = lax.ppermute(buf, axis, fwd)
-        out = put(out, buf, k - 1 - s)
-    buf = x
-    for s in range(n - 1 - nf):
-        buf = lax.ppermute(buf, axis, bwd)
-        out = put(out, buf, k + 1 + s)
+        if s < n - 1 - nf:
+            buf_b = lax.ppermute(buf_b, axis, bwd)
+        buf_f = lax.ppermute(buf_f, axis, fwd)
+        if s < n - 1 - nf:
+            out = put(out, buf_b, k + 1 + s)
+        out = put(out, buf_f, k - 1 - s)
     return out.reshape((n * own.shape[0],) + own.shape[1:])
 
 

time: 145 us -> 156 us (1.076)
  waiting for transfers between devices: 56.6 us -> 71.2 us
  starting transfers between devices: 41.8 us -> 38.3 us
    ppermute x10, waiting for transfers between devices: 16.4 us -> 31 us  [the longest x6 22.6 us: ring_ag(): buf_f = lax.ppermute(buf_f, axis, fwd)]
    ppermute x10, starting transfers between devices: 17.1 us -> 13.6 us  [the longest x4 12.5 us: ring_ag(): buf_b = lax.ppermute(buf_b, axis, bwd)]
  transfers between devices with their start and end apart: 27 -> 27, of which waited for: 20 -> 21; matrix products, arithmetic and copies ran while one was open for 13% -> 10% of each run, Pallas kernels for 0% -> 0%
where the time goes in v17:
time: 156 us; the launch traced here: 155 us
  waiting for transfers between devices  71.2 us (46%)
  starting transfers between devices  38.3 us (25%)
  matrix products  22.2 us (14%)
  blocking collectives  14.4 us (9%)
  other arithmetic  4.5 us (3%)
  local copies, waits for them, and re-layouts  4.2 us (3%)
    ppermute x16, waiting for transfers between devices, side(): got = lax.ppermute(acc.astype(send_dtype), axis, perm).astype(jnp.float32)  36.3 us
    ppermute x16, starting transfers between devices, side(): got = lax.ppermute(acc.astype(send_dtype), axis, perm).astype(jnp.float32)  24.6 us
    ppermute x6, waiting for transfers between devices, ring_ag(): buf_f = lax.ppermute(buf_f, axis, fwd)  22.6 us
    all_gather x1, blocking collectives, on_device(): activated = lax.all_gather(activated, EMBED, axis=0, tiled=True)  14.4 us
    ppermute x4, starting transfers between devices, ring_ag(): buf_b = lax.ppermute(buf_b, axis, bwd)  12.5 us
    dot_general x9, matrix products, on_device(): jnp.dot(lax.dynamic_index_in_dim(act_blocks, i, 0, keepdims=False), down_...  8.9 us
    ppermute x4, waiting for transfers between devices, ring_ag(): buf_b = lax.ppermute(buf_b, axis, bwd)  8.46 us
    dot_general x8, matrix products, on_device(): jnp.dot(v, gate_weight, preferred_element_type=jnp.float32)  7.65 us
  transfers between devices with their start and end apart: 27, of which 21 were waited for; matrix products, arithmetic and copies ran while one was open for 10% of the time, Pallas kernels for 0%

profile of v17, /device:TPU:2, one launch (start us, length us, event | category | flops | bytes accessed | tf_op | source)
XLA Modules:
  0.0 155.3 jit_solution(6271615242214060387)
XLA Ops:
  0.0 3.0 %collective-permute-start = (bf16[16,2048]{1,0:T(8,128)(2,1)}, bf16[16,2048]{1,0:T(8,128)(2,1)S(1)}, u32[]{:S(2)}, u32[]{:S(2)}) collective-permute-start(bf16[16,2048]{1,0:T(8,128)(2,1)} %param.4), channel_id=1, source_target_pairs={{0,24},{8,0},{16,8},{24,16},{1,25},{9,1},{17,9},{25,17},{2,26},{10... | collective-permute-start | bytes 196616 | tf_op jit(solution)/shard_map/ppermute | solution.py:21
  3.0 0.9 bitcast_dynamic-update-slice_fusion.3
  3.9 4.8 %collective-permute-done.1 = bf16[16,2048]{1,0:T(8,128)(2,1)S(1)} collective-permute-done((bf16[16,2048]{1,0:T(8,128)(2,1)}, bf16[16,2048]{1,0:T(8,128)(2,1)S(1)}, u32[]{:S(2)}, u32[]{:S(2)}) %collective-permute-start.1) | collective-permute-done | bytes 65568 | tf_op jit(solution)/shard_map/ppermute | solution.py:22
  8.7 5.4 %collective-permute-done.2 = bf16[16,2048]{1,0:T(8,128)(2,1)S(1)} collective-permute-done((bf16[16,2048]{1,0:T(8,128)(2,1)S(1)}, bf16[16,2048]{1,0:T(8,128)(2,1)S(1)}, u32[]{:S(2)}, u32[]{:S(2)}) %collective-permute-start.2) | collective-permute-done | bytes 65568 | tf_op jit(solution)/shard_map/ppermute | solution.py:22
  14.2 5.9 %collective-permute-start.3 = (bf16[64,2048]{1,0:T(8,128)(2,1)S(1)}, bf16[64,2048]{1,0:T(8,128)(2,1)S(1)}, u32[]{:S(2)}, u32[]{:S(2)}) collective-permute-start(bf16[64,2048]{1,0:T(8,128)(2,1)S(1)} %bitcast.169), channel_id=1, source_target_pairs={{0,7},{1,0},{2,1},{3,2},{4,3},{5,4},{6,5},{7,6},{8,15},{9,8},{10,9... | collective-permute-start | bytes 786440 | tf_op jit(solution)/shard_map/ppermute | solution.py:21
  20.1 2.7 %fusion.64 = f32[64,896]{1,0:T(8,128)S(1)} fusion(bf16[64,2048]{1,0:T(8,128)(2,1)S(1)} %bitcast.171, bf16[2048,896]{1,0:T(8,128)(2,1)} %param.5), kind=kOutput, calls=%fused_computation.86 | convolution fusion | flops 234881024 | bytes 4161536 | tf_op jit(solution)/shard_map/dot_general | solution.py:86
  22.9 0.7 fusion.65
  24.0 0.9 copy-done.1
  24.9 0.7 fusion.66
  25.6 0.7 fusion.67
  26.3 1.4 collective-permute-done.4
  27.7 0.7 fusion.68
  28.4 0.7 fusion.69
  29.1 1.9 %collective-permute-start.5 = (bf16[64,2048]{1,0:T(8,128)(2,1)S(1)}, bf16[64,2048]{1,0:T(8,128)(2,1)S(1)}, u32[]{:S(2)}, u32[]{:S(2)}) collective-permute-start(bf16[64,2048]{1,0:T(8,128)(2,1)S(1)} %collective-permute-done.3), channel_id=1, source_target_pairs={{0,7},{1,0},{2,1},{3,2},{4,3},{5,4},{6,5},{7,6},{8,15},{9,8},{10,9... | collective-permute-start | bytes 786440 | tf_op jit(solution)/shard_map/ppermute | solution.py:21
  31.4 4.2 %collective-permute-done.5 = bf16[64,2048]{1,0:T(8,128)(2,1)S(1)} collective-permute-done((bf16[64,2048]{1,0:T(8,128)(2,1)S(1)}, bf16[64,2048]{1,0:T(8,128)(2,1)S(1)}, u32[]{:S(2)}, u32[]{:S(2)}) %collective-permute-start.5) | collective-permute-done | bytes 262176 | tf_op jit(solution)/shard_map/ppermute | solution.py:21
  35.6 0.7 fusion.70
  36.3 0.7 fusion.71
  37.0 1.8 %collective-permute-done.6 = bf16[64,2048]{1,0:T(8,128)(2,1)S(1)} collective-permute-done((bf16[64,2048]{1,0:T(8,128)(2,1)S(1)}, bf16[64,2048]{1,0:T(8,128)(2,1)S(1)}, u32[]{:S(2)}, u32[]{:S(2)}) %collective-permute-start.6) | collective-permute-done | bytes 262176 | tf_op jit(solution)/shard_map/ppermute | solution.py:22
  38.8 0.7 fusion.72
  39.5 0.7 fusion.73
  40.2 1.6 %collective-permute-start.7 = (bf16[64,2048]{1,0:T(8,128)(2,1)S(1)}, bf16[64,2048]{1,0:T(8,128)(2,1)S(1)}, u32[]{:S(2)}, u32[]{:S(2)}) collective-permute-start(bf16[64,2048]{1,0:T(8,128)(2,1)S(1)} %collective-permute-done.5), channel_id=1, source_target_pairs={{0,7},{1,0},{2,1},{3,2},{4,3},{5,4},{6,5},{7,6},{8,15},{9,8},{10,9... | collective-permute-start | bytes 786440 | tf_op jit(solution)/shard_map/ppermute | solution.py:21
  41.8 0.8 collective-permute-start.8
  42.6 4.2 %collective-permute-done.7 = bf16[64,2048]{1,0:T(8,128)(2,1)S(1)} collective-permute-done((bf16[64,2048]{1,0:T(8,128)(2,1)S(1)}, bf16[64,2048]{1,0:T(8,128)(2,1)S(1)}, u32[]{:S(2)}, u32[]{:S(2)}) %collective-permute-start.7) | collective-permute-done | bytes 262176 | tf_op jit(solution)/shard_map/ppermute | solution.py:21
  46.8 0.7 fusion.74
  47.5 0.7 fusion.75
  48.2 1.7 %collective-permute-done.8 = bf16[64,2048]{1,0:T(8,128)(2,1)S(1)} collective-permute-done((bf16[64,2048]{1,0:T(8,128)(2,1)S(1)}, bf16[64,2048]{1,0:T(8,128)(2,1)S(1)}, u32[]{:S(2)}, u32[]{:S(2)}) %collective-permute-start.8) | collective-permute-done | bytes 262176 | tf_op jit(solution)/shard_map/ppermute | solution.py:22
  50.0 0.7 fusion.76
  50.7 0.7 fusion.77
  51.6 7.5 %collective-permute-done.9 = bf16[64,2048]{1,0:T(8,128)(2,1)S(1)} collective-permute-done((bf16[64,2048]{1,0:T(8,128)(2,1)S(1)}, bf16[64,2048]{1,0:T(8,128)(2,1)S(1)}, u32[]{:S(2)}, u32[]{:S(2)}) %collective-permute-start.9) | collective-permute-done | bytes 262176 | tf_op jit(solution)/shard_map/ppermute | solution.py:22
  59.1 0.7 fusion.78
  59.8 0.7 fusion.79
  60.5 1.8 %copy-done.3 = f32[8,64,1792]{2,1,0:T(8,128)} copy-done((f32[8,64,1792]{2,1,0:T(8,128)}, f32[8,64,1792]{2,1,0:T(8,128)S(1)}, u32[]{:S(2)}) %copy-start.3) | copy-done | bytes 3670040
  62.6 3.9 %collective-permute-done.10 = f32[4,64,1792]{2,1,0:T(8,128)} collective-permute-done((f32[4,64,1792]{2,1,0:T(8,128)S(1)}, f32[4,64,1792]{2,1,0:T(8,128)}, u32[]{:S(2)}, u32[]{:S(2)}) %collective-permute-start.10) | collective-permute-done | bytes 1835040 | tf_op jit(solution)/shard_map/ppermute | solution.py:69
  66.4 2.2 %bitcast_add_fusion = f32[4,64,1792]{2,1,0:T(8,128)S(1)} fusion(f32[4,64,1792]{2,1,0:T(8,128)} %collective-permute-done.10, f32[4,2,64,1792]{3,2,1,0:T(8,128)} %bitcast.159, s32[]{:T(128)S(6)} %select_n.206), kind=kLoop, calls=%fused_computation | loop fusion | flops 458752 | bytes 5505028 | tf_op jit(solution)/shard_map/add | solution.py:70
  68.8 1.6 %collective-permute-start.11 = (f32[64,896]{1,0:T(8,128)S(1)}, f32[64,896]{1,0:T(8,128)S(1)}, u32[]{:S(2)}, u32[]{:S(2)}) collective-permute-start(f32[64,896]{1,0:T(8,128)S(1)} %slice.36), channel_id=1, source_target_pairs={{0,64},{64,128},{128,192},{192,0},{1,65},{65,129},{129,193},{193,1... | collective-permute-start | bytes 688136 | tf_op jit(solution)/shard_map/ppermute | solution.py:42
  71.0 5.5 %collective-permute-done.11 = f32[64,896]{1,0:T(8,128)S(1)} collective-permute-done((f32[64,896]{1,0:T(8,128)S(1)}, f32[64,896]{1,0:T(8,128)S(1)}, u32[]{:S(2)}, u32[]{:S(2)}) %collective-permute-start.11) | collective-permute-done | bytes 229408 | tf_op jit(solution)/shard_map/ppermute | solution.py:42
  76.5 1.3 collective-permute-done.13
  77.9 1.3 collective-permute-start.12
  79.2 0.8 collective-permute-start.14
  80.0 9.4 %collective-permute-done.12 = f32[64,1792]{1,0:T(8,128)S(1)} collective-permute-done((f32[64,1792]{1,0:T(8,128)S(1)}, f32[64,1792]{1,0:T(8,128)S(1)}, u32[]{:S(2)}, u32[]{:S(2)}) %collective-permute-start.12) | collective-permute-done | bytes 458784 | tf_op jit(solution)/shard_map/ppermute | solution.py:42
  89.4 1.0 collective-permute-done.14
  90.4 1.1 fusion.8
  91.6 14.4 %all_gather.3 = bf16[512,896]{1,0:T(8,128)(2,1)S(1)} all-gather(bf16[64,896]{1,0:T(8,128)(2,1)S(1)} %fusion.9), channel_id=1, replica_groups=mesh['ex'=4,'ec'=2,'hy'=4,'hz'=8] {'ex','ec'}, dimensions={0}, use_global_device_ids=true | all-gather | bytes 1032192 | tf_op jit(solution)/shard_map/all_gather | solution.py:94
  106.0 2.8 %fusion.24 = bf16[64,2048]{1,0:T(8,128)(2,1)S(1)} fusion(bf16[896,2048]{1,0:T(8,128)(2,1)} %param.7, bf16[8,64,896]{2,1,0:T(8,128)(2,1)S(1)} %bitcast.160, s32[]{:T(128)S(6)} %select_n.221), kind=kOutput, calls=%fused_computation.52 | convolution fusion | flops 234881024 | bytes 4046852 | tf_op jit(solution)/shard_map/dot_general | solution.py:96
  108.9 0.8 fusion.14
  109.7 3.5 %collective-permute-start.19 = (bf16[64,1024]{1,0:T(8,128)(2,1)S(1)}, bf16[64,1024]{1,0:T(8,128)(2,1)S(1)}, u32[]{:S(2)}, u32[]{:S(2)}) collective-permute-start(bf16[64,1024]{1,0:T(8,128)(2,1)S(1)} %slice.50), channel_id=1, source_target_pairs={{0,7},{1,0},{2,1},{3,2},{4,3},{5,4},{6,5},{7,6},{8,15},{9,8},{10,9... | collective-permute-start | bytes 393224 | tf_op jit(solution)/shard_map/ppermute | solution.py:42
  113.2 2.6 %collective-permute-done.15 = bf16[64,1024]{1,0:T(8,128)(2,1)S(1)} collective-permute-done((bf16[64,1024]{1,0:T(8,128)(2,1)S(1)}, bf16[64,1024]{1,0:T(8,128)(2,1)S(1)}, u32[]{:S(2)}, u32[]{:S(2)}) %collective-permute-start.15) | collective-permute-done | bytes 131104 | tf_op jit(solution)/shard_map/ppermute | solution.py:42
  115.8 0.8 add_convert_fusion.5
  116.7 0.8 add_convert_fusion.2
  117.5 3.3 %collective-permute-start.20 = (bf16[64,2048]{1,0:T(8,128)(2,1)S(1)}, bf16[64,2048]{1,0:T(8,128)(2,1)S(1)}, u32[]{:S(2)}, u32[]{:S(2)}) collective-permute-start(bf16[64,2048]{1,0:T(8,128)(2,1)S(1)} %add_convert_fusion.2), channel_id=1, source_target_pairs={{0,7},{1,0},{2,1},{3,2},{4,3},{5,4},{6,5},{7,6},{8,15},{9,8},{10,9... | collective-permute-start | bytes 786440 | tf_op jit(solution)/shard_map/ppermute | solution.py:42
  120.8 4.9 %collective-permute-done.16 = bf16[64,2048]{1,0:T(8,128)(2,1)S(1)} collective-permute-done((bf16[64,2048]{1,0:T(8,128)(2,1)S(1)}, bf16[64,2048]{1,0:T(8,128)(2,1)S(1)}, u32[]{:S(2)}, u32[]{:S(2)}) %collective-permute-start.16) | collective-permute-done | bytes 262176 | tf_op jit(solution)/shard_map/ppermute | solution.py:42
  125.6 0.8 add_convert_fusion.4
  126.5 0.8 add_convert_fusion.1
  127.3 3.3 %collective-permute-start.21 = (bf16[64,2048]{1,0:T(8,128)(2,1)S(1)}, bf16[64,2048]{1,0:T(8,128)(2,1)S(1)}, u32[]{:S(2)}, u32[]{:S(2)}) collective-permute-start(bf16[64,2048]{1,0:T(8,128)(2,1)S(1)} %add_convert_fusion.1), channel_id=1, source_target_pairs={{0,7},{1,0},{2,1},{3,2},{4,3},{5,4},{6,5},{7,6},{8,15},{9,8},{10,9... | collective-permute-start | bytes 786440 | tf_op jit(solution)/shard_map/ppermute | solution.py:42
  130.6 4.0 %collective-permute-done.17 = bf16[64,2048]{1,0:T(8,128)(2,1)S(1)} collective-permute-done((bf16[64,2048]{1,0:T(8,128)(2,1)S(1)}, bf16[64,2048]{1,0:T(8,128)(2,1)S(1)}, u32[]{:S(2)}, u32[]{:S(2)}) %collective-permute-start.17) | collective-permute-done | bytes 262176 | tf_op jit(solution)/shard_map/ppermute | solution.py:42
  134.5 0.8 add_convert_fusion.3
  135.4 0.8 add_convert_fusion
  136.2 3.3 %collective-permute-start.22 = (bf16[64,2048]{1,0:T(8,128)(2,1)S(1)}, bf16[64,2048]{1,0:T(8,128)(2,1)S(1)}, u32[]{:S(2)}, u32[]{:S(2)}) collective-permute-start(bf16[64,2048]{1,0:T(8,128)(2,1)S(1)} %add_convert_fusion), channel_id=1, source_target_pairs={{0,7},{1,0},{2,1},{3,2},{4,3},{5,4},{6,5},{7,6},{8,15},{9,8},{10,9... | collective-permute-start | bytes 786440 | tf_op jit(solution)/shard_map/ppermute | solution.py:42
  139.5 0.8 fusion.34
  140.2 2.7 %collective-permute-done.18 = bf16[64,2048]{1,0:T(8,128)(2,1)S(1)} collective-permute-done((bf16[64,2048]{1,0:T(8,128)(2,1)S(1)}, bf16[64,2048]{1,0:T(8,128)(2,1)S(1)}, u32[]{:S(2)}, u32[]{:S(2)}) %collective-permute-start.18) | collective-permute-done | bytes 262176 | tf_op jit(solution)/shard_map/ppermute | solution.py:42
  143.6 3.2 %collective-permute-start.25 = (bf16[16,1024]{1,0:T(8,128)(2,1)S(1)}, bf16[16,1024]{1,0:T(8,128)(2,1)S(1)}, u32[]{:S(2)}, u32[]{:S(2)}) collective-permute-start(bf16[16,1024]{1,0:T(8,128)(2,1)S(1)} %slice.43), channel_id=1, source_target_pairs={{0,24},{8,0},{16,8},{24,16},{1,25},{9,1},{17,9},{25,17},{2,26},{10... | collective-permute-start | bytes 98312 | tf_op jit(solution)/shard_map/ppermute | solution.py:42
  146.8 2.2 %collective-permute-done.23 = bf16[16,1024]{1,0:T(8,128)(2,1)S(1)} collective-permute-done((bf16[16,1024]{1,0:T(8,128)(2,1)S(1)}, bf16[16,1024]{1,0:T(8,128)(2,1)S(1)}, u32[]{:S(2)}, u32[]{:S(2)}) %collective-permute-start.23) | collective-permute-done | bytes 32800 | tf_op jit(solution)/shard_map/ppermute | solution.py:42
  149.1 3.2 %collective-permute-start.26 = (bf16[16,2048]{1,0:T(8,128)(2,1)S(1)}, bf16[16,2048]{1,0:T(8,128)(2,1)S(1)}, u32[]{:S(2)}, u32[]{:S(2)}) collective-permute-start(bf16[16,2048]{1,0:T(8,128)(2,1)S(1)} %get-tuple-element.10), channel_id=1, source_target_pairs={{0,24},{8,0},{16,8},{24,16},{1,25},{9,1},{17,9},{25,17},{2,26},{10... | collective-permute-start | bytes 196616 | tf_op jit(solution)/shard_map/ppermute | solution.py:42
  152.4 2.2 %collective-permute-done.24 = bf16[16,2048]{1,0:T(8,128)(2,1)S(1)} collective-permute-done((bf16[16,2048]{1,0:T(8,128)(2,1)S(1)}, bf16[16,2048]{1,0:T(8,128)(2,1)S(1)}, u32[]{:S(2)}, u32[]{:S(2)}) %collective-permute-start.24) | collective-permute-done | bytes 65568 | tf_op jit(solution)/shard_map/ppermute | solution.py:42
  (54 shorter events, 3.8 us)
Async XLA Ops:
  0.0 8.7 %collective-permute-start = (bf16[16,2048]{1,0:T(8,128)(2,1)}, bf16[16,2048]{1,0:T(8,128)(2,1)S(1)}, u32[]{:S(2)}, u32[]{:S(2)}) collective-permute-start(bf16[16,2048]{1,0:T(8,128)(2,1)} %param.4), channel_id=1, source_target_pairs={{0,24},{8,0},{16,8},{24,16},{1,25},{9,1},{17,9},{25,17},{2,26},{10... | collective-permute-start | bytes 196616 | tf_op jit(solution)/shard_map/ppermute | solution.py:21
  3.0 5.7 %collective-permute-start.1 = (bf16[16,2048]{1,0:T(8,128)(2,1)}, bf16[16,2048]{1,0:T(8,128)(2,1)S(1)}, u32[]{:S(2)}, u32[]{:S(2)}) collective-permute-start(bf16[16,2048]{1,0:T(8,128)(2,1)} %param.4), channel_id=1, source_target_pairs={{0,8},{8,16},{16,24},{24,0},{1,9},{9,17},{17,25},{25,1},{2,10},{10... | collective-permute-start | bytes 196616 | tf_op jit(solution)/shard_map/ppermute | solution.py:22
  3.9 18.9 %copy-start.2 = (bf16[2048,896]{1,0:T(8,128)(2,1)S(1)}, bf16[2048,896]{1,0:T(8,128)(2,1)}, u32[]{:S(2)}) copy-start(bf16[2048,896]{1,0:T(8,128)(2,1)} %param.6) | copy-start | bytes 11010052
  8.7 5.5 %collective-permute-start.2 = (bf16[16,2048]{1,0:T(8,128)(2,1)S(1)}, bf16[16,2048]{1,0:T(8,128)(2,1)S(1)}, u32[]{:S(2)}, u32[]{:S(2)}) collective-permute-start(bf16[16,2048]{1,0:T(8,128)(2,1)S(1)} %collective-permute-done.1), channel_id=1, source_target_pairs={{0,8},{8,16},{16,24},{24,0},{1,9},{9,17},{17,25},{25,1},{2,10},{10... | collective-permute-start | bytes 196616 | tf_op jit(solution)/shard_map/ppermute | solution.py:22
  14.2 9.8 %collective-permute-start.3 = (bf16[64,2048]{1,0:T(8,128)(2,1)S(1)}, bf16[64,2048]{1,0:T(8,128)(2,1)S(1)}, u32[]{:S(2)}, u32[]{:S(2)}) collective-permute-start(bf16[64,2048]{1,0:T(8,128)(2,1)S(1)} %bitcast.169), channel_id=1, source_target_pairs={{0,7},{1,0},{2,1},{3,2},{4,3},{5,4},{6,5},{7,6},{8,15},{9,8},{10,9... | collective-permute-start | bytes 786440 | tf_op jit(solution)/shard_map/ppermute | solution.py:21
  20.1 7.6 %collective-permute-start.4 = (bf16[64,2048]{1,0:T(8,128)(2,1)S(1)}, bf16[64,2048]{1,0:T(8,128)(2,1)S(1)}, u32[]{:S(2)}, u32[]{:S(2)}) collective-permute-start(bf16[64,2048]{1,0:T(8,128)(2,1)S(1)} %bitcast.170), channel_id=1, source_target_pairs={{0,1},{1,2},{2,3},{3,4},{4,5},{5,6},{6,7},{7,0},{8,9},{9,10},{10,1... | collective-permute-start | bytes 786440 | tf_op jit(solution)/shard_map/ppermute | solution.py:22
  22.9 2.0 %copy-start.1 = (bf16[2048,896]{1,0:T(8,128)(2,1)S(1)}, bf16[2048,896]{1,0:T(8,128)(2,1)}, u32[]{:S(2)}) copy-start(bf16[2048,896]{1,0:T(8,128)(2,1)} %param.5) | copy-start | bytes 11010052
  29.1 6.5 %collective-permute-start.5 = (bf16[64,2048]{1,0:T(8,128)(2,1)S(1)}, bf16[64,2048]{1,0:T(8,128)(2,1)S(1)}, u32[]{:S(2)}, u32[]{:S(2)}) collective-permute-start(bf16[64,2048]{1,0:T(8,128)(2,1)S(1)} %collective-permute-done.3), channel_id=1, source_target_pairs={{0,7},{1,0},{2,1},{3,2},{4,3},{5,4},{6,5},{7,6},{8,15},{9,8},{10,9... | collective-permute-start | bytes 786440 | tf_op jit(solution)/shard_map/ppermute | solution.py:21
  31.1 7.7 %collective-permute-start.6 = (bf16[64,2048]{1,0:T(8,128)(2,1)S(1)}, bf16[64,2048]{1,0:T(8,128)(2,1)S(1)}, u32[]{:S(2)}, u32[]{:S(2)}) collective-permute-start(bf16[64,2048]{1,0:T(8,128)(2,1)S(1)} %collective-permute-done.4), channel_id=1, source_target_pairs={{0,1},{1,2},{2,3},{3,4},{4,5},{5,6},{6,7},{7,0},{8,9},{9,10},{10,1... | collective-permute-start | bytes 786440 | tf_op jit(solution)/shard_map/ppermute | solution.py:22
  40.2 6.6 %collective-permute-start.7 = (bf16[64,2048]{1,0:T(8,128)(2,1)S(1)}, bf16[64,2048]{1,0:T(8,128)(2,1)S(1)}, u32[]{:S(2)}, u32[]{:S(2)}) collective-permute-start(bf16[64,2048]{1,0:T(8,128)(2,1)S(1)} %collective-permute-done.5), channel_id=1, source_target_pairs={{0,7},{1,0},{2,1},{3,2},{4,3},{5,4},{6,5},{7,6},{8,15},{9,8},{10,9... | collective-permute-start | bytes 786440 | tf_op jit(solution)/shard_map/ppermute | solution.py:21
  41.8 8.2 %collective-permute-start.8 = (bf16[64,2048]{1,0:T(8,128)(2,1)S(1)}, bf16[64,2048]{1,0:T(8,128)(2,1)S(1)}, u32[]{:S(2)}, u32[]{:S(2)}) collective-permute-start(bf16[64,2048]{1,0:T(8,128)(2,1)S(1)} %collective-permute-done.6), channel_id=1, source_target_pairs={{0,1},{1,2},{2,3},{3,4},{4,5},{5,6},{6,7},{7,0},{8,9},{9,10},{10,1... | collective-permute-start | bytes 786440 | tf_op jit(solution)/shard_map/ppermute | solution.py:22
  51.4 7.7 %collective-permute-start.9 = (bf16[64,2048]{1,0:T(8,128)(2,1)S(1)}, bf16[64,2048]{1,0:T(8,128)(2,1)S(1)}, u32[]{:S(2)}, u32[]{:S(2)}) collective-permute-start(bf16[64,2048]{1,0:T(8,128)(2,1)S(1)} %collective-permute-done.8), channel_id=1, source_target_pairs={{0,1},{1,2},{2,3},{3,4},{4,5},{5,6},{6,7},{7,0},{8,9},{9,10},{10,1... | collective-permute-start | bytes 786440 | tf_op jit(solution)/shard_map/ppermute | solution.py:22
  60.5 1.8 %copy-start.3 = (f32[8,64,1792]{2,1,0:T(8,128)}, f32[8,64,1792]{2,1,0:T(8,128)S(1)}, u32[]{:S(2)}) copy-start(f32[8,64,1792]{2,1,0:T(8,128)S(1)} %fusion.7) | copy-start | bytes 11010052
  62.4 4.0 %collective-permute-start.10 = (f32[4,64,1792]{2,1,0:T(8,128)S(1)}, f32[4,64,1792]{2,1,0:T(8,128)}, u32[]{:S(2)}, u32[]{:S(2)}) collective-permute-start(f32[4,64,1792]{2,1,0:T(8,128)S(1)} %dynamic-slice_bitcast_fusion), channel_id=1, source_target_pairs={{0,32},{32,0},{1,33},{33,1},{2,34},{34,2},{3,35},{35,3},{4,36},{36... | collective-permute-start | bytes 5505032 | tf_op jit(solution)/shard_map/ppermute | solution.py:69
  68.8 7.7 %collective-permute-start.11 = (f32[64,896]{1,0:T(8,128)S(1)}, f32[64,896]{1,0:T(8,128)S(1)}, u32[]{:S(2)}, u32[]{:S(2)}) collective-permute-start(f32[64,896]{1,0:T(8,128)S(1)} %slice.36), channel_id=1, source_target_pairs={{0,64},{64,128},{128,192},{192,0},{1,65},{65,129},{129,193},{193,1... | collective-permute-start | bytes 688136 | tf_op jit(solution)/shard_map/ppermute | solution.py:42
  70.4 7.4 %collective-permute-start.13 = (f32[64,896]{1,0:T(8,128)S(1)}, f32[64,896]{1,0:T(8,128)S(1)}, u32[]{:S(2)}, u32[]{:S(2)}) collective-permute-start(f32[64,896]{1,0:T(8,128)S(1)} %slice.37), channel_id=1, source_target_pairs={{0,192},{64,0},{128,64},{192,128},{1,193},{65,1},{129,65},{193,129... | collective-permute-start | bytes 688136 | tf_op jit(solution)/shard_map/ppermute | solution.py:42
  77.9 11.5 %collective-permute-start.12 = (f32[64,1792]{1,0:T(8,128)S(1)}, f32[64,1792]{1,0:T(8,128)S(1)}, u32[]{:S(2)}, u32[]{:S(2)}) collective-permute-start(f32[64,1792]{1,0:T(8,128)S(1)} %get-tuple-element.5), channel_id=1, source_target_pairs={{0,64},{64,128},{128,192},{192,0},{1,65},{65,129},{129,193},{193,1... | collective-permute-start | bytes 1376264 | tf_op jit(solution)/shard_map/ppermute | solution.py:42
  79.2 11.2 %collective-permute-start.14 = (f32[64,1792]{1,0:T(8,128)S(1)}, f32[64,1792]{1,0:T(8,128)}, u32[]{:S(2)}, u32[]{:S(2)}) collective-permute-start(f32[64,1792]{1,0:T(8,128)S(1)} %get-tuple-element.6), channel_id=1, source_target_pairs={{0,192},{64,0},{128,64},{192,128},{1,193},{65,1},{129,65},{193,129... | collective-permute-start | bytes 1376264 | tf_op jit(solution)/shard_map/ppermute | solution.py:42
  80.0 28.9 %copy-start = (bf16[896,2048]{1,0:T(8,128)(2,1)S(1)}, bf16[896,2048]{1,0:T(8,128)(2,1)}, u32[]{:S(2)}) copy-start(bf16[896,2048]{1,0:T(8,128)(2,1)} %param.7) | copy-start | bytes 11010052
  108.8 7.0 %collective-permute-start.15 = (bf16[64,1024]{1,0:T(8,128)(2,1)S(1)}, bf16[64,1024]{1,0:T(8,128)(2,1)S(1)}, u32[]{:S(2)}, u32[]{:S(2)}) collective-permute-start(bf16[64,1024]{1,0:T(8,128)(2,1)S(1)} %slice.51), channel_id=1, source_target_pairs={{0,1},{1,2},{2,3},{3,4},{4,5},{5,6},{6,7},{7,0},{8,9},{9,10},{10,1... | collective-permute-start | bytes 393224 | tf_op jit(solution)/shard_map/ppermute | solution.py:42
  109.7 7.0 %collective-permute-start.19 = (bf16[64,1024]{1,0:T(8,128)(2,1)S(1)}, bf16[64,1024]{1,0:T(8,128)(2,1)S(1)}, u32[]{:S(2)}, u32[]{:S(2)}) collective-permute-start(bf16[64,1024]{1,0:T(8,128)(2,1)S(1)} %slice.50), channel_id=1, source_target_pairs={{0,7},{1,0},{2,1},{3,2},{4,3},{5,4},{6,5},{7,6},{8,15},{9,8},{10,9... | collective-permute-start | bytes 393224 | tf_op jit(solution)/shard_map/ppermute | solution.py:42
  116.6 9.0 %collective-permute-start.16 = (bf16[64,2048]{1,0:T(8,128)(2,1)S(1)}, bf16[64,2048]{1,0:T(8,128)(2,1)S(1)}, u32[]{:S(2)}, u32[]{:S(2)}) collective-permute-start(bf16[64,2048]{1,0:T(8,128)(2,1)S(1)} %add_convert_fusion.5), channel_id=1, source_target_pairs={{0,1},{1,2},{2,3},{3,4},{4,5},{5,6},{6,7},{7,0},{8,9},{9,10},{10,1... | collective-permute-start | bytes 786440 | tf_op jit(solution)/shard_map/ppermute | solution.py:42
  117.5 9.0 %collective-permute-start.20 = (bf16[64,2048]{1,0:T(8,128)(2,1)S(1)}, bf16[64,2048]{1,0:T(8,128)(2,1)S(1)}, u32[]{:S(2)}, u32[]{:S(2)}) collective-permute-start(bf16[64,2048]{1,0:T(8,128)(2,1)S(1)} %add_convert_fusion.2), channel_id=1, source_target_pairs={{0,7},{1,0},{2,1},{3,2},{4,3},{5,4},{6,5},{7,6},{8,15},{9,8},{10,9... | collective-permute-start | bytes 786440 | tf_op jit(solution)/shard_map/ppermute | solution.py:42
  126.4 8.1 %collective-permute-start.17 = (bf16[64,2048]{1,0:T(8,128)(2,1)S(1)}, bf16[64,2048]{1,0:T(8,128)(2,1)S(1)}, u32[]{:S(2)}, u32[]{:S(2)}) collective-permute-start(bf16[64,2048]{1,0:T(8,128)(2,1)S(1)} %add_convert_fusion.4), channel_id=1, source_target_pairs={{0,1},{1,2},{2,3},{3,4},{4,5},{5,6},{6,7},{7,0},{8,9},{9,10},{10,1... | collective-permute-start | bytes 786440 | tf_op jit(solution)/shard_map/ppermute | solution.py:42
  127.3 8.1 %collective-permute-start.21 = (bf16[64,2048]{1,0:T(8,128)(2,1)S(1)}, bf16[64,2048]{1,0:T(8,128)(2,1)S(1)}, u32[]{:S(2)}, u32[]{:S(2)}) collective-permute-start(bf16[64,2048]{1,0:T(8,128)(2,1)S(1)} %add_convert_fusion.1), channel_id=1, source_target_pairs={{0,7},{1,0},{2,1},{3,2},{4,3},{5,4},{6,5},{7,6},{8,15},{9,8},{10,9... | collective-permute-start | bytes 786440 | tf_op jit(solution)/shard_map/ppermute | solution.py:42
  135.3 7.7 %collective-permute-start.18 = (bf16[64,2048]{1,0:T(8,128)(2,1)S(1)}, bf16[64,2048]{1,0:T(8,128)(2,1)S(1)}, u32[]{:S(2)}, u32[]{:S(2)}) collective-permute-start(bf16[64,2048]{1,0:T(8,128)(2,1)S(1)} %add_convert_fusion.3), channel_id=1, source_target_pairs={{0,1},{1,2},{2,3},{3,4},{4,5},{5,6},{6,7},{7,0},{8,9},{9,10},{10,1... | collective-permute-start | bytes 786440 | tf_op jit(solution)/shard_map/ppermute | solution.py:42
  136.2 7.2 %collective-permute-start.22 = (bf16[64,2048]{1,0:T(8,128)(2,1)S(1)}, bf16[64,2048]{1,0:T(8,128)(2,1)S(1)}, u32[]{:S(2)}, u32[]{:S(2)}) collective-permute-start(bf16[64,2048]{1,0:T(8,128)(2,1)S(1)} %add_convert_fusion), channel_id=1, source_target_pairs={{0,7},{1,0},{2,1},{3,2},{4,3},{5,4},{6,5},{7,6},{8,15},{9,8},{10,9... | collective-permute-start | bytes 786440 | tf_op jit(solution)/shard_map/ppermute | solution.py:42
  143.5 5.5 %collective-permute-start.23 = (bf16[16,1024]{1,0:T(8,128)(2,1)S(1)}, bf16[16,1024]{1,0:T(8,128)(2,1)S(1)}, u32[]{:S(2)}, u32[]{:S(2)}) collective-permute-start(bf16[16,1024]{1,0:T(8,128)(2,1)S(1)} %slice.42), channel_id=1, source_target_pairs={{0,8},{8,16},{16,24},{24,0},{1,9},{9,17},{17,25},{25,1},{2,10},{10... | collective-permute-start | bytes 98312 | tf_op jit(solution)/shard_map/ppermute | solution.py:42
  143.6 5.4 %collective-permute-start.25 = (bf16[16,1024]{1,0:T(8,128)(2,1)S(1)}, bf16[16,1024]{1,0:T(8,128)(2,1)S(1)}, u32[]{:S(2)}, u32[]{:S(2)}) collective-permute-start(bf16[16,1024]{1,0:T(8,128)(2,1)S(1)} %slice.43), channel_id=1, source_target_pairs={{0,24},{8,0},{16,8},{24,16},{1,25},{9,1},{17,9},{25,17},{2,26},{10... | collective-permute-start | bytes 98312 | tf_op jit(solution)/shard_map/ppermute | solution.py:42
  149.1 5.6 %collective-permute-start.24 = (bf16[16,2048]{1,0:T(8,128)(2,1)S(1)}, bf16[16,2048]{1,0:T(8,128)(2,1)S(1)}, u32[]{:S(2)}, u32[]{:S(2)}) collective-permute-start(bf16[16,2048]{1,0:T(8,128)(2,1)S(1)} %get-tuple-element.9), channel_id=1, source_target_pairs={{0,8},{8,16},{16,24},{24,0},{1,9},{9,17},{17,25},{25,1},{2,10},{10... | collective-permute-start | bytes 196616 | tf_op jit(solution)/shard_map/ppermute | solution.py:42
  149.1 5.5 %collective-permute-start.26 = (bf16[16,2048]{1,0:T(8,128)(2,1)S(1)}, bf16[16,2048]{1,0:T(8,128)(2,1)S(1)}, u32[]{:S(2)}, u32[]{:S(2)}) collective-permute-start(bf16[16,2048]{1,0:T(8,128)(2,1)S(1)} %get-tuple-element.10), channel_id=1, source_target_pairs={{0,24},{8,0},{16,8},{24,16},{1,25},{9,1},{17,9},{25,17},{2,26},{10... | collective-permute-start | bytes 196616 | tf_op jit(solution)/shard_map/ppermute | solution.py:42
